TPU v7x, 32 devices: a whole 2x2x4 slice. The times are simulated.
32 devices in a mesh: row: 8 (over y, x, core), col: 4 (over z).
Axes of the slice: x: 2, y: 2, z: 4, core: 2. Of those that a mesh axis runs over, the one named last changes fastest.
Arguments:
- a_blocks: bfloat16 [8, 4, 16, 128, 128], P('row', 'col'), may hold values from -6 to 6
- b_blocks: bfloat16 [8, 4, 16, 128, 128], P('row', 'col'), may hold values from -0.21875 to 0.21875
- a_send: int32 [8, 4, 4, 4], P('row', 'col'), may hold values from -1 to 15, as said below
- b_send: int32 [8, 4, 8, 2], P('row', 'col'), may hold values from -1 to 15, as said below
- triples: int32 [8, 4, 4, 3, 384], P('row', 'col'), may hold values from -1 to 15, as said below
- c_send: int32 [8, 4, 32], P('row', 'col'), may hold values from -1 to 15, as said below
Outputs:
- returned: bfloat16 [8, 4, 32, 128, 128], P('row', 'col')
Inputs may be any that keep to these rules, and one draw needn't show every extreme that they name: In a_send[r, j], every block 0 to 15 appears exactly once; in every grid row one owner column receives 4 blocks from every column, which one is drawn. In b_send[i, c], every block 0 to 15 appears exactly once; in every grid column one owner row receives 2 blocks from every row, which one is drawn. Left slots are below 16, right slots below 16, result blocks below 16; live triples name panel slots that hold a stored block wherever the panel meeting there holds any; in each stack the live triples come first, or all three entries are -1; each stack holds 192 to 384 live triples, and at every stop some device holds 384. `c_send`: each device returns each of its 16 result blocks to exactly one device; one drawn device receives a block from every device.
All inputs are finite; a program needn't handle non-finite values.
Results may differ from a plain program's by a relative error of at most 0.0049.
Values may be sent and summed in bfloat16 or wider, within the bound.
No kernel may reach another device: no remote copies, remote signals or barrier semaphores. Data moves between devices by JAX's collectives and lax.ppermute only.
A program may use at most 64 MiB of HBM per device.

v0:
```python
import functools

import jax
import jax.numpy as jnp
from jax import lax
from jax.experimental import pallas as pl
from jax.experimental.pallas import tpu as pltpu
from jax.sharding import PartitionSpec as P

STOPS = 4


def passed_along(value, axis, steps):
    count = lax.axis_size(axis)
    pairs = [(source, (source + steps) % count) for source in range(count)]
    return lax.ppermute(value, axis, pairs)


def bucketize(blocks, index):
    picked = jnp.take(blocks, jnp.maximum(index, 0), axis=0)
    return jnp.where((index >= 0)[..., None, None], picked, jnp.zeros_like(picked))


def sort_stack(stack, left_count, right_count, result_count):
    live = stack[0] >= 0
    target = jnp.clip(stack[2], 0, result_count - 1)
    keys = jnp.where(live, target, result_count)
    order = jnp.argsort(keys, stable=True)
    left_sorted = jnp.clip(jnp.take(stack[0], order), 0, left_count - 1)
    right_sorted = jnp.clip(jnp.take(stack[1], order), 0, right_count - 1)
    counts = jnp.sum(
        (keys[:, None] == jnp.arange(result_count, dtype=jnp.int32)[None, :]).astype(jnp.int32),
        axis=0,
    )
    offsets = jnp.concatenate([jnp.zeros((1,), jnp.int32), jnp.cumsum(counts).astype(jnp.int32)])
    return left_sorted.astype(jnp.int32), right_sorted.astype(jnp.int32), offsets


def stop_kernel(ls_ref, rs_ref, off_ref, left_ref, right_ref, acc_in_ref, acc_out_ref):
    result_count = acc_out_ref.shape[0]

    def per_target(t, carry):
        def per_triple(i, acc):
            a = left_ref[ls_ref[i]]
            b = right_ref[rs_ref[i]]
            return acc + jnp.dot(a, b, preferred_element_type=jnp.float32)

        acc = lax.fori_loop(off_ref[t], off_ref[t + 1], per_triple, acc_in_ref[t])
        acc_out_ref[t] = acc
        return carry

    lax.fori_loop(0, result_count, per_target, 0)


def run_stop(total, left, right, stack):
    result_count = total.shape[0]
    ls, rs, off = sort_stack(stack, left.shape[0], right.shape[0], result_count)
    full = lambda shape: pl.BlockSpec(shape, lambda *_: (0,) * len(shape))
    grid_spec = pltpu.PrefetchScalarGridSpec(
        num_scalar_prefetch=3,
        grid=(1,),
        in_specs=[full(left.shape), full(right.shape), full(total.shape)],
        out_specs=full(total.shape),
    )
    return pl.pallas_call(
        stop_kernel,
        grid_spec=grid_spec,
        out_shape=jax.ShapeDtypeStruct(total.shape, jnp.float32),
        input_output_aliases={5: 0},
    )(ls, rs, off, left, right, total)


def on_device(a_blocks, b_blocks, a_send, b_send, triples, c_send):
    rows_n = lax.axis_size("row")
    cols_n = lax.axis_size("col")
    count = rows_n * cols_n
    result_count = count // 2
    edge = a_blocks.shape[-1]
    left_out = bucketize(a_blocks[0, 0], a_send[0, 0])
    left_home = lax.all_to_all(left_out, "col", split_axis=0, concat_axis=0, tiled=True)
    left_home = left_home.reshape(-1, edge, edge)
    right_out = bucketize(b_blocks[0, 0], b_send[0, 0])
    right_home = lax.all_to_all(right_out, "row", split_axis=0, concat_axis=0, tiled=True)
    right_home = right_home.reshape(-1, edge, edge)
    total = jnp.zeros((result_count, edge, edge), jnp.float32)
    left_now = left_home
    right_now = right_home
    for stop_index in range(STOPS):
        if stop_index > 0:
            left_now = passed_along(left_now, "col", -1)
            right_now = passed_along(right_now, "row", -1)
        total = run_stop(total, left_now, right_now, triples[0, 0, stop_index])
    result = total.astype(jnp.bfloat16)
    outgoing = bucketize(result, c_send[0, 0])
    arrived = lax.all_to_all(outgoing, ("row", "col"), split_axis=0, concat_axis=0, tiled=True)
    return arrived[None, None]


def solution(mesh):
    placed = (
        P("row", "col", None, None, None),
        P("row", "col", None, None, None),
        P("row", "col", None, None),
        P("row", "col", None, None),
        P("row", "col", None, None, None),
        P("row", "col", None),
    )
    return jax.shard_map(
        on_device,
        mesh=mesh,
        in_specs=placed,
        out_specs=P("row", "col", None, None, None),
        check_vma=False,
    )
```

profile of v0, /device:TPU:1, one launch (start us, length us, event | category | flops | bytes accessed | tf_op | source)
XLA Modules:
  0.0 328.8 jit_solution(12645824110571943160)
XLA Ops:
  0.0 0.8 compare_bitcast_fusion.1
  1.8 0.9 select_select_fusion.1
  2.7 5.4 %all-to-all-start.1 = ((bf16[8,2,128,128]{3,2,1,0:T(8,128)(2,1)}), bf16[8,2,128,128]{3,2,1,0:T(8,128)(2,1)S(1)}, u32[]{:S(2)}, u32[]{:S(2)}) async-start(bf16[8,2,128,128]{3,2,1,0:T(8,128)(2,1)} %select_select_fusion.1), calls=%async_computation.1 | async-start | bytes 1048576 | tf_op jit(solution)/shard_map/all_to_all | solution.py:83
  8.3 3.8 %sort.62 = (s32[384]{0:T(512)}, s32[384]{0:T(512)S(1)}) sort(s32[384]{0:T(512)S(1)} %get-tuple-element.40, s32[384]{0:T(512)S(1)} %iota.23), dimensions={0}, to_apply=%region_9.11 | sort | flops 3456 | bytes 6144 | tf_op jit(solution)/shard_map/jit(argsort)/sort | solution.py:28
  12.1 2.8 gather_fusion.9
  14.9 2.8 gather_fusion.10
  18.7 3.8 %sort.61 = (s32[384]{0:T(512)}, s32[384]{0:T(512)S(1)}) sort(s32[384]{0:T(512)S(1)} %get-tuple-element.41, s32[384]{0:T(512)S(1)} %iota.22), dimensions={0}, to_apply=%region_6.8 | sort | flops 3456 | bytes 6144 | tf_op jit(solution)/shard_map/jit(argsort)/sort | solution.py:28
  22.5 2.8 gather_fusion.7
  25.3 3.8 %sort.60 = (s32[384]{0:T(512)}, s32[384]{0:T(512)S(1)}) sort(s32[384]{0:T(512)S(1)} %get-tuple-element.42, s32[384]{0:T(512)S(1)} %iota.21), dimensions={0}, to_apply=%region_3.5 | sort | flops 3456 | bytes 6144 | tf_op jit(solution)/shard_map/jit(argsort)/sort | solution.py:28
  29.8 0.9 select_select_fusion.2
  30.7 4.6 %all-to-all-start = ((bf16[4,4,128,128]{3,2,1,0:T(8,128)(2,1)}), bf16[4,4,128,128]{3,2,1,0:T(8,128)(2,1)S(1)}, u32[]{:S(2)}, u32[]{:S(2)}) async-start(bf16[4,4,128,128]{3,2,1,0:T(8,128)(2,1)} %select_select_fusion.2), calls=%async_computation | async-start | bytes 1048576 | tf_op jit(solution)/shard_map/all_to_all | solution.py:80
  35.3 2.8 gather_fusion.8
  38.4 2.8 gather_fusion.5
  41.2 2.8 gather_fusion.6
  44.3 3.8 %sort.59 = (s32[384]{0:T(512)}, s32[384]{0:T(512)S(1)}) sort(s32[384]{0:T(512)S(1)} %get-tuple-element.43, s32[384]{0:T(512)S(1)} %iota.20), dimensions={0}, to_apply=%region_0.1 | sort | flops 3456 | bytes 6144 | tf_op jit(solution)/shard_map/jit(argsort)/sort | solution.py:28
  48.1 2.8 gather_fusion.3
  50.9 2.8 gather_fusion.4
  55.7 3.5 %collective-permute-start = (bf16[16,128,128]{2,1,0:T(8,128)(2,1)S(1)}, bf16[16,128,128]{2,1,0:T(8,128)(2,1)S(1)}, u32[]{:S(2)}, u32[]{:S(2)}) collective-permute-start(bf16[16,128,128]{2,1,0:T(8,128)(2,1)S(1)} %bitcast.33), channel_id=1, source_target_pairs={{0,3},{1,0},{2,1},{3,2},{4,7},{5,4},{6,5},{7,6},{8,11},{9,8},{10,9... | collective-permute-start | bytes 1572872 | tf_op jit(solution)/shard_map/ppermute | solution.py:16
  59.2 5.2 %collective-permute-done.3.right_ref = bf16[16,128,128]{2,1,0:T(8,128)(2,1)S(1)} collective-permute-done((bf16[16,128,128]{2,1,0:T(8,128)(2,1)S(1)}, bf16[16,128,128]{2,1,0:T(8,128)(2,1)S(1)}, u32[]{:S(2)}, u32[]{:S(2)}) %collective-permute-start.3) | collective-permute-done | bytes 524320 | tf_op jit(solution)/shard_map/ppermute | solution.py:16
  64.7 3.6 %collective-permute-done.left_ref = bf16[16,128,128]{2,1,0:T(8,128)(2,1)S(1)} collective-permute-done((bf16[16,128,128]{2,1,0:T(8,128)(2,1)S(1)}, bf16[16,128,128]{2,1,0:T(8,128)(2,1)S(1)}, u32[]{:S(2)}, u32[]{:S(2)}) %collective-permute-start) | collective-permute-done | bytes 524320 | tf_op jit(solution)/shard_map/ppermute | solution.py:16
  68.3 4.0 %collective-permute-start.1 = (bf16[16,128,128]{2,1,0:T(8,128)(2,1)S(1)}, bf16[16,128,128]{2,1,0:T(8,128)(2,1)S(1)}, u32[]{:S(2)}, u32[]{:S(2)}) collective-permute-start(bf16[16,128,128]{2,1,0:T(8,128)(2,1)S(1)} %collective-permute-done.left_ref), channel_id=1, source_target_pairs={{0,3},{1,0},{2,1},{3,2},{4,7},{5,4},{6,5},{7,6},{8,11},{9,8},{10,9... | collective-permute-start | bytes 1572872 | tf_op jit(solution)/shard_map/ppermute | solution.py:16
  74.1 3.3 %collective-permute-start.5 = (bf16[16,128,128]{2,1,0:T(8,128)(2,1)S(1)}, bf16[16,128,128]{2,1,0:T(8,128)(2,1)}, u32[]{:S(2)}, u32[]{:S(2)}) collective-permute-start(bf16[16,128,128]{2,1,0:T(8,128)(2,1)S(1)} %collective-permute-done.4.right_ref), channel_id=1, source_target_pairs={{0,28},{4,0},{8,4},{12,8},{16,12},{20,16},{24,20},{28,24},{1,29},{... | collective-permute-start | bytes 1572872 | tf_op jit(solution)/shard_map/ppermute | solution.py:16
  77.4 3.1 collective-permute-done.1.left_ref
  80.5 4.0 %collective-permute-start.2 = (bf16[16,128,128]{2,1,0:T(8,128)(2,1)S(1)}, bf16[16,128,128]{2,1,0:T(8,128)(2,1)}, u32[]{:S(2)}, u32[]{:S(2)}) collective-permute-start(bf16[16,128,128]{2,1,0:T(8,128)(2,1)S(1)} %collective-permute-done.1.left_ref), channel_id=1, source_target_pairs={{0,3},{1,0},{2,1},{3,2},{4,7},{5,4},{6,5},{7,6},{8,11},{9,8},{10,9... | collective-permute-start | bytes 1572872 | tf_op jit(solution)/shard_map/ppermute | solution.py:16
  86.3 1.1 broadcast_in_dim.104.acc_in_ref
  87.3 42.0 %shard_map.64.acc_in_ref = f32[16,128,128]{2,1,0:T(8,128)} custom-call(s32[384]{0:T(512)} %get-tuple-element.27.ls_ref, s32[384]{0:T(512)} %get-tuple-element.26.rs_ref, s32[17]{0:T(128)} %pad_add_fusion.off_ref, bf16[16,128,128]{2,1,0:T(8,128)(2,1)} %bitcast.34, bf16[16,128,128]{2,1,0:T(8,128)(2,1)} %bitcast.32, ...), custom_call_target="tpu_custom_call", output_to_operand_aliasing={{}: (5, {})} | custom-call | tf_op jit(solution)/shard_map/pallas_call | solution.py:65
  129.3 52.6 %shard_map.65.acc_in_ref = f32[16,128,128]{2,1,0:T(8,128)} custom-call(s32[384]{0:T(512)} %get-tuple-element.29.ls_ref, s32[384]{0:T(512)} %get-tuple-element.28.rs_ref, s32[17]{0:T(128)} %pad_add_fusion.1.off_ref, bf16[16,128,128]{2,1,0:T(8,128)(2,1)} %copy-done.5, bf16[16,128,128]{2,1,0:T(8,128)(2,1)} %copy-done.4, ...), custom_call_target="tpu_custom_call", output_to_operand_aliasing={{}: (5, {})} | custom-call | tf_op jit(solution)/shard_map/pallas_call | solution.py:65
  182.0 38.8 %shard_map.66.acc_in_ref = f32[16,128,128]{2,1,0:T(8,128)} custom-call(s32[384]{0:T(512)} %get-tuple-element.31.ls_ref, s32[384]{0:T(512)} %get-tuple-element.30.rs_ref, s32[17]{0:T(128)} %pad_add_fusion.2.off_ref, bf16[16,128,128]{2,1,0:T(8,128)(2,1)} %copy-done.7, bf16[16,128,128]{2,1,0:T(8,128)(2,1)} %copy-done.6, ...), custom_call_target="tpu_custom_call", output_to_operand_aliasing={{}: (5, {})} | custom-call | tf_op jit(solution)/shard_map/pallas_call | solution.py:65
  220.8 32.3 %shard_map.67 = f32[16,128,128]{2,1,0:T(8,128)} custom-call(s32[384]{0:T(512)} %get-tuple-element.35.ls_ref, s32[384]{0:T(512)} %get-tuple-element.34.rs_ref, s32[17]{0:T(128)} %pad_add_fusion.3.off_ref, bf16[16,128,128]{2,1,0:T(8,128)(2,1)} %collective-permute-done.2.left_ref, ...), custom_call_target="tpu_custom_call", output_to_operand_aliasing={{}: (5, {})} | custom-call | tf_op jit(solution)/shard_map/pallas_call | solution.py:65
  253.1 1.3 convert_element_type.19
  255.4 72.4 %all_to_all.15 = bf16[32,128,128]{2,1,0:T(8,128)(2,1)S(1)} all-to-all(bf16[32,128,128]{2,1,0:T(8,128)(2,1)S(1)} %select_select_fusion), channel_id=1, replica_groups=mesh['row'=8,'col'=4] {'row','col'}, dimensions={0} | all-to-all | bytes 2097152 | tf_op jit(solution)/shard_map/all_to_all | solution.py:95
  327.8 1.0 copy.37
  (87 shorter events, 10.3 us)
Async XLA Ops:
  0.0 1.1 copy-start
  0.0 0.8 copy-start.10
  2.7 5.4 %copy-start.8 = (s32[1,1,4,3,384]{4,2,3,1,0:T(4,128)S(1)}, s32[1,1,4,3,384]{4,2,3,1,0:T(4,128)}, u32[]{:S(2)}) copy-start(s32[1,1,4,3,384]{4,2,3,1,0:T(4,128)} %param.12) | copy-start | bytes 55300
  2.7 28.0 %all-to-all-start.1 = ((bf16[8,2,128,128]{3,2,1,0:T(8,128)(2,1)}), bf16[8,2,128,128]{3,2,1,0:T(8,128)(2,1)S(1)}, u32[]{:S(2)}, u32[]{:S(2)}) async-start(bf16[8,2,128,128]{3,2,1,0:T(8,128)(2,1)} %select_select_fusion.1), calls=%async_computation.1 | async-start | bytes 1048576 | tf_op jit(solution)/shard_map/all_to_all | solution.py:83
  17.8 0.7 copy-start.9
  22.5 6.6 %copy-start.3 = (bf16[1,1,16,128,128]{4,3,2,1,0:T(8,128)(2,1)S(1)}, bf16[1,1,16,128,128]{4,3,2,1,0:T(8,128)(2,1)}, u32[]{:S(2)}) copy-start(bf16[1,1,16,128,128]{4,3,2,1,0:T(8,128)(2,1)} %param.8) | copy-start | bytes 1572868
  30.7 24.6 %copy-start.1 = (bf16[8,2,128,128]{3,2,1,0:T(8,128)(2,1)}, bf16[8,2,128,128]{3,2,1,0:T(8,128)(2,1)S(1)}, u32[]{:S(2)}) copy-start(bf16[8,2,128,128]{3,2,1,0:T(8,128)(2,1)S(1)} %all-to-all-done.1) | copy-start | bytes 1572868
  30.7 24.9 %all-to-all-start = ((bf16[4,4,128,128]{3,2,1,0:T(8,128)(2,1)}), bf16[4,4,128,128]{3,2,1,0:T(8,128)(2,1)S(1)}, u32[]{:S(2)}, u32[]{:S(2)}) async-start(bf16[4,4,128,128]{3,2,1,0:T(8,128)(2,1)} %select_select_fusion.2), calls=%async_computation | async-start | bytes 1048576 | tf_op jit(solution)/shard_map/all_to_all | solution.py:80
  55.4 3.8 %copy-start.11 = (s32[1,1,32]{2,1,0:T(1,128)S(1)}, s32[1,1,32]{2,1,0:T(1,128)}, u32[]{:S(2)}) copy-start(s32[1,1,32]{2,1,0:T(1,128)} %param.13) | copy-start | bytes 388
  55.4 9.1 %collective-permute-start.3 = (bf16[16,128,128]{2,1,0:T(8,128)(2,1)S(1)}, bf16[16,128,128]{2,1,0:T(8,128)(2,1)S(1)}, u32[]{:S(2)}, u32[]{:S(2)}) collective-permute-start(bf16[16,128,128]{2,1,0:T(8,128)(2,1)S(1)} %bitcast.31), channel_id=1, source_target_pairs={{0,28},{4,0},{8,4},{12,8},{16,12},{20,16},{24,20},{28,24},{1,29},{... | collective-permute-start | bytes 1572872 | tf_op jit(solution)/shard_map/ppermute | solution.py:16
  55.7 31.7 %copy-start.2 = (bf16[4,4,128,128]{3,2,1,0:T(8,128)(2,1)}, bf16[4,4,128,128]{3,2,1,0:T(8,128)(2,1)S(1)}, u32[]{:S(2)}) copy-start(bf16[4,4,128,128]{3,2,1,0:T(8,128)(2,1)S(1)} %all-to-all-done) | copy-start | bytes 1572868
  55.7 12.6 %collective-permute-start = (bf16[16,128,128]{2,1,0:T(8,128)(2,1)S(1)}, bf16[16,128,128]{2,1,0:T(8,128)(2,1)S(1)}, u32[]{:S(2)}, u32[]{:S(2)}) collective-permute-start(bf16[16,128,128]{2,1,0:T(8,128)(2,1)S(1)} %bitcast.33), channel_id=1, source_target_pairs={{0,3},{1,0},{2,1},{3,2},{4,7},{5,4},{6,5},{7,6},{8,11},{9,8},{10,9... | collective-permute-start | bytes 1572872 | tf_op jit(solution)/shard_map/ppermute | solution.py:16
  64.4 22.9 %copy-start.4 = (bf16[16,128,128]{2,1,0:T(8,128)(2,1)}, bf16[16,128,128]{2,1,0:T(8,128)(2,1)S(1)}, u32[]{:S(2)}) copy-start(bf16[16,128,128]{2,1,0:T(8,128)(2,1)S(1)} %collective-permute-done.3.right_ref) | copy-start | bytes 1572868
  64.4 9.7 %collective-permute-start.4 = (bf16[16,128,128]{2,1,0:T(8,128)(2,1)S(1)}, bf16[16,128,128]{2,1,0:T(8,128)(2,1)S(1)}, u32[]{:S(2)}, u32[]{:S(2)}) collective-permute-start(bf16[16,128,128]{2,1,0:T(8,128)(2,1)S(1)} %collective-permute-done.3.right_ref), channel_id=1, source_target_pairs={{0,28},{4,0},{8,4},{12,8},{16,12},{20,16},{24,20},{28,24},{1,29},{... | collective-permute-start | bytes 1572872 | tf_op jit(solution)/shard_map/ppermute | solution.py:16
  68.3 61.0 %copy-start.5 = (bf16[16,128,128]{2,1,0:T(8,128)(2,1)}, bf16[16,128,128]{2,1,0:T(8,128)(2,1)S(1)}, u32[]{:S(2)}) copy-start(bf16[16,128,128]{2,1,0:T(8,128)(2,1)S(1)} %collective-permute-done.left_ref) | copy-start | bytes 1572868
  68.3 12.2 %collective-permute-start.1 = (bf16[16,128,128]{2,1,0:T(8,128)(2,1)S(1)}, bf16[16,128,128]{2,1,0:T(8,128)(2,1)S(1)}, u32[]{:S(2)}, u32[]{:S(2)}) collective-permute-start(bf16[16,128,128]{2,1,0:T(8,128)(2,1)S(1)} %collective-permute-done.left_ref), channel_id=1, source_target_pairs={{0,3},{1,0},{2,1},{3,2},{4,7},{5,4},{6,5},{7,6},{8,11},{9,8},{10,9... | collective-permute-start | bytes 1572872 | tf_op jit(solution)/shard_map/ppermute | solution.py:16
  74.1 55.2 %copy-start.6 = (bf16[16,128,128]{2,1,0:T(8,128)(2,1)}, bf16[16,128,128]{2,1,0:T(8,128)(2,1)S(1)}, u32[]{:S(2)}) copy-start(bf16[16,128,128]{2,1,0:T(8,128)(2,1)S(1)} %collective-permute-done.4.right_ref) | copy-start | bytes 1572868
  74.1 146.7 %collective-permute-start.5 = (bf16[16,128,128]{2,1,0:T(8,128)(2,1)S(1)}, bf16[16,128,128]{2,1,0:T(8,128)(2,1)}, u32[]{:S(2)}, u32[]{:S(2)}) collective-permute-start(bf16[16,128,128]{2,1,0:T(8,128)(2,1)S(1)} %collective-permute-done.4.right_ref), channel_id=1, source_target_pairs={{0,28},{4,0},{8,4},{12,8},{16,12},{20,16},{24,20},{28,24},{1,29},{... | collective-permute-start | bytes 1572872 | tf_op jit(solution)/shard_map/ppermute | solution.py:16
  80.5 48.9 %copy-start.7 = (bf16[16,128,128]{2,1,0:T(8,128)(2,1)}, bf16[16,128,128]{2,1,0:T(8,128)(2,1)S(1)}, u32[]{:S(2)}) copy-start(bf16[16,128,128]{2,1,0:T(8,128)(2,1)S(1)} %collective-permute-done.1.left_ref) | copy-start | bytes 1572868
  80.5 140.3 %collective-permute-start.2 = (bf16[16,128,128]{2,1,0:T(8,128)(2,1)S(1)}, bf16[16,128,128]{2,1,0:T(8,128)(2,1)}, u32[]{:S(2)}, u32[]{:S(2)}) collective-permute-start(bf16[16,128,128]{2,1,0:T(8,128)(2,1)S(1)} %collective-permute-done.1.left_ref), channel_id=1, source_target_pairs={{0,3},{1,0},{2,1},{3,2},{4,7},{5,4},{6,5},{7,6},{8,11},{9,8},{10,9... | collective-permute-start | bytes 1572872 | tf_op jit(solution)/shard_map/ppermute | solution.py:16
where the time goes:
time: 325 us; the launch traced here: 329 us
  Pallas kernels  166 us (51%)
  blocking collectives  72.4 us (22%)
  local copies, waits for them, and re-layouts  27.8 us (9%)
  starting transfers between devices  25.4 us (8%)
  other arithmetic  25.3 us (8%)
  waiting for transfers between devices  11.8 us (4%)
    pallas_call x4, Pallas kernels, run_stop(): pl.pallas_call(stop_kernel, grid_spec=grid_spec, out_shape=jax.ShapeDtype...  166 us
    all_to_all x1, blocking collectives, on_device(): lax.all_to_all(outgoing, ('row', 'col'), split_axis=0, concat_axis=0, til...  72.4 us
    ppermute x6, starting transfers between devices, passed_along(): return lax.ppermute(value, axis, pairs)  15.5 us
    sort x4, other arithmetic, sort_stack(): order = jnp.argsort(keys, stable=True)  15.1 us
    ppermute x6, waiting for transfers between devices, passed_along(): return lax.ppermute(value, axis, pairs)  11.8 us
    gather x4, local copies, waits for them, and re-layouts, sort_stack(): left_sorted = jnp.clip(jnp.take(stack[0], order), 0, left_count - 1)  11.2 us
    gather x4, local copies, waits for them, and re-layouts, sort_stack(): right_sorted = jnp.clip(jnp.take(stack[1], order), 0, right_count - 1)  11.2 us
  transfers between devices with their start and end apart: 8, of which 3 were waited for; matrix products, arithmetic and copies ran while one was open for 14% of the time, Pallas kernels for 41%

commit v1 on v0

--- a/solution.py
+++ b/solution.py
@@ -21,43 +21,40 @@
     return jnp.where((index >= 0)[..., None, None], picked, jnp.zeros_like(picked))
 
 
-def sort_stack(stack, left_count, right_count, result_count):
-    live = stack[0] >= 0
-    target = jnp.clip(stack[2], 0, result_count - 1)
-    keys = jnp.where(live, target, result_count)
-    order = jnp.argsort(keys, stable=True)
-    left_sorted = jnp.clip(jnp.take(stack[0], order), 0, left_count - 1)
-    right_sorted = jnp.clip(jnp.take(stack[1], order), 0, right_count - 1)
-    counts = jnp.sum(
-        (keys[:, None] == jnp.arange(result_count, dtype=jnp.int32)[None, :]).astype(jnp.int32),
-        axis=0,
-    )
-    offsets = jnp.concatenate([jnp.zeros((1,), jnp.int32), jnp.cumsum(counts).astype(jnp.int32)])
-    return left_sorted.astype(jnp.int32), right_sorted.astype(jnp.int32), offsets
+GROUP = 32
 
 
-def stop_kernel(ls_ref, rs_ref, off_ref, left_ref, right_ref, acc_in_ref, acc_out_ref):
-    result_count = acc_out_ref.shape[0]
+def stop_kernel(ls_ref, rs_ref, ts_ref, n_ref, left_ref, right_ref, acc_in_ref, acc_out_ref):
+    live_count = n_ref[0]
 
-    def per_target(t, carry):
-        def per_triple(i, acc):
-            a = left_ref[ls_ref[i]]
-            b = right_ref[rs_ref[i]]
-            return acc + jnp.dot(a, b, preferred_element_type=jnp.float32)
-
-        acc = lax.fori_loop(off_ref[t], off_ref[t + 1], per_triple, acc_in_ref[t])
-        acc_out_ref[t] = acc
+    def per_group(g, carry):
+        base = g * GROUP
+        prods = []
+        for k in range(GROUP):
+            i = base + k
+            p = jnp.dot(left_ref[ls_ref[i]], right_ref[rs_ref[i]], preferred_element_type=jnp.float32)
+            p = p.astype(jnp.bfloat16).astype(jnp.float32)
+            prods.append(jnp.where(i < live_count, p, 0.0))
+        for k in range(GROUP):
+            t = ts_ref[base + k]
+            acc_out_ref[t] = acc_out_ref[t] + prods[k]
         return carry
 
-    lax.fori_loop(0, result_count, per_target, 0)
+    acc_out_ref[...] = acc_in_ref[...]
+    lax.fori_loop(0, (live_count + GROUP - 1) // GROUP, per_group, 0)
 
 
 def run_stop(total, left, right, stack):
     result_count = total.shape[0]
-    ls, rs, off = sort_stack(stack, left.shape[0], right.shape[0], result_count)
+    slots = stack.shape[1]
+    assert slots % GROUP == 0
+    ls = jnp.clip(stack[0], 0, left.shape[0] - 1).astype(jnp.int32)
+    rs = jnp.clip(stack[1], 0, right.shape[0] - 1).astype(jnp.int32)
+    ts = jnp.clip(stack[2], 0, result_count - 1).astype(jnp.int32)
+    live_count = jnp.sum((stack[0] >= 0).astype(jnp.int32)).reshape(1)
     full = lambda shape: pl.BlockSpec(shape, lambda *_: (0,) * len(shape))
     grid_spec = pltpu.PrefetchScalarGridSpec(
-        num_scalar_prefetch=3,
+        num_scalar_prefetch=4,
         grid=(1,),
         in_specs=[full(left.shape), full(right.shape), full(total.shape)],
         out_specs=full(total.shape),
@@ -66,8 +63,8 @@
         stop_kernel,
         grid_spec=grid_spec,
         out_shape=jax.ShapeDtypeStruct(total.shape, jnp.float32),
-        input_output_aliases={5: 0},
-    )(ls, rs, off, left, right, total)
+        input_output_aliases={6: 0},
+    )(ls, rs, ts, live_count, left, right, total)
 
 
 def on_device(a_blocks, b_blocks, a_send, b_send, triples, c_send):

time: 325 us -> 134 us (0.41); the launches traced: 329 us -> 133 us
  Pallas kernels: 166 us -> 31.3 us
  blocking collectives: 72.4 us -> 36.2 us
  local copies, waits for them, and re-layouts: 27.8 us -> 5.38 us
  other arithmetic: 25.3 us -> 5.01 us
  waiting for transfers between devices: 11.8 us -> 24 us
  starting transfers between devices: 25.4 us -> 30.7 us
    pallas_call x4, Pallas kernels: 166 us -> 31.3 us  [run_stop(): pl.pallas_call(stop_kernel, grid_spec=grid_spec, out_shape=jax.ShapeDtype...]
    all_to_all x1, blocking collectives: 72.4 us -> 36.2 us  [on_device(): lax.all_to_all(outgoing, ('row', 'col'), split_axis=0, concat_axis=0, til...]
    gather x8 -> x0, local copies, waits for them, and re-layouts: 22.3 us -> none  [the longest x4 11.2 us: sort_stack(): left_sorted = jnp.clip(jnp.take(stack[0], order), 0, left_count - 1)]
    sort x4 -> x0, other arithmetic: 15.1 us -> none  [sort_stack(): order = jnp.argsort(keys, stable=True)]
    all_to_all x1, waiting for transfers between devices: 0.01 us -> 7.63 us  [on_device(): lax.all_to_all(left_out, 'col', split_axis=0, concat_axis=0, tiled=True)]
    ppermute x6, starting transfers between devices: 15.5 us -> 20.6 us  [passed_along(): return lax.ppermute(value, axis, pairs)]
    all_to_all x1, waiting for transfers between devices: 0.01 us -> 5.01 us  [on_device(): lax.all_to_all(right_out, 'row', split_axis=0, concat_axis=0, tiled=True)]
  transfers between devices with their start and end apart: 8 -> 8, of which waited for: 3 -> 4; matrix products, arithmetic and copies ran while one was open for 14% -> 3% of each run, Pallas kernels for 41% -> 17%
where the time goes in v1:
time: 134 us; the launch traced here: 133 us
  blocking collectives  36.2 us (27%)
  Pallas kernels  31.3 us (23%)
  starting transfers between devices  30.7 us (23%)
  waiting for transfers between devices  24 us (18%)
  local copies, waits for them, and re-layouts  5.38 us (4%)
  other arithmetic  5.01 us (4%)
    all_to_all x1, blocking collectives, on_device(): lax.all_to_all(outgoing, ('row', 'col'), split_axis=0, concat_axis=0, til...  36.2 us
    pallas_call x4, Pallas kernels, run_stop(): pl.pallas_call(stop_kernel, grid_spec=grid_spec, out_shape=jax.ShapeDtype...  31.3 us
    ppermute x6, starting transfers between devices, passed_along(): return lax.ppermute(value, axis, pairs)  20.6 us
    ppermute x6, waiting for transfers between devices, passed_along(): return lax.ppermute(value, axis, pairs)  11.3 us
    all_to_all x1, waiting for transfers between devices, on_device(): lax.all_to_all(left_out, 'col', split_axis=0, concat_axis=0, tiled=True)  7.63 us
    all_to_all x1, starting transfers between devices, on_device(): lax.all_to_all(right_out, 'row', split_axis=0, concat_axis=0, tiled=True)  5.35 us
    all_to_all x1, waiting for transfers between devices, on_device(): lax.all_to_all(right_out, 'row', split_axis=0, concat_axis=0, tiled=True)  5.01 us
    all_to_all x1, starting transfers between devices, on_device(): lax.all_to_all(left_out, 'col', split_axis=0, concat_axis=0, tiled=True)  4.72 us
  transfers between devices with their start and end apart: 8, of which 4 were waited for; matrix products, arithmetic and copies ran while one was open for 3% of the time, Pallas kernels for 17%

profile of v1, /device:TPU:1, one launch (start us, length us, event | category | flops | bytes accessed | tf_op | source)
XLA Modules:
  0.0 132.7 jit_solution(5054923242000484876)
XLA Ops:
  0.0 0.8 compare_bitcast_fusion.1
  0.8 0.1 copy.14
  0.9 0.1 copy.15
  1.1 0.6 gather_fusion.1
  1.8 0.9 select_select_fusion.1
  2.7 5.4 %all-to-all-start.1 = ((bf16[8,2,128,128]{3,2,1,0:T(8,128)(2,1)}), bf16[8,2,128,128]{3,2,1,0:T(8,128)(2,1)S(1)}, u32[]{:S(2)}, u32[]{:S(2)}) async-start(bf16[8,2,128,128]{3,2,1,0:T(8,128)(2,1)} %select_select_fusion.1), calls=%async_computation.1 | async-start | bytes 1048576 | tf_op jit(solution)/shard_map/all_to_all | solution.py:80
  8.1 0.1 reshape.185
  8.2 0.6 gather_fusion
  8.9 0.9 select_select_fusion.2
  9.8 5.0 %all-to-all-done.1 = bf16[8,2,128,128]{3,2,1,0:T(8,128)(2,1)S(1)} async-done(((bf16[8,2,128,128]{3,2,1,0:T(8,128)(2,1)}), bf16[8,2,128,128]{3,2,1,0:T(8,128)(2,1)S(1)}, u32[]{:S(2)}, u32[]{:S(2)}) %all-to-all-start.1) | async-done | bytes 524320 | tf_op jit(solution)/shard_map/all_to_all | solution.py:80
  14.8 4.7 %all-to-all-start = ((bf16[4,4,128,128]{3,2,1,0:T(8,128)(2,1)}), bf16[4,4,128,128]{3,2,1,0:T(8,128)(2,1)S(1)}, u32[]{:S(2)}, u32[]{:S(2)}) async-start(bf16[4,4,128,128]{3,2,1,0:T(8,128)(2,1)} %select_select_fusion.2), calls=%async_computation | async-start | bytes 1048576 | tf_op jit(solution)/shard_map/all_to_all | solution.py:77
  19.6 3.3 %collective-permute-start.3 = (bf16[16,128,128]{2,1,0:T(8,128)(2,1)S(1)}, bf16[16,128,128]{2,1,0:T(8,128)(2,1)S(1)}, u32[]{:S(2)}, u32[]{:S(2)}) collective-permute-start(bf16[16,128,128]{2,1,0:T(8,128)(2,1)S(1)} %bitcast.31), channel_id=1, source_target_pairs={{0,28},{4,0},{8,4},{12,8},{16,12},{20,16},{24,20},{28,24},{1,29},{... | collective-permute-start | bytes 1572872 | tf_op jit(solution)/shard_map/ppermute | solution.py:16
  22.9 7.6 %all-to-all-done = bf16[4,4,128,128]{3,2,1,0:T(8,128)(2,1)S(1)} async-done(((bf16[4,4,128,128]{3,2,1,0:T(8,128)(2,1)}), bf16[4,4,128,128]{3,2,1,0:T(8,128)(2,1)S(1)}, u32[]{:S(2)}, u32[]{:S(2)}) %all-to-all-start) | async-done | bytes 524320 | tf_op jit(solution)/shard_map/all_to_all | solution.py:77
  30.5 3.5 %collective-permute-start = (bf16[16,128,128]{2,1,0:T(8,128)(2,1)S(1)}, bf16[16,128,128]{2,1,0:T(8,128)(2,1)S(1)}, u32[]{:S(2)}, u32[]{:S(2)}) collective-permute-start(bf16[16,128,128]{2,1,0:T(8,128)(2,1)S(1)} %bitcast.33), channel_id=1, source_target_pairs={{0,3},{1,0},{2,1},{3,2},{4,7},{5,4},{6,5},{7,6},{8,11},{9,8},{10,9... | collective-permute-start | bytes 1572872 | tf_op jit(solution)/shard_map/ppermute | solution.py:16
  34.0 2.5 %collective-permute-start.4 = (bf16[16,128,128]{2,1,0:T(8,128)(2,1)S(1)}, bf16[16,128,128]{2,1,0:T(8,128)(2,1)S(1)}, u32[]{:S(2)}, u32[]{:S(2)}) collective-permute-start(bf16[16,128,128]{2,1,0:T(8,128)(2,1)S(1)} %collective-permute-done.3.right_ref), channel_id=1, source_target_pairs={{0,28},{4,0},{8,4},{12,8},{16,12},{20,16},{24,20},{28,24},{1,29},{... | collective-permute-start | bytes 1572872 | tf_op jit(solution)/shard_map/ppermute | solution.py:16
  36.5 6.6 %collective-permute-done.left_ref = bf16[16,128,128]{2,1,0:T(8,128)(2,1)S(1)} collective-permute-done((bf16[16,128,128]{2,1,0:T(8,128)(2,1)S(1)}, bf16[16,128,128]{2,1,0:T(8,128)(2,1)S(1)}, u32[]{:S(2)}, u32[]{:S(2)}) %collective-permute-start) | collective-permute-done | bytes 524320 | tf_op jit(solution)/shard_map/ppermute | solution.py:16
  43.1 4.0 %collective-permute-start.1 = (bf16[16,128,128]{2,1,0:T(8,128)(2,1)S(1)}, bf16[16,128,128]{2,1,0:T(8,128)(2,1)S(1)}, u32[]{:S(2)}, u32[]{:S(2)}) collective-permute-start(bf16[16,128,128]{2,1,0:T(8,128)(2,1)S(1)} %collective-permute-done.left_ref), channel_id=1, source_target_pairs={{0,3},{1,0},{2,1},{3,2},{4,7},{5,4},{6,5},{7,6},{8,11},{9,8},{10,9... | collective-permute-start | bytes 1572872 | tf_op jit(solution)/shard_map/ppermute | solution.py:16
  47.1 3.4 %collective-permute-start.5 = (bf16[16,128,128]{2,1,0:T(8,128)(2,1)S(1)}, bf16[16,128,128]{2,1,0:T(8,128)(2,1)S(1)}, u32[]{:S(2)}, u32[]{:S(2)}) collective-permute-start(bf16[16,128,128]{2,1,0:T(8,128)(2,1)S(1)} %collective-permute-done.4.right_ref), channel_id=1, source_target_pairs={{0,28},{4,0},{8,4},{12,8},{16,12},{20,16},{24,20},{28,24},{1,29},{... | collective-permute-start | bytes 1572872 | tf_op jit(solution)/shard_map/ppermute | solution.py:16
  50.4 4.7 %collective-permute-done.1.left_ref = bf16[16,128,128]{2,1,0:T(8,128)(2,1)S(1)} collective-permute-done((bf16[16,128,128]{2,1,0:T(8,128)(2,1)S(1)}, bf16[16,128,128]{2,1,0:T(8,128)(2,1)S(1)}, u32[]{:S(2)}, u32[]{:S(2)}) %collective-permute-start.1) | collective-permute-done | bytes 524320 | tf_op jit(solution)/shard_map/ppermute | solution.py:16
  55.2 4.0 %collective-permute-start.2 = (bf16[16,128,128]{2,1,0:T(8,128)(2,1)S(1)}, bf16[16,128,128]{2,1,0:T(8,128)(2,1)}, u32[]{:S(2)}, u32[]{:S(2)}) collective-permute-start(bf16[16,128,128]{2,1,0:T(8,128)(2,1)S(1)} %collective-permute-done.1.left_ref), channel_id=1, source_target_pairs={{0,3},{1,0},{2,1},{3,2},{4,7},{5,4},{6,5},{7,6},{8,11},{9,8},{10,9... | collective-permute-start | bytes 1572872 | tf_op jit(solution)/shard_map/ppermute | solution.py:16
  59.2 0.8 fusion.3
  60.0 1.1 broadcast_in_dim.82.acc_in_ref
  61.1 7.8 %shard_map.64.acc_in_ref = f32[16,128,128]{2,1,0:T(8,128)} custom-call(s32[384]{0:T(512)} %get-tuple-element.9.ls_ref, s32[384]{0:T(512)} %get-tuple-element.20.rs_ref, s32[384]{0:T(512)} %get-tuple-element.19.ts_ref, s32[1]{0:T(128)} %bitcast.15.n_ref, bf16[16,128,128]{2,1,0:T(8,128)(2,1)} %bitcast.34, ...), custom_call_target="tpu_custom_call", output_to_operand_aliasing={{}: (6, {})} | custom-call | tf_op jit(solution)/shard_map/pallas_call | solution.py:62
  68.9 7.2 %shard_map.65.acc_in_ref = f32[16,128,128]{2,1,0:T(8,128)} custom-call(s32[384]{0:T(512)} %get-tuple-element.12.ls_ref, s32[384]{0:T(512)} %get-tuple-element.11.rs_ref, s32[384]{0:T(512)} %get-tuple-element.10.ts_ref, s32[1]{0:T(128)} %bitcast.14.n_ref, bf16[16,128,128]{2,1,0:T(8,128)(2,1)} %copy-done.8, ...), custom_call_target="tpu_custom_call", output_to_operand_aliasing={{}: (6, {})} | custom-call | tf_op jit(solution)/shard_map/pallas_call | solution.py:62
  76.1 7.2 %shard_map.66.acc_in_ref = f32[16,128,128]{2,1,0:T(8,128)} custom-call(s32[384]{0:T(512)} %get-tuple-element.15.ls_ref, s32[384]{0:T(512)} %get-tuple-element.14.rs_ref, s32[384]{0:T(512)} %get-tuple-element.13.ts_ref, s32[1]{0:T(128)} %bitcast.13.n_ref, bf16[16,128,128]{2,1,0:T(8,128)(2,1)} %copy-done.6, ...), custom_call_target="tpu_custom_call", output_to_operand_aliasing={{}: (6, {})} | custom-call | tf_op jit(solution)/shard_map/pallas_call | solution.py:62
  83.3 0.8 copy-done.7
  84.1 9.1 %shard_map.67 = f32[16,128,128]{2,1,0:T(8,128)} custom-call(s32[384]{0:T(512)} %get-tuple-element.18.ls_ref, s32[384]{0:T(512)} %get-tuple-element.17.rs_ref, s32[384]{0:T(512)} %get-tuple-element.16.ts_ref, s32[1]{0:T(128)} %bitcast.2.n_ref, bf16[16,128,128]{2,1,0:T(8,128)(2,1)} %collective-permute-done.2.left_ref, ...), custom_call_target="tpu_custom_call", output_to_operand_aliasing={{}: (6, {})} | custom-call | tf_op jit(solution)/shard_map/pallas_call | solution.py:62
  93.3 1.3 convert_element_type.23
  94.6 0.7 gather_fusion.2
  95.3 0.2 select_select_fusion
  95.5 36.2 %all_to_all.15 = bf16[32,128,128]{2,1,0:T(8,128)(2,1)S(1)} all-to-all(bf16[32,128,128]{2,1,0:T(8,128)(2,1)S(1)} %select_select_fusion), channel_id=1, replica_groups=mesh['row'=8,'col'=4] {'row','col'}, dimensions={0} | all-to-all | bytes 2097152 | tf_op jit(solution)/shard_map/all_to_all | solution.py:92
  131.7 1.0 copy.22
  (39 shorter events, 0.3 us)
Async XLA Ops:
  0.0 1.1 copy-start
  0.0 0.8 copy-start.11
  2.7 5.4 %copy-start.10 = (s32[1,1,4,4]{3,2,1,0:T(4,128)S(1)}, s32[1,1,4,4]{3,2,1,0:T(4,128)}, u32[]{:S(2)}) copy-start(s32[1,1,4,4]{3,2,1,0:T(4,128)} %param.8) | copy-start | bytes 196
  2.7 5.5 %copy-start.3 = (bf16[1,1,16,128,128]{4,3,2,1,0:T(8,128)(2,1)S(1)}, bf16[1,1,16,128,128]{4,3,2,1,0:T(8,128)(2,1)}, u32[]{:S(2)}) copy-start(bf16[1,1,16,128,128]{4,3,2,1,0:T(8,128)(2,1)} %param.6) | copy-start | bytes 1572868
  2.7 12.1 %all-to-all-start.1 = ((bf16[8,2,128,128]{3,2,1,0:T(8,128)(2,1)}), bf16[8,2,128,128]{3,2,1,0:T(8,128)(2,1)S(1)}, u32[]{:S(2)}, u32[]{:S(2)}) async-start(bf16[8,2,128,128]{3,2,1,0:T(8,128)(2,1)} %select_select_fusion.1), calls=%async_computation.1 | async-start | bytes 1048576 | tf_op jit(solution)/shard_map/all_to_all | solution.py:80
  14.8 4.7 %copy-start.1 = (bf16[8,2,128,128]{3,2,1,0:T(8,128)(2,1)}, bf16[8,2,128,128]{3,2,1,0:T(8,128)(2,1)S(1)}, u32[]{:S(2)}) copy-start(bf16[8,2,128,128]{3,2,1,0:T(8,128)(2,1)S(1)} %all-to-all-done.1) | copy-start | bytes 1572868
  14.8 44.4 %copy-start.9 = (s32[1,1,4,3,384]{4,2,3,1,0:T(4,128)S(1)}, s32[1,1,4,3,384]{4,2,3,1,0:T(4,128)}, u32[]{:S(2)}) copy-start(s32[1,1,4,3,384]{4,2,3,1,0:T(4,128)} %param.10) | copy-start | bytes 55300
  14.8 15.7 %all-to-all-start = ((bf16[4,4,128,128]{3,2,1,0:T(8,128)(2,1)}), bf16[4,4,128,128]{3,2,1,0:T(8,128)(2,1)S(1)}, u32[]{:S(2)}, u32[]{:S(2)}) async-start(bf16[4,4,128,128]{3,2,1,0:T(8,128)(2,1)} %select_select_fusion.2), calls=%async_computation | async-start | bytes 1048576 | tf_op jit(solution)/shard_map/all_to_all | solution.py:77
  19.6 39.6 %copy-start.12 = (s32[1,1,32]{2,1,0:T(1,128)S(1)}, s32[1,1,32]{2,1,0:T(1,128)}, u32[]{:S(2)}) copy-start(s32[1,1,32]{2,1,0:T(1,128)} %param.11) | copy-start | bytes 388
  19.6 14.5 %collective-permute-start.3 = (bf16[16,128,128]{2,1,0:T(8,128)(2,1)S(1)}, bf16[16,128,128]{2,1,0:T(8,128)(2,1)S(1)}, u32[]{:S(2)}, u32[]{:S(2)}) collective-permute-start(bf16[16,128,128]{2,1,0:T(8,128)(2,1)S(1)} %bitcast.31), channel_id=1, source_target_pairs={{0,28},{4,0},{8,4},{12,8},{16,12},{20,16},{24,20},{28,24},{1,29},{... | collective-permute-start | bytes 1572872 | tf_op jit(solution)/shard_map/ppermute | solution.py:16
  30.5 30.6 %copy-start.2 = (bf16[4,4,128,128]{3,2,1,0:T(8,128)(2,1)}, bf16[4,4,128,128]{3,2,1,0:T(8,128)(2,1)S(1)}, u32[]{:S(2)}) copy-start(bf16[4,4,128,128]{3,2,1,0:T(8,128)(2,1)S(1)} %all-to-all-done) | copy-start | bytes 1572868
  30.5 12.6 %collective-permute-start = (bf16[16,128,128]{2,1,0:T(8,128)(2,1)S(1)}, bf16[16,128,128]{2,1,0:T(8,128)(2,1)S(1)}, u32[]{:S(2)}, u32[]{:S(2)}) collective-permute-start(bf16[16,128,128]{2,1,0:T(8,128)(2,1)S(1)} %bitcast.33), channel_id=1, source_target_pairs={{0,3},{1,0},{2,1},{3,2},{4,7},{5,4},{6,5},{7,6},{8,11},{9,8},{10,9... | collective-permute-start | bytes 1572872 | tf_op jit(solution)/shard_map/ppermute | solution.py:16
  34.0 27.1 %copy-start.4 = (bf16[16,128,128]{2,1,0:T(8,128)(2,1)}, bf16[16,128,128]{2,1,0:T(8,128)(2,1)S(1)}, u32[]{:S(2)}) copy-start(bf16[16,128,128]{2,1,0:T(8,128)(2,1)S(1)} %collective-permute-done.3.right_ref) | copy-start | bytes 1572868
  34.0 13.0 %collective-permute-start.4 = (bf16[16,128,128]{2,1,0:T(8,128)(2,1)S(1)}, bf16[16,128,128]{2,1,0:T(8,128)(2,1)S(1)}, u32[]{:S(2)}, u32[]{:S(2)}) collective-permute-start(bf16[16,128,128]{2,1,0:T(8,128)(2,1)S(1)} %collective-permute-done.3.right_ref), channel_id=1, source_target_pairs={{0,28},{4,0},{8,4},{12,8},{16,12},{20,16},{24,20},{28,24},{1,29},{... | collective-permute-start | bytes 1572872 | tf_op jit(solution)/shard_map/ppermute | solution.py:16
  43.1 12.1 %copy-start.8 = (bf16[16,128,128]{2,1,0:T(8,128)(2,1)}, bf16[16,128,128]{2,1,0:T(8,128)(2,1)S(1)}, u32[]{:S(2)}) copy-start(bf16[16,128,128]{2,1,0:T(8,128)(2,1)S(1)} %collective-permute-done.left_ref) | copy-start | bytes 1572868
  43.1 12.1 %collective-permute-start.1 = (bf16[16,128,128]{2,1,0:T(8,128)(2,1)S(1)}, bf16[16,128,128]{2,1,0:T(8,128)(2,1)S(1)}, u32[]{:S(2)}, u32[]{:S(2)}) collective-permute-start(bf16[16,128,128]{2,1,0:T(8,128)(2,1)S(1)} %collective-permute-done.left_ref), channel_id=1, source_target_pairs={{0,3},{1,0},{2,1},{3,2},{4,7},{5,4},{6,5},{7,6},{8,11},{9,8},{10,9... | collective-permute-start | bytes 1572872 | tf_op jit(solution)/shard_map/ppermute | solution.py:16
  47.1 21.8 %copy-start.5 = (bf16[16,128,128]{2,1,0:T(8,128)(2,1)}, bf16[16,128,128]{2,1,0:T(8,128)(2,1)S(1)}, u32[]{:S(2)}) copy-start(bf16[16,128,128]{2,1,0:T(8,128)(2,1)S(1)} %collective-permute-done.4.right_ref) | copy-start | bytes 1572868
  47.1 36.2 %collective-permute-start.5 = (bf16[16,128,128]{2,1,0:T(8,128)(2,1)S(1)}, bf16[16,128,128]{2,1,0:T(8,128)(2,1)S(1)}, u32[]{:S(2)}, u32[]{:S(2)}) collective-permute-start(bf16[16,128,128]{2,1,0:T(8,128)(2,1)S(1)} %collective-permute-done.4.right_ref), channel_id=1, source_target_pairs={{0,28},{4,0},{8,4},{12,8},{16,12},{20,16},{24,20},{28,24},{1,29},{... | collective-permute-start | bytes 1572872 | tf_op jit(solution)/shard_map/ppermute | solution.py:16
  55.2 13.7 %copy-start.6 = (bf16[16,128,128]{2,1,0:T(8,128)(2,1)}, bf16[16,128,128]{2,1,0:T(8,128)(2,1)S(1)}, u32[]{:S(2)}) copy-start(bf16[16,128,128]{2,1,0:T(8,128)(2,1)S(1)} %collective-permute-done.1.left_ref) | copy-start | bytes 1572868
  55.2 28.1 %collective-permute-start.2 = (bf16[16,128,128]{2,1,0:T(8,128)(2,1)S(1)}, bf16[16,128,128]{2,1,0:T(8,128)(2,1)}, u32[]{:S(2)}, u32[]{:S(2)}) collective-permute-start(bf16[16,128,128]{2,1,0:T(8,128)(2,1)S(1)} %collective-permute-done.1.left_ref), channel_id=1, source_target_pairs={{0,3},{1,0},{2,1},{3,2},{4,7},{5,4},{6,5},{7,6},{8,11},{9,8},{10,9... | collective-permute-start | bytes 1572872 | tf_op jit(solution)/shard_map/ppermute | solution.py:16
  83.3 0.8 copy-start.7

commit v2 on v1

--- a/solution.py
+++ b/solution.py
@@ -80,13 +80,10 @@
     right_home = lax.all_to_all(right_out, "row", split_axis=0, concat_axis=0, tiled=True)
     right_home = right_home.reshape(-1, edge, edge)
     total = jnp.zeros((result_count, edge, edge), jnp.float32)
-    left_now = left_home
-    right_now = right_home
+    lefts = [left_home] + [passed_along(left_home, "col", -s) for s in range(1, STOPS)]
+    rights = [right_home] + [passed_along(right_home, "row", -s) for s in range(1, STOPS)]
     for stop_index in range(STOPS):
-        if stop_index > 0:
-            left_now = passed_along(left_now, "col", -1)
-            right_now = passed_along(right_now, "row", -1)
-        total = run_stop(total, left_now, right_now, triples[0, 0, stop_index])
+        total = run_stop(total, lefts[stop_index], rights[stop_index], triples[0, 0, stop_index])
     result = total.astype(jnp.bfloat16)
     outgoing = bucketize(result, c_send[0, 0])
     arrived = lax.all_to_all(outgoing, ("row", "col"), split_axis=0, concat_axis=0, tiled=True)

time: 134 us -> 133 us (level)
  starting transfers between devices: 30.7 us -> 20.9 us
  waiting for transfers between devices: 24 us -> 33.3 us
  blocking collectives: 36.2 us -> 31.6 us
  Pallas kernels: 31.3 us -> 34.5 us
    ppermute x6, waiting for transfers between devices: 11.3 us -> 23.2 us  [passed_along(): return lax.ppermute(value, axis, pairs)]
    ppermute x6, starting transfers between devices: 20.6 us -> 10.9 us  [passed_along(): return lax.ppermute(value, axis, pairs)]
    all_to_all x1, blocking collectives: 36.2 us -> 31.6 us  [on_device(): lax.all_to_all(outgoing, ('row', 'col'), split_axis=0, concat_axis=0, til...]
    pallas_call x4, Pallas kernels: 31.3 us -> 34.5 us  [run_stop(): pl.pallas_call(stop_kernel, grid_spec=grid_spec, out_shape=jax.ShapeDtype...]
    all_to_all x1, waiting for transfers between devices: 7.63 us -> 5.15 us  [on_device(): lax.all_to_all(left_out, 'col', split_axis=0, concat_axis=0, tiled=True)]
  transfers between devices with their start and end apart: 8 -> 8, of which waited for: 4 -> 4; matrix products, arithmetic and copies ran while one was open for 3% -> 3% of each run, Pallas kernels for 17% -> 20%
where the time goes in v2:
time: 133 us; the launch traced here: 131 us
  Pallas kernels  34.5 us (26%)
  waiting for transfers between devices  33.3 us (25%)
  blocking collectives  31.6 us (24%)
  starting transfers between devices  20.9 us (16%)
  local copies, waits for them, and re-layouts  5.54 us (4%)
  other arithmetic  5 us (4%)
    pallas_call x4, Pallas kernels, run_stop(): pl.pallas_call(stop_kernel, grid_spec=grid_spec, out_shape=jax.ShapeDtype...  34.5 us
    all_to_all x1, blocking collectives, on_device(): lax.all_to_all(outgoing, ('row', 'col'), split_axis=0, concat_axis=0, til...  31.6 us
    ppermute x6, waiting for transfers between devices, passed_along(): return lax.ppermute(value, axis, pairs)  23.2 us
    ppermute x6, starting transfers between devices, passed_along(): return lax.ppermute(value, axis, pairs)  10.9 us
    all_to_all x1, starting transfers between devices, on_device(): lax.all_to_all(right_out, 'row', split_axis=0, concat_axis=0, tiled=True)  5.35 us
    all_to_all x1, waiting for transfers between devices, on_device(): lax.all_to_all(left_out, 'col', split_axis=0, concat_axis=0, tiled=True)  5.15 us
    all_to_all x1, waiting for transfers between devices, on_device(): lax.all_to_all(right_out, 'row', split_axis=0, concat_axis=0, tiled=True)  5.01 us
    all_to_all x1, starting transfers between devices, on_device(): lax.all_to_all(left_out, 'col', split_axis=0, concat_axis=0, tiled=True)  4.72 us
  transfers between devices with their start and end apart: 8, of which 4 were waited for; matrix products, arithmetic and copies ran while one was open for 3% of the time, Pallas kernels for 20%

profile of v2, /device:TPU:1, one launch (start us, length us, event | category | flops | bytes accessed | tf_op | source)
XLA Modules:
  0.0 131.0 jit_solution(13633752007374196480)
XLA Ops:
  0.0 0.8 compare_bitcast_fusion.1
  0.8 0.1 copy.14
  0.9 0.1 copy.15
  1.1 0.6 gather_fusion.1
  1.8 0.9 select_select_fusion.1
  2.7 5.4 %all-to-all-start.1 = ((bf16[8,2,128,128]{3,2,1,0:T(8,128)(2,1)}), bf16[8,2,128,128]{3,2,1,0:T(8,128)(2,1)S(1)}, u32[]{:S(2)}, u32[]{:S(2)}) async-start(bf16[8,2,128,128]{3,2,1,0:T(8,128)(2,1)} %select_select_fusion.1), calls=%async_computation.1 | async-start | bytes 1048576 | tf_op jit(solution)/shard_map/all_to_all | solution.py:80
  8.1 0.1 reshape.185
  8.2 0.6 gather_fusion
  8.9 0.9 select_select_fusion.2
  9.8 5.0 %all-to-all-done.1 = bf16[8,2,128,128]{3,2,1,0:T(8,128)(2,1)S(1)} async-done(((bf16[8,2,128,128]{3,2,1,0:T(8,128)(2,1)}), bf16[8,2,128,128]{3,2,1,0:T(8,128)(2,1)S(1)}, u32[]{:S(2)}, u32[]{:S(2)}) %all-to-all-start.1) | async-done | bytes 524320 | tf_op jit(solution)/shard_map/all_to_all | solution.py:80
  14.8 4.7 %all-to-all-start = ((bf16[4,4,128,128]{3,2,1,0:T(8,128)(2,1)}), bf16[4,4,128,128]{3,2,1,0:T(8,128)(2,1)S(1)}, u32[]{:S(2)}, u32[]{:S(2)}) async-start(bf16[4,4,128,128]{3,2,1,0:T(8,128)(2,1)} %select_select_fusion.2), calls=%async_computation | async-start | bytes 1048576 | tf_op jit(solution)/shard_map/all_to_all | solution.py:77
  19.6 3.3 %collective-permute-start.5 = (bf16[16,128,128]{2,1,0:T(8,128)(2,1)S(1)}, bf16[16,128,128]{2,1,0:T(8,128)(2,1)}, u32[]{:S(2)}, u32[]{:S(2)}) collective-permute-start(bf16[16,128,128]{2,1,0:T(8,128)(2,1)S(1)} %bitcast.31), channel_id=1, source_target_pairs={{0,28},{4,0},{8,4},{12,8},{16,12},{20,16},{24,20},{28,24},{1,29},{... | collective-permute-start | bytes 1572872 | tf_op jit(solution)/shard_map/ppermute | solution.py:16
  22.9 0.3 collective-permute-start.3
  23.1 2.2 %collective-permute-start.1 = (bf16[16,128,128]{2,1,0:T(8,128)(2,1)S(1)}, bf16[16,128,128]{2,1,0:T(8,128)(2,1)S(1)}, u32[]{:S(2)}, u32[]{:S(2)}) collective-permute-start(bf16[16,128,128]{2,1,0:T(8,128)(2,1)S(1)} %bitcast.33), channel_id=1, source_target_pairs={{0,20},{4,24},{8,28},{12,0},{16,4},{20,8},{24,12},{28,16},{1,21},{... | collective-permute-start | bytes 1572872 | tf_op jit(solution)/shard_map/ppermute | solution.py:16
  25.3 5.1 %all-to-all-done = bf16[4,4,128,128]{3,2,1,0:T(8,128)(2,1)S(1)} async-done(((bf16[4,4,128,128]{3,2,1,0:T(8,128)(2,1)}), bf16[4,4,128,128]{3,2,1,0:T(8,128)(2,1)S(1)}, u32[]{:S(2)}, u32[]{:S(2)}) %all-to-all-start) | async-done | bytes 524320 | tf_op jit(solution)/shard_map/all_to_all | solution.py:77
  30.5 3.5 %collective-permute-start.4 = (bf16[16,128,128]{2,1,0:T(8,128)(2,1)S(1)}, bf16[16,128,128]{2,1,0:T(8,128)(2,1)}, u32[]{:S(2)}, u32[]{:S(2)}) collective-permute-start(bf16[16,128,128]{2,1,0:T(8,128)(2,1)S(1)} %bitcast.35), channel_id=1, source_target_pairs={{0,3},{1,0},{2,1},{3,2},{4,7},{5,4},{6,5},{7,6},{8,11},{9,8},{10,9... | collective-permute-start | bytes 1572872 | tf_op jit(solution)/shard_map/ppermute | solution.py:16
  34.0 0.8 collective-permute-done.5.right_ref
  34.8 1.6 %collective-permute-start = (bf16[16,128,128]{2,1,0:T(8,128)(2,1)S(1)}, bf16[16,128,128]{2,1,0:T(8,128)(2,1)S(1)}, u32[]{:S(2)}, u32[]{:S(2)}) collective-permute-start(bf16[16,128,128]{2,1,0:T(8,128)(2,1)S(1)} %bitcast.37), channel_id=1, source_target_pairs={{0,1},{1,2},{2,3},{3,0},{4,5},{5,6},{6,7},{7,4},{8,9},{9,10},{10,1... | collective-permute-start | bytes 1572872 | tf_op jit(solution)/shard_map/ppermute | solution.py:16
  36.4 0.8 fusion.3
  37.2 1.1 broadcast_in_dim.82.acc_in_ref
  38.3 8.2 %shard_map.64.acc_in_ref = f32[16,128,128]{2,1,0:T(8,128)} custom-call(s32[384]{0:T(512)} %get-tuple-element.9.ls_ref, s32[384]{0:T(512)} %get-tuple-element.20.rs_ref, s32[384]{0:T(512)} %get-tuple-element.19.ts_ref, s32[1]{0:T(128)} %bitcast.15.n_ref, bf16[16,128,128]{2,1,0:T(8,128)(2,1)} %bitcast.38, ...), custom_call_target="tpu_custom_call", output_to_operand_aliasing={{}: (6, {})} | custom-call | tf_op jit(solution)/shard_map/pallas_call | solution.py:62
  46.5 8.6 %shard_map.65.acc_in_ref = f32[16,128,128]{2,1,0:T(8,128)} custom-call(s32[384]{0:T(512)} %get-tuple-element.12.ls_ref, s32[384]{0:T(512)} %get-tuple-element.11.rs_ref, s32[384]{0:T(512)} %get-tuple-element.10.ts_ref, s32[1]{0:T(128)} %bitcast.14.n_ref, bf16[16,128,128]{2,1,0:T(8,128)(2,1)} %collective-permute-done.4.left_ref, ...), custom_call_target="tpu_custom_call", output_to_operand_aliasing={{}: (6, {})} | custom-call | tf_op jit(solution)/shard_map/pallas_call | solution.py:62
  55.0 22.4 %collective-permute-done.2.left_ref = bf16[16,128,128]{2,1,0:T(8,128)(2,1)} collective-permute-done((bf16[16,128,128]{2,1,0:T(8,128)(2,1)S(1)}, bf16[16,128,128]{2,1,0:T(8,128)(2,1)}, u32[]{:S(2)}, u32[]{:S(2)}) %collective-permute-start.2) | collective-permute-done | bytes 524320 | tf_op jit(solution)/shard_map/ppermute | solution.py:16
  77.4 9.5 %shard_map.66.acc_in_ref = f32[16,128,128]{2,1,0:T(8,128)} custom-call(s32[384]{0:T(512)} %get-tuple-element.15.ls_ref, s32[384]{0:T(512)} %get-tuple-element.14.rs_ref, s32[384]{0:T(512)} %get-tuple-element.13.ts_ref, s32[1]{0:T(128)} %bitcast.13.n_ref, bf16[16,128,128]{2,1,0:T(8,128)(2,1)} %collective-permute-done.2.left_ref, ...), custom_call_target="tpu_custom_call", output_to_operand_aliasing={{}: (6, {})} | custom-call | tf_op jit(solution)/shard_map/pallas_call | solution.py:62
  87.0 0.8 copy-done.4
  87.8 0.2 copy-done.6
  88.0 8.2 %shard_map.67 = f32[16,128,128]{2,1,0:T(8,128)} custom-call(s32[384]{0:T(512)} %get-tuple-element.18.ls_ref, s32[384]{0:T(512)} %get-tuple-element.17.rs_ref, s32[384]{0:T(512)} %get-tuple-element.16.ts_ref, s32[1]{0:T(128)} %bitcast.2.n_ref, bf16[16,128,128]{2,1,0:T(8,128)(2,1)} %copy-done.6, ...), custom_call_target="tpu_custom_call", output_to_operand_aliasing={{}: (6, {})} | custom-call | tf_op jit(solution)/shard_map/pallas_call | solution.py:62
  96.2 1.3 %convert_element_type.23 = bf16[16,128,128]{2,1,0:T(8,128)(2,1)S(1)} convert(f32[16,128,128]{2,1,0:T(8,128)} %shard_map.67) | non-fusion elementwise | flops 262144 | bytes 1572864 | tf_op jit(solution)/shard_map/convert_element_type | solution.py:87
  97.5 0.7 gather_fusion.2
  98.2 0.2 select_select_fusion
  98.4 31.6 %all_to_all.15 = bf16[32,128,128]{2,1,0:T(8,128)(2,1)S(1)} all-to-all(bf16[32,128,128]{2,1,0:T(8,128)(2,1)S(1)} %select_select_fusion), channel_id=1, replica_groups=mesh['row'=8,'col'=4] {'row','col'}, dimensions={0} | all-to-all | bytes 2097152 | tf_op jit(solution)/shard_map/all_to_all | solution.py:89
  130.0 1.0 copy.22
  (35 shorter events, 0.3 us)
Async XLA Ops:
  0.0 1.1 copy-start
  0.0 0.8 copy-start.9
  2.7 5.4 %copy-start.8 = (s32[1,1,4,4]{3,2,1,0:T(4,128)S(1)}, s32[1,1,4,4]{3,2,1,0:T(4,128)}, u32[]{:S(2)}) copy-start(s32[1,1,4,4]{3,2,1,0:T(4,128)} %param.8) | copy-start | bytes 196
  2.7 5.5 %copy-start.3 = (bf16[1,1,16,128,128]{4,3,2,1,0:T(8,128)(2,1)S(1)}, bf16[1,1,16,128,128]{4,3,2,1,0:T(8,128)(2,1)}, u32[]{:S(2)}) copy-start(bf16[1,1,16,128,128]{4,3,2,1,0:T(8,128)(2,1)} %param.6) | copy-start | bytes 1572868
  2.7 12.1 %all-to-all-start.1 = ((bf16[8,2,128,128]{3,2,1,0:T(8,128)(2,1)}), bf16[8,2,128,128]{3,2,1,0:T(8,128)(2,1)S(1)}, u32[]{:S(2)}, u32[]{:S(2)}) async-start(bf16[8,2,128,128]{3,2,1,0:T(8,128)(2,1)} %select_select_fusion.1), calls=%async_computation.1 | async-start | bytes 1048576 | tf_op jit(solution)/shard_map/all_to_all | solution.py:80
  14.8 8.3 %copy-start.1 = (bf16[8,2,128,128]{3,2,1,0:T(8,128)(2,1)}, bf16[8,2,128,128]{3,2,1,0:T(8,128)(2,1)S(1)}, u32[]{:S(2)}) copy-start(bf16[8,2,128,128]{3,2,1,0:T(8,128)(2,1)S(1)} %all-to-all-done.1) | copy-start | bytes 1572868
  14.8 21.5 %copy-start.7 = (s32[1,1,4,3,384]{4,2,3,1,0:T(4,128)S(1)}, s32[1,1,4,3,384]{4,2,3,1,0:T(4,128)}, u32[]{:S(2)}) copy-start(s32[1,1,4,3,384]{4,2,3,1,0:T(4,128)} %param.10) | copy-start | bytes 55300
  14.8 15.7 %all-to-all-start = ((bf16[4,4,128,128]{3,2,1,0:T(8,128)(2,1)}), bf16[4,4,128,128]{3,2,1,0:T(8,128)(2,1)S(1)}, u32[]{:S(2)}, u32[]{:S(2)}) async-start(bf16[4,4,128,128]{3,2,1,0:T(8,128)(2,1)} %select_select_fusion.2), calls=%async_computation | async-start | bytes 1048576 | tf_op jit(solution)/shard_map/all_to_all | solution.py:77
  19.5 16.8 %copy-start.10 = (s32[1,1,32]{2,1,0:T(1,128)S(1)}, s32[1,1,32]{2,1,0:T(1,128)}, u32[]{:S(2)}) copy-start(s32[1,1,32]{2,1,0:T(1,128)} %param.11) | copy-start | bytes 388
  19.6 15.2 %collective-permute-start.5 = (bf16[16,128,128]{2,1,0:T(8,128)(2,1)S(1)}, bf16[16,128,128]{2,1,0:T(8,128)(2,1)}, u32[]{:S(2)}, u32[]{:S(2)}) collective-permute-start(bf16[16,128,128]{2,1,0:T(8,128)(2,1)S(1)} %bitcast.31), channel_id=1, source_target_pairs={{0,28},{4,0},{8,4},{12,8},{16,12},{20,16},{24,20},{28,24},{1,29},{... | collective-permute-start | bytes 1572872 | tf_op jit(solution)/shard_map/ppermute | solution.py:16
  22.9 32.2 %collective-permute-start.3 = (bf16[16,128,128]{2,1,0:T(8,128)(2,1)S(1)}, bf16[16,128,128]{2,1,0:T(8,128)(2,1)S(1)}, u32[]{:S(2)}, u32[]{:S(2)}) collective-permute-start(bf16[16,128,128]{2,1,0:T(8,128)(2,1)S(1)} %bitcast.32), channel_id=1, source_target_pairs={{0,24},{4,28},{8,0},{12,4},{16,8},{20,12},{24,16},{28,20},{1,25},{... | collective-permute-start | bytes 1572872 | tf_op jit(solution)/shard_map/ppermute | solution.py:16
  23.1 63.8 %collective-permute-start.1 = (bf16[16,128,128]{2,1,0:T(8,128)(2,1)S(1)}, bf16[16,128,128]{2,1,0:T(8,128)(2,1)S(1)}, u32[]{:S(2)}, u32[]{:S(2)}) collective-permute-start(bf16[16,128,128]{2,1,0:T(8,128)(2,1)S(1)} %bitcast.33), channel_id=1, source_target_pairs={{0,20},{4,24},{8,28},{12,0},{16,4},{20,8},{24,12},{28,16},{1,21},{... | collective-permute-start | bytes 1572872 | tf_op jit(solution)/shard_map/ppermute | solution.py:16
  30.5 7.8 %copy-start.2 = (bf16[4,4,128,128]{3,2,1,0:T(8,128)(2,1)}, bf16[4,4,128,128]{3,2,1,0:T(8,128)(2,1)S(1)}, u32[]{:S(2)}) copy-start(bf16[4,4,128,128]{3,2,1,0:T(8,128)(2,1)S(1)} %all-to-all-done) | copy-start | bytes 1572868
  30.5 16.0 %collective-permute-start.4 = (bf16[16,128,128]{2,1,0:T(8,128)(2,1)S(1)}, bf16[16,128,128]{2,1,0:T(8,128)(2,1)}, u32[]{:S(2)}, u32[]{:S(2)}) collective-permute-start(bf16[16,128,128]{2,1,0:T(8,128)(2,1)S(1)} %bitcast.35), channel_id=1, source_target_pairs={{0,3},{1,0},{2,1},{3,2},{4,7},{5,4},{6,5},{7,6},{8,11},{9,8},{10,9... | collective-permute-start | bytes 1572872 | tf_op jit(solution)/shard_map/ppermute | solution.py:16
  34.0 43.4 %collective-permute-start.2 = (bf16[16,128,128]{2,1,0:T(8,128)(2,1)S(1)}, bf16[16,128,128]{2,1,0:T(8,128)(2,1)}, u32[]{:S(2)}, u32[]{:S(2)}) collective-permute-start(bf16[16,128,128]{2,1,0:T(8,128)(2,1)S(1)} %bitcast.36), channel_id=1, source_target_pairs={{0,2},{1,3},{2,0},{3,1},{4,6},{5,7},{6,4},{7,5},{8,10},{9,11},{10,... | collective-permute-start | bytes 1572872 | tf_op jit(solution)/shard_map/ppermute | solution.py:16
  34.8 52.2 %collective-permute-start = (bf16[16,128,128]{2,1,0:T(8,128)(2,1)S(1)}, bf16[16,128,128]{2,1,0:T(8,128)(2,1)S(1)}, u32[]{:S(2)}, u32[]{:S(2)}) collective-permute-start(bf16[16,128,128]{2,1,0:T(8,128)(2,1)S(1)} %bitcast.37), channel_id=1, source_target_pairs={{0,1},{1,2},{2,3},{3,0},{4,5},{5,6},{6,7},{7,4},{8,9},{9,10},{10,1... | collective-permute-start | bytes 1572872 | tf_op jit(solution)/shard_map/ppermute | solution.py:16
  55.0 22.4 %copy-start.5 = (bf16[16,128,128]{2,1,0:T(8,128)(2,1)}, bf16[16,128,128]{2,1,0:T(8,128)(2,1)S(1)}, u32[]{:S(2)}) copy-start(bf16[16,128,128]{2,1,0:T(8,128)(2,1)S(1)} %collective-permute-done.3.right_ref) | copy-start | bytes 1572868
  87.0 0.8 copy-start.4
  87.0 1.0 copy-start.6

commit v3 on v2

--- a/solution.py
+++ b/solution.py
@@ -24,7 +24,7 @@
 GROUP = 32
 
 
-def stop_kernel(ls_ref, rs_ref, ts_ref, n_ref, left_ref, right_ref, acc_in_ref, acc_out_ref):
+def stop_kernel(ls_ref, rs_ref, ts_ref, ok_ref, n_ref, left_ref, right_ref, acc_in_ref, acc_out_ref):
     live_count = n_ref[0]
 
     def per_group(g, carry):
@@ -34,7 +34,7 @@
             i = base + k
             p = jnp.dot(left_ref[ls_ref[i]], right_ref[rs_ref[i]], preferred_element_type=jnp.float32)
             p = p.astype(jnp.bfloat16).astype(jnp.float32)
-            prods.append(jnp.where(i < live_count, p, 0.0))
+            prods.append(jnp.where((i < live_count) & (ok_ref[i] > 0), p, 0.0))
         for k in range(GROUP):
             t = ts_ref[base + k]
             acc_out_ref[t] = acc_out_ref[t] + prods[k]
@@ -44,17 +44,20 @@
     lax.fori_loop(0, (live_count + GROUP - 1) // GROUP, per_group, 0)
 
 
-def run_stop(total, left, right, stack):
+def run_stop(total, left, right, stack, left_map):
     result_count = total.shape[0]
     slots = stack.shape[1]
     assert slots % GROUP == 0
-    ls = jnp.clip(stack[0], 0, left.shape[0] - 1).astype(jnp.int32)
+    live = stack[0] >= 0
+    mapped = jnp.take(left_map, jnp.clip(stack[0], 0, left_map.shape[0] - 1))
+    ok = (live & (mapped >= 0)).astype(jnp.int32)
+    ls = jnp.clip(mapped, 0, left.shape[0] - 1).astype(jnp.int32)
     rs = jnp.clip(stack[1], 0, right.shape[0] - 1).astype(jnp.int32)
     ts = jnp.clip(stack[2], 0, result_count - 1).astype(jnp.int32)
-    live_count = jnp.sum((stack[0] >= 0).astype(jnp.int32)).reshape(1)
+    live_count = jnp.sum(live.astype(jnp.int32)).reshape(1)
     full = lambda shape: pl.BlockSpec(shape, lambda *_: (0,) * len(shape))
     grid_spec = pltpu.PrefetchScalarGridSpec(
-        num_scalar_prefetch=4,
+        num_scalar_prefetch=5,
         grid=(1,),
         in_specs=[full(left.shape), full(right.shape), full(total.shape)],
         out_specs=full(total.shape),
@@ -63,8 +66,8 @@
         stop_kernel,
         grid_spec=grid_spec,
         out_shape=jax.ShapeDtypeStruct(total.shape, jnp.float32),
-        input_output_aliases={6: 0},
-    )(ls, rs, ts, live_count, left, right, total)
+        input_output_aliases={7: 0},
+    )(ls, rs, ts, ok, live_count, left, right, total)
 
 
 def on_device(a_blocks, b_blocks, a_send, b_send, triples, c_send):
@@ -73,17 +76,23 @@
     count = rows_n * cols_n
     result_count = count // 2
     edge = a_blocks.shape[-1]
-    left_out = bucketize(a_blocks[0, 0], a_send[0, 0])
-    left_home = lax.all_to_all(left_out, "col", split_axis=0, concat_axis=0, tiled=True)
-    left_home = left_home.reshape(-1, edge, edge)
+    held = a_blocks.shape[2]
+    left_all = lax.all_gather(a_blocks[0, 0], "col", axis=0, tiled=True)
+    send_all = lax.all_gather(a_send[0, 0], "col", axis=0, tiled=False)
+    col_at = lax.axis_index("col")
+    column_base = (jnp.arange(cols_n, dtype=jnp.int32) * held)[:, None]
+    left_maps = []
+    for stop_index in range(STOPS):
+        owner = (col_at + stop_index) % cols_n
+        picked = jnp.take(send_all, owner, axis=1)
+        left_maps.append(jnp.where(picked >= 0, picked + column_base, -1).reshape(-1).astype(jnp.int32))
     right_out = bucketize(b_blocks[0, 0], b_send[0, 0])
     right_home = lax.all_to_all(right_out, "row", split_axis=0, concat_axis=0, tiled=True)
     right_home = right_home.reshape(-1, edge, edge)
     total = jnp.zeros((result_count, edge, edge), jnp.float32)
-    lefts = [left_home] + [passed_along(left_home, "col", -s) for s in range(1, STOPS)]
     rights = [right_home] + [passed_along(right_home, "row", -s) for s in range(1, STOPS)]
     for stop_index in range(STOPS):
-        total = run_stop(total, lefts[stop_index], rights[stop_index], triples[0, 0, stop_index])
+        total = run_stop(total, left_all, rights[stop_index], triples[0, 0, stop_index], left_maps[stop_index])
     result = total.astype(jnp.bfloat16)
     outgoing = bucketize(result, c_send[0, 0])
     arrived = lax.all_to_all(outgoing, ("row", "col"), split_axis=0, concat_axis=0, tiled=True)

time: 133 us -> 163 us (1.23); the launches traced: 131 us -> 163 us
  other arithmetic: 5 us -> 51.6 us
  waiting for transfers between devices: 33.3 us -> 0.72 us
  between operations: 0.11 us -> 13.6 us
  starting transfers between devices: 20.9 us -> 10.7 us
  blocking collectives: 31.6 us -> 41.1 us
  local copies, waits for them, and re-layouts: 5.54 us -> 9.39 us
    convert_element_type x0 -> x4, other arithmetic: none -> 41.9 us  [run_stop(): ok = (live & (mapped >= 0)).astype(jnp.int32)]
    ppermute x6 -> x3, waiting for transfers between devices: 23.2 us -> 0.01 us  [passed_along(): return lax.ppermute(value, axis, pairs)]
    all_gather x0 -> x1, blocking collectives: none -> 9.8 us  [on_device(): send_all = lax.all_gather(a_send[0, 0], 'col', axis=0, tiled=False)]
    ppermute x6 -> x3, starting transfers between devices: 10.9 us -> 5.46 us  [passed_along(): return lax.ppermute(value, axis, pairs)]
    all_to_all x1 -> x0, waiting for transfers between devices: 5.15 us -> none  [on_device(): lax.all_to_all(left_out, 'col', split_axis=0, concat_axis=0, tiled=True)]
    all_to_all x1, waiting for transfers between devices: 5.01 us -> 0.01 us  [on_device(): lax.all_to_all(right_out, 'row', split_axis=0, concat_axis=0, tiled=True)]
    all_to_all x1 -> x0, starting transfers between devices: 4.72 us -> none  [on_device(): lax.all_to_all(left_out, 'col', split_axis=0, concat_axis=0, tiled=True)]
    min x0 -> x5, other arithmetic: none -> 3.04 us  [the longest x4 2.37 us: run_stop(): ls = jnp.clip(mapped, 0, left.shape[0] - 1).astype(jnp.int32)]
  transfers between devices with their start and end apart: 8 -> 5, of which waited for: 4 -> 0; matrix products, arithmetic and copies ran while one was open for 3% -> 32% of each run, Pallas kernels for 20% -> 16%
where the time goes in v3:
time: 163 us
  other arithmetic  51.6 us (32%)
  blocking collectives  41.1 us (25%)
  Pallas kernels  35.8 us (22%)
  between operations  13.6 us (8%)
  starting transfers between devices  10.7 us (7%)
  local copies, waits for them, and re-layouts  9.39 us (6%)
    convert_element_type x4, other arithmetic, run_stop(): ok = (live & (mapped >= 0)).astype(jnp.int32)  41.9 us
    pallas_call x4, Pallas kernels, run_stop(): pl.pallas_call(stop_kernel, grid_spec=grid_spec, out_shape=jax.ShapeDtype...  35.8 us
    all_to_all x1, blocking collectives, on_device(): lax.all_to_all(outgoing, ('row', 'col'), split_axis=0, concat_axis=0, til...  31.3 us
    all_gather x1, blocking collectives, on_device(): send_all = lax.all_gather(a_send[0, 0], 'col', axis=0, tiled=False)  9.8 us
    ppermute x3, starting transfers between devices, passed_along(): return lax.ppermute(value, axis, pairs)  5.46 us
    all_to_all x1, starting transfers between devices, on_device(): lax.all_to_all(right_out, 'row', split_axis=0, concat_axis=0, tiled=True)  5.22 us
    unnamed x17, local copies, waits for them, and re-layouts  3.38 us
  transfers between devices with their start and end apart: 5, of which 0 were waited for; matrix products, arithmetic and copies ran while one was open for 32% of the time, Pallas kernels for 16%

profile of v3, /device:TPU:1, one launch (start us, length us, event | category | flops | bytes accessed | tf_op | source)
XLA Modules:
  0.0 162.8 jit_solution(12650747522561581160)
XLA Ops:
  6.5 0.7 compare_bitcast_fusion.1
  7.3 0.7 broadcast_maximum_fusion
  8.3 0.6 gather_fusion
  9.0 0.9 select_select_fusion.1
  9.9 5.2 %all-to-all-start = ((bf16[8,2,128,128]{3,2,1,0:T(8,128)(2,1)}), bf16[8,2,128,128]{3,2,1,0:T(8,128)(2,1)S(1)}, u32[]{:S(2)}, u32[]{:S(2)}) async-start(bf16[8,2,128,128]{3,2,1,0:T(8,128)(2,1)} %select_select_fusion.1), calls=%async_computation | async-start | bytes 1048576 | tf_op jit(solution)/shard_map/all_to_all | solution.py:90
  15.2 0.7 all-gather.4.cloned.1.call-update
  16.0 9.8 %all-gather = s32[4,1,4,4]{3,2,1,0:T(4,128)S(1)} all-gather(s32[1,1,4,4]{3,2,1,0:T(4,128)S(1)} %copy-done.6), channel_id=2, replica_groups=mesh['row'=8,'col'=4] {'col'}, dimensions={0}, use_global_device_ids=true | all-gather | bytes 320 | tf_op jit(solution)/shard_map/all_gather | solution.py:81
  26.7 0.7 convert_reduce_fusion.1
  27.6 0.7 fusion
  28.3 0.7 fusion.1
  29.0 0.7 fusion.2
  29.7 0.7 fusion.3
  30.4 0.7 clamp_reduce_fusion
  31.1 10.5 %and_convert_fusion = (s32[384]{0:T(512)}, s32[384]{0:T(512)S(1)}) fusion(pred[384]{0:T(512)(128)(4,1)S(1)} %get-tuple-element.18, s32[]{:T(128)} %bitcast.80, s32[]{:T(128)} %bitcast.79, s32[]{:T(128)} %bitcast.78, s32[]{:T(128)} %bitcast.77, s32[]{:T(128)} %bitcast.76, s32[]{:T(128)} %bitcast.75, s32[]{:T(128)} %bitcast.74, s32[]{:T(128)} %bitcast.73, ...), kind=kLoop, calls=%fused_computation.30 | loop fusion | flops 15360 | bytes 5056 | tf_op jit(solution)/shard_map/convert_element_type | solution.py:53
  42.2 10.5 %and_convert_fusion.1 = (s32[384]{0:T(512)}, s32[384]{0:T(512)S(1)}) fusion(pred[384]{0:T(512)(128)(4,1)S(1)} %get-tuple-element.21, s32[]{:T(128)} %bitcast.62, s32[]{:T(128)} %bitcast.61, s32[]{:T(128)} %bitcast.60, s32[]{:T(128)} %bitcast.59, s32[]{:T(128)} %bitcast.58, s32[]{:T(128)} %bitcast.57, s32[]{:T(128)} %bitcast.56, s32[]{:T(128)} %bitcast.55, ...), kind=kLoop, calls=%fused_computation.31 | loop fusion | flops 15360 | bytes 5056 | tf_op jit(solution)/shard_map/convert_element_type | solution.py:53
  53.9 10.4 %and_convert_fusion.2 = (s32[384]{0:T(512)}, s32[384]{0:T(512)S(1)}) fusion(pred[384]{0:T(512)(128)(4,1)S(1)} %get-tuple-element.20, s32[]{:T(128)} %bitcast.44, s32[]{:T(128)} %bitcast.43, s32[]{:T(128)} %bitcast.42, s32[]{:T(128)} %bitcast.41, s32[]{:T(128)} %bitcast.40, s32[]{:T(128)} %bitcast.39, s32[]{:T(128)} %bitcast.38, s32[]{:T(128)} %bitcast.37, ...), kind=kLoop, calls=%fused_computation.32 | loop fusion | flops 15360 | bytes 5056 | tf_op jit(solution)/shard_map/convert_element_type | solution.py:53
  64.9 2.3 %collective-permute-start.2 = (bf16[16,128,128]{2,1,0:T(8,128)(2,1)S(1)}, bf16[16,128,128]{2,1,0:T(8,128)(2,1)S(1)}, u32[]{:S(2)}, u32[]{:S(2)}) collective-permute-start(bf16[16,128,128]{2,1,0:T(8,128)(2,1)S(1)} %bitcast.97), channel_id=1, source_target_pairs={{0,28},{4,0},{8,4},{12,8},{16,12},{20,16},{24,20},{28,24},{1,29},{... | collective-permute-start | bytes 1572872 | tf_op jit(solution)/shard_map/ppermute | solution.py:16
  67.2 2.6 %collective-permute-start.1 = (bf16[16,128,128]{2,1,0:T(8,128)(2,1)S(1)}, bf16[16,128,128]{2,1,0:T(8,128)(2,1)S(1)}, u32[]{:S(2)}, u32[]{:S(2)}) collective-permute-start(bf16[16,128,128]{2,1,0:T(8,128)(2,1)S(1)} %bitcast.98), channel_id=1, source_target_pairs={{0,24},{4,28},{8,0},{12,4},{16,8},{20,12},{24,16},{28,20},{1,25},{... | collective-permute-start | bytes 1572872 | tf_op jit(solution)/shard_map/ppermute | solution.py:16
  70.4 0.7 convert_reduce_fusion.3
  71.1 10.5 %and_convert_fusion.3 = (s32[384]{0:T(512)}, s32[384]{0:T(512)S(1)}) fusion(pred[384]{0:T(512)(128)(4,1)S(1)} %get-tuple-element.19, s32[]{:T(128)} %bitcast.19, s32[]{:T(128)} %bitcast.18, s32[]{:T(128)} %bitcast.17, s32[]{:T(128)} %bitcast.16, s32[]{:T(128)} %bitcast.15, s32[]{:T(128)} %bitcast.14, s32[]{:T(128)} %bitcast.13, s32[]{:T(128)} %bitcast.12, ...), kind=kLoop, calls=%fused_computation.35 | loop fusion | flops 15360 | bytes 5056 | tf_op jit(solution)/shard_map/convert_element_type | solution.py:53
  82.2 1.1 broadcast_in_dim.77.acc_in_ref
  83.3 8.2 %shard_map.64.acc_in_ref = f32[16,128,128]{2,1,0:T(8,128)} custom-call(s32[384]{0:T(512)} %broadcast_clamp_fusion.ls_ref, s32[384]{0:T(512)} %get-tuple-element.33.rs_ref, s32[384]{0:T(512)} %get-tuple-element.22.ts_ref, s32[384]{0:T(512)} %get-tuple-element.34.ok_ref, s32[1]{0:T(128)} %bitcast.81.n_ref, ...), custom_call_target="tpu_custom_call", output_to_operand_aliasing={{}: (7, {})} | custom-call | tf_op jit(solution)/shard_map/pallas_call | solution.py:65
  91.4 0.8 copy-done.4
  92.2 9.2 %shard_map.65.acc_in_ref = f32[16,128,128]{2,1,0:T(8,128)} custom-call(s32[384]{0:T(512)} %broadcast_clamp_fusion.1.ls_ref, s32[384]{0:T(512)} %get-tuple-element.25.rs_ref, s32[384]{0:T(512)} %get-tuple-element.24.ts_ref, s32[384]{0:T(512)} %get-tuple-element.36.ok_ref, s32[1]{0:T(128)} %bitcast.63.n_ref, ...), custom_call_target="tpu_custom_call", output_to_operand_aliasing={{}: (7, {})} | custom-call | tf_op jit(solution)/shard_map/pallas_call | solution.py:65
  101.4 0.8 copy-done.3
  102.2 9.2 %shard_map.66.acc_in_ref = f32[16,128,128]{2,1,0:T(8,128)} custom-call(s32[384]{0:T(512)} %broadcast_clamp_fusion.2.ls_ref, s32[384]{0:T(512)} %get-tuple-element.28.rs_ref, s32[384]{0:T(512)} %get-tuple-element.27.ts_ref, s32[384]{0:T(512)} %get-tuple-element.38.ok_ref, s32[1]{0:T(128)} %bitcast.45.n_ref, ...), custom_call_target="tpu_custom_call", output_to_operand_aliasing={{}: (7, {})} | custom-call | tf_op jit(solution)/shard_map/pallas_call | solution.py:65
  111.4 0.8 copy-done.2
  112.2 9.2 %shard_map.67 = f32[16,128,128]{2,1,0:T(8,128)} custom-call(s32[384]{0:T(512)} %broadcast_clamp_fusion.3.ls_ref, s32[384]{0:T(512)} %get-tuple-element.31.rs_ref, s32[384]{0:T(512)} %get-tuple-element.30.ts_ref, s32[384]{0:T(512)} %get-tuple-element.40.ok_ref, s32[1]{0:T(128)} %bitcast.20.n_ref, ...), custom_call_target="tpu_custom_call", output_to_operand_aliasing={{}: (7, {})} | custom-call | tf_op jit(solution)/shard_map/pallas_call | solution.py:65
  121.4 1.3 convert_element_type.35
  122.7 0.7 gather_fusion.1
  123.7 31.3 %all_to_all.10 = bf16[32,128,128]{2,1,0:T(8,128)(2,1)S(1)} all-to-all(bf16[32,128,128]{2,1,0:T(8,128)(2,1)S(1)} %select_select_fusion), channel_id=1, replica_groups=mesh['row'=8,'col'=4] {'row','col'}, dimensions={0} | all-to-all | bytes 2097152 | tf_op jit(solution)/shard_map/all_to_all | solution.py:98
  155.0 1.0 copy.26
  (43 shorter events, 5.2 us)
Async XLA Ops:
  6.5 1.8 %copy-start = (bf16[1,1,16,128,128]{4,3,2,1,0:T(8,128)(2,1)S(1)}, bf16[1,1,16,128,128]{4,3,2,1,0:T(8,128)(2,1)}, u32[]{:S(2)}) copy-start(bf16[1,1,16,128,128]{4,3,2,1,0:T(8,128)(2,1)} %param.11) | copy-start | bytes 1572868
  6.5 9.4 %copy-start.6 = (s32[1,1,4,4]{3,2,1,0:T(4,128)S(1)}, s32[1,1,4,4]{3,2,1,0:T(4,128)}, u32[]{:S(2)}) copy-start(s32[1,1,4,4]{3,2,1,0:T(4,128)} %param.12) | copy-start | bytes 196
  6.5 19.4 %copy-start.5 = (s32[1,1,4,3,384]{4,2,3,1,0:T(4,128)S(1)}, s32[1,1,4,3,384]{4,2,3,1,0:T(4,128)}, u32[]{:S(2)}) copy-start(s32[1,1,4,3,384]{4,2,3,1,0:T(4,128)} %param.14) | copy-start | bytes 55300
  6.5 21.0 %copy-start.7 = (s32[1,1,32]{2,1,0:T(1,128)S(1)}, s32[1,1,32]{2,1,0:T(1,128)}, u32[]{:S(2)}) copy-start(s32[1,1,32]{2,1,0:T(1,128)} %param.15) | copy-start | bytes 388
  9.9 55.0 %all-to-all-start = ((bf16[8,2,128,128]{3,2,1,0:T(8,128)(2,1)}), bf16[8,2,128,128]{3,2,1,0:T(8,128)(2,1)S(1)}, u32[]{:S(2)}, u32[]{:S(2)}) async-start(bf16[8,2,128,128]{3,2,1,0:T(8,128)(2,1)} %select_select_fusion.1), calls=%async_computation | async-start | bytes 1048576 | tf_op jit(solution)/shard_map/all_to_all | solution.py:90
  15.2 67.0 %all-gather.4.cloned.1.call-start = ((), (), s32[]{:S(2)}) async-start(), calls=%async_computation.2 | async-start | bytes 2621440 | tf_op jit(solution)/shard_map/all_gather | solution.py:80
  64.9 18.3 %copy-start.1 = (bf16[8,2,128,128]{3,2,1,0:T(8,128)(2,1)}, bf16[8,2,128,128]{3,2,1,0:T(8,128)(2,1)S(1)}, u32[]{:S(2)}) copy-start(bf16[8,2,128,128]{3,2,1,0:T(8,128)(2,1)S(1)} %all-to-all-done) | copy-start | bytes 1572868
  64.9 26.5 %collective-permute-start.2 = (bf16[16,128,128]{2,1,0:T(8,128)(2,1)S(1)}, bf16[16,128,128]{2,1,0:T(8,128)(2,1)S(1)}, u32[]{:S(2)}, u32[]{:S(2)}) collective-permute-start(bf16[16,128,128]{2,1,0:T(8,128)(2,1)S(1)} %bitcast.97), channel_id=1, source_target_pairs={{0,28},{4,0},{8,4},{12,8},{16,12},{20,16},{24,20},{28,24},{1,29},{... | collective-permute-start | bytes 1572872 | tf_op jit(solution)/shard_map/ppermute | solution.py:16
  67.2 34.2 %collective-permute-start.1 = (bf16[16,128,128]{2,1,0:T(8,128)(2,1)S(1)}, bf16[16,128,128]{2,1,0:T(8,128)(2,1)S(1)}, u32[]{:S(2)}, u32[]{:S(2)}) collective-permute-start(bf16[16,128,128]{2,1,0:T(8,128)(2,1)S(1)} %bitcast.98), channel_id=1, source_target_pairs={{0,24},{4,28},{8,0},{12,4},{16,8},{20,12},{24,16},{28,20},{1,25},{... | collective-permute-start | bytes 1572872 | tf_op jit(solution)/shard_map/ppermute | solution.py:16
  69.9 41.5 %collective-permute-start = (bf16[16,128,128]{2,1,0:T(8,128)(2,1)S(1)}, bf16[16,128,128]{2,1,0:T(8,128)(2,1)S(1)}, u32[]{:S(2)}, u32[]{:S(2)}) collective-permute-start(bf16[16,128,128]{2,1,0:T(8,128)(2,1)S(1)} %bitcast.99), channel_id=1, source_target_pairs={{0,20},{4,24},{8,28},{12,0},{16,4},{20,8},{24,12},{28,16},{1,21},{... | collective-permute-start | bytes 1572872 | tf_op jit(solution)/shard_map/ppermute | solution.py:16
  91.4 0.8 copy-start.4
  101.4 0.8 copy-start.3
  111.4 0.8 copy-start.2
Sparse Core Ops, SparseCore 0:
  17.5 46.9 all-gather.3

commit v4 on v3

--- a/solution.py
+++ b/solution.py
@@ -24,19 +24,30 @@
 GROUP = 32
 
 
-def stop_kernel(ls_ref, rs_ref, ts_ref, ok_ref, n_ref, left_ref, right_ref, acc_in_ref, acc_out_ref):
+def stop_kernel(stack_ref, map_ref, n_ref, left_ref, right_ref, acc_in_ref, acc_out_ref):
     live_count = n_ref[0]
+    slots = map_ref.shape[0]
+    left_count = left_ref.shape[0]
+    right_count = right_ref.shape[0]
+    result_count = acc_out_ref.shape[0]
 
     def per_group(g, carry):
         base = g * GROUP
         prods = []
+        targets = []
         for k in range(GROUP):
             i = base + k
-            p = jnp.dot(left_ref[ls_ref[i]], right_ref[rs_ref[i]], preferred_element_type=jnp.float32)
+            slot = stack_ref[0, i]
+            mapped = map_ref[jnp.clip(slot, 0, slots - 1)]
+            ok = (i < live_count) & (slot >= 0) & (mapped >= 0)
+            a = left_ref[jnp.clip(mapped, 0, left_count - 1)]
+            b = right_ref[jnp.clip(stack_ref[1, i], 0, right_count - 1)]
+            p = jnp.dot(a, b, preferred_element_type=jnp.float32)
             p = p.astype(jnp.bfloat16).astype(jnp.float32)
-            prods.append(jnp.where((i < live_count) & (ok_ref[i] > 0), p, 0.0))
+            prods.append(jnp.where(ok, p, 0.0))
+            targets.append(jnp.clip(stack_ref[2, i], 0, result_count - 1))
         for k in range(GROUP):
-            t = ts_ref[base + k]
+            t = targets[k]
             acc_out_ref[t] = acc_out_ref[t] + prods[k]
         return carry
 
@@ -45,19 +56,12 @@
 
 
 def run_stop(total, left, right, stack, left_map):
-    result_count = total.shape[0]
     slots = stack.shape[1]
     assert slots % GROUP == 0
-    live = stack[0] >= 0
-    mapped = jnp.take(left_map, jnp.clip(stack[0], 0, left_map.shape[0] - 1))
-    ok = (live & (mapped >= 0)).astype(jnp.int32)
-    ls = jnp.clip(mapped, 0, left.shape[0] - 1).astype(jnp.int32)
-    rs = jnp.clip(stack[1], 0, right.shape[0] - 1).astype(jnp.int32)
-    ts = jnp.clip(stack[2], 0, result_count - 1).astype(jnp.int32)
-    live_count = jnp.sum(live.astype(jnp.int32)).reshape(1)
+    live_count = jnp.sum((stack[0] >= 0).astype(jnp.int32)).reshape(1)
     full = lambda shape: pl.BlockSpec(shape, lambda *_: (0,) * len(shape))
     grid_spec = pltpu.PrefetchScalarGridSpec(
-        num_scalar_prefetch=5,
+        num_scalar_prefetch=3,
         grid=(1,),
         in_specs=[full(left.shape), full(right.shape), full(total.shape)],
         out_specs=full(total.shape),
@@ -66,8 +70,8 @@
         stop_kernel,
         grid_spec=grid_spec,
         out_shape=jax.ShapeDtypeStruct(total.shape, jnp.float32),
-        input_output_aliases={7: 0},
-    )(ls, rs, ts, ok, live_count, left, right, total)
+        input_output_aliases={5: 0},
+    )(stack.astype(jnp.int32), left_map, live_count, left, right, total)
 
 
 def on_device(a_blocks, b_blocks, a_send, b_send, triples, c_send):

time: 163 us -> 142 us (0.87)
  other arithmetic: 51.6 us -> 4.63 us
  waiting for transfers between devices: 0.72 us -> 21.4 us
  Pallas kernels: 35.8 us -> 38.2 us
    convert_element_type x4 -> x0, other arithmetic: 41.9 us -> none  [run_stop(): ok = (live & (mapped >= 0)).astype(jnp.int32)]
    all_gather x1, waiting for transfers between devices: 0.01 us -> 20.7 us  [on_device(): left_all = lax.all_gather(a_blocks[0, 0], 'col', axis=0, tiled=True)]
    min x5 -> x0, other arithmetic: 3.04 us -> none  [the longest x4 2.37 us: run_stop(): ls = jnp.clip(mapped, 0, left.shape[0] - 1).astype(jnp.int32)]
    gather x4 -> x0, local copies, waits for them, and re-layouts: 2.84 us -> none  [run_stop(): mapped = jnp.take(left_map, jnp.clip(stack[0], 0, left_map.shape[0] - 1))]
    pallas_call x4, Pallas kernels: 35.8 us -> 38.2 us  [run_stop(): pl.pallas_call(stop_kernel, grid_spec=grid_spec, out_shape=jax.ShapeDtype...]
    reshape x4, local copies, waits for them, and re-layouts: 0.33 us -> 2.45 us  [on_device(): jnp.where(picked >= 0, picked + column_base, -1).reshape(-1)]
    reduce_sum x4 -> x1, other arithmetic: 2.68 us -> 0.69 us  [run_stop(): live_count = jnp.sum((stack[0] >= 0).astype(jnp.int32)).reshape(1)]
    unnamed x17 -> x19, local copies, waits for them, and re-layouts: 3.38 us -> 4.56 us
  transfers between devices with their start and end apart: 5 -> 5, of which waited for: 0 -> 1; matrix products, arithmetic and copies ran while one was open for 32% -> 7% of each run, Pallas kernels for 16% -> 19%
where the time goes in v4:
time: 142 us; the launch traced here: 141 us
  blocking collectives  42.3 us (30%)
  Pallas kernels  38.2 us (27%)
  waiting for transfers between devices  21.4 us (15%)
  between operations  13.5 us (10%)
  starting transfers between devices  10.7 us (8%)
  local copies, waits for them, and re-layouts  10.5 us (7%)
  other arithmetic  4.63 us (3%)
    pallas_call x4, Pallas kernels, run_stop(): pl.pallas_call(stop_kernel, grid_spec=grid_spec, out_shape=jax.ShapeDtype...  38.2 us
    all_to_all x1, blocking collectives, on_device(): lax.all_to_all(outgoing, ('row', 'col'), split_axis=0, concat_axis=0, til...  32.3 us
    all_gather x1, waiting for transfers between devices, on_device(): left_all = lax.all_gather(a_blocks[0, 0], 'col', axis=0, tiled=True)  20.7 us
    all_gather x1, blocking collectives, on_device(): send_all = lax.all_gather(a_send[0, 0], 'col', axis=0, tiled=False)  10 us
    ppermute x3, starting transfers between devices, passed_along(): return lax.ppermute(value, axis, pairs)  5.45 us
    all_to_all x1, starting transfers between devices, on_device(): lax.all_to_all(right_out, 'row', split_axis=0, concat_axis=0, tiled=True)  5.22 us
    unnamed x19, local copies, waits for them, and re-layouts  4.56 us
  transfers between devices with their start and end apart: 5, of which 1 were waited for; matrix products, arithmetic and copies ran while one was open for 7% of the time, Pallas kernels for 19%

profile of v4, /device:TPU:1, one launch (start us, length us, event | category | flops | bytes accessed | tf_op | source)
XLA Modules:
  0.0 141.1 jit_solution(5938100092430247387)
XLA Ops:
  6.6 0.7 all-gather.4.cloned.1.call-update
  7.3 0.7 compare_bitcast_fusion.1
  8.2 0.7 broadcast_maximum_fusion
  9.0 0.6 gather_fusion
  9.7 0.9 select_select_fusion.1
  10.6 5.2 %all-to-all-start = ((bf16[8,2,128,128]{3,2,1,0:T(8,128)(2,1)}), bf16[8,2,128,128]{3,2,1,0:T(8,128)(2,1)S(1)}, u32[]{:S(2)}, u32[]{:S(2)}) async-start(bf16[8,2,128,128]{3,2,1,0:T(8,128)(2,1)} %select_select_fusion.1), calls=%async_computation | async-start | bytes 1048576 | tf_op jit(solution)/shard_map/all_to_all | solution.py:94
  15.8 10.0 %all-gather = s32[4,1,4,4]{3,2,1,0:T(4,128)S(1)} all-gather(s32[1,1,4,4]{3,2,1,0:T(4,128)S(1)} %copy-done.6), channel_id=2, replica_groups=mesh['row'=8,'col'=4] {'col'}, dimensions={0}, use_global_device_ids=true | all-gather | bytes 320 | tf_op jit(solution)/shard_map/all_gather | solution.py:85
  25.9 0.6 reshape.117.map_ref
  26.5 0.6 copy.41
  27.1 0.6 reshape.115.map_ref
  27.7 0.6 copy.42
  28.3 0.6 reshape.113.map_ref
  28.9 0.7 reshape.110.map_ref
  29.6 0.7 fusion.3
  30.3 2.3 %collective-permute-start.2 = (bf16[16,128,128]{2,1,0:T(8,128)(2,1)S(1)}, bf16[16,128,128]{2,1,0:T(8,128)(2,1)S(1)}, u32[]{:S(2)}, u32[]{:S(2)}) collective-permute-start(bf16[16,128,128]{2,1,0:T(8,128)(2,1)S(1)} %bitcast.44), channel_id=1, source_target_pairs={{0,28},{4,0},{8,4},{12,8},{16,12},{20,16},{24,20},{28,24},{1,29},{... | collective-permute-start | bytes 1572872 | tf_op jit(solution)/shard_map/ppermute | solution.py:16
  32.6 2.7 %collective-permute-start.1 = (bf16[16,128,128]{2,1,0:T(8,128)(2,1)S(1)}, bf16[16,128,128]{2,1,0:T(8,128)(2,1)S(1)}, u32[]{:S(2)}, u32[]{:S(2)}) collective-permute-start(bf16[16,128,128]{2,1,0:T(8,128)(2,1)S(1)} %bitcast.45), channel_id=1, source_target_pairs={{0,24},{4,28},{8,0},{12,4},{16,8},{20,12},{24,16},{28,20},{1,25},{... | collective-permute-start | bytes 1572872 | tf_op jit(solution)/shard_map/ppermute | solution.py:16
  35.3 0.5 collective-permute-start
  35.8 0.6 copy_bitcast_fusion.2
  36.4 20.7 %all-gather.4.cloned.1.call-done = bf16[1,1,64,128,128]{4,3,1,0,2:T(8,128)(2,1)} async-done(((bf16[1,1,16,128,128]{4,3,1,0,2:T(8,128)(2,1)}), bf16[1,1,64,128,128]{4,3,1,0,2:T(8,128)(2,1)}) %all-gather.4.cloned.1.call-update) | async-done | bytes 2097168 | tf_op jit(solution)/shard_map/all_gather | solution.py:84
  57.1 1.1 broadcast_in_dim.71.acc_in_ref
  58.2 9.4 %shard_map.64.acc_in_ref = f32[16,128,128]{2,1,0:T(8,128)} custom-call(s32[3,384]{1,0:T(4,128)} %bitcast.51, s32[16]{0:T(128)} %reshape.117.map_ref, s32[1]{0:T(128)} %bitcast.21.n_ref, bf16[64,128,128]{2,1,0:T(8,128)(2,1)} %bitcast.38, bf16[16,128,128]{2,1,0:T(8,128)(2,1)} %bitcast.47, ...), custom_call_target="tpu_custom_call", output_to_operand_aliasing={{}: (5, {})} | custom-call | tf_op jit(solution)/shard_map/pallas_call | solution.py:69
  67.6 0.8 copy-done.4
  68.4 8.9 %shard_map.65.acc_in_ref = f32[16,128,128]{2,1,0:T(8,128)} custom-call(s32[3,384]{1,0:T(4,128)} %bitcast.50, s32[16]{0:T(128)} %reshape.115.map_ref, s32[1]{0:T(128)} %bitcast.18.n_ref, bf16[64,128,128]{2,1,0:T(8,128)(2,1)} %bitcast.39, bf16[16,128,128]{2,1,0:T(8,128)(2,1)} %copy-done.4, ...), custom_call_target="tpu_custom_call", output_to_operand_aliasing={{}: (5, {})} | custom-call | tf_op jit(solution)/shard_map/pallas_call | solution.py:69
  77.3 0.8 copy-done.3
  78.1 8.9 %shard_map.66.acc_in_ref = f32[16,128,128]{2,1,0:T(8,128)} custom-call(s32[3,384]{1,0:T(4,128)} %get-tuple-element.37.stack_ref, s32[16]{0:T(128)} %reshape.113.map_ref, s32[1]{0:T(128)} %bitcast.15.n_ref, bf16[64,128,128]{2,1,0:T(8,128)(2,1)} %bitcast.40, bf16[16,128,128]{2,1,0:T(8,128)(2,1)} %copy-done.3, ...), custom_call_target="tpu_custom_call", output_to_operand_aliasing={{}: (5, {})} | custom-call | tf_op jit(solution)/shard_map/pallas_call | solution.py:69
  86.9 0.8 copy-done.2
  87.7 11.0 %shard_map.67 = f32[16,128,128]{2,1,0:T(8,128)} custom-call(s32[3,384]{1,0:T(4,128)} %get-tuple-element.38.stack_ref, s32[16]{0:T(128)} %reshape.110.map_ref, s32[1]{0:T(128)} %bitcast.5.n_ref, bf16[64,128,128]{2,1,0:T(8,128)(2,1)} %bitcast.41, bf16[16,128,128]{2,1,0:T(8,128)(2,1)} %copy-done.2, ...), custom_call_target="tpu_custom_call", output_to_operand_aliasing={{}: (5, {})} | custom-call | tf_op jit(solution)/shard_map/pallas_call | solution.py:69
  98.7 1.3 convert_element_type.23
  100.1 0.7 gather_fusion.1
  100.8 0.2 select_select_fusion
  101.0 32.3 %all_to_all.10 = bf16[32,128,128]{2,1,0:T(8,128)(2,1)S(1)} all-to-all(bf16[32,128,128]{2,1,0:T(8,128)(2,1)S(1)} %select_select_fusion), channel_id=1, replica_groups=mesh['row'=8,'col'=4] {'row','col'}, dimensions={0} | all-to-all | bytes 2097152 | tf_op jit(solution)/shard_map/all_to_all | solution.py:102
  133.3 1.0 copy.48
  (30 shorter events, 0.6 us)
Async XLA Ops:
  6.5 2.5 %copy-start = (bf16[1,1,16,128,128]{4,3,2,1,0:T(8,128)(2,1)S(1)}, bf16[1,1,16,128,128]{4,3,2,1,0:T(8,128)(2,1)}, u32[]{:S(2)}) copy-start(bf16[1,1,16,128,128]{4,3,2,1,0:T(8,128)(2,1)} %param.9) | copy-start | bytes 1572868
  6.5 9.3 %copy-start.6 = (s32[1,1,4,4]{3,2,1,0:T(4,128)S(1)}, s32[1,1,4,4]{3,2,1,0:T(4,128)}, u32[]{:S(2)}) copy-start(s32[1,1,4,4]{3,2,1,0:T(4,128)} %param.10) | copy-start | bytes 196
  6.5 20.0 %copy-start.5 = (s32[1,1,4,3,384]{4,2,3,1,0:T(4,128)S(1)}, s32[1,1,4,3,384]{4,2,3,1,0:T(4,128)}, u32[]{:S(2)}) copy-start(s32[1,1,4,3,384]{4,2,3,1,0:T(4,128)} %param.12) | copy-start | bytes 55300
  6.5 23.8 %copy-start.7 = (s32[1,1,32]{2,1,0:T(1,128)S(1)}, s32[1,1,32]{2,1,0:T(1,128)}, u32[]{:S(2)}) copy-start(s32[1,1,32]{2,1,0:T(1,128)} %param.13) | copy-start | bytes 388
  6.5 50.6 %all-gather.4.cloned.1.call-start = ((), (), s32[]{:S(2)}) async-start(), calls=%async_computation.2 | async-start | bytes 2621440 | tf_op jit(solution)/shard_map/all_gather | solution.py:84
  10.6 19.7 %all-to-all-start = ((bf16[8,2,128,128]{3,2,1,0:T(8,128)(2,1)}), bf16[8,2,128,128]{3,2,1,0:T(8,128)(2,1)S(1)}, u32[]{:S(2)}, u32[]{:S(2)}) async-start(bf16[8,2,128,128]{3,2,1,0:T(8,128)(2,1)} %select_select_fusion.1), calls=%async_computation | async-start | bytes 1048576 | tf_op jit(solution)/shard_map/all_to_all | solution.py:94
  30.3 27.9 %copy-start.1 = (bf16[8,2,128,128]{3,2,1,0:T(8,128)(2,1)}, bf16[8,2,128,128]{3,2,1,0:T(8,128)(2,1)S(1)}, u32[]{:S(2)}) copy-start(bf16[8,2,128,128]{3,2,1,0:T(8,128)(2,1)S(1)} %all-to-all-done) | copy-start | bytes 1572868
  30.3 37.3 %collective-permute-start.2 = (bf16[16,128,128]{2,1,0:T(8,128)(2,1)S(1)}, bf16[16,128,128]{2,1,0:T(8,128)(2,1)S(1)}, u32[]{:S(2)}, u32[]{:S(2)}) collective-permute-start(bf16[16,128,128]{2,1,0:T(8,128)(2,1)S(1)} %bitcast.44), channel_id=1, source_target_pairs={{0,28},{4,0},{8,4},{12,8},{16,12},{20,16},{24,20},{28,24},{1,29},{... | collective-permute-start | bytes 1572872 | tf_op jit(solution)/shard_map/ppermute | solution.py:16
  32.6 44.7 %collective-permute-start.1 = (bf16[16,128,128]{2,1,0:T(8,128)(2,1)S(1)}, bf16[16,128,128]{2,1,0:T(8,128)(2,1)S(1)}, u32[]{:S(2)}, u32[]{:S(2)}) collective-permute-start(bf16[16,128,128]{2,1,0:T(8,128)(2,1)S(1)} %bitcast.45), channel_id=1, source_target_pairs={{0,24},{4,28},{8,0},{12,4},{16,8},{20,12},{24,16},{28,20},{1,25},{... | collective-permute-start | bytes 1572872 | tf_op jit(solution)/shard_map/ppermute | solution.py:16
  35.3 51.7 %collective-permute-start = (bf16[16,128,128]{2,1,0:T(8,128)(2,1)S(1)}, bf16[16,128,128]{2,1,0:T(8,128)(2,1)S(1)}, u32[]{:S(2)}, u32[]{:S(2)}) collective-permute-start(bf16[16,128,128]{2,1,0:T(8,128)(2,1)S(1)} %bitcast.46), channel_id=1, source_target_pairs={{0,20},{4,24},{8,28},{12,0},{16,4},{20,8},{24,12},{28,16},{1,21},{... | collective-permute-start | bytes 1572872 | tf_op jit(solution)/shard_map/ppermute | solution.py:16
  67.6 0.8 copy-start.4
  77.3 0.8 copy-start.3
  86.9 0.8 copy-start.2
Sparse Core Ops, SparseCore 0:
  8.9 48.1 all-gather.3

commit v5 on v1

--- a/solution.py
+++ b/solution.py
@@ -86,6 +86,8 @@
         if stop_index > 0:
             left_now = passed_along(left_now, "col", -1)
             right_now = passed_along(right_now, "row", -1)
+        if stop_index > 0:
+            left_now, right_now, total = lax.optimization_barrier((left_now, right_now, total))
         total = run_stop(total, left_now, right_now, triples[0, 0, stop_index])
     result = total.astype(jnp.bfloat16)
     outgoing = bucketize(result, c_send[0, 0])

time: 134 us -> 120 us (0.90)
  waiting for transfers between devices: 24 us -> 17.1 us
  starting transfers between devices: 30.7 us -> 26.9 us
  blocking collectives: 36.2 us -> 34.5 us
    ppermute x6, waiting for transfers between devices: 11.3 us -> 4.48 us  [passed_along(): return lax.ppermute(value, axis, pairs)]
    ppermute x6, starting transfers between devices: 20.6 us -> 16.9 us  [passed_along(): return lax.ppermute(value, axis, pairs)]
    all_to_all x1, blocking collectives: 36.2 us -> 34.5 us  [on_device(): lax.all_to_all(outgoing, ('row', 'col'), split_axis=0, concat_axis=0, til...]
  transfers between devices with their start and end apart: 8 -> 8, of which waited for: 4 -> 5; matrix products, arithmetic and copies ran while one was open for 3% -> 3% of each run, Pallas kernels for 17% -> 20%
where the time goes in v5:
time: 120 us
  blocking collectives  34.5 us (29%)
  Pallas kernels  30.9 us (26%)
  starting transfers between devices  26.9 us (22%)
  waiting for transfers between devices  17.1 us (14%)
  local copies, waits for them, and re-layouts  5.39 us (4%)
  other arithmetic  5.01 us (4%)
    all_to_all x1, blocking collectives, on_device(): lax.all_to_all(outgoing, ('row', 'col'), split_axis=0, concat_axis=0, til...  34.5 us
    pallas_call x4, Pallas kernels, run_stop(): pl.pallas_call(stop_kernel, grid_spec=grid_spec, out_shape=jax.ShapeDtype...  30.9 us
    ppermute x6, starting transfers between devices, passed_along(): return lax.ppermute(value, axis, pairs)  16.9 us
    all_to_all x1, waiting for transfers between devices, on_device(): lax.all_to_all(left_out, 'col', split_axis=0, concat_axis=0, tiled=True)  7.63 us
    all_to_all x1, starting transfers between devices, on_device(): lax.all_to_all(right_out, 'row', split_axis=0, concat_axis=0, tiled=True)  5.35 us
    all_to_all x1, waiting for transfers between devices, on_device(): lax.all_to_all(right_out, 'row', split_axis=0, concat_axis=0, tiled=True)  5.01 us
    all_to_all x1, starting transfers between devices, on_device(): lax.all_to_all(left_out, 'col', split_axis=0, concat_axis=0, tiled=True)  4.59 us
    ppermute x6, waiting for transfers between devices, passed_along(): return lax.ppermute(value, axis, pairs)  4.48 us
  transfers between devices with their start and end apart: 8, of which 5 were waited for; matrix products, arithmetic and copies ran while one was open for 3% of the time, Pallas kernels for 20%

profile of v5, /device:TPU:1, one launch (start us, length us, event | category | flops | bytes accessed | tf_op | source)
XLA Modules:
  0.0 119.9 jit_solution(5524404227439211148)
XLA Ops:
  0.0 0.8 compare_bitcast_fusion.1
  0.8 0.1 copy.14
  0.9 0.1 copy.15
  1.1 0.6 gather_fusion.1
  1.8 0.9 select_select_fusion.1
  2.7 5.4 %all-to-all-start.1 = ((bf16[8,2,128,128]{3,2,1,0:T(8,128)(2,1)}), bf16[8,2,128,128]{3,2,1,0:T(8,128)(2,1)S(1)}, u32[]{:S(2)}, u32[]{:S(2)}) async-start(bf16[8,2,128,128]{3,2,1,0:T(8,128)(2,1)} %select_select_fusion.1), calls=%async_computation.1 | async-start | bytes 1048576 | tf_op jit(solution)/shard_map/all_to_all | solution.py:80
  8.1 0.1 reshape.185
  8.2 0.6 gather_fusion
  8.9 0.9 select_select_fusion.2
  9.8 5.0 %all-to-all-done.1 = bf16[8,2,128,128]{3,2,1,0:T(8,128)(2,1)S(1)} async-done(((bf16[8,2,128,128]{3,2,1,0:T(8,128)(2,1)}), bf16[8,2,128,128]{3,2,1,0:T(8,128)(2,1)S(1)}, u32[]{:S(2)}, u32[]{:S(2)}) %all-to-all-start.1) | async-done | bytes 524320 | tf_op jit(solution)/shard_map/all_to_all | solution.py:80
  14.8 4.6 %all-to-all-start = ((bf16[4,4,128,128]{3,2,1,0:T(8,128)(2,1)}), bf16[4,4,128,128]{3,2,1,0:T(8,128)(2,1)S(1)}, u32[]{:S(2)}, u32[]{:S(2)}) async-start(bf16[4,4,128,128]{3,2,1,0:T(8,128)(2,1)} %select_select_fusion.2), calls=%async_computation | async-start | bytes 1048576 | tf_op jit(solution)/shard_map/all_to_all | solution.py:77
  19.4 3.3 %collective-permute-start.1 = (bf16[16,128,128]{2,1,0:T(8,128)(2,1)S(1)}, bf16[16,128,128]{2,1,0:T(8,128)(2,1)S(1)}, u32[]{:S(2)}, u32[]{:S(2)}) collective-permute-start(bf16[16,128,128]{2,1,0:T(8,128)(2,1)S(1)} %bitcast.31), channel_id=1, source_target_pairs={{0,28},{4,0},{8,4},{12,8},{16,12},{20,16},{24,20},{28,24},{1,29},{... | collective-permute-start | bytes 1572872 | tf_op jit(solution)/shard_map/ppermute | solution.py:16
  22.7 7.6 %all-to-all-done = bf16[4,4,128,128]{3,2,1,0:T(8,128)(2,1)S(1)} async-done(((bf16[4,4,128,128]{3,2,1,0:T(8,128)(2,1)}), bf16[4,4,128,128]{3,2,1,0:T(8,128)(2,1)S(1)}, u32[]{:S(2)}, u32[]{:S(2)}) %all-to-all-start) | async-done | bytes 524320 | tf_op jit(solution)/shard_map/all_to_all | solution.py:77
  30.4 3.5 %collective-permute-start = (bf16[16,128,128]{2,1,0:T(8,128)(2,1)S(1)}, bf16[16,128,128]{2,1,0:T(8,128)(2,1)S(1)}, u32[]{:S(2)}, u32[]{:S(2)}) collective-permute-start(bf16[16,128,128]{2,1,0:T(8,128)(2,1)S(1)} %bitcast.33), channel_id=1, source_target_pairs={{0,3},{1,0},{2,1},{3,2},{4,7},{5,4},{6,5},{7,6},{8,11},{9,8},{10,9... | collective-permute-start | bytes 1572872 | tf_op jit(solution)/shard_map/ppermute | solution.py:16
  33.9 0.8 fusion.3
  34.7 1.1 broadcast_in_dim.82.acc_in_ref
  35.8 7.3 %shard_map.64.acc_in_ref = f32[16,128,128]{2,1,0:T(8,128)} custom-call(s32[384]{0:T(512)} %get-tuple-element.33.ls_ref, s32[384]{0:T(512)} %get-tuple-element.32.rs_ref, s32[384]{0:T(512)} %get-tuple-element.31.ts_ref, s32[1]{0:T(128)} %bitcast.13.n_ref, bf16[16,128,128]{2,1,0:T(8,128)(2,1)} %bitcast.34, ...), custom_call_target="tpu_custom_call", output_to_operand_aliasing={{}: (6, {})} | custom-call | tf_op jit(solution)/shard_map/pallas_call | solution.py:62
  43.1 3.8 %collective-permute-start.2 = (bf16[16,128,128]{2,1,0:T(8,128)(2,1)S(1)}, bf16[16,128,128]{2,1,0:T(8,128)(2,1)S(1)}, u32[]{:S(2)}, u32[]{:S(2)}) collective-permute-start(bf16[16,128,128]{2,1,0:T(8,128)(2,1)S(1)} %collective-permute-done.left_ref), channel_id=1, source_target_pairs={{0,3},{1,0},{2,1},{3,2},{4,7},{5,4},{6,5},{7,6},{8,11},{9,8},{10,9... | collective-permute-start | bytes 1572872 | tf_op jit(solution)/shard_map/ppermute | solution.py:16
  46.9 3.4 %collective-permute-start.3 = (bf16[16,128,128]{2,1,0:T(8,128)(2,1)S(1)}, bf16[16,128,128]{2,1,0:T(8,128)(2,1)S(1)}, u32[]{:S(2)}, u32[]{:S(2)}) collective-permute-start(bf16[16,128,128]{2,1,0:T(8,128)(2,1)S(1)} %collective-permute-done.1.right_ref), channel_id=1, source_target_pairs={{0,28},{4,0},{8,4},{12,8},{16,12},{20,16},{24,20},{28,24},{1,29},{... | collective-permute-start | bytes 1572872 | tf_op jit(solution)/shard_map/ppermute | solution.py:16
  50.3 7.2 %shard_map.65.acc_in_ref = f32[16,128,128]{2,1,0:T(8,128)} custom-call(s32[384]{0:T(512)} %get-tuple-element.30.ls_ref, s32[384]{0:T(512)} %get-tuple-element.29.rs_ref, s32[384]{0:T(512)} %get-tuple-element.28.ts_ref, s32[1]{0:T(128)} %bitcast.14.n_ref, bf16[16,128,128]{2,1,0:T(8,128)(2,1)} %copy-done.5, ...), custom_call_target="tpu_custom_call", output_to_operand_aliasing={{}: (6, {})} | custom-call | tf_op jit(solution)/shard_map/pallas_call | solution.py:62
  57.5 3.0 %collective-permute-done.3.right_ref = bf16[16,128,128]{2,1,0:T(8,128)(2,1)S(1)} collective-permute-done((bf16[16,128,128]{2,1,0:T(8,128)(2,1)S(1)}, bf16[16,128,128]{2,1,0:T(8,128)(2,1)S(1)}, u32[]{:S(2)}, u32[]{:S(2)}) %collective-permute-start.3) | collective-permute-done | bytes 524320 | tf_op jit(solution)/shard_map/ppermute | solution.py:16
  60.5 2.9 %collective-permute-start.5 = (bf16[16,128,128]{2,1,0:T(8,128)(2,1)S(1)}, bf16[16,128,128]{2,1,0:T(8,128)(2,1)S(1)}, u32[]{:S(2)}, u32[]{:S(2)}) collective-permute-start(bf16[16,128,128]{2,1,0:T(8,128)(2,1)S(1)} %collective-permute-done.3.right_ref), channel_id=1, source_target_pairs={{0,28},{4,0},{8,4},{12,8},{16,12},{20,16},{24,20},{28,24},{1,29},{... | collective-permute-start | bytes 1572872 | tf_op jit(solution)/shard_map/ppermute | solution.py:16
  63.4 9.2 %shard_map.66.acc_in_ref = f32[16,128,128]{2,1,0:T(8,128)} custom-call(s32[384]{0:T(512)} %get-tuple-element.27.ls_ref, s32[384]{0:T(512)} %get-tuple-element.38.rs_ref, s32[384]{0:T(512)} %get-tuple-element.37.ts_ref, s32[1]{0:T(128)} %bitcast.15.n_ref, bf16[16,128,128]{2,1,0:T(8,128)(2,1)} %copy-done.6, ...), custom_call_target="tpu_custom_call", output_to_operand_aliasing={{}: (6, {})} | custom-call | tf_op jit(solution)/shard_map/pallas_call | solution.py:62
  72.6 0.5 collective-permute-done.4.left_ref
  73.2 1.0 collective-permute-done.5.right_ref
  74.1 0.8 copy-done.9
  75.0 7.2 %shard_map.67 = f32[16,128,128]{2,1,0:T(8,128)} custom-call(s32[384]{0:T(512)} %get-tuple-element.36.ls_ref, s32[384]{0:T(512)} %get-tuple-element.35.rs_ref, s32[384]{0:T(512)} %get-tuple-element.34.ts_ref, s32[1]{0:T(128)} %bitcast.2.n_ref, bf16[16,128,128]{2,1,0:T(8,128)(2,1)} %copy-done.8, ...), custom_call_target="tpu_custom_call", output_to_operand_aliasing={{}: (6, {})} | custom-call | tf_op jit(solution)/shard_map/pallas_call | solution.py:62
  82.1 1.3 %convert_element_type.23 = bf16[16,128,128]{2,1,0:T(8,128)(2,1)S(1)} convert(f32[16,128,128]{2,1,0:T(8,128)} %shard_map.67) | non-fusion elementwise | flops 262144 | bytes 1572864 | tf_op jit(solution)/shard_map/convert_element_type | solution.py:92
  83.5 0.7 gather_fusion.2
  84.2 0.2 select_select_fusion
  84.4 34.5 %all_to_all.15 = bf16[32,128,128]{2,1,0:T(8,128)(2,1)S(1)} all-to-all(bf16[32,128,128]{2,1,0:T(8,128)(2,1)S(1)} %select_select_fusion), channel_id=1, replica_groups=mesh['row'=8,'col'=4] {'row','col'}, dimensions={0} | all-to-all | bytes 2097152 | tf_op jit(solution)/shard_map/all_to_all | solution.py:94
  118.9 1.0 copy.22
  (41 shorter events, 0.3 us)
Async XLA Ops:
  0.0 1.1 copy-start
  0.0 0.8 copy-start.12
  2.7 5.4 %copy-start.11 = (s32[1,1,4,4]{3,2,1,0:T(4,128)S(1)}, s32[1,1,4,4]{3,2,1,0:T(4,128)}, u32[]{:S(2)}) copy-start(s32[1,1,4,4]{3,2,1,0:T(4,128)} %param.8) | copy-start | bytes 196
  2.7 5.5 %copy-start.3 = (bf16[1,1,16,128,128]{4,3,2,1,0:T(8,128)(2,1)S(1)}, bf16[1,1,16,128,128]{4,3,2,1,0:T(8,128)(2,1)}, u32[]{:S(2)}) copy-start(bf16[1,1,16,128,128]{4,3,2,1,0:T(8,128)(2,1)} %param.6) | copy-start | bytes 1572868
  2.7 12.1 %all-to-all-start.1 = ((bf16[8,2,128,128]{3,2,1,0:T(8,128)(2,1)}), bf16[8,2,128,128]{3,2,1,0:T(8,128)(2,1)S(1)}, u32[]{:S(2)}, u32[]{:S(2)}) async-start(bf16[8,2,128,128]{3,2,1,0:T(8,128)(2,1)} %select_select_fusion.1), calls=%async_computation.1 | async-start | bytes 1048576 | tf_op jit(solution)/shard_map/all_to_all | solution.py:80
  9.8 24.1 %copy-start.10 = (s32[1,1,4,3,384]{4,2,3,1,0:T(4,128)S(1)}, s32[1,1,4,3,384]{4,2,3,1,0:T(4,128)}, u32[]{:S(2)}) copy-start(s32[1,1,4,3,384]{4,2,3,1,0:T(4,128)} %param.10) | copy-start | bytes 55300
  14.8 4.6 %copy-start.1 = (bf16[8,2,128,128]{3,2,1,0:T(8,128)(2,1)}, bf16[8,2,128,128]{3,2,1,0:T(8,128)(2,1)S(1)}, u32[]{:S(2)}) copy-start(bf16[8,2,128,128]{3,2,1,0:T(8,128)(2,1)S(1)} %all-to-all-done.1) | copy-start | bytes 1572868
  14.8 15.5 %all-to-all-start = ((bf16[4,4,128,128]{3,2,1,0:T(8,128)(2,1)}), bf16[4,4,128,128]{3,2,1,0:T(8,128)(2,1)S(1)}, u32[]{:S(2)}, u32[]{:S(2)}) async-start(bf16[4,4,128,128]{3,2,1,0:T(8,128)(2,1)} %select_select_fusion.2), calls=%async_computation | async-start | bytes 1048576 | tf_op jit(solution)/shard_map/all_to_all | solution.py:77
  19.4 23.7 %collective-permute-start.1 = (bf16[16,128,128]{2,1,0:T(8,128)(2,1)S(1)}, bf16[16,128,128]{2,1,0:T(8,128)(2,1)S(1)}, u32[]{:S(2)}, u32[]{:S(2)}) collective-permute-start(bf16[16,128,128]{2,1,0:T(8,128)(2,1)S(1)} %bitcast.31), channel_id=1, source_target_pairs={{0,28},{4,0},{8,4},{12,8},{16,12},{20,16},{24,20},{28,24},{1,29},{... | collective-permute-start | bytes 1572872 | tf_op jit(solution)/shard_map/ppermute | solution.py:16
  30.4 5.4 %copy-start.2 = (bf16[4,4,128,128]{3,2,1,0:T(8,128)(2,1)}, bf16[4,4,128,128]{3,2,1,0:T(8,128)(2,1)S(1)}, u32[]{:S(2)}) copy-start(bf16[4,4,128,128]{3,2,1,0:T(8,128)(2,1)S(1)} %all-to-all-done) | copy-start | bytes 1572868
  30.4 12.7 %collective-permute-start = (bf16[16,128,128]{2,1,0:T(8,128)(2,1)S(1)}, bf16[16,128,128]{2,1,0:T(8,128)(2,1)S(1)}, u32[]{:S(2)}, u32[]{:S(2)}) collective-permute-start(bf16[16,128,128]{2,1,0:T(8,128)(2,1)S(1)} %bitcast.33), channel_id=1, source_target_pairs={{0,3},{1,0},{2,1},{3,2},{4,7},{5,4},{6,5},{7,6},{8,11},{9,8},{10,9... | collective-permute-start | bytes 1572872 | tf_op jit(solution)/shard_map/ppermute | solution.py:16
  43.1 7.2 %copy-start.4 = (bf16[16,128,128]{2,1,0:T(8,128)(2,1)}, bf16[16,128,128]{2,1,0:T(8,128)(2,1)S(1)}, u32[]{:S(2)}) copy-start(bf16[16,128,128]{2,1,0:T(8,128)(2,1)S(1)} %collective-permute-done.1.right_ref) | copy-start | bytes 1572868
  43.1 7.2 %copy-start.5 = (bf16[16,128,128]{2,1,0:T(8,128)(2,1)}, bf16[16,128,128]{2,1,0:T(8,128)(2,1)S(1)}, u32[]{:S(2)}) copy-start(bf16[16,128,128]{2,1,0:T(8,128)(2,1)S(1)} %collective-permute-done.left_ref) | copy-start | bytes 1572868
  43.1 14.4 %collective-permute-start.2 = (bf16[16,128,128]{2,1,0:T(8,128)(2,1)S(1)}, bf16[16,128,128]{2,1,0:T(8,128)(2,1)S(1)}, u32[]{:S(2)}, u32[]{:S(2)}) collective-permute-start(bf16[16,128,128]{2,1,0:T(8,128)(2,1)S(1)} %collective-permute-done.left_ref), channel_id=1, source_target_pairs={{0,3},{1,0},{2,1},{3,2},{4,7},{5,4},{6,5},{7,6},{8,11},{9,8},{10,9... | collective-permute-start | bytes 1572872 | tf_op jit(solution)/shard_map/ppermute | solution.py:16
  46.9 13.6 %collective-permute-start.3 = (bf16[16,128,128]{2,1,0:T(8,128)(2,1)S(1)}, bf16[16,128,128]{2,1,0:T(8,128)(2,1)S(1)}, u32[]{:S(2)}, u32[]{:S(2)}) collective-permute-start(bf16[16,128,128]{2,1,0:T(8,128)(2,1)S(1)} %collective-permute-done.1.right_ref), channel_id=1, source_target_pairs={{0,28},{4,0},{8,4},{12,8},{16,12},{20,16},{24,20},{28,24},{1,29},{... | collective-permute-start | bytes 1572872 | tf_op jit(solution)/shard_map/ppermute | solution.py:16
  50.3 13.1 %copy-start.13 = (s32[1,1,32]{2,1,0:T(1,128)S(1)}, s32[1,1,32]{2,1,0:T(1,128)}, u32[]{:S(2)}) copy-start(s32[1,1,32]{2,1,0:T(1,128)} %param.11) | copy-start | bytes 388
  57.5 5.9 %copy-start.6 = (bf16[16,128,128]{2,1,0:T(8,128)(2,1)}, bf16[16,128,128]{2,1,0:T(8,128)(2,1)S(1)}, u32[]{:S(2)}) copy-start(bf16[16,128,128]{2,1,0:T(8,128)(2,1)S(1)} %collective-permute-done.2.left_ref) | copy-start | bytes 1572868
  60.5 3.0 %copy-start.7 = (bf16[16,128,128]{2,1,0:T(8,128)(2,1)}, bf16[16,128,128]{2,1,0:T(8,128)(2,1)S(1)}, u32[]{:S(2)}) copy-start(bf16[16,128,128]{2,1,0:T(8,128)(2,1)S(1)} %collective-permute-done.3.right_ref) | copy-start | bytes 1572868
  60.5 12.7 %collective-permute-start.4 = (bf16[16,128,128]{2,1,0:T(8,128)(2,1)S(1)}, bf16[16,128,128]{2,1,0:T(8,128)(2,1)S(1)}, u32[]{:S(2)}, u32[]{:S(2)}) collective-permute-start(bf16[16,128,128]{2,1,0:T(8,128)(2,1)S(1)} %collective-permute-done.2.left_ref), channel_id=1, source_target_pairs={{0,3},{1,0},{2,1},{3,2},{4,7},{5,4},{6,5},{7,6},{8,11},{9,8},{10,9... | collective-permute-start | bytes 1572872 | tf_op jit(solution)/shard_map/ppermute | solution.py:16
  60.5 13.6 %collective-permute-start.5 = (bf16[16,128,128]{2,1,0:T(8,128)(2,1)S(1)}, bf16[16,128,128]{2,1,0:T(8,128)(2,1)S(1)}, u32[]{:S(2)}, u32[]{:S(2)}) collective-permute-start(bf16[16,128,128]{2,1,0:T(8,128)(2,1)S(1)} %collective-permute-done.3.right_ref), channel_id=1, source_target_pairs={{0,28},{4,0},{8,4},{12,8},{16,12},{20,16},{24,20},{28,24},{1,29},{... | collective-permute-start | bytes 1572872 | tf_op jit(solution)/shard_map/ppermute | solution.py:16
  73.2 1.0 copy-start.8
  74.1 0.8 copy-start.9

commit v6 on v4

--- a/solution.py
+++ b/solution.py
@@ -80,23 +80,32 @@
     count = rows_n * cols_n
     result_count = count // 2
     edge = a_blocks.shape[-1]
-    held = a_blocks.shape[2]
-    left_all = lax.all_gather(a_blocks[0, 0], "col", axis=0, tiled=True)
-    send_all = lax.all_gather(a_send[0, 0], "col", axis=0, tiled=False)
+    left_out = bucketize(a_blocks[0, 0], a_send[0, 0])
+    cap = left_out.shape[1]
     col_at = lax.axis_index("col")
-    column_base = (jnp.arange(cols_n, dtype=jnp.int32) * held)[:, None]
+    pieces = [jnp.take(left_out, col_at, axis=0)]
+    for shift in range(1, cols_n):
+        bucket = jnp.take(left_out, (col_at + shift) % cols_n, axis=0)
+        pieces.append(passed_along(bucket, "col", shift))
+    left_home = jnp.concatenate(pieces, axis=0)
+    slot = jnp.arange(cols_n * cap, dtype=jnp.int32)
     left_maps = []
     for stop_index in range(STOPS):
         owner = (col_at + stop_index) % cols_n
-        picked = jnp.take(send_all, owner, axis=1)
-        left_maps.append(jnp.where(picked >= 0, picked + column_base, -1).reshape(-1).astype(jnp.int32))
+        left_maps.append((((owner - slot // cap) % cols_n) * cap + slot % cap).astype(jnp.int32))
     right_out = bucketize(b_blocks[0, 0], b_send[0, 0])
     right_home = lax.all_to_all(right_out, "row", split_axis=0, concat_axis=0, tiled=True)
     right_home = right_home.reshape(-1, edge, edge)
     total = jnp.zeros((result_count, edge, edge), jnp.float32)
-    rights = [right_home] + [passed_along(right_home, "row", -s) for s in range(1, STOPS)]
+    left_now = left_home
+    right_now = right_home
     for stop_index in range(STOPS):
-        total = run_stop(total, left_all, rights[stop_index], triples[0, 0, stop_index], left_maps[stop_index])
+        if stop_index > 0:
+            left_now = passed_along(left_now, "col", -1)
+            right_now = passed_along(right_now, "row", -1)
+        if stop_index > 0:
+            left_now, right_now, total = lax.optimization_barrier((left_now, right_now, total))
+        total = run_stop(total, left_now, right_now, triples[0, 0, stop_index], left_maps[stop_index])
     result = total.astype(jnp.bfloat16)
     outgoing = bucketize(result, c_send[0, 0])
     arrived = lax.all_to_all(outgoing, ("row", "col"), split_axis=0, concat_axis=0, tiled=True)

time: 142 us -> 114 us (0.80)
  between operations: 13.5 us -> 0.25 us
  waiting for transfers between devices: 21.4 us -> 9.01 us
  blocking collectives: 42.3 us -> 31.7 us
  starting transfers between devices: 10.7 us -> 18.5 us
  local copies, waits for them, and re-layouts: 10.5 us -> 7.93 us
  other arithmetic: 4.63 us -> 6.61 us
  Pallas kernels: 38.2 us -> 39.7 us
    all_gather x1 -> x0, waiting for transfers between devices: 20.7 us -> none  [on_device(): left_all = lax.all_gather(a_blocks[0, 0], 'col', axis=0, tiled=True)]
    all_gather x1 -> x0, blocking collectives: 10 us -> none  [on_device(): send_all = lax.all_gather(a_send[0, 0], 'col', axis=0, tiled=False)]
    ppermute x3 -> x9, waiting for transfers between devices: 0.01 us -> 9 us  [passed_along(): return lax.ppermute(value, axis, pairs)]
    ppermute x3 -> x9, starting transfers between devices: 5.45 us -> 13.1 us  [passed_along(): return lax.ppermute(value, axis, pairs)]
    reshape x4 -> x0, local copies, waits for them, and re-layouts: 2.45 us -> none  [on_device(): jnp.where(picked >= 0, picked + column_base, -1).reshape(-1)]
    add x0 -> x4, other arithmetic: none -> 2.35 us  [on_device(): (owner - slot // cap) % cols_n * cap + slot % cap]
    pallas_call x4, Pallas kernels: 38.2 us -> 39.7 us  [run_stop(): pl.pallas_call(stop_kernel, grid_spec=grid_spec, out_shape=jax.ShapeDtype...]
    unnamed x19 -> x33, local copies, waits for them, and re-layouts: 4.56 us -> 4.35 us
  transfers between devices with their start and end apart: 5 -> 10, of which waited for: 1 -> 3; matrix products, arithmetic and copies ran while one was open for 7% -> 7% of each run, Pallas kernels for 19% -> 27%
where the time goes in v6:
time: 114 us
  Pallas kernels  39.7 us (35%)
  blocking collectives  31.7 us (28%)
  starting transfers between devices  18.5 us (16%)
  waiting for transfers between devices  9.01 us (8%)
  local copies, waits for them, and re-layouts  7.93 us (7%)
  other arithmetic  6.61 us (6%)
    pallas_call x4, Pallas kernels, run_stop(): pl.pallas_call(stop_kernel, grid_spec=grid_spec, out_shape=jax.ShapeDtype...  39.7 us
    all_to_all x1, blocking collectives, on_device(): lax.all_to_all(outgoing, ('row', 'col'), split_axis=0, concat_axis=0, til...  31.7 us
    ppermute x9, starting transfers between devices, passed_along(): return lax.ppermute(value, axis, pairs)  13.1 us
    ppermute x9, waiting for transfers between devices, passed_along(): return lax.ppermute(value, axis, pairs)  9 us
    all_to_all x1, starting transfers between devices, on_device(): lax.all_to_all(right_out, 'row', split_axis=0, concat_axis=0, tiled=True)  5.35 us
    unnamed x33, local copies, waits for them, and re-layouts  4.35 us
    add x4, other arithmetic, on_device(): (owner - slot // cap) % cols_n * cap + slot % cap  2.35 us
  transfers between devices with their start and end apart: 10, of which 3 were waited for; matrix products, arithmetic and copies ran while one was open for 7% of the time, Pallas kernels for 27%

profile of v6, /device:TPU:1, one launch (start us, length us, event | category | flops | bytes accessed | tf_op | source)
XLA Modules:
  0.0 113.7 jit_solution(1133918494593525710)
XLA Ops:
  0.0 0.8 compare_bitcast_fusion.1
  1.1 0.6 gather_fusion.1
  1.8 0.9 select_select_fusion.1
  2.7 5.4 %all-to-all-start = ((bf16[8,2,128,128]{3,2,1,0:T(8,128)(2,1)}), bf16[8,2,128,128]{3,2,1,0:T(8,128)(2,1)S(1)}, u32[]{:S(2)}, u32[]{:S(2)}) async-start(bf16[8,2,128,128]{3,2,1,0:T(8,128)(2,1)} %select_select_fusion.1), calls=%async_computation | async-start | bytes 1048576 | tf_op jit(solution)/shard_map/all_to_all | solution.py:97
  8.2 0.6 gather_fusion
  9.1 1.3 %collective-permute-start = (bf16[4,128,128]{2,1,0:T(8,128)(2,1)S(1)}, bf16[4,128,128]{2,1,0:T(8,128)(2,1)S(1)}, u32[]{:S(2)}, u32[]{:S(2)}) collective-permute-start(bf16[4,128,128]{2,1,0:T(8,128)(2,1)S(1)} %get-tuple-element.42), channel_id=1, source_target_pairs={{0,1},{1,2},{2,3},{3,0},{4,5},{5,6},{6,7},{7,4},{8,9},{9,10},{10,1... | collective-permute-start | bytes 393224 | tf_op jit(solution)/shard_map/ppermute | solution.py:16
  10.5 2.3 %collective-permute-start.1 = (bf16[4,128,128]{2,1,0:T(8,128)(2,1)S(1)}, bf16[4,128,128]{2,1,0:T(8,128)(2,1)S(1)}, u32[]{:S(2)}, u32[]{:S(2)}) collective-permute-start(bf16[4,128,128]{2,1,0:T(8,128)(2,1)S(1)} %get-tuple-element.41), channel_id=1, source_target_pairs={{0,2},{1,3},{2,0},{3,1},{4,6},{5,7},{6,4},{7,5},{8,10},{9,11},{10,... | collective-permute-start | bytes 393224 | tf_op jit(solution)/shard_map/ppermute | solution.py:16
  12.8 1.1 collective-permute-start.2
  13.9 2.4 %collective-permute-done = bf16[4,128,128]{2,1,0:T(8,128)(2,1)S(1)} collective-permute-done((bf16[4,128,128]{2,1,0:T(8,128)(2,1)S(1)}, bf16[4,128,128]{2,1,0:T(8,128)(2,1)S(1)}, u32[]{:S(2)}, u32[]{:S(2)}) %collective-permute-start) | collective-permute-done | bytes 131104 | tf_op jit(solution)/shard_map/ppermute | solution.py:16
  16.3 5.8 %collective-permute-done.1 = bf16[4,128,128]{2,1,0:T(8,128)(2,1)S(1)} collective-permute-done((bf16[4,128,128]{2,1,0:T(8,128)(2,1)S(1)}, bf16[4,128,128]{2,1,0:T(8,128)(2,1)S(1)}, u32[]{:S(2)}, u32[]{:S(2)}) %collective-permute-start.1) | collective-permute-done | bytes 131104 | tf_op jit(solution)/shard_map/ppermute | solution.py:16
  22.2 3.9 %collective-permute-start.3 = (bf16[16,128,128]{2,1,0:T(8,128)(2,1)S(1)}, bf16[16,128,128]{2,1,0:T(8,128)(2,1)S(1)}, u32[]{:S(2)}, u32[]{:S(2)}) collective-permute-start(bf16[16,128,128]{2,1,0:T(8,128)(2,1)S(1)} %pad_maximum_fusion.left_ref), channel_id=1, source_target_pairs={{0,3},{1,0},{2,1},{3,2},{4,7},{5,4},{6,5},{7,6},{8,11},{9,8},{10,9... | collective-permute-start | bytes 1572872 | tf_op jit(solution)/shard_map/ppermute | solution.py:16
  26.1 1.1 collective-permute-start.4
  27.2 0.6 copy.35
  27.8 0.6 fusion.7.map_ref
  28.4 0.7 fusion.3
  29.1 1.1 broadcast_in_dim.91.acc_in_ref
  30.2 10.6 %shard_map.64.acc_in_ref = f32[16,128,128]{2,1,0:T(8,128)} custom-call(s32[3,384]{1,0:T(4,128)} %bitcast.55, s32[16]{0:T(128)} %fusion.7.map_ref, s32[1]{0:T(128)} %bitcast.18.n_ref, bf16[16,128,128]{2,1,0:T(8,128)(2,1)} %copy-done.2, bf16[16,128,128]{2,1,0:T(8,128)(2,1)} %bitcast.49, ...), custom_call_target="tpu_custom_call", output_to_operand_aliasing={{}: (5, {})} | custom-call | tf_op jit(solution)/shard_map/pallas_call | solution.py:69
  40.9 1.7 %collective-permute-start.6 = (bf16[16,128,128]{2,1,0:T(8,128)(2,1)S(1)}, bf16[16,128,128]{2,1,0:T(8,128)(2,1)S(1)}, u32[]{:S(2)}, u32[]{:S(2)}) collective-permute-start(bf16[16,128,128]{2,1,0:T(8,128)(2,1)S(1)} %collective-permute-done.4.right_ref), channel_id=1, source_target_pairs={{0,28},{4,0},{8,4},{12,8},{16,12},{20,16},{24,20},{28,24},{1,29},{... | collective-permute-start | bytes 1572872 | tf_op jit(solution)/shard_map/ppermute | solution.py:16
  42.6 0.6 copy.34
  43.2 0.6 copy.33
  43.8 0.6 copy.36
  45.5 0.6 fusion.5.map_ref
  46.1 9.5 %shard_map.65.acc_in_ref = f32[16,128,128]{2,1,0:T(8,128)} custom-call(s32[3,384]{1,0:T(4,128)} %bitcast.56, s32[16]{0:T(128)} %fusion.9.map_ref, s32[1]{0:T(128)} %bitcast.20.n_ref, bf16[16,128,128]{2,1,0:T(8,128)(2,1)} %copy-done.3, bf16[16,128,128]{2,1,0:T(8,128)(2,1)} %copy-done.4, ...), custom_call_target="tpu_custom_call", output_to_operand_aliasing={{}: (5, {})} | custom-call | tf_op jit(solution)/shard_map/pallas_call | solution.py:69
  55.7 1.7 %collective-permute-start.8 = (bf16[16,128,128]{2,1,0:T(8,128)(2,1)S(1)}, bf16[16,128,128]{2,1,0:T(8,128)(2,1)S(1)}, u32[]{:S(2)}, u32[]{:S(2)}) collective-permute-start(bf16[16,128,128]{2,1,0:T(8,128)(2,1)S(1)} %collective-permute-done.6.right_ref), channel_id=1, source_target_pairs={{0,28},{4,0},{8,4},{12,8},{16,12},{20,16},{24,20},{28,24},{1,29},{... | collective-permute-start | bytes 1572872 | tf_op jit(solution)/shard_map/ppermute | solution.py:16
  57.4 10.6 %shard_map.66.acc_in_ref = f32[16,128,128]{2,1,0:T(8,128)} custom-call(s32[3,384]{1,0:T(4,128)} %bitcast.54, s32[16]{0:T(128)} %fusion.11.map_ref, s32[1]{0:T(128)} %bitcast.22.n_ref, bf16[16,128,128]{2,1,0:T(8,128)(2,1)} %copy-done.5, bf16[16,128,128]{2,1,0:T(8,128)(2,1)} %copy-done.6, ...), custom_call_target="tpu_custom_call", output_to_operand_aliasing={{}: (5, {})} | custom-call | tf_op jit(solution)/shard_map/pallas_call | solution.py:69
  68.0 0.7 collective-permute-done.7.left_ref
  68.8 0.8 copy-done.7
  69.7 9.0 %shard_map.67 = f32[16,128,128]{2,1,0:T(8,128)} custom-call(s32[3,384]{1,0:T(4,128)} %bitcast.53, s32[16]{0:T(128)} %fusion.5.map_ref, s32[1]{0:T(128)} %bitcast.3.n_ref, bf16[16,128,128]{2,1,0:T(8,128)(2,1)} %copy-done.7, bf16[16,128,128]{2,1,0:T(8,128)(2,1)} %copy-done.8, f32[16,128,128]{2,1,0:T(8,128)} %shard_map.66.acc_in_ref), custom_call_target="tpu_custom_call", output_to_operand_aliasing={{}: (5, {})} | custom-call | tf_op jit(solution)/shard_map/pallas_call | solution.py:69
  78.7 1.3 %convert_element_type.23 = bf16[16,128,128]{2,1,0:T(8,128)(2,1)S(1)} convert(f32[16,128,128]{2,1,0:T(8,128)} %shard_map.67) | non-fusion elementwise | flops 262144 | bytes 1572864 | tf_op jit(solution)/shard_map/convert_element_type | solution.py:109
  80.0 0.7 gather_fusion.2
  81.0 31.7 %all_to_all.10 = bf16[32,128,128]{2,1,0:T(8,128)(2,1)S(1)} all-to-all(bf16[32,128,128]{2,1,0:T(8,128)(2,1)S(1)} %select_select_fusion), channel_id=1, replica_groups=mesh['row'=8,'col'=4] {'row','col'}, dimensions={0} | all-to-all | bytes 2097152 | tf_op jit(solution)/shard_map/all_to_all | solution.py:111
  112.8 1.0 copy.42
  (56 shorter events, 2.5 us)
Async XLA Ops:
  0.0 1.1 copy-start
  0.0 0.8 copy-start.12
  2.7 5.4 %copy-start.11 = (s32[1,1,4,4]{3,2,1,0:T(4,128)S(1)}, s32[1,1,4,4]{3,2,1,0:T(4,128)}, u32[]{:S(2)}) copy-start(s32[1,1,4,4]{3,2,1,0:T(4,128)} %param.10) | copy-start | bytes 196
  2.7 5.5 %copy-start.9 = (bf16[1,1,16,128,128]{4,3,2,1,0:T(8,128)(2,1)S(1)}, bf16[1,1,16,128,128]{4,3,2,1,0:T(8,128)(2,1)}, u32[]{:S(2)}) copy-start(bf16[1,1,16,128,128]{4,3,2,1,0:T(8,128)(2,1)} %param.8) | copy-start | bytes 1572868
  2.7 23.4 %all-to-all-start = ((bf16[8,2,128,128]{3,2,1,0:T(8,128)(2,1)}), bf16[8,2,128,128]{3,2,1,0:T(8,128)(2,1)S(1)}, u32[]{:S(2)}, u32[]{:S(2)}) async-start(bf16[8,2,128,128]{3,2,1,0:T(8,128)(2,1)} %select_select_fusion.1), calls=%async_computation | async-start | bytes 1048576 | tf_op jit(solution)/shard_map/all_to_all | solution.py:97
  9.1 7.1 %collective-permute-start = (bf16[4,128,128]{2,1,0:T(8,128)(2,1)S(1)}, bf16[4,128,128]{2,1,0:T(8,128)(2,1)S(1)}, u32[]{:S(2)}, u32[]{:S(2)}) collective-permute-start(bf16[4,128,128]{2,1,0:T(8,128)(2,1)S(1)} %get-tuple-element.42), channel_id=1, source_target_pairs={{0,1},{1,2},{2,3},{3,0},{4,5},{5,6},{6,7},{7,4},{8,9},{9,10},{10,1... | collective-permute-start | bytes 393224 | tf_op jit(solution)/shard_map/ppermute | solution.py:16
  10.5 11.6 %collective-permute-start.1 = (bf16[4,128,128]{2,1,0:T(8,128)(2,1)S(1)}, bf16[4,128,128]{2,1,0:T(8,128)(2,1)S(1)}, u32[]{:S(2)}, u32[]{:S(2)}) collective-permute-start(bf16[4,128,128]{2,1,0:T(8,128)(2,1)S(1)} %get-tuple-element.41), channel_id=1, source_target_pairs={{0,2},{1,3},{2,0},{3,1},{4,6},{5,7},{6,4},{7,5},{8,10},{9,11},{10,... | collective-permute-start | bytes 393224 | tf_op jit(solution)/shard_map/ppermute | solution.py:16
  12.8 9.3 %collective-permute-start.2 = (bf16[4,128,128]{2,1,0:T(8,128)(2,1)S(1)}, bf16[4,128,128]{2,1,0:T(8,128)(2,1)S(1)}, u32[]{:S(2)}, u32[]{:S(2)}) collective-permute-start(bf16[4,128,128]{2,1,0:T(8,128)(2,1)S(1)} %get-tuple-element.40), channel_id=1, source_target_pairs={{0,3},{1,0},{2,1},{3,2},{4,7},{5,4},{6,5},{7,6},{8,11},{9,8},{10,9... | collective-permute-start | bytes 393224 | tf_op jit(solution)/shard_map/ppermute | solution.py:16
  22.1 5.0 %copy-start.10 = (s32[1,1,4,3,384]{4,2,3,1,0:T(4,128)S(1)}, s32[1,1,4,3,384]{4,2,3,1,0:T(4,128)}, u32[]{:S(2)}) copy-start(s32[1,1,4,3,384]{4,2,3,1,0:T(4,128)} %param.12) | copy-start | bytes 55300
  22.2 8.0 %copy-start.2 = (bf16[16,128,128]{2,1,0:T(8,128)(2,1)}, bf16[16,128,128]{2,1,0:T(8,128)(2,1)S(1)}, u32[]{:S(2)}) copy-start(bf16[16,128,128]{2,1,0:T(8,128)(2,1)S(1)} %pad_maximum_fusion.left_ref) | copy-start | bytes 1572868
  22.2 18.6 %collective-permute-start.3 = (bf16[16,128,128]{2,1,0:T(8,128)(2,1)S(1)}, bf16[16,128,128]{2,1,0:T(8,128)(2,1)S(1)}, u32[]{:S(2)}, u32[]{:S(2)}) collective-permute-start(bf16[16,128,128]{2,1,0:T(8,128)(2,1)S(1)} %pad_maximum_fusion.left_ref), channel_id=1, source_target_pairs={{0,3},{1,0},{2,1},{3,2},{4,7},{5,4},{6,5},{7,6},{8,11},{9,8},{10,9... | collective-permute-start | bytes 1572872 | tf_op jit(solution)/shard_map/ppermute | solution.py:16
  26.1 4.1 %copy-start.1 = (bf16[8,2,128,128]{3,2,1,0:T(8,128)(2,1)}, bf16[8,2,128,128]{3,2,1,0:T(8,128)(2,1)S(1)}, u32[]{:S(2)}) copy-start(bf16[8,2,128,128]{3,2,1,0:T(8,128)(2,1)S(1)} %all-to-all-done) | copy-start | bytes 1572868
  26.1 14.7 %collective-permute-start.4 = (bf16[16,128,128]{2,1,0:T(8,128)(2,1)S(1)}, bf16[16,128,128]{2,1,0:T(8,128)(2,1)S(1)}, u32[]{:S(2)}, u32[]{:S(2)}) collective-permute-start(bf16[16,128,128]{2,1,0:T(8,128)(2,1)S(1)} %bitcast.48), channel_id=1, source_target_pairs={{0,28},{4,0},{8,4},{12,8},{16,12},{20,16},{24,20},{28,24},{1,29},{... | collective-permute-start | bytes 1572872 | tf_op jit(solution)/shard_map/ppermute | solution.py:16
  40.8 5.3 %copy-start.3 = (bf16[16,128,128]{2,1,0:T(8,128)(2,1)}, bf16[16,128,128]{2,1,0:T(8,128)(2,1)S(1)}, u32[]{:S(2)}) copy-start(bf16[16,128,128]{2,1,0:T(8,128)(2,1)S(1)} %collective-permute-done.3.left_ref) | copy-start | bytes 1572868
  40.8 5.3 %copy-start.4 = (bf16[16,128,128]{2,1,0:T(8,128)(2,1)}, bf16[16,128,128]{2,1,0:T(8,128)(2,1)S(1)}, u32[]{:S(2)}) copy-start(bf16[16,128,128]{2,1,0:T(8,128)(2,1)S(1)} %collective-permute-done.4.right_ref) | copy-start | bytes 1572868
  40.8 14.8 %collective-permute-start.5 = (bf16[16,128,128]{2,1,0:T(8,128)(2,1)S(1)}, bf16[16,128,128]{2,1,0:T(8,128)(2,1)S(1)}, u32[]{:S(2)}, u32[]{:S(2)}) collective-permute-start(bf16[16,128,128]{2,1,0:T(8,128)(2,1)S(1)} %collective-permute-done.3.left_ref), channel_id=1, source_target_pairs={{0,3},{1,0},{2,1},{3,2},{4,7},{5,4},{6,5},{7,6},{8,11},{9,8},{10,9... | collective-permute-start | bytes 1572872 | tf_op jit(solution)/shard_map/ppermute | solution.py:16
  40.9 14.7 %collective-permute-start.6 = (bf16[16,128,128]{2,1,0:T(8,128)(2,1)S(1)}, bf16[16,128,128]{2,1,0:T(8,128)(2,1)S(1)}, u32[]{:S(2)}, u32[]{:S(2)}) collective-permute-start(bf16[16,128,128]{2,1,0:T(8,128)(2,1)S(1)} %collective-permute-done.4.right_ref), channel_id=1, source_target_pairs={{0,28},{4,0},{8,4},{12,8},{16,12},{20,16},{24,20},{28,24},{1,29},{... | collective-permute-start | bytes 1572872 | tf_op jit(solution)/shard_map/ppermute | solution.py:16
  46.1 11.3 %copy-start.13 = (s32[1,1,32]{2,1,0:T(1,128)S(1)}, s32[1,1,32]{2,1,0:T(1,128)}, u32[]{:S(2)}) copy-start(s32[1,1,32]{2,1,0:T(1,128)} %param.13) | copy-start | bytes 388
  55.6 1.8 %copy-start.5 = (bf16[16,128,128]{2,1,0:T(8,128)(2,1)}, bf16[16,128,128]{2,1,0:T(8,128)(2,1)S(1)}, u32[]{:S(2)}) copy-start(bf16[16,128,128]{2,1,0:T(8,128)(2,1)S(1)} %collective-permute-done.5.left_ref) | copy-start | bytes 1572868
  55.6 1.8 %copy-start.6 = (bf16[16,128,128]{2,1,0:T(8,128)(2,1)}, bf16[16,128,128]{2,1,0:T(8,128)(2,1)S(1)}, u32[]{:S(2)}) copy-start(bf16[16,128,128]{2,1,0:T(8,128)(2,1)S(1)} %collective-permute-done.6.right_ref) | copy-start | bytes 1572868
  55.6 13.1 %collective-permute-start.7 = (bf16[16,128,128]{2,1,0:T(8,128)(2,1)S(1)}, bf16[16,128,128]{2,1,0:T(8,128)(2,1)S(1)}, u32[]{:S(2)}, u32[]{:S(2)}) collective-permute-start(bf16[16,128,128]{2,1,0:T(8,128)(2,1)S(1)} %collective-permute-done.5.left_ref), channel_id=1, source_target_pairs={{0,3},{1,0},{2,1},{3,2},{4,7},{5,4},{6,5},{7,6},{8,11},{9,8},{10,9... | collective-permute-start | bytes 1572872 | tf_op jit(solution)/shard_map/ppermute | solution.py:16
  55.7 13.1 %collective-permute-start.8 = (bf16[16,128,128]{2,1,0:T(8,128)(2,1)S(1)}, bf16[16,128,128]{2,1,0:T(8,128)(2,1)S(1)}, u32[]{:S(2)}, u32[]{:S(2)}) collective-permute-start(bf16[16,128,128]{2,1,0:T(8,128)(2,1)S(1)} %collective-permute-done.6.right_ref), channel_id=1, source_target_pairs={{0,28},{4,0},{8,4},{12,8},{16,12},{20,16},{24,20},{28,24},{1,29},{... | collective-permute-start | bytes 1572872 | tf_op jit(solution)/shard_map/ppermute | solution.py:16
  68.8 0.8 copy-start.7
  68.8 1.0 copy-start.8

commit v7 on v6

v7 whole, which is shorter than its diff:
```python
import functools

import jax
import jax.numpy as jnp
from jax import lax
from jax.experimental import pallas as pl
from jax.experimental.pallas import tpu as pltpu
from jax.sharding import PartitionSpec as P

STOPS = 4


def passed_along(value, axis, steps):
    count = lax.axis_size(axis)
    pairs = [(source, (source + steps) % count) for source in range(count)]
    return lax.ppermute(value, axis, pairs)


def bucketize(blocks, index):
    picked = jnp.take(blocks, jnp.maximum(index, 0), axis=0)
    return jnp.where((index >= 0)[..., None, None], picked, jnp.zeros_like(picked))


GROUP = 32


def stop_kernel(stop, first, last, stack_ref, map_ref, n_ref, left_ref, right_ref, *refs):
    if first:
        acc_out_ref, acc_ref = refs[0], refs[-1]
    else:
        acc_in_ref, acc_out_ref, acc_ref = refs[0], refs[1], refs[-1]
    live_count = n_ref[stop]
    slots = map_ref.shape[1]
    left_count = left_ref.shape[0]
    right_count = right_ref.shape[0]
    result_count = acc_out_ref.shape[0]

    def per_group(g, carry):
        base = g * GROUP
        prods = []
        targets = []
        for k in range(GROUP):
            i = base + k
            slot = stack_ref[stop, 0, i]
            mapped = map_ref[stop, jnp.clip(slot, 0, slots - 1)]
            ok = (i < live_count) & (slot >= 0) & (mapped >= 0)
            a = left_ref[jnp.clip(mapped, 0, left_count - 1)]
            b = right_ref[jnp.clip(stack_ref[stop, 1, i], 0, right_count - 1)]
            p = jnp.dot(a, b, preferred_element_type=jnp.float32)
            p = p.astype(jnp.bfloat16).astype(jnp.float32)
            prods.append(jnp.where(ok, p, 0.0))
            targets.append(jnp.clip(stack_ref[stop, 2, i], 0, result_count - 1))
        for k in range(GROUP):
            t = targets[k]
            acc_ref[t] = acc_ref[t] + prods[k]
        return carry

    if first:
        acc_ref[...] = jnp.zeros(acc_ref.shape, jnp.float32)
    else:
        acc_ref[...] = acc_in_ref[...]
    lax.fori_loop(0, (live_count + GROUP - 1) // GROUP, per_group, 0)
    acc_out_ref[...] = acc_ref[...].astype(acc_out_ref.dtype)


def run_stop(total, left, right, stacks, left_maps, live_counts, stop, last, result_shape):
    assert stacks.shape[-1] % GROUP == 0
    first = total is None
    full = lambda shape: pl.BlockSpec(shape, lambda *_: (0,) * len(shape))
    in_specs = [full(left.shape), full(right.shape)]
    operands = [stacks, left_maps, live_counts, left, right]
    aliases = {}
    if not first:
        in_specs.append(full(result_shape))
        operands.append(total)
        if not last:
            aliases = {5: 0}
    scratch = [pltpu.VMEM(result_shape, jnp.float32)]
    out_dtype = jnp.bfloat16 if last else jnp.float32
    grid_spec = pltpu.PrefetchScalarGridSpec(
        num_scalar_prefetch=3,
        grid=(1,),
        in_specs=in_specs,
        out_specs=full(result_shape),
        scratch_shapes=scratch,
    )
    return pl.pallas_call(
        functools.partial(stop_kernel, stop, first, last),
        grid_spec=grid_spec,
        out_shape=jax.ShapeDtypeStruct(result_shape, out_dtype),
        input_output_aliases=aliases,
    )(*operands)


def on_device(a_blocks, b_blocks, a_send, b_send, triples, c_send):
    rows_n = lax.axis_size("row")
    cols_n = lax.axis_size("col")
    count = rows_n * cols_n
    result_count = count // 2
    edge = a_blocks.shape[-1]
    left_out = bucketize(a_blocks[0, 0], a_send[0, 0])
    cap = left_out.shape[1]
    col_at = lax.axis_index("col")
    pieces = [jnp.take(left_out, col_at, axis=0)]
    for shift in range(1, cols_n):
        bucket = jnp.take(left_out, (col_at + shift) % cols_n, axis=0)
        pieces.append(passed_along(bucket, "col", shift))
    left_home = jnp.concatenate(pieces, axis=0)
    slot = jnp.arange(cols_n * cap, dtype=jnp.int32)[None, :]
    owner = (col_at + jnp.arange(STOPS, dtype=jnp.int32)[:, None]) % cols_n
    left_maps = (((owner - slot // cap) % cols_n) * cap + slot % cap).astype(jnp.int32)
    stacks = triples[0, 0].astype(jnp.int32)
    live_counts = jnp.sum((stacks[:, 0, :] >= 0).astype(jnp.int32), axis=1)
    right_out = bucketize(b_blocks[0, 0], b_send[0, 0])
    right_home = lax.all_to_all(right_out, "row", split_axis=0, concat_axis=0, tiled=True)
    right_home = right_home.reshape(-1, edge, edge)
    total = None
    result_shape = (result_count, edge, edge)
    left_now = left_home
    right_now = right_home
    for stop_index in range(STOPS):
        if stop_index > 0:
            left_now = passed_along(left_now, "col", -1)
            right_now = passed_along(right_now, "row", -1)
        if stop_index > 0:
            left_now, right_now, total = lax.optimization_barrier((left_now, right_now, total))
        total = run_stop(total, left_now, right_now, stacks, left_maps, live_counts, stop_index,
                         stop_index == STOPS - 1, result_shape)
    result = total
    outgoing = bucketize(result, c_send[0, 0])
    arrived = lax.all_to_all(outgoing, ("row", "col"), split_axis=0, concat_axis=0, tiled=True)
    return arrived[None, None]


def solution(mesh):
    placed = (
        P("row", "col", None, None, None),
        P("row", "col", None, None, None),
        P("row", "col", None, None),
        P("row", "col", None, None),
        P("row", "col", None, None, None),
        P("row", "col", None),
    )
    return jax.shard_map(
        on_device,
        mesh=mesh,
        in_specs=placed,
        out_specs=P("row", "col", None, None, None),
        check_vma=False,
    )
```

time: 114 us -> 113 us (level)
  starting transfers between devices: 18.5 us -> 23.6 us
  Pallas kernels: 39.7 us -> 36.1 us
  other arithmetic: 6.61 us -> 3.57 us
  local copies, waits for them, and re-layouts: 7.93 us -> 6.16 us
    ppermute x9, starting transfers between devices: 13.1 us -> 18.2 us  [passed_along(): return lax.ppermute(value, axis, pairs)]
    pallas_call x4, Pallas kernels: 39.7 us -> 36.1 us  [run_stop(): pl.pallas_call(functools.partial(stop_kernel, stop, first, last), grid_sp...]
    unnamed x33 -> x30, local copies, waits for them, and re-layouts: 4.35 us -> 2.64 us
    add x4 -> x1, other arithmetic: 2.35 us -> 0.67 us  [on_device(): (owner - slot // cap) % cols_n * cap + slot % cap]
    convert_element_type x1 -> x0, other arithmetic: 1.31 us -> none  [on_device(): result = total.astype(jnp.bfloat16)]
  transfers between devices with their start and end apart: 10 -> 10, of which waited for: 3 -> 3; matrix products, arithmetic and copies ran while one was open for 7% -> 2% of each run, Pallas kernels for 27% -> 25%
where the time goes in v7:
time: 113 us; the launch traced here: 112 us
  Pallas kernels  36.1 us (32%)
  blocking collectives  32.5 us (29%)
  starting transfers between devices  23.6 us (21%)
  waiting for transfers between devices  9.53 us (8%)
  local copies, waits for them, and re-layouts  6.16 us (5%)
  other arithmetic  3.57 us (3%)
    pallas_call x4, Pallas kernels, run_stop(): pl.pallas_call(functools.partial(stop_kernel, stop, first, last), grid_sp...  36.1 us
    all_to_all x1, blocking collectives, on_device(): lax.all_to_all(outgoing, ('row', 'col'), split_axis=0, concat_axis=0, til...  32.5 us
    ppermute x9, starting transfers between devices, passed_along(): return lax.ppermute(value, axis, pairs)  18.2 us
    ppermute x9, waiting for transfers between devices, passed_along(): return lax.ppermute(value, axis, pairs)  9.52 us
    all_to_all x1, starting transfers between devices, on_device(): lax.all_to_all(right_out, 'row', split_axis=0, concat_axis=0, tiled=True)  5.35 us
    gather x3, local copies, waits for them, and re-layouts, bucketize(): picked = jnp.take(blocks, jnp.maximum(index, 0), axis=0)  3.08 us
    unnamed x30, local copies, waits for them, and re-layouts  2.64 us
  transfers between devices with their start and end apart: 10, of which 3 were waited for; matrix products, arithmetic and copies ran while one was open for 2% of the time, Pallas kernels for 25%

profile of v7, /device:TPU:1, one launch (start us, length us, event | category | flops | bytes accessed | tf_op | source)
XLA Modules:
  0.0 111.7 jit_solution(7784974947995916896)
XLA Ops:
  0.0 0.8 compare_bitcast_fusion.1
  0.8 0.1 copy.14
  0.9 0.1 copy.15
  1.1 0.6 gather_fusion.1
  1.8 0.9 select_select_fusion.1
  2.7 5.4 %all-to-all-start = ((bf16[8,2,128,128]{3,2,1,0:T(8,128)(2,1)}), bf16[8,2,128,128]{3,2,1,0:T(8,128)(2,1)S(1)}, u32[]{:S(2)}, u32[]{:S(2)}) async-start(bf16[8,2,128,128]{3,2,1,0:T(8,128)(2,1)} %select_select_fusion.1), calls=%async_computation | async-start | bytes 1048576 | tf_op jit(solution)/shard_map/all_to_all | solution.py:115
  8.2 0.6 gather_fusion
  8.9 0.1 select_select_fusion.2
  9.2 1.3 %collective-permute-start = (bf16[4,128,128]{2,1,0:T(8,128)(2,1)S(1)}, bf16[4,128,128]{2,1,0:T(8,128)(2,1)S(1)}, u32[]{:S(2)}, u32[]{:S(2)}) collective-permute-start(bf16[4,128,128]{2,1,0:T(8,128)(2,1)S(1)} %get-tuple-element.38), channel_id=1, source_target_pairs={{0,1},{1,2},{2,3},{3,0},{4,5},{5,6},{6,7},{7,4},{8,9},{9,10},{10,1... | collective-permute-start | bytes 393224 | tf_op jit(solution)/shard_map/ppermute | solution.py:16
  10.5 2.3 %collective-permute-start.1 = (bf16[4,128,128]{2,1,0:T(8,128)(2,1)S(1)}, bf16[4,128,128]{2,1,0:T(8,128)(2,1)S(1)}, u32[]{:S(2)}, u32[]{:S(2)}) collective-permute-start(bf16[4,128,128]{2,1,0:T(8,128)(2,1)S(1)} %get-tuple-element.37), channel_id=1, source_target_pairs={{0,2},{1,3},{2,0},{3,1},{4,6},{5,7},{6,4},{7,5},{8,10},{9,11},{10,... | collective-permute-start | bytes 393224 | tf_op jit(solution)/shard_map/ppermute | solution.py:16
  12.8 1.1 collective-permute-start.2
  13.9 2.4 %collective-permute-done = bf16[4,128,128]{2,1,0:T(8,128)(2,1)S(1)} collective-permute-done((bf16[4,128,128]{2,1,0:T(8,128)(2,1)S(1)}, bf16[4,128,128]{2,1,0:T(8,128)(2,1)S(1)}, u32[]{:S(2)}, u32[]{:S(2)}) %collective-permute-start) | collective-permute-done | bytes 131104 | tf_op jit(solution)/shard_map/ppermute | solution.py:16
  16.3 5.8 %collective-permute-done.1 = bf16[4,128,128]{2,1,0:T(8,128)(2,1)S(1)} collective-permute-done((bf16[4,128,128]{2,1,0:T(8,128)(2,1)S(1)}, bf16[4,128,128]{2,1,0:T(8,128)(2,1)S(1)}, u32[]{:S(2)}, u32[]{:S(2)}) %collective-permute-start.1) | collective-permute-done | bytes 131104 | tf_op jit(solution)/shard_map/ppermute | solution.py:16
  22.2 3.9 %collective-permute-start.3 = (bf16[16,128,128]{2,1,0:T(8,128)(2,1)S(1)}, bf16[16,128,128]{2,1,0:T(8,128)(2,1)S(1)}, u32[]{:S(2)}, u32[]{:S(2)}) collective-permute-start(bf16[16,128,128]{2,1,0:T(8,128)(2,1)S(1)} %pad_maximum_fusion.left_ref), channel_id=1, source_target_pairs={{0,3},{1,0},{2,1},{3,2},{4,7},{5,4},{6,5},{7,6},{8,11},{9,8},{10,9... | collective-permute-start | bytes 1572872 | tf_op jit(solution)/shard_map/ppermute | solution.py:16
  26.1 1.1 collective-permute-start.4
  27.2 0.7 fusion.n_ref
  27.9 0.7 fusion.2.map_ref
  28.6 9.0 %shard_map.64.refs_0_ = f32[16,128,128]{2,1,0:T(8,128)} custom-call(s32[4,3,384]{2,1,0:T(4,128)} %bitcast.40, s32[4,16]{1,0:T(4,128)} %fusion.2.map_ref, s32[4]{0:T(128)} %fusion.n_ref, bf16[16,128,128]{2,1,0:T(8,128)(2,1)} %copy-done.2, bf16[16,128,128]{2,1,0:T(8,128)(2,1)} %bitcast.38), custom_call_target="tpu_custom_call" | custom-call | tf_op jit(solution)/shard_map/pallas_call | solution.py:87
  37.5 3.1 %collective-permute-start.5 = (bf16[16,128,128]{2,1,0:T(8,128)(2,1)S(1)}, bf16[16,128,128]{2,1,0:T(8,128)(2,1)S(1)}, u32[]{:S(2)}, u32[]{:S(2)}) collective-permute-start(bf16[16,128,128]{2,1,0:T(8,128)(2,1)S(1)} %collective-permute-done.3.left_ref), channel_id=1, source_target_pairs={{0,3},{1,0},{2,1},{3,2},{4,7},{5,4},{6,5},{7,6},{8,11},{9,8},{10,9... | collective-permute-start | bytes 1572872 | tf_op jit(solution)/shard_map/ppermute | solution.py:16
  40.6 2.0 %collective-permute-start.6 = (bf16[16,128,128]{2,1,0:T(8,128)(2,1)S(1)}, bf16[16,128,128]{2,1,0:T(8,128)(2,1)}, u32[]{:S(2)}, u32[]{:S(2)}) collective-permute-start(bf16[16,128,128]{2,1,0:T(8,128)(2,1)S(1)} %collective-permute-done.4.right_ref), channel_id=1, source_target_pairs={{0,28},{4,0},{8,4},{12,8},{16,12},{20,16},{24,20},{28,24},{1,29},{... | collective-permute-start | bytes 1572872 | tf_op jit(solution)/shard_map/ppermute | solution.py:16
  42.6 10.9 %shard_map.65.refs_0_ = f32[16,128,128]{2,1,0:T(8,128)} custom-call(s32[4,3,384]{2,1,0:T(4,128)} %bitcast.41, s32[4,16]{1,0:T(4,128)} %fusion.2.map_ref, s32[4]{0:T(128)} %fusion.n_ref, bf16[16,128,128]{2,1,0:T(8,128)(2,1)} %copy-done.7, bf16[16,128,128]{2,1,0:T(8,128)(2,1)} %copy-done.8, ...), custom_call_target="tpu_custom_call", output_to_operand_aliasing={{}: (5, {})} | custom-call | tf_op jit(solution)/shard_map/pallas_call | solution.py:87
  53.5 0.7 collective-permute-start.7
  54.1 2.9 %collective-permute-start.8 = (bf16[16,128,128]{2,1,0:T(8,128)(2,1)}, bf16[16,128,128]{2,1,0:T(8,128)(2,1)S(1)}, u32[]{:S(2)}, u32[]{:S(2)}) collective-permute-start(bf16[16,128,128]{2,1,0:T(8,128)(2,1)} %collective-permute-done.6.right_ref), channel_id=1, source_target_pairs={{0,28},{4,0},{8,4},{12,8},{16,12},{20,16},{24,20},{28,24},{1,29},{... | collective-permute-start | bytes 1572872 | tf_op jit(solution)/shard_map/ppermute | solution.py:16
  57.1 8.5 %shard_map.66.refs_0_ = f32[16,128,128]{2,1,0:T(8,128)} custom-call(s32[4,3,384]{2,1,0:T(4,128)} %bitcast.42, s32[4,16]{1,0:T(4,128)} %fusion.2.map_ref, s32[4]{0:T(128)} %fusion.n_ref, bf16[16,128,128]{2,1,0:T(8,128)(2,1)} %copy-done.9, bf16[16,128,128]{2,1,0:T(8,128)(2,1)} %collective-permute-done.6.right_ref, ...), custom_call_target="tpu_custom_call", output_to_operand_aliasing={{}: (5, {})} | custom-call | tf_op jit(solution)/shard_map/pallas_call | solution.py:87
  65.6 1.3 %collective-permute-done.7.left_ref = bf16[16,128,128]{2,1,0:T(8,128)(2,1)S(1)} collective-permute-done((bf16[16,128,128]{2,1,0:T(8,128)(2,1)S(1)}, bf16[16,128,128]{2,1,0:T(8,128)(2,1)S(1)}, u32[]{:S(2)}, u32[]{:S(2)}) %collective-permute-start.7) | collective-permute-done | bytes 524320 | tf_op jit(solution)/shard_map/ppermute | solution.py:16
  66.9 0.8 copy-done.4
  67.7 0.8 copy-done.5
  68.5 7.7 %shard_map.67 = bf16[16,128,128]{2,1,0:T(8,128)(2,1)} custom-call(s32[4,3,384]{2,1,0:T(4,128)} %bitcast.43, s32[4,16]{1,0:T(4,128)} %fusion.2.map_ref, s32[4]{0:T(128)} %fusion.n_ref, bf16[16,128,128]{2,1,0:T(8,128)(2,1)} %copy-done.4, bf16[16,128,128]{2,1,0:T(8,128)(2,1)} %copy-done.5, f32[16,128,128]{2,1,0:T(8,128)} %shard_map.66.refs_0_), custom_call_target="tpu_custom_call" | custom-call | tf_op jit(solution)/shard_map/pallas_call | solution.py:87
  76.2 1.8 %gather_fusion.2 = bf16[32,128,128]{2,1,0:T(8,128)(2,1)S(1)} fusion(bf16[16,128,128]{2,1,0:T(8,128)(2,1)} %shard_map.67, s32[1024]{0:T(1024)S(1)} %pad_clamp_fusion), kind=kCustom, calls=%fused_computation.2 | custom fusion | bytes 2097280 | tf_op jit(solution)/shard_map/jit(_take)/gather | solution.py:20
  78.0 0.2 select_select_fusion
  78.2 32.5 %all_to_all.10 = bf16[32,128,128]{2,1,0:T(8,128)(2,1)S(1)} all-to-all(bf16[32,128,128]{2,1,0:T(8,128)(2,1)S(1)} %select_select_fusion), channel_id=1, replica_groups=mesh['row'=8,'col'=4] {'row','col'}, dimensions={0} | all-to-all | bytes 2097152 | tf_op jit(solution)/shard_map/all_to_all | solution.py:131
  110.7 1.0 copy.22
  (49 shorter events, 0.5 us)
Async XLA Ops:
  0.0 1.1 %copy-start = (bf16[1,1,16,128,128]{4,3,2,1,0:T(8,128)(2,1)S(1)}, bf16[1,1,16,128,128]{4,3,2,1,0:T(8,128)(2,1)}, u32[]{:S(2)}) copy-start(bf16[1,1,16,128,128]{4,3,2,1,0:T(8,128)(2,1)} %param.9) | copy-start | bytes 1572868
  0.0 0.8 copy-start.12
  2.7 5.4 %copy-start.11 = (s32[1,1,4,4]{3,2,1,0:T(4,128)S(1)}, s32[1,1,4,4]{3,2,1,0:T(4,128)}, u32[]{:S(2)}) copy-start(s32[1,1,4,4]{3,2,1,0:T(4,128)} %param.10) | copy-start | bytes 196
  2.7 5.5 %copy-start.6 = (bf16[1,1,16,128,128]{4,3,2,1,0:T(8,128)(2,1)S(1)}, bf16[1,1,16,128,128]{4,3,2,1,0:T(8,128)(2,1)}, u32[]{:S(2)}) copy-start(bf16[1,1,16,128,128]{4,3,2,1,0:T(8,128)(2,1)} %param.8) | copy-start | bytes 1572868
  2.7 23.4 %all-to-all-start = ((bf16[8,2,128,128]{3,2,1,0:T(8,128)(2,1)}), bf16[8,2,128,128]{3,2,1,0:T(8,128)(2,1)S(1)}, u32[]{:S(2)}, u32[]{:S(2)}) async-start(bf16[8,2,128,128]{3,2,1,0:T(8,128)(2,1)} %select_select_fusion.1), calls=%async_computation | async-start | bytes 1048576 | tf_op jit(solution)/shard_map/all_to_all | solution.py:115
  9.1 4.8 %copy-start.10 = (s32[1,1,4,3,384]{4,2,3,1,0:T(4,128)S(1)}, s32[1,1,4,3,384]{4,2,3,1,0:T(4,128)}, u32[]{:S(2)}) copy-start(s32[1,1,4,3,384]{4,2,3,1,0:T(4,128)} %param.12) | copy-start | bytes 55300
  9.2 7.1 %collective-permute-start = (bf16[4,128,128]{2,1,0:T(8,128)(2,1)S(1)}, bf16[4,128,128]{2,1,0:T(8,128)(2,1)S(1)}, u32[]{:S(2)}, u32[]{:S(2)}) collective-permute-start(bf16[4,128,128]{2,1,0:T(8,128)(2,1)S(1)} %get-tuple-element.38), channel_id=1, source_target_pairs={{0,1},{1,2},{2,3},{3,0},{4,5},{5,6},{6,7},{7,4},{8,9},{9,10},{10,1... | collective-permute-start | bytes 393224 | tf_op jit(solution)/shard_map/ppermute | solution.py:16
  10.5 11.6 %collective-permute-start.1 = (bf16[4,128,128]{2,1,0:T(8,128)(2,1)S(1)}, bf16[4,128,128]{2,1,0:T(8,128)(2,1)S(1)}, u32[]{:S(2)}, u32[]{:S(2)}) collective-permute-start(bf16[4,128,128]{2,1,0:T(8,128)(2,1)S(1)} %get-tuple-element.37), channel_id=1, source_target_pairs={{0,2},{1,3},{2,0},{3,1},{4,6},{5,7},{6,4},{7,5},{8,10},{9,11},{10,... | collective-permute-start | bytes 393224 | tf_op jit(solution)/shard_map/ppermute | solution.py:16
  12.8 9.3 %collective-permute-start.2 = (bf16[4,128,128]{2,1,0:T(8,128)(2,1)S(1)}, bf16[4,128,128]{2,1,0:T(8,128)(2,1)S(1)}, u32[]{:S(2)}, u32[]{:S(2)}) collective-permute-start(bf16[4,128,128]{2,1,0:T(8,128)(2,1)S(1)} %get-tuple-element.36), channel_id=1, source_target_pairs={{0,3},{1,0},{2,1},{3,2},{4,7},{5,4},{6,5},{7,6},{8,11},{9,8},{10,9... | collective-permute-start | bytes 393224 | tf_op jit(solution)/shard_map/ppermute | solution.py:16
  13.9 13.3 %copy-start.3 = (s32[1,1,4,3,384]{4,3,2,1,0:T(4,128)}, s32[1,1,4,3,384]{4,3,2,1,0:T(4,128)S(1)}, u32[]{:S(2)}) copy-start(s32[1,1,4,3,384]{4,3,2,1,0:T(4,128)S(1)} %copy.18) | copy-start | bytes 55300
  22.2 6.3 %copy-start.2 = (bf16[16,128,128]{2,1,0:T(8,128)(2,1)}, bf16[16,128,128]{2,1,0:T(8,128)(2,1)S(1)}, u32[]{:S(2)}) copy-start(bf16[16,128,128]{2,1,0:T(8,128)(2,1)S(1)} %pad_maximum_fusion.left_ref) | copy-start | bytes 1572868
  22.2 15.3 %collective-permute-start.3 = (bf16[16,128,128]{2,1,0:T(8,128)(2,1)S(1)}, bf16[16,128,128]{2,1,0:T(8,128)(2,1)S(1)}, u32[]{:S(2)}, u32[]{:S(2)}) collective-permute-start(bf16[16,128,128]{2,1,0:T(8,128)(2,1)S(1)} %pad_maximum_fusion.left_ref), channel_id=1, source_target_pairs={{0,3},{1,0},{2,1},{3,2},{4,7},{5,4},{6,5},{7,6},{8,11},{9,8},{10,9... | collective-permute-start | bytes 1572872 | tf_op jit(solution)/shard_map/ppermute | solution.py:16
  26.1 2.4 %copy-start.1 = (bf16[8,2,128,128]{3,2,1,0:T(8,128)(2,1)}, bf16[8,2,128,128]{3,2,1,0:T(8,128)(2,1)S(1)}, u32[]{:S(2)}) copy-start(bf16[8,2,128,128]{3,2,1,0:T(8,128)(2,1)S(1)} %all-to-all-done) | copy-start | bytes 1572868
  26.1 11.4 %collective-permute-start.4 = (bf16[16,128,128]{2,1,0:T(8,128)(2,1)S(1)}, bf16[16,128,128]{2,1,0:T(8,128)(2,1)S(1)}, u32[]{:S(2)}, u32[]{:S(2)}) collective-permute-start(bf16[16,128,128]{2,1,0:T(8,128)(2,1)S(1)} %bitcast.37), channel_id=1, source_target_pairs={{0,28},{4,0},{8,4},{12,8},{16,12},{20,16},{24,20},{28,24},{1,29},{... | collective-permute-start | bytes 1572872 | tf_op jit(solution)/shard_map/ppermute | solution.py:16
  37.5 19.5 %copy-start.13 = (s32[1,1,32]{2,1,0:T(1,128)S(1)}, s32[1,1,32]{2,1,0:T(1,128)}, u32[]{:S(2)}) copy-start(s32[1,1,32]{2,1,0:T(1,128)} %param.13) | copy-start | bytes 388
  37.5 5.1 %copy-start.7 = (bf16[16,128,128]{2,1,0:T(8,128)(2,1)}, bf16[16,128,128]{2,1,0:T(8,128)(2,1)S(1)}, u32[]{:S(2)}) copy-start(bf16[16,128,128]{2,1,0:T(8,128)(2,1)S(1)} %collective-permute-done.3.left_ref) | copy-start | bytes 1572868
  37.5 5.0 %copy-start.8 = (bf16[16,128,128]{2,1,0:T(8,128)(2,1)}, bf16[16,128,128]{2,1,0:T(8,128)(2,1)S(1)}, u32[]{:S(2)}) copy-start(bf16[16,128,128]{2,1,0:T(8,128)(2,1)S(1)} %collective-permute-done.4.right_ref) | copy-start | bytes 1572868
  37.5 15.9 %collective-permute-start.5 = (bf16[16,128,128]{2,1,0:T(8,128)(2,1)S(1)}, bf16[16,128,128]{2,1,0:T(8,128)(2,1)S(1)}, u32[]{:S(2)}, u32[]{:S(2)}) collective-permute-start(bf16[16,128,128]{2,1,0:T(8,128)(2,1)S(1)} %collective-permute-done.3.left_ref), channel_id=1, source_target_pairs={{0,3},{1,0},{2,1},{3,2},{4,7},{5,4},{6,5},{7,6},{8,11},{9,8},{10,9... | collective-permute-start | bytes 1572872 | tf_op jit(solution)/shard_map/ppermute | solution.py:16
  40.6 12.9 %collective-permute-start.6 = (bf16[16,128,128]{2,1,0:T(8,128)(2,1)S(1)}, bf16[16,128,128]{2,1,0:T(8,128)(2,1)}, u32[]{:S(2)}, u32[]{:S(2)}) collective-permute-start(bf16[16,128,128]{2,1,0:T(8,128)(2,1)S(1)} %collective-permute-done.4.right_ref), channel_id=1, source_target_pairs={{0,28},{4,0},{8,4},{12,8},{16,12},{20,16},{24,20},{28,24},{1,29},{... | collective-permute-start | bytes 1572872 | tf_op jit(solution)/shard_map/ppermute | solution.py:16
  53.5 3.6 %copy-start.9 = (bf16[16,128,128]{2,1,0:T(8,128)(2,1)}, bf16[16,128,128]{2,1,0:T(8,128)(2,1)S(1)}, u32[]{:S(2)}) copy-start(bf16[16,128,128]{2,1,0:T(8,128)(2,1)S(1)} %collective-permute-done.5.left_ref) | copy-start | bytes 1572868
  53.5 13.4 %collective-permute-start.7 = (bf16[16,128,128]{2,1,0:T(8,128)(2,1)S(1)}, bf16[16,128,128]{2,1,0:T(8,128)(2,1)S(1)}, u32[]{:S(2)}, u32[]{:S(2)}) collective-permute-start(bf16[16,128,128]{2,1,0:T(8,128)(2,1)S(1)} %collective-permute-done.5.left_ref), channel_id=1, source_target_pairs={{0,3},{1,0},{2,1},{3,2},{4,7},{5,4},{6,5},{7,6},{8,11},{9,8},{10,9... | collective-permute-start | bytes 1572872 | tf_op jit(solution)/shard_map/ppermute | solution.py:16
  54.1 12.7 %collective-permute-start.8 = (bf16[16,128,128]{2,1,0:T(8,128)(2,1)}, bf16[16,128,128]{2,1,0:T(8,128)(2,1)S(1)}, u32[]{:S(2)}, u32[]{:S(2)}) collective-permute-start(bf16[16,128,128]{2,1,0:T(8,128)(2,1)} %collective-permute-done.6.right_ref), channel_id=1, source_target_pairs={{0,28},{4,0},{8,4},{12,8},{16,12},{20,16},{24,20},{28,24},{1,29},{... | collective-permute-start | bytes 1572872 | tf_op jit(solution)/shard_map/ppermute | solution.py:16
  66.9 0.8 copy-start.4
  67.7 0.8 copy-start.5

commit v8 on v7

--- a/solution.py
+++ b/solution.py
@@ -21,7 +21,7 @@
     return jnp.where((index >= 0)[..., None, None], picked, jnp.zeros_like(picked))
 
 
-GROUP = 32
+GROUP = 64
 
 
 def stop_kernel(stop, first, last, stack_ref, map_ref, n_ref, left_ref, right_ref, *refs):

time: 113 us -> 112 us (level)
  Pallas kernels: 36.1 us -> 32.9 us
  starting transfers between devices: 23.6 us -> 26.6 us
    pallas_call x4, Pallas kernels: 36.1 us -> 32.9 us  [run_stop(): pl.pallas_call(functools.partial(stop_kernel, stop, first, last), grid_sp...]
    ppermute x9, starting transfers between devices: 18.2 us -> 21.3 us  [passed_along(): return lax.ppermute(value, axis, pairs)]
  transfers between devices with their start and end apart: 10 -> 10, of which waited for: 3 -> 3; matrix products, arithmetic and copies ran while one was open for 2% -> 2% of each run, Pallas kernels for 25% -> 22%
where the time goes in v8:
time: 112 us
  Pallas kernels  32.9 us (29%)
  blocking collectives  32.7 us (29%)
  starting transfers between devices  26.6 us (24%)
  waiting for transfers between devices  9.49 us (8%)
  local copies, waits for them, and re-layouts  6.16 us (6%)
  other arithmetic  3.57 us (3%)
    pallas_call x4, Pallas kernels, run_stop(): pl.pallas_call(functools.partial(stop_kernel, stop, first, last), grid_sp...  32.9 us
    all_to_all x1, blocking collectives, on_device(): lax.all_to_all(outgoing, ('row', 'col'), split_axis=0, concat_axis=0, til...  32.7 us
    ppermute x9, starting transfers between devices, passed_along(): return lax.ppermute(value, axis, pairs)  21.3 us
    ppermute x9, waiting for transfers between devices, passed_along(): return lax.ppermute(value, axis, pairs)  9.49 us
    all_to_all x1, starting transfers between devices, on_device(): lax.all_to_all(right_out, 'row', split_axis=0, concat_axis=0, tiled=True)  5.35 us
    gather x3, local copies, waits for them, and re-layouts, bucketize(): picked = jnp.take(blocks, jnp.maximum(index, 0), axis=0)  3.08 us
    unnamed x30, local copies, waits for them, and re-layouts  2.64 us
  transfers between devices with their start and end apart: 10, of which 3 were waited for; matrix products, arithmetic and copies ran while one was open for 2% of the time, Pallas kernels for 22%

profile of v8, /device:TPU:1, one launch (start us, length us, event | category | flops | bytes accessed | tf_op | source)
XLA Modules:
  0.0 111.6 jit_solution(6284783240641920486)
XLA Ops:
  0.0 0.8 compare_bitcast_fusion.1
  0.8 0.1 copy.14
  0.9 0.1 copy.15
  1.1 0.6 gather_fusion.1
  1.8 0.9 select_select_fusion.1
  2.7 5.4 %all-to-all-start = ((bf16[8,2,128,128]{3,2,1,0:T(8,128)(2,1)}), bf16[8,2,128,128]{3,2,1,0:T(8,128)(2,1)S(1)}, u32[]{:S(2)}, u32[]{:S(2)}) async-start(bf16[8,2,128,128]{3,2,1,0:T(8,128)(2,1)} %select_select_fusion.1), calls=%async_computation | async-start | bytes 1048576 | tf_op jit(solution)/shard_map/all_to_all | solution.py:115
  8.2 0.6 gather_fusion
  8.9 0.1 select_select_fusion.2
  9.2 1.3 %collective-permute-start = (bf16[4,128,128]{2,1,0:T(8,128)(2,1)S(1)}, bf16[4,128,128]{2,1,0:T(8,128)(2,1)S(1)}, u32[]{:S(2)}, u32[]{:S(2)}) collective-permute-start(bf16[4,128,128]{2,1,0:T(8,128)(2,1)S(1)} %get-tuple-element.38), channel_id=1, source_target_pairs={{0,1},{1,2},{2,3},{3,0},{4,5},{5,6},{6,7},{7,4},{8,9},{9,10},{10,1... | collective-permute-start | bytes 393224 | tf_op jit(solution)/shard_map/ppermute | solution.py:16
  10.5 2.3 %collective-permute-start.1 = (bf16[4,128,128]{2,1,0:T(8,128)(2,1)S(1)}, bf16[4,128,128]{2,1,0:T(8,128)(2,1)S(1)}, u32[]{:S(2)}, u32[]{:S(2)}) collective-permute-start(bf16[4,128,128]{2,1,0:T(8,128)(2,1)S(1)} %get-tuple-element.37), channel_id=1, source_target_pairs={{0,2},{1,3},{2,0},{3,1},{4,6},{5,7},{6,4},{7,5},{8,10},{9,11},{10,... | collective-permute-start | bytes 393224 | tf_op jit(solution)/shard_map/ppermute | solution.py:16
  12.8 1.1 collective-permute-start.2
  13.9 2.4 %collective-permute-done = bf16[4,128,128]{2,1,0:T(8,128)(2,1)S(1)} collective-permute-done((bf16[4,128,128]{2,1,0:T(8,128)(2,1)S(1)}, bf16[4,128,128]{2,1,0:T(8,128)(2,1)S(1)}, u32[]{:S(2)}, u32[]{:S(2)}) %collective-permute-start) | collective-permute-done | bytes 131104 | tf_op jit(solution)/shard_map/ppermute | solution.py:16
  16.3 5.8 %collective-permute-done.1 = bf16[4,128,128]{2,1,0:T(8,128)(2,1)S(1)} collective-permute-done((bf16[4,128,128]{2,1,0:T(8,128)(2,1)S(1)}, bf16[4,128,128]{2,1,0:T(8,128)(2,1)S(1)}, u32[]{:S(2)}, u32[]{:S(2)}) %collective-permute-start.1) | collective-permute-done | bytes 131104 | tf_op jit(solution)/shard_map/ppermute | solution.py:16
  22.2 3.9 %collective-permute-start.3 = (bf16[16,128,128]{2,1,0:T(8,128)(2,1)S(1)}, bf16[16,128,128]{2,1,0:T(8,128)(2,1)S(1)}, u32[]{:S(2)}, u32[]{:S(2)}) collective-permute-start(bf16[16,128,128]{2,1,0:T(8,128)(2,1)S(1)} %pad_maximum_fusion.left_ref), channel_id=1, source_target_pairs={{0,3},{1,0},{2,1},{3,2},{4,7},{5,4},{6,5},{7,6},{8,11},{9,8},{10,9... | collective-permute-start | bytes 1572872 | tf_op jit(solution)/shard_map/ppermute | solution.py:16
  26.1 1.1 collective-permute-start.4
  27.2 0.7 fusion.n_ref
  27.9 0.7 fusion.2.map_ref
  28.6 7.4 %shard_map.64.refs_0_ = f32[16,128,128]{2,1,0:T(8,128)} custom-call(s32[4,3,384]{2,1,0:T(4,128)} %bitcast.40, s32[4,16]{1,0:T(4,128)} %fusion.2.map_ref, s32[4]{0:T(128)} %fusion.n_ref, bf16[16,128,128]{2,1,0:T(8,128)(2,1)} %copy-done.2, bf16[16,128,128]{2,1,0:T(8,128)(2,1)} %bitcast.38), custom_call_target="tpu_custom_call" | custom-call | tf_op jit(solution)/shard_map/pallas_call | solution.py:87
  36.0 1.2 %collective-permute-done.3.left_ref = bf16[16,128,128]{2,1,0:T(8,128)(2,1)S(1)} collective-permute-done((bf16[16,128,128]{2,1,0:T(8,128)(2,1)S(1)}, bf16[16,128,128]{2,1,0:T(8,128)(2,1)S(1)}, u32[]{:S(2)}, u32[]{:S(2)}) %collective-permute-start.3) | collective-permute-done | bytes 524320 | tf_op jit(solution)/shard_map/ppermute | solution.py:16
  37.3 3.4 %collective-permute-start.5 = (bf16[16,128,128]{2,1,0:T(8,128)(2,1)S(1)}, bf16[16,128,128]{2,1,0:T(8,128)(2,1)S(1)}, u32[]{:S(2)}, u32[]{:S(2)}) collective-permute-start(bf16[16,128,128]{2,1,0:T(8,128)(2,1)S(1)} %collective-permute-done.3.left_ref), channel_id=1, source_target_pairs={{0,3},{1,0},{2,1},{3,2},{4,7},{5,4},{6,5},{7,6},{8,11},{9,8},{10,9... | collective-permute-start | bytes 1572872 | tf_op jit(solution)/shard_map/ppermute | solution.py:16
  40.6 2.0 %collective-permute-start.6 = (bf16[16,128,128]{2,1,0:T(8,128)(2,1)S(1)}, bf16[16,128,128]{2,1,0:T(8,128)(2,1)}, u32[]{:S(2)}, u32[]{:S(2)}) collective-permute-start(bf16[16,128,128]{2,1,0:T(8,128)(2,1)S(1)} %collective-permute-done.4.right_ref), channel_id=1, source_target_pairs={{0,28},{4,0},{8,4},{12,8},{16,12},{20,16},{24,20},{28,24},{1,29},{... | collective-permute-start | bytes 1572872 | tf_op jit(solution)/shard_map/ppermute | solution.py:16
  42.6 8.2 %shard_map.65.refs_0_ = f32[16,128,128]{2,1,0:T(8,128)} custom-call(s32[4,3,384]{2,1,0:T(4,128)} %bitcast.41, s32[4,16]{1,0:T(4,128)} %fusion.2.map_ref, s32[4]{0:T(128)} %fusion.n_ref, bf16[16,128,128]{2,1,0:T(8,128)(2,1)} %copy-done.7, bf16[16,128,128]{2,1,0:T(8,128)(2,1)} %copy-done.8, ...), custom_call_target="tpu_custom_call", output_to_operand_aliasing={{}: (5, {})} | custom-call | tf_op jit(solution)/shard_map/pallas_call | solution.py:87
  50.8 3.4 %collective-permute-start.7 = (bf16[16,128,128]{2,1,0:T(8,128)(2,1)S(1)}, bf16[16,128,128]{2,1,0:T(8,128)(2,1)S(1)}, u32[]{:S(2)}, u32[]{:S(2)}) collective-permute-start(bf16[16,128,128]{2,1,0:T(8,128)(2,1)S(1)} %collective-permute-done.5.left_ref), channel_id=1, source_target_pairs={{0,3},{1,0},{2,1},{3,2},{4,7},{5,4},{6,5},{7,6},{8,11},{9,8},{10,9... | collective-permute-start | bytes 1572872 | tf_op jit(solution)/shard_map/ppermute | solution.py:16
  54.1 2.9 %collective-permute-start.8 = (bf16[16,128,128]{2,1,0:T(8,128)(2,1)}, bf16[16,128,128]{2,1,0:T(8,128)(2,1)S(1)}, u32[]{:S(2)}, u32[]{:S(2)}) collective-permute-start(bf16[16,128,128]{2,1,0:T(8,128)(2,1)} %collective-permute-done.6.right_ref), channel_id=1, source_target_pairs={{0,28},{4,0},{8,4},{12,8},{16,12},{20,16},{24,20},{28,24},{1,29},{... | collective-permute-start | bytes 1572872 | tf_op jit(solution)/shard_map/ppermute | solution.py:16
  57.1 9.3 %shard_map.66.refs_0_ = f32[16,128,128]{2,1,0:T(8,128)} custom-call(s32[4,3,384]{2,1,0:T(4,128)} %bitcast.42, s32[4,16]{1,0:T(4,128)} %fusion.2.map_ref, s32[4]{0:T(128)} %fusion.n_ref, bf16[16,128,128]{2,1,0:T(8,128)(2,1)} %copy-done.9, bf16[16,128,128]{2,1,0:T(8,128)(2,1)} %collective-permute-done.6.right_ref, ...), custom_call_target="tpu_custom_call", output_to_operand_aliasing={{}: (5, {})} | custom-call | tf_op jit(solution)/shard_map/pallas_call | solution.py:87
  66.4 0.8 copy-done.4
  67.2 0.8 copy-done.5
  68.0 8.0 %shard_map.67 = bf16[16,128,128]{2,1,0:T(8,128)(2,1)} custom-call(s32[4,3,384]{2,1,0:T(4,128)} %bitcast.43, s32[4,16]{1,0:T(4,128)} %fusion.2.map_ref, s32[4]{0:T(128)} %fusion.n_ref, bf16[16,128,128]{2,1,0:T(8,128)(2,1)} %copy-done.4, bf16[16,128,128]{2,1,0:T(8,128)(2,1)} %copy-done.5, f32[16,128,128]{2,1,0:T(8,128)} %shard_map.66.refs_0_), custom_call_target="tpu_custom_call" | custom-call | tf_op jit(solution)/shard_map/pallas_call | solution.py:87
  76.0 1.8 %gather_fusion.2 = bf16[32,128,128]{2,1,0:T(8,128)(2,1)S(1)} fusion(bf16[16,128,128]{2,1,0:T(8,128)(2,1)} %shard_map.67, s32[1024]{0:T(1024)S(1)} %pad_clamp_fusion), kind=kCustom, calls=%fused_computation.2 | custom fusion | bytes 2097280 | tf_op jit(solution)/shard_map/jit(_take)/gather | solution.py:20
  77.8 0.2 select_select_fusion
  78.0 32.7 %all_to_all.10 = bf16[32,128,128]{2,1,0:T(8,128)(2,1)S(1)} all-to-all(bf16[32,128,128]{2,1,0:T(8,128)(2,1)S(1)} %select_select_fusion), channel_id=1, replica_groups=mesh['row'=8,'col'=4] {'row','col'}, dimensions={0} | all-to-all | bytes 2097152 | tf_op jit(solution)/shard_map/all_to_all | solution.py:131
  110.7 1.0 copy.22
  (49 shorter events, 0.5 us)
Async XLA Ops:
  0.0 1.1 %copy-start = (bf16[1,1,16,128,128]{4,3,2,1,0:T(8,128)(2,1)S(1)}, bf16[1,1,16,128,128]{4,3,2,1,0:T(8,128)(2,1)}, u32[]{:S(2)}) copy-start(bf16[1,1,16,128,128]{4,3,2,1,0:T(8,128)(2,1)} %param.9) | copy-start | bytes 1572868
  0.0 0.8 copy-start.12
  2.7 5.4 %copy-start.11 = (s32[1,1,4,4]{3,2,1,0:T(4,128)S(1)}, s32[1,1,4,4]{3,2,1,0:T(4,128)}, u32[]{:S(2)}) copy-start(s32[1,1,4,4]{3,2,1,0:T(4,128)} %param.10) | copy-start | bytes 196
  2.7 5.5 %copy-start.6 = (bf16[1,1,16,128,128]{4,3,2,1,0:T(8,128)(2,1)S(1)}, bf16[1,1,16,128,128]{4,3,2,1,0:T(8,128)(2,1)}, u32[]{:S(2)}) copy-start(bf16[1,1,16,128,128]{4,3,2,1,0:T(8,128)(2,1)} %param.8) | copy-start | bytes 1572868
  2.7 23.4 %all-to-all-start = ((bf16[8,2,128,128]{3,2,1,0:T(8,128)(2,1)}), bf16[8,2,128,128]{3,2,1,0:T(8,128)(2,1)S(1)}, u32[]{:S(2)}, u32[]{:S(2)}) async-start(bf16[8,2,128,128]{3,2,1,0:T(8,128)(2,1)} %select_select_fusion.1), calls=%async_computation | async-start | bytes 1048576 | tf_op jit(solution)/shard_map/all_to_all | solution.py:115
  9.1 4.8 %copy-start.10 = (s32[1,1,4,3,384]{4,2,3,1,0:T(4,128)S(1)}, s32[1,1,4,3,384]{4,2,3,1,0:T(4,128)}, u32[]{:S(2)}) copy-start(s32[1,1,4,3,384]{4,2,3,1,0:T(4,128)} %param.12) | copy-start | bytes 55300
  9.2 7.1 %collective-permute-start = (bf16[4,128,128]{2,1,0:T(8,128)(2,1)S(1)}, bf16[4,128,128]{2,1,0:T(8,128)(2,1)S(1)}, u32[]{:S(2)}, u32[]{:S(2)}) collective-permute-start(bf16[4,128,128]{2,1,0:T(8,128)(2,1)S(1)} %get-tuple-element.38), channel_id=1, source_target_pairs={{0,1},{1,2},{2,3},{3,0},{4,5},{5,6},{6,7},{7,4},{8,9},{9,10},{10,1... | collective-permute-start | bytes 393224 | tf_op jit(solution)/shard_map/ppermute | solution.py:16
  10.5 11.6 %collective-permute-start.1 = (bf16[4,128,128]{2,1,0:T(8,128)(2,1)S(1)}, bf16[4,128,128]{2,1,0:T(8,128)(2,1)S(1)}, u32[]{:S(2)}, u32[]{:S(2)}) collective-permute-start(bf16[4,128,128]{2,1,0:T(8,128)(2,1)S(1)} %get-tuple-element.37), channel_id=1, source_target_pairs={{0,2},{1,3},{2,0},{3,1},{4,6},{5,7},{6,4},{7,5},{8,10},{9,11},{10,... | collective-permute-start | bytes 393224 | tf_op jit(solution)/shard_map/ppermute | solution.py:16
  12.8 9.3 %collective-permute-start.2 = (bf16[4,128,128]{2,1,0:T(8,128)(2,1)S(1)}, bf16[4,128,128]{2,1,0:T(8,128)(2,1)S(1)}, u32[]{:S(2)}, u32[]{:S(2)}) collective-permute-start(bf16[4,128,128]{2,1,0:T(8,128)(2,1)S(1)} %get-tuple-element.36), channel_id=1, source_target_pairs={{0,3},{1,0},{2,1},{3,2},{4,7},{5,4},{6,5},{7,6},{8,11},{9,8},{10,9... | collective-permute-start | bytes 393224 | tf_op jit(solution)/shard_map/ppermute | solution.py:16
  13.9 13.3 %copy-start.3 = (s32[1,1,4,3,384]{4,3,2,1,0:T(4,128)}, s32[1,1,4,3,384]{4,3,2,1,0:T(4,128)S(1)}, u32[]{:S(2)}) copy-start(s32[1,1,4,3,384]{4,3,2,1,0:T(4,128)S(1)} %copy.18) | copy-start | bytes 55300
  22.2 6.3 %copy-start.2 = (bf16[16,128,128]{2,1,0:T(8,128)(2,1)}, bf16[16,128,128]{2,1,0:T(8,128)(2,1)S(1)}, u32[]{:S(2)}) copy-start(bf16[16,128,128]{2,1,0:T(8,128)(2,1)S(1)} %pad_maximum_fusion.left_ref) | copy-start | bytes 1572868
  22.2 15.0 %collective-permute-start.3 = (bf16[16,128,128]{2,1,0:T(8,128)(2,1)S(1)}, bf16[16,128,128]{2,1,0:T(8,128)(2,1)S(1)}, u32[]{:S(2)}, u32[]{:S(2)}) collective-permute-start(bf16[16,128,128]{2,1,0:T(8,128)(2,1)S(1)} %pad_maximum_fusion.left_ref), channel_id=1, source_target_pairs={{0,3},{1,0},{2,1},{3,2},{4,7},{5,4},{6,5},{7,6},{8,11},{9,8},{10,9... | collective-permute-start | bytes 1572872 | tf_op jit(solution)/shard_map/ppermute | solution.py:16
  26.1 2.4 %copy-start.1 = (bf16[8,2,128,128]{3,2,1,0:T(8,128)(2,1)}, bf16[8,2,128,128]{3,2,1,0:T(8,128)(2,1)S(1)}, u32[]{:S(2)}) copy-start(bf16[8,2,128,128]{3,2,1,0:T(8,128)(2,1)S(1)} %all-to-all-done) | copy-start | bytes 1572868
  26.1 11.1 %collective-permute-start.4 = (bf16[16,128,128]{2,1,0:T(8,128)(2,1)S(1)}, bf16[16,128,128]{2,1,0:T(8,128)(2,1)S(1)}, u32[]{:S(2)}, u32[]{:S(2)}) collective-permute-start(bf16[16,128,128]{2,1,0:T(8,128)(2,1)S(1)} %bitcast.37), channel_id=1, source_target_pairs={{0,28},{4,0},{8,4},{12,8},{16,12},{20,16},{24,20},{28,24},{1,29},{... | collective-permute-start | bytes 1572872 | tf_op jit(solution)/shard_map/ppermute | solution.py:16
  36.0 21.0 %copy-start.13 = (s32[1,1,32]{2,1,0:T(1,128)S(1)}, s32[1,1,32]{2,1,0:T(1,128)}, u32[]{:S(2)}) copy-start(s32[1,1,32]{2,1,0:T(1,128)} %param.13) | copy-start | bytes 388
  37.2 5.3 %copy-start.7 = (bf16[16,128,128]{2,1,0:T(8,128)(2,1)}, bf16[16,128,128]{2,1,0:T(8,128)(2,1)S(1)}, u32[]{:S(2)}) copy-start(bf16[16,128,128]{2,1,0:T(8,128)(2,1)S(1)} %collective-permute-done.3.left_ref) | copy-start | bytes 1572868
  37.3 5.3 %copy-start.8 = (bf16[16,128,128]{2,1,0:T(8,128)(2,1)}, bf16[16,128,128]{2,1,0:T(8,128)(2,1)S(1)}, u32[]{:S(2)}) copy-start(bf16[16,128,128]{2,1,0:T(8,128)(2,1)S(1)} %collective-permute-done.4.right_ref) | copy-start | bytes 1572868
  37.3 13.5 %collective-permute-start.5 = (bf16[16,128,128]{2,1,0:T(8,128)(2,1)S(1)}, bf16[16,128,128]{2,1,0:T(8,128)(2,1)S(1)}, u32[]{:S(2)}, u32[]{:S(2)}) collective-permute-start(bf16[16,128,128]{2,1,0:T(8,128)(2,1)S(1)} %collective-permute-done.3.left_ref), channel_id=1, source_target_pairs={{0,3},{1,0},{2,1},{3,2},{4,7},{5,4},{6,5},{7,6},{8,11},{9,8},{10,9... | collective-permute-start | bytes 1572872 | tf_op jit(solution)/shard_map/ppermute | solution.py:16
  40.6 10.2 %collective-permute-start.6 = (bf16[16,128,128]{2,1,0:T(8,128)(2,1)S(1)}, bf16[16,128,128]{2,1,0:T(8,128)(2,1)}, u32[]{:S(2)}, u32[]{:S(2)}) collective-permute-start(bf16[16,128,128]{2,1,0:T(8,128)(2,1)S(1)} %collective-permute-done.4.right_ref), channel_id=1, source_target_pairs={{0,28},{4,0},{8,4},{12,8},{16,12},{20,16},{24,20},{28,24},{1,29},{... | collective-permute-start | bytes 1572872 | tf_op jit(solution)/shard_map/ppermute | solution.py:16
  50.8 6.3 %copy-start.9 = (bf16[16,128,128]{2,1,0:T(8,128)(2,1)}, bf16[16,128,128]{2,1,0:T(8,128)(2,1)S(1)}, u32[]{:S(2)}) copy-start(bf16[16,128,128]{2,1,0:T(8,128)(2,1)S(1)} %collective-permute-done.5.left_ref) | copy-start | bytes 1572868
  50.8 15.6 %collective-permute-start.7 = (bf16[16,128,128]{2,1,0:T(8,128)(2,1)S(1)}, bf16[16,128,128]{2,1,0:T(8,128)(2,1)S(1)}, u32[]{:S(2)}, u32[]{:S(2)}) collective-permute-start(bf16[16,128,128]{2,1,0:T(8,128)(2,1)S(1)} %collective-permute-done.5.left_ref), channel_id=1, source_target_pairs={{0,3},{1,0},{2,1},{3,2},{4,7},{5,4},{6,5},{7,6},{8,11},{9,8},{10,9... | collective-permute-start | bytes 1572872 | tf_op jit(solution)/shard_map/ppermute | solution.py:16
  54.1 12.2 %collective-permute-start.8 = (bf16[16,128,128]{2,1,0:T(8,128)(2,1)}, bf16[16,128,128]{2,1,0:T(8,128)(2,1)S(1)}, u32[]{:S(2)}, u32[]{:S(2)}) collective-permute-start(bf16[16,128,128]{2,1,0:T(8,128)(2,1)} %collective-permute-done.6.right_ref), channel_id=1, source_target_pairs={{0,28},{4,0},{8,4},{12,8},{16,12},{20,16},{24,20},{28,24},{1,29},{... | collective-permute-start | bytes 1572872 | tf_op jit(solution)/shard_map/ppermute | solution.py:16
  66.4 0.8 copy-start.4
  67.2 0.8 copy-start.5

commit v9 on v7

--- a/solution.py
+++ b/solution.py
@@ -24,7 +24,7 @@
 GROUP = 32
 
 
-def stop_kernel(stop, first, last, stack_ref, map_ref, n_ref, left_ref, right_ref, *refs):
+def stop_kernel(stop, first, last, stack_ref, map_ref, n_ref, send_ref, left_ref, right_ref, *refs):
     if first:
         acc_out_ref, acc_ref = refs[0], refs[-1]
     else:
@@ -60,34 +60,44 @@
     else:
         acc_ref[...] = acc_in_ref[...]
     lax.fori_loop(0, (live_count + GROUP - 1) // GROUP, per_group, 0)
-    acc_out_ref[...] = acc_ref[...].astype(acc_out_ref.dtype)
+    if last:
+        def per_slot(e, carry):
+            wanted = send_ref[e]
+            block = acc_ref[jnp.clip(wanted, 0, result_count - 1)]
+            acc_out_ref[e] = jnp.where(wanted >= 0, block, 0.0).astype(acc_out_ref.dtype)
+            return carry
+
+        lax.fori_loop(0, acc_out_ref.shape[0], per_slot, 0)
+    else:
+        acc_out_ref[...] = acc_ref[...]
 
 
-def run_stop(total, left, right, stacks, left_maps, live_counts, stop, last, result_shape):
+def run_stop(total, left, right, stacks, left_maps, live_counts, c_send, stop, last, result_shape):
     assert stacks.shape[-1] % GROUP == 0
     first = total is None
     full = lambda shape: pl.BlockSpec(shape, lambda *_: (0,) * len(shape))
     in_specs = [full(left.shape), full(right.shape)]
-    operands = [stacks, left_maps, live_counts, left, right]
+    operands = [stacks, left_maps, live_counts, c_send, left, right]
     aliases = {}
     if not first:
         in_specs.append(full(result_shape))
         operands.append(total)
         if not last:
-            aliases = {5: 0}
+            aliases = {6: 0}
     scratch = [pltpu.VMEM(result_shape, jnp.float32)]
     out_dtype = jnp.bfloat16 if last else jnp.float32
+    out_shape = (c_send.shape[0],) + result_shape[1:] if last else result_shape
     grid_spec = pltpu.PrefetchScalarGridSpec(
-        num_scalar_prefetch=3,
+        num_scalar_prefetch=4,
         grid=(1,),
         in_specs=in_specs,
-        out_specs=full(result_shape),
+        out_specs=full(out_shape),
         scratch_shapes=scratch,
     )
     return pl.pallas_call(
         functools.partial(stop_kernel, stop, first, last),
         grid_spec=grid_spec,
-        out_shape=jax.ShapeDtypeStruct(result_shape, out_dtype),
+        out_shape=jax.ShapeDtypeStruct(out_shape, out_dtype),
         input_output_aliases=aliases,
     )(*operands)
 
@@ -124,10 +134,9 @@
             right_now = passed_along(right_now, "row", -1)
         if stop_index > 0:
             left_now, right_now, total = lax.optimization_barrier((left_now, right_now, total))
-        total = run_stop(total, left_now, right_now, stacks, left_maps, live_counts, stop_index,
+        total = run_stop(total, left_now, right_now, stacks, left_maps, live_counts, c_send[0, 0], stop_index,
                          stop_index == STOPS - 1, result_shape)
-    result = total
-    outgoing = bucketize(result, c_send[0, 0])
+    outgoing = total
     arrived = lax.all_to_all(outgoing, ("row", "col"), split_axis=0, concat_axis=0, tiled=True)
     return arrived[None, None]
 

time: 113 us -> 112 us (level); the launches traced: 112 us -> 113 us
  starting transfers between devices: 23.6 us -> 17.4 us
  Pallas kernels: 36.1 us -> 40.3 us
  blocking collectives: 32.5 us -> 36.2 us
  waiting for transfers between devices: 9.53 us -> 11.4 us
  local copies, waits for them, and re-layouts: 6.16 us -> 4.37 us
    ppermute x9, starting transfers between devices: 18.2 us -> 12 us  [passed_along(): return lax.ppermute(value, axis, pairs)]
    pallas_call x4, Pallas kernels: 36.1 us -> 40.3 us  [run_stop(): pl.pallas_call(functools.partial(stop_kernel, stop, first, last), grid_sp...]
    all_to_all x1, blocking collectives: 32.5 us -> 36.2 us  [on_device(): lax.all_to_all(outgoing, ('row', 'col'), split_axis=0, concat_axis=0, til...]
    ppermute x9, waiting for transfers between devices: 9.52 us -> 11.4 us  [passed_along(): return lax.ppermute(value, axis, pairs)]
    gather x3 -> x2, local copies, waits for them, and re-layouts: 3.08 us -> 1.3 us  [bucketize(): picked = jnp.take(blocks, jnp.maximum(index, 0), axis=0)]
  transfers between devices with their start and end apart: 10 -> 10, of which waited for: 3 -> 3; matrix products, arithmetic and copies ran while one was open for 2% -> 2% of each run, Pallas kernels for 25% -> 27%
where the time goes in v9:
time: 112 us; the launch traced here: 113 us
  Pallas kernels  40.3 us (36%)
  blocking collectives  36.2 us (32%)
  starting transfers between devices  17.4 us (16%)
  waiting for transfers between devices  11.4 us (10%)
  local copies, waits for them, and re-layouts  4.37 us (4%)
  other arithmetic  3.33 us (3%)
    pallas_call x4, Pallas kernels, run_stop(): pl.pallas_call(functools.partial(stop_kernel, stop, first, last), grid_sp...  40.3 us
    all_to_all x1, blocking collectives, on_device(): lax.all_to_all(outgoing, ('row', 'col'), split_axis=0, concat_axis=0, til...  36.2 us
    ppermute x9, starting transfers between devices, passed_along(): return lax.ppermute(value, axis, pairs)  12 us
    ppermute x9, waiting for transfers between devices, passed_along(): return lax.ppermute(value, axis, pairs)  11.4 us
    all_to_all x1, starting transfers between devices, on_device(): lax.all_to_all(right_out, 'row', split_axis=0, concat_axis=0, tiled=True)  5.35 us
    unnamed x30, local copies, waits for them, and re-layouts  2.64 us
  transfers between devices with their start and end apart: 10, of which 3 were waited for; matrix products, arithmetic and copies ran while one was open for 2% of the time, Pallas kernels for 27%

profile of v9, /device:TPU:1, one launch (start us, length us, event | category | flops | bytes accessed | tf_op | source)
XLA Modules:
  0.0 113.2 jit_solution(9492256485259026804)
XLA Ops:
  0.0 0.8 broadcast_maximum_fusion.1
  0.8 0.1 copy.14
  0.9 0.1 copy.15
  1.0 0.1 copy.16
  1.0 0.1 reshape.223
  1.1 0.6 gather_fusion.1
  1.8 0.9 select_select_fusion
  2.7 5.4 %all-to-all-start = ((bf16[8,2,128,128]{3,2,1,0:T(8,128)(2,1)}), bf16[8,2,128,128]{3,2,1,0:T(8,128)(2,1)S(1)}, u32[]{:S(2)}, u32[]{:S(2)}) async-start(bf16[8,2,128,128]{3,2,1,0:T(8,128)(2,1)} %select_select_fusion), calls=%async_computation | async-start | bytes 1048576 | tf_op jit(solution)/shard_map/all_to_all | solution.py:125
  8.1 0.1 reshape.215
  8.2 0.6 gather_fusion
  8.9 0.1 select_select_fusion.1
  9.2 3.4 %collective-permute-start.2 = (bf16[4,128,128]{2,1,0:T(8,128)(2,1)S(1)}, bf16[4,128,128]{2,1,0:T(8,128)(2,1)S(1)}, u32[]{:S(2)}, u32[]{:S(2)}) collective-permute-start(bf16[4,128,128]{2,1,0:T(8,128)(2,1)S(1)} %get-tuple-element.36), channel_id=1, source_target_pairs={{0,3},{1,0},{2,1},{3,2},{4,7},{5,4},{6,5},{7,6},{8,11},{9,8},{10,9... | collective-permute-start | bytes 393224 | tf_op jit(solution)/shard_map/ppermute | solution.py:16
  12.5 0.5 collective-permute-start
  13.0 2.5 %collective-permute-done.2 = bf16[4,128,128]{2,1,0:T(8,128)(2,1)S(1)} collective-permute-done((bf16[4,128,128]{2,1,0:T(8,128)(2,1)S(1)}, bf16[4,128,128]{2,1,0:T(8,128)(2,1)S(1)}, u32[]{:S(2)}, u32[]{:S(2)}) %collective-permute-start.2) | collective-permute-done | bytes 131104 | tf_op jit(solution)/shard_map/ppermute | solution.py:16
  15.5 8.6 %collective-permute-done.1 = bf16[4,128,128]{2,1,0:T(8,128)(2,1)S(1)} collective-permute-done((bf16[4,128,128]{2,1,0:T(8,128)(2,1)S(1)}, bf16[4,128,128]{2,1,0:T(8,128)(2,1)S(1)}, u32[]{:S(2)}, u32[]{:S(2)}) %collective-permute-start.1) | collective-permute-done | bytes 131104 | tf_op jit(solution)/shard_map/ppermute | solution.py:16
  24.1 0.1 pad_maximum_fusion.left_ref
  24.3 2.0 %collective-permute-start.4 = (bf16[16,128,128]{2,1,0:T(8,128)(2,1)S(1)}, bf16[16,128,128]{2,1,0:T(8,128)(2,1)S(1)}, u32[]{:S(2)}, u32[]{:S(2)}) collective-permute-start(bf16[16,128,128]{2,1,0:T(8,128)(2,1)S(1)} %bitcast.30), channel_id=1, source_target_pairs={{0,28},{4,0},{8,4},{12,8},{16,12},{20,16},{24,20},{28,24},{1,29},{... | collective-permute-start | bytes 1572872 | tf_op jit(solution)/shard_map/ppermute | solution.py:16
  26.3 0.7 fusion.n_ref
  27.0 0.7 fusion.2.map_ref
  27.7 9.5 %shard_map.64.refs_0_ = f32[16,128,128]{2,1,0:T(8,128)} custom-call(s32[4,3,384]{2,1,0:T(4,128)} %bitcast.35, s32[4,16]{1,0:T(4,128)} %fusion.2.map_ref, s32[4]{0:T(128)} %fusion.n_ref, s32[32]{0:T(128)} %bitcast.40, bf16[16,128,128]{2,1,0:T(8,128)(2,1)} %copy-done.2, bf16[16,128,128]{2,1,0:T(8,128)(2,1)} %bitcast.31), custom_call_target="tpu_custom_call" | custom-call | tf_op jit(solution)/shard_map/pallas_call | solution.py:97
  37.2 0.6 collective-permute-start.5
  37.8 3.0 %collective-permute-start.6 = (bf16[16,128,128]{2,1,0:T(8,128)(2,1)S(1)}, bf16[16,128,128]{2,1,0:T(8,128)(2,1)S(1)}, u32[]{:S(2)}, u32[]{:S(2)}) collective-permute-start(bf16[16,128,128]{2,1,0:T(8,128)(2,1)S(1)} %collective-permute-done.4.right_ref), channel_id=1, source_target_pairs={{0,28},{4,0},{8,4},{12,8},{16,12},{20,16},{24,20},{28,24},{1,29},{... | collective-permute-start | bytes 1572872 | tf_op jit(solution)/shard_map/ppermute | solution.py:16
  40.7 10.9 %shard_map.65.refs_0_ = f32[16,128,128]{2,1,0:T(8,128)} custom-call(s32[4,3,384]{2,1,0:T(4,128)} %bitcast.36, s32[4,16]{1,0:T(4,128)} %fusion.2.map_ref, s32[4]{0:T(128)} %fusion.n_ref, s32[32]{0:T(128)} %bitcast.41, bf16[16,128,128]{2,1,0:T(8,128)(2,1)} %copy-done.4, bf16[16,128,128]{2,1,0:T(8,128)(2,1)} %copy-done.5, ...), custom_call_target="tpu_custom_call", output_to_operand_aliasing={{}: (6, {})} | custom-call | tf_op jit(solution)/shard_map/pallas_call | solution.py:97
  51.7 1.3 %collective-permute-start.7 = (bf16[16,128,128]{2,1,0:T(8,128)(2,1)S(1)}, bf16[16,128,128]{2,1,0:T(8,128)(2,1)S(1)}, u32[]{:S(2)}, u32[]{:S(2)}) collective-permute-start(bf16[16,128,128]{2,1,0:T(8,128)(2,1)S(1)} %collective-permute-done.5.left_ref), channel_id=1, source_target_pairs={{0,3},{1,0},{2,1},{3,2},{4,7},{5,4},{6,5},{7,6},{8,11},{9,8},{10,9... | collective-permute-start | bytes 1572872 | tf_op jit(solution)/shard_map/ppermute | solution.py:16
  53.0 1.3 %collective-permute-start.8 = (bf16[16,128,128]{2,1,0:T(8,128)(2,1)S(1)}, bf16[16,128,128]{2,1,0:T(8,128)(2,1)S(1)}, u32[]{:S(2)}, u32[]{:S(2)}) collective-permute-start(bf16[16,128,128]{2,1,0:T(8,128)(2,1)S(1)} %collective-permute-done.6.right_ref), channel_id=1, source_target_pairs={{0,28},{4,0},{8,4},{12,8},{16,12},{20,16},{24,20},{28,24},{1,29},{... | collective-permute-start | bytes 1572872 | tf_op jit(solution)/shard_map/ppermute | solution.py:16
  54.3 10.3 %shard_map.66.refs_0_ = f32[16,128,128]{2,1,0:T(8,128)} custom-call(s32[4,3,384]{2,1,0:T(4,128)} %bitcast.37, s32[4,16]{1,0:T(4,128)} %fusion.2.map_ref, s32[4]{0:T(128)} %fusion.n_ref, s32[32]{0:T(128)} %bitcast.42, bf16[16,128,128]{2,1,0:T(8,128)(2,1)} %copy-done.6, bf16[16,128,128]{2,1,0:T(8,128)(2,1)} %copy-done.7, ...), custom_call_target="tpu_custom_call", output_to_operand_aliasing={{}: (6, {})} | custom-call | tf_op jit(solution)/shard_map/pallas_call | solution.py:97
  64.5 0.3 collective-permute-done.7.left_ref
  64.8 0.8 copy-done.8
  65.7 0.8 copy-done.9
  66.4 9.5 %shard_map.67 = bf16[32,128,128]{2,1,0:T(8,128)(2,1)} custom-call(s32[4,3,384]{2,1,0:T(4,128)} %bitcast.38, s32[4,16]{1,0:T(4,128)} %fusion.2.map_ref, s32[4]{0:T(128)} %fusion.n_ref, s32[32]{0:T(128)} %bitcast.43, bf16[16,128,128]{2,1,0:T(8,128)(2,1)} %copy-done.8, bf16[16,128,128]{2,1,0:T(8,128)(2,1)} %copy-done.9, f32[16,128,128]{2,1,0:T(8,128)} %shard_map.66.refs_0_), custom_call_target="tpu_custom_call" | custom-call | tf_op jit(solution)/shard_map/pallas_call | solution.py:97
  76.0 36.2 %all_to_all.10 = bf16[32,128,128]{2,1,0:T(8,128)(2,1)S(1)} all-to-all(bf16[32,128,128]{2,1,0:T(8,128)(2,1)} %shard_map.67), channel_id=1, replica_groups=mesh['row'=8,'col'=4] {'row','col'}, dimensions={0} | all-to-all | bytes 2097152 | tf_op jit(solution)/shard_map/all_to_all | solution.py:140
  112.2 1.0 copy.22
  (44 shorter events, 0.2 us)
Async XLA Ops:
  0.0 1.1 %copy-start = (bf16[1,1,16,128,128]{4,3,2,1,0:T(8,128)(2,1)S(1)}, bf16[1,1,16,128,128]{4,3,2,1,0:T(8,128)(2,1)}, u32[]{:S(2)}) copy-start(bf16[1,1,16,128,128]{4,3,2,1,0:T(8,128)(2,1)} %param.9) | copy-start | bytes 1572868
  0.0 0.8 copy-start.13
  2.7 5.4 %copy-start.12 = (s32[1,1,4,4]{3,2,1,0:T(4,128)S(1)}, s32[1,1,4,4]{3,2,1,0:T(4,128)}, u32[]{:S(2)}) copy-start(s32[1,1,4,4]{3,2,1,0:T(4,128)} %param.10) | copy-start | bytes 196
  2.7 5.5 %copy-start.10 = (bf16[1,1,16,128,128]{4,3,2,1,0:T(8,128)(2,1)S(1)}, bf16[1,1,16,128,128]{4,3,2,1,0:T(8,128)(2,1)}, u32[]{:S(2)}) copy-start(bf16[1,1,16,128,128]{4,3,2,1,0:T(8,128)(2,1)} %param.8) | copy-start | bytes 1572868
  2.7 21.5 %all-to-all-start = ((bf16[8,2,128,128]{3,2,1,0:T(8,128)(2,1)}), bf16[8,2,128,128]{3,2,1,0:T(8,128)(2,1)S(1)}, u32[]{:S(2)}, u32[]{:S(2)}) async-start(bf16[8,2,128,128]{3,2,1,0:T(8,128)(2,1)} %select_select_fusion), calls=%async_computation | async-start | bytes 1048576 | tf_op jit(solution)/shard_map/all_to_all | solution.py:125
  9.1 3.9 %copy-start.11 = (s32[1,1,4,3,384]{4,2,3,1,0:T(4,128)S(1)}, s32[1,1,4,3,384]{4,2,3,1,0:T(4,128)}, u32[]{:S(2)}) copy-start(s32[1,1,4,3,384]{4,2,3,1,0:T(4,128)} %param.12) | copy-start | bytes 55300
  9.2 6.3 %collective-permute-start.2 = (bf16[4,128,128]{2,1,0:T(8,128)(2,1)S(1)}, bf16[4,128,128]{2,1,0:T(8,128)(2,1)S(1)}, u32[]{:S(2)}, u32[]{:S(2)}) collective-permute-start(bf16[4,128,128]{2,1,0:T(8,128)(2,1)S(1)} %get-tuple-element.36), channel_id=1, source_target_pairs={{0,3},{1,0},{2,1},{3,2},{4,7},{5,4},{6,5},{7,6},{8,11},{9,8},{10,9... | collective-permute-start | bytes 393224 | tf_op jit(solution)/shard_map/ppermute | solution.py:16
  12.5 11.6 %collective-permute-start.1 = (bf16[4,128,128]{2,1,0:T(8,128)(2,1)S(1)}, bf16[4,128,128]{2,1,0:T(8,128)(2,1)S(1)}, u32[]{:S(2)}, u32[]{:S(2)}) collective-permute-start(bf16[4,128,128]{2,1,0:T(8,128)(2,1)S(1)} %get-tuple-element.37), channel_id=1, source_target_pairs={{0,2},{1,3},{2,0},{3,1},{4,6},{5,7},{6,4},{7,5},{8,10},{9,11},{10,... | collective-permute-start | bytes 393224 | tf_op jit(solution)/shard_map/ppermute | solution.py:16
  12.5 11.6 %collective-permute-start = (bf16[4,128,128]{2,1,0:T(8,128)(2,1)S(1)}, bf16[4,128,128]{2,1,0:T(8,128)(2,1)S(1)}, u32[]{:S(2)}, u32[]{:S(2)}) collective-permute-start(bf16[4,128,128]{2,1,0:T(8,128)(2,1)S(1)} %get-tuple-element.38), channel_id=1, source_target_pairs={{0,1},{1,2},{2,3},{3,0},{4,5},{5,6},{6,7},{7,4},{8,9},{9,10},{10,1... | collective-permute-start | bytes 393224 | tf_op jit(solution)/shard_map/ppermute | solution.py:16
  13.0 13.3 %copy-start.3 = (s32[1,1,4,3,384]{4,3,2,1,0:T(4,128)}, s32[1,1,4,3,384]{4,3,2,1,0:T(4,128)S(1)}, u32[]{:S(2)}) copy-start(s32[1,1,4,3,384]{4,3,2,1,0:T(4,128)S(1)} %copy.18) | copy-start | bytes 55300
  24.2 3.5 %copy-start.2 = (bf16[16,128,128]{2,1,0:T(8,128)(2,1)}, bf16[16,128,128]{2,1,0:T(8,128)(2,1)S(1)}, u32[]{:S(2)}) copy-start(bf16[16,128,128]{2,1,0:T(8,128)(2,1)S(1)} %pad_maximum_fusion.left_ref) | copy-start | bytes 1572868
  24.2 13.0 %collective-permute-start.3 = (bf16[16,128,128]{2,1,0:T(8,128)(2,1)S(1)}, bf16[16,128,128]{2,1,0:T(8,128)(2,1)S(1)}, u32[]{:S(2)}, u32[]{:S(2)}) collective-permute-start(bf16[16,128,128]{2,1,0:T(8,128)(2,1)S(1)} %pad_maximum_fusion.left_ref), channel_id=1, source_target_pairs={{0,3},{1,0},{2,1},{3,2},{4,7},{5,4},{6,5},{7,6},{8,11},{9,8},{10,9... | collective-permute-start | bytes 1572872 | tf_op jit(solution)/shard_map/ppermute | solution.py:16
  24.3 3.4 %copy-start.1 = (bf16[8,2,128,128]{3,2,1,0:T(8,128)(2,1)}, bf16[8,2,128,128]{3,2,1,0:T(8,128)(2,1)S(1)}, u32[]{:S(2)}) copy-start(bf16[8,2,128,128]{3,2,1,0:T(8,128)(2,1)S(1)} %all-to-all-done) | copy-start | bytes 1572868
  24.3 12.9 %collective-permute-start.4 = (bf16[16,128,128]{2,1,0:T(8,128)(2,1)S(1)}, bf16[16,128,128]{2,1,0:T(8,128)(2,1)S(1)}, u32[]{:S(2)}, u32[]{:S(2)}) collective-permute-start(bf16[16,128,128]{2,1,0:T(8,128)(2,1)S(1)} %bitcast.30), channel_id=1, source_target_pairs={{0,28},{4,0},{8,4},{12,8},{16,12},{20,16},{24,20},{28,24},{1,29},{... | collective-permute-start | bytes 1572872 | tf_op jit(solution)/shard_map/ppermute | solution.py:16
  37.2 3.5 %copy-start.4 = (bf16[16,128,128]{2,1,0:T(8,128)(2,1)}, bf16[16,128,128]{2,1,0:T(8,128)(2,1)S(1)}, u32[]{:S(2)}) copy-start(bf16[16,128,128]{2,1,0:T(8,128)(2,1)S(1)} %collective-permute-done.3.left_ref) | copy-start | bytes 1572868
  37.2 3.5 %copy-start.5 = (bf16[16,128,128]{2,1,0:T(8,128)(2,1)}, bf16[16,128,128]{2,1,0:T(8,128)(2,1)S(1)}, u32[]{:S(2)}) copy-start(bf16[16,128,128]{2,1,0:T(8,128)(2,1)S(1)} %collective-permute-done.4.right_ref) | copy-start | bytes 1572868
  37.2 14.4 %collective-permute-start.5 = (bf16[16,128,128]{2,1,0:T(8,128)(2,1)S(1)}, bf16[16,128,128]{2,1,0:T(8,128)(2,1)S(1)}, u32[]{:S(2)}, u32[]{:S(2)}) collective-permute-start(bf16[16,128,128]{2,1,0:T(8,128)(2,1)S(1)} %collective-permute-done.3.left_ref), channel_id=1, source_target_pairs={{0,3},{1,0},{2,1},{3,2},{4,7},{5,4},{6,5},{7,6},{8,11},{9,8},{10,9... | collective-permute-start | bytes 1572872 | tf_op jit(solution)/shard_map/ppermute | solution.py:16
  37.8 13.9 %collective-permute-start.6 = (bf16[16,128,128]{2,1,0:T(8,128)(2,1)S(1)}, bf16[16,128,128]{2,1,0:T(8,128)(2,1)S(1)}, u32[]{:S(2)}, u32[]{:S(2)}) collective-permute-start(bf16[16,128,128]{2,1,0:T(8,128)(2,1)S(1)} %collective-permute-done.4.right_ref), channel_id=1, source_target_pairs={{0,28},{4,0},{8,4},{12,8},{16,12},{20,16},{24,20},{28,24},{1,29},{... | collective-permute-start | bytes 1572872 | tf_op jit(solution)/shard_map/ppermute | solution.py:16
  51.7 2.6 %copy-start.6 = (bf16[16,128,128]{2,1,0:T(8,128)(2,1)}, bf16[16,128,128]{2,1,0:T(8,128)(2,1)S(1)}, u32[]{:S(2)}) copy-start(bf16[16,128,128]{2,1,0:T(8,128)(2,1)S(1)} %collective-permute-done.5.left_ref) | copy-start | bytes 1572868
  51.7 2.6 %copy-start.7 = (bf16[16,128,128]{2,1,0:T(8,128)(2,1)}, bf16[16,128,128]{2,1,0:T(8,128)(2,1)S(1)}, u32[]{:S(2)}) copy-start(bf16[16,128,128]{2,1,0:T(8,128)(2,1)S(1)} %collective-permute-done.6.right_ref) | copy-start | bytes 1572868
  51.7 13.2 %collective-permute-start.7 = (bf16[16,128,128]{2,1,0:T(8,128)(2,1)S(1)}, bf16[16,128,128]{2,1,0:T(8,128)(2,1)S(1)}, u32[]{:S(2)}, u32[]{:S(2)}) collective-permute-start(bf16[16,128,128]{2,1,0:T(8,128)(2,1)S(1)} %collective-permute-done.5.left_ref), channel_id=1, source_target_pairs={{0,3},{1,0},{2,1},{3,2},{4,7},{5,4},{6,5},{7,6},{8,11},{9,8},{10,9... | collective-permute-start | bytes 1572872 | tf_op jit(solution)/shard_map/ppermute | solution.py:16
  53.0 11.9 %collective-permute-start.8 = (bf16[16,128,128]{2,1,0:T(8,128)(2,1)S(1)}, bf16[16,128,128]{2,1,0:T(8,128)(2,1)S(1)}, u32[]{:S(2)}, u32[]{:S(2)}) collective-permute-start(bf16[16,128,128]{2,1,0:T(8,128)(2,1)S(1)} %collective-permute-done.6.right_ref), channel_id=1, source_target_pairs={{0,28},{4,0},{8,4},{12,8},{16,12},{20,16},{24,20},{28,24},{1,29},{... | collective-permute-start | bytes 1572872 | tf_op jit(solution)/shard_map/ppermute | solution.py:16
  64.8 0.8 copy-start.8
  65.7 0.8 copy-start.9

commit v10 on v9

--- a/solution.py
+++ b/solution.py
@@ -61,13 +61,10 @@
         acc_ref[...] = acc_in_ref[...]
     lax.fori_loop(0, (live_count + GROUP - 1) // GROUP, per_group, 0)
     if last:
-        def per_slot(e, carry):
+        for e in range(acc_out_ref.shape[0]):
             wanted = send_ref[e]
-            block = acc_ref[jnp.clip(wanted, 0, result_count - 1)]
-            acc_out_ref[e] = jnp.where(wanted >= 0, block, 0.0).astype(acc_out_ref.dtype)
-            return carry
-
-        lax.fori_loop(0, acc_out_ref.shape[0], per_slot, 0)
+            block = acc_ref[jnp.clip(wanted, 0, result_count - 1)].astype(acc_out_ref.dtype)
+            acc_out_ref[e] = jnp.where(wanted >= 0, block, jnp.zeros_like(block))
     else:
         acc_out_ref[...] = acc_ref[...]
 
@@ -137,8 +134,7 @@
         total = run_stop(total, left_now, right_now, stacks, left_maps, live_counts, c_send[0, 0], stop_index,
                          stop_index == STOPS - 1, result_shape)
     outgoing = total
-    arrived = lax.all_to_all(outgoing, ("row", "col"), split_axis=0, concat_axis=0, tiled=True)
-    return arrived[None, None]
+    return lax.all_to_all(outgoing[None, None], ("row", "col"), split_axis=2, concat_axis=2, tiled=True)
 
 
 def solution(mesh):

time: 112 us -> 113 us (level); the launches traced: 113 us -> 110 us
  blocking collectives: 36.2 us -> 32.4 us
    all_to_all x1, blocking collectives: 36.2 us -> 32.4 us  [on_device(): lax.all_to_all(outgoing[None, None], ('row', 'col'), split_axis=2, concat...]
  transfers between devices with their start and end apart: 10 -> 10, of which waited for: 3 -> 4; matrix products, arithmetic and copies ran while one was open for 2% -> 2% of each run, Pallas kernels for 27% -> 27%
where the time goes in v10:
time: 113 us; the launch traced here: 110 us
  Pallas kernels  40 us (35%)
  blocking collectives  32.4 us (29%)
  starting transfers between devices  18.3 us (16%)
  waiting for transfers between devices  11.7 us (10%)
  local copies, waits for them, and re-layouts  4.37 us (4%)
  other arithmetic  3.33 us (3%)
    pallas_call x4, Pallas kernels, run_stop(): pl.pallas_call(functools.partial(stop_kernel, stop, first, last), grid_sp...  40 us
    all_to_all x1, blocking collectives, on_device(): lax.all_to_all(outgoing[None, None], ('row', 'col'), split_axis=2, concat...  32.4 us
    ppermute x9, starting transfers between devices, passed_along(): return lax.ppermute(value, axis, pairs)  12.9 us
    ppermute x9, waiting for transfers between devices, passed_along(): return lax.ppermute(value, axis, pairs)  11.7 us
    all_to_all x1, starting transfers between devices, on_device(): lax.all_to_all(right_out, 'row', split_axis=0, concat_axis=0, tiled=True)  5.35 us
    unnamed x30, local copies, waits for them, and re-layouts  2.64 us
  transfers between devices with their start and end apart: 10, of which 4 were waited for; matrix products, arithmetic and copies ran while one was open for 2% of the time, Pallas kernels for 27%

profile of v10, /device:TPU:1, one launch (start us, length us, event | category | flops | bytes accessed | tf_op | source)
XLA Modules:
  0.0 110.4 jit_solution(1114446670691404436)
XLA Ops:
  0.0 0.8 broadcast_maximum_fusion.1
  0.8 0.1 copy.18
  0.9 0.1 copy.19
  1.0 0.1 copy.20
  1.0 0.1 reshape.223
  1.1 0.6 gather_fusion.1
  1.8 0.9 select_select_fusion
  2.7 5.4 %all-to-all-start = ((bf16[8,2,128,128]{3,2,1,0:T(8,128)(2,1)}), bf16[8,2,128,128]{3,2,1,0:T(8,128)(2,1)S(1)}, u32[]{:S(2)}, u32[]{:S(2)}) async-start(bf16[8,2,128,128]{3,2,1,0:T(8,128)(2,1)} %select_select_fusion), calls=%async_computation | async-start | bytes 1048576 | tf_op jit(solution)/shard_map/all_to_all | solution.py:122
  8.1 0.1 reshape.215
  8.2 0.6 gather_fusion
  8.9 0.1 select_select_fusion.1
  9.2 3.4 %collective-permute-start.2 = (bf16[4,128,128]{2,1,0:T(8,128)(2,1)S(1)}, bf16[4,128,128]{2,1,0:T(8,128)(2,1)S(1)}, u32[]{:S(2)}, u32[]{:S(2)}) collective-permute-start(bf16[4,128,128]{2,1,0:T(8,128)(2,1)S(1)} %get-tuple-element.36), channel_id=1, source_target_pairs={{0,3},{1,0},{2,1},{3,2},{4,7},{5,4},{6,5},{7,6},{8,11},{9,8},{10,9... | collective-permute-start | bytes 393224 | tf_op jit(solution)/shard_map/ppermute | solution.py:16
  12.5 0.5 collective-permute-start
  13.0 2.5 %collective-permute-done.2 = bf16[4,128,128]{2,1,0:T(8,128)(2,1)S(1)} collective-permute-done((bf16[4,128,128]{2,1,0:T(8,128)(2,1)S(1)}, bf16[4,128,128]{2,1,0:T(8,128)(2,1)S(1)}, u32[]{:S(2)}, u32[]{:S(2)}) %collective-permute-start.2) | collective-permute-done | bytes 131104 | tf_op jit(solution)/shard_map/ppermute | solution.py:16
  15.5 8.6 %collective-permute-done.1 = bf16[4,128,128]{2,1,0:T(8,128)(2,1)S(1)} collective-permute-done((bf16[4,128,128]{2,1,0:T(8,128)(2,1)S(1)}, bf16[4,128,128]{2,1,0:T(8,128)(2,1)S(1)}, u32[]{:S(2)}, u32[]{:S(2)}) %collective-permute-start.1) | collective-permute-done | bytes 131104 | tf_op jit(solution)/shard_map/ppermute | solution.py:16
  24.3 2.0 %collective-permute-start.4 = (bf16[16,128,128]{2,1,0:T(8,128)(2,1)S(1)}, bf16[16,128,128]{2,1,0:T(8,128)(2,1)S(1)}, u32[]{:S(2)}, u32[]{:S(2)}) collective-permute-start(bf16[16,128,128]{2,1,0:T(8,128)(2,1)S(1)} %bitcast.34), channel_id=1, source_target_pairs={{0,28},{4,0},{8,4},{12,8},{16,12},{20,16},{24,20},{28,24},{1,29},{... | collective-permute-start | bytes 1572872 | tf_op jit(solution)/shard_map/ppermute | solution.py:16
  26.3 0.7 fusion.n_ref
  27.0 0.7 fusion.2.map_ref
  27.7 9.0 %shard_map.64.refs_0_ = f32[16,128,128]{2,1,0:T(8,128)} custom-call(s32[4,3,384]{2,1,0:T(4,128)} %bitcast.39, s32[4,16]{1,0:T(4,128)} %fusion.2.map_ref, s32[4]{0:T(128)} %fusion.n_ref, s32[32]{0:T(128)} %bitcast.44, bf16[16,128,128]{2,1,0:T(8,128)(2,1)} %copy-done.2, bf16[16,128,128]{2,1,0:T(8,128)(2,1)} %bitcast.35), custom_call_target="tpu_custom_call" | custom-call | tf_op jit(solution)/shard_map/pallas_call | solution.py:94
  36.6 0.2 collective-permute-done.3.left_ref
  36.9 0.9 collective-permute-start.5
  37.8 3.3 %collective-permute-start.6 = (bf16[16,128,128]{2,1,0:T(8,128)(2,1)S(1)}, bf16[16,128,128]{2,1,0:T(8,128)(2,1)S(1)}, u32[]{:S(2)}, u32[]{:S(2)}) collective-permute-start(bf16[16,128,128]{2,1,0:T(8,128)(2,1)S(1)} %collective-permute-done.4.right_ref), channel_id=1, source_target_pairs={{0,28},{4,0},{8,4},{12,8},{16,12},{20,16},{24,20},{28,24},{1,29},{... | collective-permute-start | bytes 1572872 | tf_op jit(solution)/shard_map/ppermute | solution.py:16
  41.1 10.3 %shard_map.65.refs_0_ = f32[16,128,128]{2,1,0:T(8,128)} custom-call(s32[4,3,384]{2,1,0:T(4,128)} %bitcast.40, s32[4,16]{1,0:T(4,128)} %fusion.2.map_ref, s32[4]{0:T(128)} %fusion.n_ref, s32[32]{0:T(128)} %bitcast.45, bf16[16,128,128]{2,1,0:T(8,128)(2,1)} %copy-done.4, bf16[16,128,128]{2,1,0:T(8,128)(2,1)} %copy-done.5, ...), custom_call_target="tpu_custom_call", output_to_operand_aliasing={{}: (6, {})} | custom-call | tf_op jit(solution)/shard_map/pallas_call | solution.py:94
  51.4 0.9 collective-permute-start.7
  52.4 1.9 %collective-permute-start.8 = (bf16[16,128,128]{2,1,0:T(8,128)(2,1)S(1)}, bf16[16,128,128]{2,1,0:T(8,128)(2,1)S(1)}, u32[]{:S(2)}, u32[]{:S(2)}) collective-permute-start(bf16[16,128,128]{2,1,0:T(8,128)(2,1)S(1)} %collective-permute-done.6.right_ref), channel_id=1, source_target_pairs={{0,28},{4,0},{8,4},{12,8},{16,12},{20,16},{24,20},{28,24},{1,29},{... | collective-permute-start | bytes 1572872 | tf_op jit(solution)/shard_map/ppermute | solution.py:16
  54.3 10.3 %shard_map.66.refs_0_ = f32[16,128,128]{2,1,0:T(8,128)} custom-call(s32[4,3,384]{2,1,0:T(4,128)} %bitcast.41, s32[4,16]{1,0:T(4,128)} %fusion.2.map_ref, s32[4]{0:T(128)} %fusion.n_ref, s32[32]{0:T(128)} %bitcast.46, bf16[16,128,128]{2,1,0:T(8,128)(2,1)} %copy-done.6, bf16[16,128,128]{2,1,0:T(8,128)(2,1)} %copy-done.7, ...), custom_call_target="tpu_custom_call", output_to_operand_aliasing={{}: (6, {})} | custom-call | tf_op jit(solution)/shard_map/pallas_call | solution.py:94
  64.5 0.3 collective-permute-done.7.left_ref
  64.9 0.8 copy-done.8
  65.7 0.8 copy-done.9
  66.5 10.5 %shard_map.67 = bf16[32,128,128]{2,1,0:T(8,128)(2,1)} custom-call(s32[4,3,384]{2,1,0:T(4,128)} %bitcast.42, s32[4,16]{1,0:T(4,128)} %fusion.2.map_ref, s32[4]{0:T(128)} %fusion.n_ref, s32[32]{0:T(128)} %bitcast.47, bf16[16,128,128]{2,1,0:T(8,128)(2,1)} %copy-done.8, bf16[16,128,128]{2,1,0:T(8,128)(2,1)} %copy-done.9, f32[16,128,128]{2,1,0:T(8,128)} %shard_map.66.refs_0_), custom_call_target="tpu_custom_call" | custom-call | tf_op jit(solution)/shard_map/pallas_call | solution.py:94
  77.0 32.4 %all_to_all.10 = bf16[1,1,32,128,128]{4,3,1,0,2:T(8,128)(2,1)S(1)} all-to-all(bf16[1,1,32,128,128]{4,3,1,0,2:T(8,128)(2,1)} %bitcast.32), channel_id=1, replica_groups=mesh['row'=8,'col'=4] {'row','col'}, dimensions={2} | all-to-all | bytes 2097152 | tf_op jit(solution)/shard_map/all_to_all | solution.py:137
  109.4 1.0 copy.28
  (44 shorter events, 0.3 us)
Async XLA Ops:
  0.0 1.1 %copy-start = (bf16[1,1,16,128,128]{4,3,2,1,0:T(8,128)(2,1)S(1)}, bf16[1,1,16,128,128]{4,3,2,1,0:T(8,128)(2,1)}, u32[]{:S(2)}) copy-start(bf16[1,1,16,128,128]{4,3,2,1,0:T(8,128)(2,1)} %param.9) | copy-start | bytes 1572868
  0.0 0.8 copy-start.13
  2.7 5.4 %copy-start.12 = (s32[1,1,4,4]{3,2,1,0:T(4,128)S(1)}, s32[1,1,4,4]{3,2,1,0:T(4,128)}, u32[]{:S(2)}) copy-start(s32[1,1,4,4]{3,2,1,0:T(4,128)} %param.10) | copy-start | bytes 196
  2.7 5.5 %copy-start.10 = (bf16[1,1,16,128,128]{4,3,2,1,0:T(8,128)(2,1)S(1)}, bf16[1,1,16,128,128]{4,3,2,1,0:T(8,128)(2,1)}, u32[]{:S(2)}) copy-start(bf16[1,1,16,128,128]{4,3,2,1,0:T(8,128)(2,1)} %param.8) | copy-start | bytes 1572868
  2.7 21.5 %all-to-all-start = ((bf16[8,2,128,128]{3,2,1,0:T(8,128)(2,1)}), bf16[8,2,128,128]{3,2,1,0:T(8,128)(2,1)S(1)}, u32[]{:S(2)}, u32[]{:S(2)}) async-start(bf16[8,2,128,128]{3,2,1,0:T(8,128)(2,1)} %select_select_fusion), calls=%async_computation | async-start | bytes 1048576 | tf_op jit(solution)/shard_map/all_to_all | solution.py:122
  9.1 3.9 %copy-start.11 = (s32[1,1,4,3,384]{4,2,3,1,0:T(4,128)S(1)}, s32[1,1,4,3,384]{4,2,3,1,0:T(4,128)}, u32[]{:S(2)}) copy-start(s32[1,1,4,3,384]{4,2,3,1,0:T(4,128)} %param.12) | copy-start | bytes 55300
  9.2 6.3 %collective-permute-start.2 = (bf16[4,128,128]{2,1,0:T(8,128)(2,1)S(1)}, bf16[4,128,128]{2,1,0:T(8,128)(2,1)S(1)}, u32[]{:S(2)}, u32[]{:S(2)}) collective-permute-start(bf16[4,128,128]{2,1,0:T(8,128)(2,1)S(1)} %get-tuple-element.36), channel_id=1, source_target_pairs={{0,3},{1,0},{2,1},{3,2},{4,7},{5,4},{6,5},{7,6},{8,11},{9,8},{10,9... | collective-permute-start | bytes 393224 | tf_op jit(solution)/shard_map/ppermute | solution.py:16
  12.5 11.6 %collective-permute-start.1 = (bf16[4,128,128]{2,1,0:T(8,128)(2,1)S(1)}, bf16[4,128,128]{2,1,0:T(8,128)(2,1)S(1)}, u32[]{:S(2)}, u32[]{:S(2)}) collective-permute-start(bf16[4,128,128]{2,1,0:T(8,128)(2,1)S(1)} %get-tuple-element.37), channel_id=1, source_target_pairs={{0,2},{1,3},{2,0},{3,1},{4,6},{5,7},{6,4},{7,5},{8,10},{9,11},{10,... | collective-permute-start | bytes 393224 | tf_op jit(solution)/shard_map/ppermute | solution.py:16
  12.5 11.6 %collective-permute-start = (bf16[4,128,128]{2,1,0:T(8,128)(2,1)S(1)}, bf16[4,128,128]{2,1,0:T(8,128)(2,1)S(1)}, u32[]{:S(2)}, u32[]{:S(2)}) collective-permute-start(bf16[4,128,128]{2,1,0:T(8,128)(2,1)S(1)} %get-tuple-element.38), channel_id=1, source_target_pairs={{0,1},{1,2},{2,3},{3,0},{4,5},{5,6},{6,7},{7,4},{8,9},{9,10},{10,1... | collective-permute-start | bytes 393224 | tf_op jit(solution)/shard_map/ppermute | solution.py:16
  13.0 13.3 %copy-start.3 = (s32[1,1,4,3,384]{4,3,2,1,0:T(4,128)}, s32[1,1,4,3,384]{4,3,2,1,0:T(4,128)S(1)}, u32[]{:S(2)}) copy-start(s32[1,1,4,3,384]{4,3,2,1,0:T(4,128)S(1)} %copy.24) | copy-start | bytes 55300
  24.2 3.5 %copy-start.2 = (bf16[16,128,128]{2,1,0:T(8,128)(2,1)}, bf16[16,128,128]{2,1,0:T(8,128)(2,1)S(1)}, u32[]{:S(2)}) copy-start(bf16[16,128,128]{2,1,0:T(8,128)(2,1)S(1)} %pad_maximum_fusion.left_ref) | copy-start | bytes 1572868
  24.2 12.7 %collective-permute-start.3 = (bf16[16,128,128]{2,1,0:T(8,128)(2,1)S(1)}, bf16[16,128,128]{2,1,0:T(8,128)(2,1)S(1)}, u32[]{:S(2)}, u32[]{:S(2)}) collective-permute-start(bf16[16,128,128]{2,1,0:T(8,128)(2,1)S(1)} %pad_maximum_fusion.left_ref), channel_id=1, source_target_pairs={{0,3},{1,0},{2,1},{3,2},{4,7},{5,4},{6,5},{7,6},{8,11},{9,8},{10,9... | collective-permute-start | bytes 1572872 | tf_op jit(solution)/shard_map/ppermute | solution.py:16
  24.3 3.4 %copy-start.1 = (bf16[8,2,128,128]{3,2,1,0:T(8,128)(2,1)}, bf16[8,2,128,128]{3,2,1,0:T(8,128)(2,1)S(1)}, u32[]{:S(2)}) copy-start(bf16[8,2,128,128]{3,2,1,0:T(8,128)(2,1)S(1)} %all-to-all-done) | copy-start | bytes 1572868
  24.3 12.6 %collective-permute-start.4 = (bf16[16,128,128]{2,1,0:T(8,128)(2,1)S(1)}, bf16[16,128,128]{2,1,0:T(8,128)(2,1)S(1)}, u32[]{:S(2)}, u32[]{:S(2)}) collective-permute-start(bf16[16,128,128]{2,1,0:T(8,128)(2,1)S(1)} %bitcast.34), channel_id=1, source_target_pairs={{0,28},{4,0},{8,4},{12,8},{16,12},{20,16},{24,20},{28,24},{1,29},{... | collective-permute-start | bytes 1572872 | tf_op jit(solution)/shard_map/ppermute | solution.py:16
  36.9 4.2 %copy-start.4 = (bf16[16,128,128]{2,1,0:T(8,128)(2,1)}, bf16[16,128,128]{2,1,0:T(8,128)(2,1)S(1)}, u32[]{:S(2)}) copy-start(bf16[16,128,128]{2,1,0:T(8,128)(2,1)S(1)} %collective-permute-done.3.left_ref) | copy-start | bytes 1572868
  36.9 4.2 %copy-start.5 = (bf16[16,128,128]{2,1,0:T(8,128)(2,1)}, bf16[16,128,128]{2,1,0:T(8,128)(2,1)S(1)}, u32[]{:S(2)}) copy-start(bf16[16,128,128]{2,1,0:T(8,128)(2,1)S(1)} %collective-permute-done.4.right_ref) | copy-start | bytes 1572868
  36.9 14.6 %collective-permute-start.5 = (bf16[16,128,128]{2,1,0:T(8,128)(2,1)S(1)}, bf16[16,128,128]{2,1,0:T(8,128)(2,1)S(1)}, u32[]{:S(2)}, u32[]{:S(2)}) collective-permute-start(bf16[16,128,128]{2,1,0:T(8,128)(2,1)S(1)} %collective-permute-done.3.left_ref), channel_id=1, source_target_pairs={{0,3},{1,0},{2,1},{3,2},{4,7},{5,4},{6,5},{7,6},{8,11},{9,8},{10,9... | collective-permute-start | bytes 1572872 | tf_op jit(solution)/shard_map/ppermute | solution.py:16
  37.8 13.6 %collective-permute-start.6 = (bf16[16,128,128]{2,1,0:T(8,128)(2,1)S(1)}, bf16[16,128,128]{2,1,0:T(8,128)(2,1)S(1)}, u32[]{:S(2)}, u32[]{:S(2)}) collective-permute-start(bf16[16,128,128]{2,1,0:T(8,128)(2,1)S(1)} %collective-permute-done.4.right_ref), channel_id=1, source_target_pairs={{0,28},{4,0},{8,4},{12,8},{16,12},{20,16},{24,20},{28,24},{1,29},{... | collective-permute-start | bytes 1572872 | tf_op jit(solution)/shard_map/ppermute | solution.py:16
  51.4 2.8 %copy-start.6 = (bf16[16,128,128]{2,1,0:T(8,128)(2,1)}, bf16[16,128,128]{2,1,0:T(8,128)(2,1)S(1)}, u32[]{:S(2)}) copy-start(bf16[16,128,128]{2,1,0:T(8,128)(2,1)S(1)} %collective-permute-done.5.left_ref) | copy-start | bytes 1572868
  51.4 2.8 %copy-start.7 = (bf16[16,128,128]{2,1,0:T(8,128)(2,1)}, bf16[16,128,128]{2,1,0:T(8,128)(2,1)S(1)}, u32[]{:S(2)}) copy-start(bf16[16,128,128]{2,1,0:T(8,128)(2,1)S(1)} %collective-permute-done.6.right_ref) | copy-start | bytes 1572868
  51.4 13.4 %collective-permute-start.7 = (bf16[16,128,128]{2,1,0:T(8,128)(2,1)S(1)}, bf16[16,128,128]{2,1,0:T(8,128)(2,1)S(1)}, u32[]{:S(2)}, u32[]{:S(2)}) collective-permute-start(bf16[16,128,128]{2,1,0:T(8,128)(2,1)S(1)} %collective-permute-done.5.left_ref), channel_id=1, source_target_pairs={{0,3},{1,0},{2,1},{3,2},{4,7},{5,4},{6,5},{7,6},{8,11},{9,8},{10,9... | collective-permute-start | bytes 1572872 | tf_op jit(solution)/shard_map/ppermute | solution.py:16
  52.4 12.5 %collective-permute-start.8 = (bf16[16,128,128]{2,1,0:T(8,128)(2,1)S(1)}, bf16[16,128,128]{2,1,0:T(8,128)(2,1)S(1)}, u32[]{:S(2)}, u32[]{:S(2)}) collective-permute-start(bf16[16,128,128]{2,1,0:T(8,128)(2,1)S(1)} %collective-permute-done.6.right_ref), channel_id=1, source_target_pairs={{0,28},{4,0},{8,4},{12,8},{16,12},{20,16},{24,20},{28,24},{1,29},{... | collective-permute-start | bytes 1572872 | tf_op jit(solution)/shard_map/ppermute | solution.py:16
  64.9 0.8 copy-start.8
  65.7 0.8 copy-start.9

commit v11 on v10

--- a/solution.py
+++ b/solution.py
@@ -124,13 +124,12 @@
     total = None
     result_shape = (result_count, edge, edge)
     left_now = left_home
-    right_now = right_home
+    rights = [right_home] + [passed_along(right_home, "row", -s) for s in range(1, STOPS)]
     for stop_index in range(STOPS):
+        right_now = rights[stop_index]
         if stop_index > 0:
             left_now = passed_along(left_now, "col", -1)
-            right_now = passed_along(right_now, "row", -1)
-        if stop_index > 0:
-            left_now, right_now, total = lax.optimization_barrier((left_now, right_now, total))
+            left_now, total = lax.optimization_barrier((left_now, total))
         total = run_stop(total, left_now, right_now, stacks, left_maps, live_counts, c_send[0, 0], stop_index,
                          stop_index == STOPS - 1, result_shape)
     outgoing = total

time: 113 us -> 105 us (0.929); the launches traced: 110 us -> 105 us
  waiting for transfers between devices: 11.7 us -> 5.02 us
  Pallas kernels: 40 us -> 35.8 us
  starting transfers between devices: 18.3 us -> 21.5 us
  local copies, waits for them, and re-layouts: 4.37 us -> 7.25 us
    ppermute x9, waiting for transfers between devices: 11.7 us -> 3.5 us  [passed_along(): return lax.ppermute(value, axis, pairs)]
    pallas_call x4, Pallas kernels: 40 us -> 35.8 us  [run_stop(): pl.pallas_call(functools.partial(stop_kernel, stop, first, last), grid_sp...]
    ppermute x9, starting transfers between devices: 12.9 us -> 16 us  [passed_along(): return lax.ppermute(value, axis, pairs)]
    unnamed x30 -> x28, local copies, waits for them, and re-layouts: 2.64 us -> 5.52 us
    all_to_all x1, waiting for transfers between devices: 0.01 us -> 1.52 us  [on_device(): lax.all_to_all(right_out, 'row', split_axis=0, concat_axis=0, tiled=True)]
  transfers between devices with their start and end apart: 10 -> 10, of which waited for: 4 -> 3; matrix products, arithmetic and copies ran while one was open for 2% -> 3% of each run, Pallas kernels for 27% -> 26%
where the time goes in v11:
time: 105 us
  Pallas kernels  35.8 us (34%)
  blocking collectives  32.6 us (31%)
  starting transfers between devices  21.5 us (20%)
  local copies, waits for them, and re-layouts  7.25 us (7%)
  waiting for transfers between devices  5.02 us (5%)
  other arithmetic  2.61 us (2%)
    pallas_call x4, Pallas kernels, run_stop(): pl.pallas_call(functools.partial(stop_kernel, stop, first, last), grid_sp...  35.8 us
    all_to_all x1, blocking collectives, on_device(): lax.all_to_all(outgoing[None, None], ('row', 'col'), split_axis=2, concat...  32.6 us
    ppermute x9, starting transfers between devices, passed_along(): return lax.ppermute(value, axis, pairs)  16 us
    all_to_all x1, starting transfers between devices, on_device(): lax.all_to_all(right_out, 'row', split_axis=0, concat_axis=0, tiled=True)  5.53 us
    unnamed x28, local copies, waits for them, and re-layouts  5.52 us
    ppermute x9, waiting for transfers between devices, passed_along(): return lax.ppermute(value, axis, pairs)  3.5 us
  transfers between devices with their start and end apart: 10, of which 3 were waited for; matrix products, arithmetic and copies ran while one was open for 3% of the time, Pallas kernels for 26%

profile of v11, /device:TPU:1, one launch (start us, length us, event | category | flops | bytes accessed | tf_op | source)
XLA Modules:
  0.0 105.0 jit_solution(13977508513853530918)
XLA Ops:
  0.0 0.7 copy-done.11
  0.8 0.2 copy-done
  1.1 0.6 gather_fusion
  1.7 0.1 select_select_fusion.1
  1.9 2.2 %collective-permute-start = (bf16[4,128,128]{2,1,0:T(8,128)(2,1)S(1)}, bf16[4,128,128]{2,1,0:T(8,128)(2,1)S(1)}, u32[]{:S(2)}, u32[]{:S(2)}) collective-permute-start(bf16[4,128,128]{2,1,0:T(8,128)(2,1)S(1)} %get-tuple-element.32), channel_id=1, source_target_pairs={{0,1},{1,2},{2,3},{3,0},{4,5},{5,6},{6,7},{7,4},{8,9},{9,10},{10,1... | collective-permute-start | bytes 393224 | tf_op jit(solution)/shard_map/ppermute | solution.py:16
  4.1 2.3 %collective-permute-start.1 = (bf16[4,128,128]{2,1,0:T(8,128)(2,1)S(1)}, bf16[4,128,128]{2,1,0:T(8,128)(2,1)S(1)}, u32[]{:S(2)}, u32[]{:S(2)}) collective-permute-start(bf16[4,128,128]{2,1,0:T(8,128)(2,1)S(1)} %get-tuple-element.31), channel_id=1, source_target_pairs={{0,2},{1,3},{2,0},{3,1},{4,6},{5,7},{6,4},{7,5},{8,10},{9,11},{10,... | collective-permute-start | bytes 393224 | tf_op jit(solution)/shard_map/ppermute | solution.py:16
  6.4 1.1 %collective-permute-start.2 = (bf16[4,128,128]{2,1,0:T(8,128)(2,1)S(1)}, bf16[4,128,128]{2,1,0:T(8,128)(2,1)S(1)}, u32[]{:S(2)}, u32[]{:S(2)}) collective-permute-start(bf16[4,128,128]{2,1,0:T(8,128)(2,1)S(1)} %get-tuple-element.30), channel_id=1, source_target_pairs={{0,3},{1,0},{2,1},{3,2},{4,7},{5,4},{6,5},{7,6},{8,11},{9,8},{10,9... | collective-permute-start | bytes 393224 | tf_op jit(solution)/shard_map/ppermute | solution.py:16
  7.5 0.1 copy.18
  7.9 0.6 gather_fusion.1
  8.6 0.9 select_select_fusion
  9.5 5.5 %all-to-all-start = ((bf16[8,2,128,128]{3,2,1,0:T(8,128)(2,1)}), bf16[8,2,128,128]{3,2,1,0:T(8,128)(2,1)}, u32[]{:S(2)}, u32[]{:S(2)}) async-start(bf16[8,2,128,128]{3,2,1,0:T(8,128)(2,1)} %select_select_fusion), calls=%async_computation | async-start | bytes 1048576 | tf_op jit(solution)/shard_map/all_to_all | solution.py:122
  15.0 0.7 collective-permute-done.1
  15.8 3.2 %collective-permute-start.3 = (bf16[16,128,128]{2,1,0:T(8,128)(2,1)S(1)}, bf16[16,128,128]{2,1,0:T(8,128)(2,1)S(1)}, u32[]{:S(2)}, u32[]{:S(2)}) collective-permute-start(bf16[16,128,128]{2,1,0:T(8,128)(2,1)S(1)} %pad_maximum_fusion.left_ref), channel_id=1, source_target_pairs={{0,3},{1,0},{2,1},{3,2},{4,7},{5,4},{6,5},{7,6},{8,11},{9,8},{10,9... | collective-permute-start | bytes 1572872 | tf_op jit(solution)/shard_map/ppermute | solution.py:16
  19.0 0.7 fusion.n_ref
  19.7 0.7 fusion.2.map_ref
  20.4 1.5 %all-to-all-done = bf16[8,2,128,128]{3,2,1,0:T(8,128)(2,1)} async-done(((bf16[8,2,128,128]{3,2,1,0:T(8,128)(2,1)}), bf16[8,2,128,128]{3,2,1,0:T(8,128)(2,1)}, u32[]{:S(2)}, u32[]{:S(2)}) %all-to-all-start) | async-done | bytes 524320 | tf_op jit(solution)/shard_map/all_to_all | solution.py:122
  21.9 3.0 %collective-permute-start.5 = (bf16[16,128,128]{2,1,0:T(8,128)(2,1)}, bf16[16,128,128]{2,1,0:T(8,128)(2,1)S(1)}, u32[]{:S(2)}, u32[]{:S(2)}) collective-permute-start(bf16[16,128,128]{2,1,0:T(8,128)(2,1)} %bitcast.14.right_ref), channel_id=1, source_target_pairs={{0,28},{4,0},{8,4},{12,8},{16,12},{20,16},{24,20},{28,24},{1,29},{... | collective-permute-start | bytes 1572872 | tf_op jit(solution)/shard_map/ppermute | solution.py:16
  24.9 9.5 %shard_map.64.refs_0_ = f32[16,128,128]{2,1,0:T(8,128)} custom-call(s32[4,3,384]{2,1,0:T(4,128)} %bitcast.37, s32[4,16]{1,0:T(4,128)} %fusion.2.map_ref, s32[4]{0:T(128)} %fusion.n_ref, s32[32]{0:T(128)} %bitcast.42, bf16[16,128,128]{2,1,0:T(8,128)(2,1)} %copy-done.1, bf16[16,128,128]{2,1,0:T(8,128)(2,1)} %bitcast.14.right_ref), custom_call_target="tpu_custom_call" | custom-call | tf_op jit(solution)/shard_map/pallas_call | solution.py:94
  34.5 0.4 collective-permute-start.7
  34.9 0.4 copy-done.3
  35.3 0.8 copy-done.8
  36.1 8.5 %shard_map.65.refs_0_ = f32[16,128,128]{2,1,0:T(8,128)} custom-call(s32[4,3,384]{2,1,0:T(4,128)} %bitcast.38, s32[4,16]{1,0:T(4,128)} %fusion.2.map_ref, s32[4]{0:T(128)} %fusion.n_ref, s32[32]{0:T(128)} %bitcast.43, bf16[16,128,128]{2,1,0:T(8,128)(2,1)} %copy-done.3, bf16[16,128,128]{2,1,0:T(8,128)(2,1)} %copy-done.8, ...), custom_call_target="tpu_custom_call", output_to_operand_aliasing={{}: (6, {})} | custom-call | tf_op jit(solution)/shard_map/pallas_call | solution.py:94
  44.6 2.8 %collective-permute-done.4.left_ref = bf16[16,128,128]{2,1,0:T(8,128)(2,1)S(1)} collective-permute-done((bf16[16,128,128]{2,1,0:T(8,128)(2,1)S(1)}, bf16[16,128,128]{2,1,0:T(8,128)(2,1)S(1)}, u32[]{:S(2)}, u32[]{:S(2)}) %collective-permute-start.4) | collective-permute-done | bytes 524320 | tf_op jit(solution)/shard_map/ppermute | solution.py:16
  47.4 1.7 %collective-permute-start.6 = (bf16[16,128,128]{2,1,0:T(8,128)(2,1)S(1)}, bf16[16,128,128]{2,1,0:T(8,128)(2,1)S(1)}, u32[]{:S(2)}, u32[]{:S(2)}) collective-permute-start(bf16[16,128,128]{2,1,0:T(8,128)(2,1)S(1)} %collective-permute-done.4.left_ref), channel_id=1, source_target_pairs={{0,3},{1,0},{2,1},{3,2},{4,7},{5,4},{6,5},{7,6},{8,11},{9,8},{10,9... | collective-permute-start | bytes 1572872 | tf_op jit(solution)/shard_map/ppermute | solution.py:16
  49.1 2.1 %collective-permute-start.8 = (bf16[16,128,128]{2,1,0:T(8,128)(2,1)}, bf16[16,128,128]{2,1,0:T(8,128)(2,1)S(1)}, u32[]{:S(2)}, u32[]{:S(2)}) collective-permute-start(bf16[16,128,128]{2,1,0:T(8,128)(2,1)} %bitcast.14.right_ref), channel_id=1, source_target_pairs={{0,20},{4,24},{8,28},{12,0},{16,4},{20,8},{24,12},{28,16},{1,21},{... | collective-permute-start | bytes 1572872 | tf_op jit(solution)/shard_map/ppermute | solution.py:16
  51.2 0.8 copy-done.5
  52.0 9.7 %shard_map.66.refs_0_ = f32[16,128,128]{2,1,0:T(8,128)} custom-call(s32[4,3,384]{2,1,0:T(4,128)} %bitcast.39, s32[4,16]{1,0:T(4,128)} %fusion.2.map_ref, s32[4]{0:T(128)} %fusion.n_ref, s32[32]{0:T(128)} %bitcast.44, bf16[16,128,128]{2,1,0:T(8,128)(2,1)} %copy-done.4, bf16[16,128,128]{2,1,0:T(8,128)(2,1)} %copy-done.5, ...), custom_call_target="tpu_custom_call", output_to_operand_aliasing={{}: (6, {})} | custom-call | tf_op jit(solution)/shard_map/pallas_call | solution.py:94
  61.7 0.8 copy-done.6
  62.5 0.8 copy-done.7
  63.3 8.1 %shard_map.67 = bf16[32,128,128]{2,1,0:T(8,128)(2,1)} custom-call(s32[4,3,384]{2,1,0:T(4,128)} %bitcast.40, s32[4,16]{1,0:T(4,128)} %fusion.2.map_ref, s32[4]{0:T(128)} %fusion.n_ref, s32[32]{0:T(128)} %bitcast.45, bf16[16,128,128]{2,1,0:T(8,128)(2,1)} %copy-done.6, bf16[16,128,128]{2,1,0:T(8,128)(2,1)} %copy-done.7, f32[16,128,128]{2,1,0:T(8,128)} %shard_map.66.refs_0_), custom_call_target="tpu_custom_call" | custom-call | tf_op jit(solution)/shard_map/pallas_call | solution.py:94
  71.4 32.6 %all_to_all.10 = bf16[1,1,32,128,128]{4,3,1,0,2:T(8,128)(2,1)S(1)} all-to-all(bf16[1,1,32,128,128]{4,3,1,0,2:T(8,128)(2,1)} %bitcast.32), channel_id=1, replica_groups=mesh['row'=8,'col'=4] {'row','col'}, dimensions={2} | all-to-all | bytes 2097152 | tf_op jit(solution)/shard_map/all_to_all | solution.py:136
  104.0 1.0 copy.28
  (42 shorter events, 0.6 us)
Async XLA Ops:
  0.0 1.1 %copy-start = (bf16[1,1,16,128,128]{4,3,2,1,0:T(8,128)(2,1)S(1)}, bf16[1,1,16,128,128]{4,3,2,1,0:T(8,128)(2,1)}, u32[]{:S(2)}) copy-start(bf16[1,1,16,128,128]{4,3,2,1,0:T(8,128)(2,1)} %param.8) | copy-start | bytes 1572868
  0.0 0.7 copy-start.11
  1.9 6.0 %copy-start.9 = (bf16[1,1,16,128,128]{4,3,2,1,0:T(8,128)(2,1)S(1)}, bf16[1,1,16,128,128]{4,3,2,1,0:T(8,128)(2,1)}, u32[]{:S(2)}) copy-start(bf16[1,1,16,128,128]{4,3,2,1,0:T(8,128)(2,1)} %param.9) | copy-start | bytes 1572868
  1.9 13.1 %collective-permute-start = (bf16[4,128,128]{2,1,0:T(8,128)(2,1)S(1)}, bf16[4,128,128]{2,1,0:T(8,128)(2,1)S(1)}, u32[]{:S(2)}, u32[]{:S(2)}) collective-permute-start(bf16[4,128,128]{2,1,0:T(8,128)(2,1)S(1)} %get-tuple-element.32), channel_id=1, source_target_pairs={{0,1},{1,2},{2,3},{3,0},{4,5},{5,6},{6,7},{7,4},{8,9},{9,10},{10,1... | collective-permute-start | bytes 393224 | tf_op jit(solution)/shard_map/ppermute | solution.py:16
  4.1 3.4 %copy-start.12 = (s32[1,1,8,2]{2,3,1,0:T(2,128)S(1)}, s32[1,1,8,2]{2,3,1,0:T(2,128)}, u32[]{:S(2)}) copy-start(s32[1,1,8,2]{2,3,1,0:T(2,128)} %param.11) | copy-start | bytes 196
  4.1 11.6 %collective-permute-start.1 = (bf16[4,128,128]{2,1,0:T(8,128)(2,1)S(1)}, bf16[4,128,128]{2,1,0:T(8,128)(2,1)S(1)}, u32[]{:S(2)}, u32[]{:S(2)}) collective-permute-start(bf16[4,128,128]{2,1,0:T(8,128)(2,1)S(1)} %get-tuple-element.31), channel_id=1, source_target_pairs={{0,2},{1,3},{2,0},{3,1},{4,6},{5,7},{6,4},{7,5},{8,10},{9,11},{10,... | collective-permute-start | bytes 393224 | tf_op jit(solution)/shard_map/ppermute | solution.py:16
  6.4 9.3 %collective-permute-start.2 = (bf16[4,128,128]{2,1,0:T(8,128)(2,1)S(1)}, bf16[4,128,128]{2,1,0:T(8,128)(2,1)S(1)}, u32[]{:S(2)}, u32[]{:S(2)}) collective-permute-start(bf16[4,128,128]{2,1,0:T(8,128)(2,1)S(1)} %get-tuple-element.30), channel_id=1, source_target_pairs={{0,3},{1,0},{2,1},{3,2},{4,7},{5,4},{6,5},{7,6},{8,11},{9,8},{10,9... | collective-permute-start | bytes 393224 | tf_op jit(solution)/shard_map/ppermute | solution.py:16
  9.5 12.4 %all-to-all-start = ((bf16[8,2,128,128]{3,2,1,0:T(8,128)(2,1)}), bf16[8,2,128,128]{3,2,1,0:T(8,128)(2,1)}, u32[]{:S(2)}, u32[]{:S(2)}) async-start(bf16[8,2,128,128]{3,2,1,0:T(8,128)(2,1)} %select_select_fusion), calls=%async_computation | async-start | bytes 1048576 | tf_op jit(solution)/shard_map/all_to_all | solution.py:122
  15.7 3.3 %copy-start.10 = (s32[1,1,4,3,384]{4,2,3,1,0:T(4,128)S(1)}, s32[1,1,4,3,384]{4,2,3,1,0:T(4,128)}, u32[]{:S(2)}) copy-start(s32[1,1,4,3,384]{4,2,3,1,0:T(4,128)} %param.12) | copy-start | bytes 55300
  15.8 9.1 %copy-start.1 = (bf16[16,128,128]{2,1,0:T(8,128)(2,1)}, bf16[16,128,128]{2,1,0:T(8,128)(2,1)S(1)}, u32[]{:S(2)}) copy-start(bf16[16,128,128]{2,1,0:T(8,128)(2,1)S(1)} %pad_maximum_fusion.left_ref) | copy-start | bytes 1572868
  15.8 18.6 %collective-permute-start.3 = (bf16[16,128,128]{2,1,0:T(8,128)(2,1)S(1)}, bf16[16,128,128]{2,1,0:T(8,128)(2,1)S(1)}, u32[]{:S(2)}, u32[]{:S(2)}) collective-permute-start(bf16[16,128,128]{2,1,0:T(8,128)(2,1)S(1)} %pad_maximum_fusion.left_ref), channel_id=1, source_target_pairs={{0,3},{1,0},{2,1},{3,2},{4,7},{5,4},{6,5},{7,6},{8,11},{9,8},{10,9... | collective-permute-start | bytes 1572872 | tf_op jit(solution)/shard_map/ppermute | solution.py:16
  19.0 5.9 %copy-start.2 = (s32[1,1,4,3,384]{4,3,2,1,0:T(4,128)}, s32[1,1,4,3,384]{4,3,2,1,0:T(4,128)S(1)}, u32[]{:S(2)}) copy-start(s32[1,1,4,3,384]{4,3,2,1,0:T(4,128)S(1)} %copy.24) | copy-start | bytes 55300
  21.9 13.0 %collective-permute-start.5 = (bf16[16,128,128]{2,1,0:T(8,128)(2,1)}, bf16[16,128,128]{2,1,0:T(8,128)(2,1)S(1)}, u32[]{:S(2)}, u32[]{:S(2)}) collective-permute-start(bf16[16,128,128]{2,1,0:T(8,128)(2,1)} %bitcast.14.right_ref), channel_id=1, source_target_pairs={{0,28},{4,0},{8,4},{12,8},{16,12},{20,16},{24,20},{28,24},{1,29},{... | collective-permute-start | bytes 1572872 | tf_op jit(solution)/shard_map/ppermute | solution.py:16
  34.5 0.8 copy-start.3
  34.5 12.9 %collective-permute-start.4 = (bf16[16,128,128]{2,1,0:T(8,128)(2,1)S(1)}, bf16[16,128,128]{2,1,0:T(8,128)(2,1)S(1)}, u32[]{:S(2)}, u32[]{:S(2)}) collective-permute-start(bf16[16,128,128]{2,1,0:T(8,128)(2,1)S(1)} %collective-permute-done.3.left_ref), channel_id=1, source_target_pairs={{0,3},{1,0},{2,1},{3,2},{4,7},{5,4},{6,5},{7,6},{8,11},{9,8},{10,9... | collective-permute-start | bytes 1572872 | tf_op jit(solution)/shard_map/ppermute | solution.py:16
  34.5 16.7 %collective-permute-start.7 = (bf16[16,128,128]{2,1,0:T(8,128)(2,1)}, bf16[16,128,128]{2,1,0:T(8,128)(2,1)S(1)}, u32[]{:S(2)}, u32[]{:S(2)}) collective-permute-start(bf16[16,128,128]{2,1,0:T(8,128)(2,1)} %bitcast.14.right_ref), channel_id=1, source_target_pairs={{0,24},{4,28},{8,0},{12,4},{16,8},{20,12},{24,16},{28,20},{1,25},{... | collective-permute-start | bytes 1572872 | tf_op jit(solution)/shard_map/ppermute | solution.py:16
  35.3 0.8 copy-start.8
  47.4 3.8 %copy-start.4 = (bf16[16,128,128]{2,1,0:T(8,128)(2,1)}, bf16[16,128,128]{2,1,0:T(8,128)(2,1)S(1)}, u32[]{:S(2)}) copy-start(bf16[16,128,128]{2,1,0:T(8,128)(2,1)S(1)} %collective-permute-done.4.left_ref) | copy-start | bytes 1572868
  47.4 14.3 %collective-permute-start.6 = (bf16[16,128,128]{2,1,0:T(8,128)(2,1)S(1)}, bf16[16,128,128]{2,1,0:T(8,128)(2,1)S(1)}, u32[]{:S(2)}, u32[]{:S(2)}) collective-permute-start(bf16[16,128,128]{2,1,0:T(8,128)(2,1)S(1)} %collective-permute-done.4.left_ref), channel_id=1, source_target_pairs={{0,3},{1,0},{2,1},{3,2},{4,7},{5,4},{6,5},{7,6},{8,11},{9,8},{10,9... | collective-permute-start | bytes 1572872 | tf_op jit(solution)/shard_map/ppermute | solution.py:16
  49.1 12.6 %collective-permute-start.8 = (bf16[16,128,128]{2,1,0:T(8,128)(2,1)}, bf16[16,128,128]{2,1,0:T(8,128)(2,1)S(1)}, u32[]{:S(2)}, u32[]{:S(2)}) collective-permute-start(bf16[16,128,128]{2,1,0:T(8,128)(2,1)} %bitcast.14.right_ref), channel_id=1, source_target_pairs={{0,20},{4,24},{8,28},{12,0},{16,4},{20,8},{24,12},{28,16},{1,21},{... | collective-permute-start | bytes 1572872 | tf_op jit(solution)/shard_map/ppermute | solution.py:16
  51.2 0.8 copy-start.5
  61.7 0.8 copy-start.6
  62.5 0.8 copy-start.7

commit v12 on v11

--- a/solution.py
+++ b/solution.py
@@ -41,15 +41,12 @@
         targets = []
         for k in range(GROUP):
             i = base + k
-            slot = stack_ref[stop, 0, i]
-            mapped = map_ref[stop, jnp.clip(slot, 0, slots - 1)]
-            ok = (i < live_count) & (slot >= 0) & (mapped >= 0)
-            a = left_ref[jnp.clip(mapped, 0, left_count - 1)]
-            b = right_ref[jnp.clip(stack_ref[stop, 1, i], 0, right_count - 1)]
+            a = left_ref[stack_ref[stop, 0, i]]
+            b = right_ref[stack_ref[stop, 1, i]]
             p = jnp.dot(a, b, preferred_element_type=jnp.float32)
             p = p.astype(jnp.bfloat16).astype(jnp.float32)
-            prods.append(jnp.where(ok, p, 0.0))
-            targets.append(jnp.clip(stack_ref[stop, 2, i], 0, result_count - 1))
+            prods.append(jnp.where((i < live_count) & (stack_ref[stop, 3, i] > 0), p, 0.0))
+            targets.append(stack_ref[stop, 2, i])
         for k in range(GROUP):
             t = targets[k]
             acc_ref[t] = acc_ref[t] + prods[k]
@@ -113,11 +110,16 @@
         bucket = jnp.take(left_out, (col_at + shift) % cols_n, axis=0)
         pieces.append(passed_along(bucket, "col", shift))
     left_home = jnp.concatenate(pieces, axis=0)
-    slot = jnp.arange(cols_n * cap, dtype=jnp.int32)[None, :]
+    stacks = triples[0, 0].astype(jnp.int32)
     owner = (col_at + jnp.arange(STOPS, dtype=jnp.int32)[:, None]) % cols_n
-    left_maps = (((owner - slot // cap) % cols_n) * cap + slot % cap).astype(jnp.int32)
-    stacks = triples[0, 0].astype(jnp.int32)
-    live_counts = jnp.sum((stacks[:, 0, :] >= 0).astype(jnp.int32), axis=1)
+    slot = jnp.clip(stacks[:, 0, :], 0, cols_n * cap - 1)
+    left_index = ((owner - slot // cap) % cols_n) * cap + slot % cap
+    right_index = jnp.clip(stacks[:, 1, :], 0, rows_n * b_send.shape[-1] - 1)
+    target_index = jnp.clip(stacks[:, 2, :], 0, result_count - 1)
+    live = (stacks[:, 0, :] >= 0).astype(jnp.int32)
+    stacks = jnp.stack([left_index, right_index, target_index, live], axis=1).astype(jnp.int32)
+    left_maps = jnp.zeros((STOPS, 1), jnp.int32)
+    live_counts = jnp.sum(live, axis=1)
     right_out = bucketize(b_blocks[0, 0], b_send[0, 0])
     right_home = lax.all_to_all(right_out, "row", split_axis=0, concat_axis=0, tiled=True)
     right_home = right_home.reshape(-1, edge, edge)

time: 105 us -> 116 us (1.10); the launches traced: 105 us -> 114 us
  waiting for transfers between devices: 5.02 us -> 15.5 us
  starting transfers between devices: 21.5 us -> 19.9 us
  Pallas kernels: 35.8 us -> 34.3 us
    ppermute x9, waiting for transfers between devices: 3.5 us -> 9.97 us  [passed_along(): return lax.ppermute(value, axis, pairs)]
    all_to_all x1, waiting for transfers between devices: 1.52 us -> 5.49 us  [on_device(): lax.all_to_all(right_out, 'row', split_axis=0, concat_axis=0, tiled=True)]
    ppermute x9, starting transfers between devices: 16 us -> 13.9 us  [passed_along(): return lax.ppermute(value, axis, pairs)]
    pallas_call x4, Pallas kernels: 35.8 us -> 34.3 us  [run_stop(): pl.pallas_call(functools.partial(stop_kernel, stop, first, last), grid_sp...]
    unnamed x28 -> x26, local copies, waits for them, and re-layouts: 5.52 us -> 5.83 us
  transfers between devices with their start and end apart: 10 -> 10, of which waited for: 3 -> 4; matrix products, arithmetic and copies ran while one was open for 3% -> 3% of each run, Pallas kernels for 26% -> 24%
where the time goes in v12:
time: 116 us; the launch traced here: 114 us
  Pallas kernels  34.3 us (30%)
  blocking collectives  33.7 us (29%)
  starting transfers between devices  19.9 us (17%)
  waiting for transfers between devices  15.5 us (13%)
  local copies, waits for them, and re-layouts  8.11 us (7%)
  other arithmetic  2.6 us (2%)
    pallas_call x4, Pallas kernels, run_stop(): pl.pallas_call(functools.partial(stop_kernel, stop, first, last), grid_sp...  34.3 us
    all_to_all x1, blocking collectives, on_device(): lax.all_to_all(outgoing[None, None], ('row', 'col'), split_axis=2, concat...  33.7 us
    ppermute x9, starting transfers between devices, passed_along(): return lax.ppermute(value, axis, pairs)  13.9 us
    ppermute x9, waiting for transfers between devices, passed_along(): return lax.ppermute(value, axis, pairs)  9.97 us
    all_to_all x1, starting transfers between devices, on_device(): lax.all_to_all(right_out, 'row', split_axis=0, concat_axis=0, tiled=True)  5.98 us
    unnamed x26, local copies, waits for them, and re-layouts  5.83 us
    all_to_all x1, waiting for transfers between devices, on_device(): lax.all_to_all(right_out, 'row', split_axis=0, concat_axis=0, tiled=True)  5.49 us
  transfers between devices with their start and end apart: 10, of which 4 were waited for; matrix products, arithmetic and copies ran while one was open for 3% of the time, Pallas kernels for 24%

profile of v12, /device:TPU:1, one launch (start us, length us, event | category | flops | bytes accessed | tf_op | source)
XLA Modules:
  0.0 114.1 jit_solution(11717488101610477951)
XLA Ops:
  0.0 0.7 copy-done.10
  0.8 0.2 copy-done
  1.1 0.6 gather_fusion
  1.7 0.1 select_select_fusion.1
  1.9 2.2 %collective-permute-start = (bf16[4,128,128]{2,1,0:T(8,128)(2,1)S(1)}, bf16[4,128,128]{2,1,0:T(8,128)(2,1)S(1)}, u32[]{:S(2)}, u32[]{:S(2)}) collective-permute-start(bf16[4,128,128]{2,1,0:T(8,128)(2,1)S(1)} %get-tuple-element.34), channel_id=1, source_target_pairs={{0,1},{1,2},{2,3},{3,0},{4,5},{5,6},{6,7},{7,4},{8,9},{9,10},{10,1... | collective-permute-start | bytes 393224 | tf_op jit(solution)/shard_map/ppermute | solution.py:16
  4.1 2.3 %collective-permute-start.1 = (bf16[4,128,128]{2,1,0:T(8,128)(2,1)S(1)}, bf16[4,128,128]{2,1,0:T(8,128)(2,1)S(1)}, u32[]{:S(2)}, u32[]{:S(2)}) collective-permute-start(bf16[4,128,128]{2,1,0:T(8,128)(2,1)S(1)} %get-tuple-element.33), channel_id=1, source_target_pairs={{0,2},{1,3},{2,0},{3,1},{4,6},{5,7},{6,4},{7,5},{8,10},{9,11},{10,... | collective-permute-start | bytes 393224 | tf_op jit(solution)/shard_map/ppermute | solution.py:16
  6.4 1.1 collective-permute-start.2
  7.5 0.1 copy.18
  7.9 0.6 gather_fusion.1
  8.6 0.8 collective-permute-done
  9.4 6.3 %collective-permute-done.1 = bf16[4,128,128]{2,1,0:T(8,128)(2,1)S(1)} collective-permute-done((bf16[4,128,128]{2,1,0:T(8,128)(2,1)S(1)}, bf16[4,128,128]{2,1,0:T(8,128)(2,1)S(1)}, u32[]{:S(2)}, u32[]{:S(2)}) %collective-permute-start.1) | collective-permute-done | bytes 131104 | tf_op jit(solution)/shard_map/ppermute | solution.py:16
  15.8 3.2 %collective-permute-start.3 = (bf16[16,128,128]{2,1,0:T(8,128)(2,1)S(1)}, bf16[16,128,128]{2,1,0:T(8,128)(2,1)S(1)}, u32[]{:S(2)}, u32[]{:S(2)}) collective-permute-start(bf16[16,128,128]{2,1,0:T(8,128)(2,1)S(1)} %pad_maximum_fusion.left_ref), channel_id=1, source_target_pairs={{0,3},{1,0},{2,1},{3,2},{4,7},{5,4},{6,5},{7,6},{8,11},{9,8},{10,9... | collective-permute-start | bytes 1572872 | tf_op jit(solution)/shard_map/ppermute | solution.py:16
  19.0 0.9 select_select_fusion
  19.9 6.0 %all-to-all-start = ((bf16[8,2,128,128]{3,2,1,0:T(8,128)(2,1)}), bf16[8,2,128,128]{3,2,1,0:T(8,128)(2,1)}, u32[]{:S(2)}, u32[]{:S(2)}) async-start(bf16[8,2,128,128]{3,2,1,0:T(8,128)(2,1)} %select_select_fusion), calls=%async_computation | async-start | bytes 1048576 | tf_op jit(solution)/shard_map/all_to_all | solution.py:124
  25.9 0.7 fusion.4
  26.6 0.6 pad_add_fusion.stack_ref
  27.3 5.5 %all-to-all-done = bf16[8,2,128,128]{3,2,1,0:T(8,128)(2,1)} async-done(((bf16[8,2,128,128]{3,2,1,0:T(8,128)(2,1)}), bf16[8,2,128,128]{3,2,1,0:T(8,128)(2,1)}, u32[]{:S(2)}, u32[]{:S(2)}) %all-to-all-start) | async-done | bytes 524320 | tf_op jit(solution)/shard_map/all_to_all | solution.py:124
  32.8 3.0 %collective-permute-start.5 = (bf16[16,128,128]{2,1,0:T(8,128)(2,1)}, bf16[16,128,128]{2,1,0:T(8,128)(2,1)S(1)}, u32[]{:S(2)}, u32[]{:S(2)}) collective-permute-start(bf16[16,128,128]{2,1,0:T(8,128)(2,1)} %bitcast.14.right_ref), channel_id=1, source_target_pairs={{0,28},{4,0},{8,4},{12,8},{16,12},{20,16},{24,20},{28,24},{1,29},{... | collective-permute-start | bytes 1572872 | tf_op jit(solution)/shard_map/ppermute | solution.py:16
  35.8 0.5 jit_remainder_.2.map_ref
  36.3 8.7 %shard_map.64.refs_0_ = f32[16,128,128]{2,1,0:T(8,128)} custom-call(s32[4,4,384]{2,1,0:T(4,128)} %pad_add_fusion.stack_ref, s32[4,1]{1,0:T(4,128)} %jit_remainder_.2.map_ref, s32[4]{0:T(128)} %get-tuple-element.29.n_ref, s32[32]{0:T(128)} %bitcast.38, bf16[16,128,128]{2,1,0:T(8,128)(2,1)} %copy-done.1, bf16[16,128,128]{2,1,0:T(8,128)(2,1)} %bitcast.14.right_ref), custom_call_target="tpu_custom_call" | custom-call | tf_op jit(solution)/shard_map/pallas_call | solution.py:91
  45.2 0.7 copy-done.2
  45.9 0.8 copy-done.6
  46.7 8.6 %shard_map.65.refs_0_ = f32[16,128,128]{2,1,0:T(8,128)} custom-call(s32[4,4,384]{2,1,0:T(4,128)} %pad_add_fusion.stack_ref, s32[4,1]{1,0:T(4,128)} %jit_remainder_.2.map_ref, s32[4]{0:T(128)} %get-tuple-element.29.n_ref, s32[32]{0:T(128)} %bitcast.39, bf16[16,128,128]{2,1,0:T(8,128)(2,1)} %copy-done.2, ...), custom_call_target="tpu_custom_call", output_to_operand_aliasing={{}: (6, {})} | custom-call | tf_op jit(solution)/shard_map/pallas_call | solution.py:91
  55.3 2.8 %collective-permute-done.4.left_ref = bf16[16,128,128]{2,1,0:T(8,128)(2,1)S(1)} collective-permute-done((bf16[16,128,128]{2,1,0:T(8,128)(2,1)S(1)}, bf16[16,128,128]{2,1,0:T(8,128)(2,1)S(1)}, u32[]{:S(2)}, u32[]{:S(2)}) %collective-permute-start.4) | collective-permute-done | bytes 524320 | tf_op jit(solution)/shard_map/ppermute | solution.py:16
  58.1 2.1 %collective-permute-start.6 = (bf16[16,128,128]{2,1,0:T(8,128)(2,1)S(1)}, bf16[16,128,128]{2,1,0:T(8,128)(2,1)S(1)}, u32[]{:S(2)}, u32[]{:S(2)}) collective-permute-start(bf16[16,128,128]{2,1,0:T(8,128)(2,1)S(1)} %collective-permute-done.4.left_ref), channel_id=1, source_target_pairs={{0,3},{1,0},{2,1},{3,2},{4,7},{5,4},{6,5},{7,6},{8,11},{9,8},{10,9... | collective-permute-start | bytes 1572872 | tf_op jit(solution)/shard_map/ppermute | solution.py:16
  60.2 0.8 copy-done.4
  61.0 9.6 %shard_map.66.refs_0_ = f32[16,128,128]{2,1,0:T(8,128)} custom-call(s32[4,4,384]{2,1,0:T(4,128)} %pad_add_fusion.stack_ref, s32[4,1]{1,0:T(4,128)} %jit_remainder_.2.map_ref, s32[4]{0:T(128)} %get-tuple-element.29.n_ref, s32[32]{0:T(128)} %bitcast.40, bf16[16,128,128]{2,1,0:T(8,128)(2,1)} %copy-done.3, ...), custom_call_target="tpu_custom_call", output_to_operand_aliasing={{}: (6, {})} | custom-call | tf_op jit(solution)/shard_map/pallas_call | solution.py:91
  70.6 0.8 copy-done.5
  71.4 0.8 copy-done.7
  72.2 7.3 %shard_map.67 = bf16[32,128,128]{2,1,0:T(8,128)(2,1)} custom-call(s32[4,4,384]{2,1,0:T(4,128)} %pad_add_fusion.stack_ref, s32[4,1]{1,0:T(4,128)} %jit_remainder_.2.map_ref, s32[4]{0:T(128)} %get-tuple-element.29.n_ref, s32[32]{0:T(128)} %bitcast.41, bf16[16,128,128]{2,1,0:T(8,128)(2,1)} %copy-done.5, bf16[16,128,128]{2,1,0:T(8,128)(2,1)} %copy-done.7, ...), custom_call_target="tpu_custom_call" | custom-call | tf_op jit(solution)/shard_map/pallas_call | solution.py:91
  79.5 33.7 %all_to_all.10 = bf16[1,1,32,128,128]{4,3,1,0,2:T(8,128)(2,1)S(1)} all-to-all(bf16[1,1,32,128,128]{4,3,1,0,2:T(8,128)(2,1)} %bitcast.32), channel_id=1, replica_groups=mesh['row'=8,'col'=4] {'row','col'}, dimensions={2} | all-to-all | bytes 2097152 | tf_op jit(solution)/shard_map/all_to_all | solution.py:138
  113.2 1.0 copy.28
  (40 shorter events, 0.6 us)
Async XLA Ops:
  0.0 1.1 copy-start
  0.0 0.7 copy-start.10
  1.9 6.0 %copy-start.8 = (bf16[1,1,16,128,128]{4,3,2,1,0:T(8,128)(2,1)S(1)}, bf16[1,1,16,128,128]{4,3,2,1,0:T(8,128)(2,1)}, u32[]{:S(2)}) copy-start(bf16[1,1,16,128,128]{4,3,2,1,0:T(8,128)(2,1)} %param.9) | copy-start | bytes 1572868
  1.9 7.4 %collective-permute-start = (bf16[4,128,128]{2,1,0:T(8,128)(2,1)S(1)}, bf16[4,128,128]{2,1,0:T(8,128)(2,1)S(1)}, u32[]{:S(2)}, u32[]{:S(2)}) collective-permute-start(bf16[4,128,128]{2,1,0:T(8,128)(2,1)S(1)} %get-tuple-element.34), channel_id=1, source_target_pairs={{0,1},{1,2},{2,3},{3,0},{4,5},{5,6},{6,7},{7,4},{8,9},{9,10},{10,1... | collective-permute-start | bytes 393224 | tf_op jit(solution)/shard_map/ppermute | solution.py:16
  4.1 3.4 %copy-start.11 = (s32[1,1,8,2]{2,3,1,0:T(2,128)S(1)}, s32[1,1,8,2]{2,3,1,0:T(2,128)}, u32[]{:S(2)}) copy-start(s32[1,1,8,2]{2,3,1,0:T(2,128)} %param.11) | copy-start | bytes 196
  4.1 11.6 %collective-permute-start.1 = (bf16[4,128,128]{2,1,0:T(8,128)(2,1)S(1)}, bf16[4,128,128]{2,1,0:T(8,128)(2,1)S(1)}, u32[]{:S(2)}, u32[]{:S(2)}) collective-permute-start(bf16[4,128,128]{2,1,0:T(8,128)(2,1)S(1)} %get-tuple-element.33), channel_id=1, source_target_pairs={{0,2},{1,3},{2,0},{3,1},{4,6},{5,7},{6,4},{7,5},{8,10},{9,11},{10,... | collective-permute-start | bytes 393224 | tf_op jit(solution)/shard_map/ppermute | solution.py:16
  6.4 9.3 %collective-permute-start.2 = (bf16[4,128,128]{2,1,0:T(8,128)(2,1)S(1)}, bf16[4,128,128]{2,1,0:T(8,128)(2,1)S(1)}, u32[]{:S(2)}, u32[]{:S(2)}) collective-permute-start(bf16[4,128,128]{2,1,0:T(8,128)(2,1)S(1)} %get-tuple-element.32), channel_id=1, source_target_pairs={{0,3},{1,0},{2,1},{3,2},{4,7},{5,4},{6,5},{7,6},{8,11},{9,8},{10,9... | collective-permute-start | bytes 393224 | tf_op jit(solution)/shard_map/ppermute | solution.py:16
  15.8 4.1 %copy-start.1 = (bf16[16,128,128]{2,1,0:T(8,128)(2,1)}, bf16[16,128,128]{2,1,0:T(8,128)(2,1)S(1)}, u32[]{:S(2)}) copy-start(bf16[16,128,128]{2,1,0:T(8,128)(2,1)S(1)} %pad_maximum_fusion.left_ref) | copy-start | bytes 1572868
  15.8 29.3 %collective-permute-start.3 = (bf16[16,128,128]{2,1,0:T(8,128)(2,1)S(1)}, bf16[16,128,128]{2,1,0:T(8,128)(2,1)S(1)}, u32[]{:S(2)}, u32[]{:S(2)}) collective-permute-start(bf16[16,128,128]{2,1,0:T(8,128)(2,1)S(1)} %pad_maximum_fusion.left_ref), channel_id=1, source_target_pairs={{0,3},{1,0},{2,1},{3,2},{4,7},{5,4},{6,5},{7,6},{8,11},{9,8},{10,9... | collective-permute-start | bytes 1572872 | tf_op jit(solution)/shard_map/ppermute | solution.py:16
  19.9 6.0 %copy-start.9 = (s32[1,1,4,3,384]{4,2,3,1,0:T(4,128)S(1)}, s32[1,1,4,3,384]{4,2,3,1,0:T(4,128)}, u32[]{:S(2)}) copy-start(s32[1,1,4,3,384]{4,2,3,1,0:T(4,128)} %param.12) | copy-start | bytes 55300
  19.9 12.8 %all-to-all-start = ((bf16[8,2,128,128]{3,2,1,0:T(8,128)(2,1)}), bf16[8,2,128,128]{3,2,1,0:T(8,128)(2,1)}, u32[]{:S(2)}, u32[]{:S(2)}) async-start(bf16[8,2,128,128]{3,2,1,0:T(8,128)(2,1)} %select_select_fusion), calls=%async_computation | async-start | bytes 1048576 | tf_op jit(solution)/shard_map/all_to_all | solution.py:124
  32.8 12.4 %collective-permute-start.5 = (bf16[16,128,128]{2,1,0:T(8,128)(2,1)}, bf16[16,128,128]{2,1,0:T(8,128)(2,1)S(1)}, u32[]{:S(2)}, u32[]{:S(2)}) collective-permute-start(bf16[16,128,128]{2,1,0:T(8,128)(2,1)} %bitcast.14.right_ref), channel_id=1, source_target_pairs={{0,28},{4,0},{8,4},{12,8},{16,12},{20,16},{24,20},{28,24},{1,29},{... | collective-permute-start | bytes 1572872 | tf_op jit(solution)/shard_map/ppermute | solution.py:16
  45.1 0.8 copy-start.2
  45.1 13.0 %collective-permute-start.4 = (bf16[16,128,128]{2,1,0:T(8,128)(2,1)S(1)}, bf16[16,128,128]{2,1,0:T(8,128)(2,1)S(1)}, u32[]{:S(2)}, u32[]{:S(2)}) collective-permute-start(bf16[16,128,128]{2,1,0:T(8,128)(2,1)S(1)} %collective-permute-done.3.left_ref), channel_id=1, source_target_pairs={{0,3},{1,0},{2,1},{3,2},{4,7},{5,4},{6,5},{7,6},{8,11},{9,8},{10,9... | collective-permute-start | bytes 1572872 | tf_op jit(solution)/shard_map/ppermute | solution.py:16
  45.1 15.1 %collective-permute-start.7 = (bf16[16,128,128]{2,1,0:T(8,128)(2,1)}, bf16[16,128,128]{2,1,0:T(8,128)(2,1)S(1)}, u32[]{:S(2)}, u32[]{:S(2)}) collective-permute-start(bf16[16,128,128]{2,1,0:T(8,128)(2,1)} %bitcast.14.right_ref), channel_id=1, source_target_pairs={{0,24},{4,28},{8,0},{12,4},{16,8},{20,12},{24,16},{28,20},{1,25},{... | collective-permute-start | bytes 1572872 | tf_op jit(solution)/shard_map/ppermute | solution.py:16
  45.9 0.8 copy-start.6
  58.1 2.1 %copy-start.3 = (bf16[16,128,128]{2,1,0:T(8,128)(2,1)}, bf16[16,128,128]{2,1,0:T(8,128)(2,1)S(1)}, u32[]{:S(2)}) copy-start(bf16[16,128,128]{2,1,0:T(8,128)(2,1)S(1)} %collective-permute-done.4.left_ref) | copy-start | bytes 1572868
  58.1 12.5 %collective-permute-start.6 = (bf16[16,128,128]{2,1,0:T(8,128)(2,1)S(1)}, bf16[16,128,128]{2,1,0:T(8,128)(2,1)S(1)}, u32[]{:S(2)}, u32[]{:S(2)}) collective-permute-start(bf16[16,128,128]{2,1,0:T(8,128)(2,1)S(1)} %collective-permute-done.4.left_ref), channel_id=1, source_target_pairs={{0,3},{1,0},{2,1},{3,2},{4,7},{5,4},{6,5},{7,6},{8,11},{9,8},{10,9... | collective-permute-start | bytes 1572872 | tf_op jit(solution)/shard_map/ppermute | solution.py:16
  60.2 10.4 %collective-permute-start.8 = (bf16[16,128,128]{2,1,0:T(8,128)(2,1)}, bf16[16,128,128]{2,1,0:T(8,128)(2,1)S(1)}, u32[]{:S(2)}, u32[]{:S(2)}) collective-permute-start(bf16[16,128,128]{2,1,0:T(8,128)(2,1)} %bitcast.14.right_ref), channel_id=1, source_target_pairs={{0,20},{4,24},{8,28},{12,0},{16,4},{20,8},{24,12},{28,16},{1,21},{... | collective-permute-start | bytes 1572872 | tf_op jit(solution)/shard_map/ppermute | solution.py:16
  60.2 0.8 copy-start.4
  70.6 0.8 copy-start.5
  71.4 0.8 copy-start.7

commit v13 on v12

--- a/solution.py
+++ b/solution.py
@@ -125,6 +125,7 @@
     right_home = right_home.reshape(-1, edge, edge)
     total = None
     result_shape = (result_count, edge, edge)
+    left_home, right_home = lax.optimization_barrier((left_home, right_home))
     left_now = left_home
     rights = [right_home] + [passed_along(right_home, "row", -s) for s in range(1, STOPS)]
     for stop_index in range(STOPS):

time: 116 us -> 111 us (0.957)
  starting transfers between devices: 19.9 us -> 27.1 us
  waiting for transfers between devices: 15.5 us -> 9.56 us
  Pallas kernels: 34.3 us -> 31.9 us
  blocking collectives: 33.7 us -> 31.6 us
  local copies, waits for them, and re-layouts: 8.11 us -> 6.45 us
    ppermute x9, starting transfers between devices: 13.9 us -> 21.7 us  [passed_along(): return lax.ppermute(value, axis, pairs)]
    all_to_all x1, waiting for transfers between devices: 5.49 us -> 0.01 us  [on_device(): lax.all_to_all(right_out, 'row', split_axis=0, concat_axis=0, tiled=True)]
    pallas_call x4, Pallas kernels: 34.3 us -> 31.9 us  [run_stop(): pl.pallas_call(functools.partial(stop_kernel, stop, first, last), grid_sp...]
    all_to_all x1, blocking collectives: 33.7 us -> 31.6 us  [on_device(): lax.all_to_all(outgoing[None, None], ('row', 'col'), split_axis=2, concat...]
    unnamed x26, local copies, waits for them, and re-layouts: 5.83 us -> 4.18 us
  transfers between devices with their start and end apart: 10 -> 10, of which waited for: 4 -> 3; matrix products, arithmetic and copies ran while one was open for 3% -> 3% of each run, Pallas kernels for 24% -> 21%
where the time goes in v13:
time: 111 us; the launch traced here: 110 us
  Pallas kernels  31.9 us (29%)
  blocking collectives  31.6 us (28%)
  starting transfers between devices  27.1 us (24%)
  waiting for transfers between devices  9.56 us (9%)
  local copies, waits for them, and re-layouts  6.45 us (6%)
  other arithmetic  3.35 us (3%)
    pallas_call x4, Pallas kernels, run_stop(): pl.pallas_call(functools.partial(stop_kernel, stop, first, last), grid_sp...  31.9 us
    all_to_all x1, blocking collectives, on_device(): lax.all_to_all(outgoing[None, None], ('row', 'col'), split_axis=2, concat...  31.6 us
    ppermute x9, starting transfers between devices, passed_along(): return lax.ppermute(value, axis, pairs)  21.7 us
    ppermute x9, waiting for transfers between devices, passed_along(): return lax.ppermute(value, axis, pairs)  9.56 us
    all_to_all x1, starting transfers between devices, on_device(): lax.all_to_all(right_out, 'row', split_axis=0, concat_axis=0, tiled=True)  5.35 us
    unnamed x26, local copies, waits for them, and re-layouts  4.18 us
  transfers between devices with their start and end apart: 10, of which 3 were waited for; matrix products, arithmetic and copies ran while one was open for 3% of the time, Pallas kernels for 21%

profile of v13, /device:TPU:1, one launch (start us, length us, event | category | flops | bytes accessed | tf_op | source)
XLA Modules:
  0.0 110.0 jit_solution(2033324512327389928)
XLA Ops:
  0.0 0.8 compare_bitcast_fusion.1
  0.8 0.1 copy.18
  1.1 0.6 gather_fusion.1
  1.8 0.9 select_select_fusion
  2.7 5.4 %all-to-all-start = ((bf16[8,2,128,128]{3,2,1,0:T(8,128)(2,1)}), bf16[8,2,128,128]{3,2,1,0:T(8,128)(2,1)}, u32[]{:S(2)}, u32[]{:S(2)}) async-start(bf16[8,2,128,128]{3,2,1,0:T(8,128)(2,1)} %select_select_fusion), calls=%async_computation | async-start | bytes 1048576 | tf_op jit(solution)/shard_map/all_to_all | solution.py:124
  8.2 0.6 gather_fusion
  8.9 0.1 select_select_fusion.1
  9.1 1.7 %collective-permute-start = (bf16[4,128,128]{2,1,0:T(8,128)(2,1)S(1)}, bf16[4,128,128]{2,1,0:T(8,128)(2,1)S(1)}, u32[]{:S(2)}, u32[]{:S(2)}) collective-permute-start(bf16[4,128,128]{2,1,0:T(8,128)(2,1)S(1)} %get-tuple-element.38), channel_id=1, source_target_pairs={{0,1},{1,2},{2,3},{3,0},{4,5},{5,6},{6,7},{7,4},{8,9},{9,10},{10,1... | collective-permute-start | bytes 393224 | tf_op jit(solution)/shard_map/ppermute | solution.py:16
  10.8 2.3 %collective-permute-start.1 = (bf16[4,128,128]{2,1,0:T(8,128)(2,1)S(1)}, bf16[4,128,128]{2,1,0:T(8,128)(2,1)S(1)}, u32[]{:S(2)}, u32[]{:S(2)}) collective-permute-start(bf16[4,128,128]{2,1,0:T(8,128)(2,1)S(1)} %get-tuple-element.37), channel_id=1, source_target_pairs={{0,2},{1,3},{2,0},{3,1},{4,6},{5,7},{6,4},{7,5},{8,10},{9,11},{10,... | collective-permute-start | bytes 393224 | tf_op jit(solution)/shard_map/ppermute | solution.py:16
  13.1 1.1 collective-permute-start.2
  14.2 2.4 %collective-permute-done = bf16[4,128,128]{2,1,0:T(8,128)(2,1)S(1)} collective-permute-done((bf16[4,128,128]{2,1,0:T(8,128)(2,1)S(1)}, bf16[4,128,128]{2,1,0:T(8,128)(2,1)S(1)}, u32[]{:S(2)}, u32[]{:S(2)}) %collective-permute-start) | collective-permute-done | bytes 131104 | tf_op jit(solution)/shard_map/ppermute | solution.py:16
  16.6 5.8 %collective-permute-done.1 = bf16[4,128,128]{2,1,0:T(8,128)(2,1)S(1)} collective-permute-done((bf16[4,128,128]{2,1,0:T(8,128)(2,1)S(1)}, bf16[4,128,128]{2,1,0:T(8,128)(2,1)S(1)}, u32[]{:S(2)}, u32[]{:S(2)}) %collective-permute-start.1) | collective-permute-done | bytes 131104 | tf_op jit(solution)/shard_map/ppermute | solution.py:16
  22.5 3.7 %collective-permute-start.3 = (bf16[16,128,128]{2,1,0:T(8,128)(2,1)S(1)}, bf16[16,128,128]{2,1,0:T(8,128)(2,1)S(1)}, u32[]{:S(2)}, u32[]{:S(2)}) collective-permute-start(bf16[16,128,128]{2,1,0:T(8,128)(2,1)S(1)} %pad_maximum_fusion.left_ref), channel_id=1, source_target_pairs={{0,3},{1,0},{2,1},{3,2},{4,7},{5,4},{6,5},{7,6},{8,11},{9,8},{10,9... | collective-permute-start | bytes 1572872 | tf_op jit(solution)/shard_map/ppermute | solution.py:16
  26.3 0.7 fusion.4
  27.0 0.6 pad_add_fusion.stack_ref
  27.6 1.2 %collective-permute-start.5 = (bf16[16,128,128]{2,1,0:T(8,128)(2,1)}, bf16[16,128,128]{2,1,0:T(8,128)(2,1)S(1)}, u32[]{:S(2)}, u32[]{:S(2)}) collective-permute-start(bf16[16,128,128]{2,1,0:T(8,128)(2,1)} %bitcast.14.right_ref), channel_id=1, source_target_pairs={{0,28},{4,0},{8,4},{12,8},{16,12},{20,16},{24,20},{28,24},{1,29},{... | collective-permute-start | bytes 1572872 | tf_op jit(solution)/shard_map/ppermute | solution.py:16
  28.9 0.5 jit_remainder_.2.map_ref
  29.4 6.8 %shard_map.64.refs_0_ = f32[16,128,128]{2,1,0:T(8,128)} custom-call(s32[4,4,384]{2,1,0:T(4,128)} %pad_add_fusion.stack_ref, s32[4,1]{1,0:T(4,128)} %jit_remainder_.2.map_ref, s32[4]{0:T(128)} %get-tuple-element.33.n_ref, s32[32]{0:T(128)} %bitcast.38, bf16[16,128,128]{2,1,0:T(8,128)(2,1)} %copy-done.1, bf16[16,128,128]{2,1,0:T(8,128)(2,1)} %bitcast.14.right_ref), custom_call_target="tpu_custom_call" | custom-call | tf_op jit(solution)/shard_map/pallas_call | solution.py:91
  36.2 1.3 %collective-permute-done.3.left_ref = bf16[16,128,128]{2,1,0:T(8,128)(2,1)S(1)} collective-permute-done((bf16[16,128,128]{2,1,0:T(8,128)(2,1)S(1)}, bf16[16,128,128]{2,1,0:T(8,128)(2,1)S(1)}, u32[]{:S(2)}, u32[]{:S(2)}) %collective-permute-start.3) | collective-permute-done | bytes 524320 | tf_op jit(solution)/shard_map/ppermute | solution.py:16
  37.5 3.0 %collective-permute-start.4 = (bf16[16,128,128]{2,1,0:T(8,128)(2,1)S(1)}, bf16[16,128,128]{2,1,0:T(8,128)(2,1)S(1)}, u32[]{:S(2)}, u32[]{:S(2)}) collective-permute-start(bf16[16,128,128]{2,1,0:T(8,128)(2,1)S(1)} %collective-permute-done.3.left_ref), channel_id=1, source_target_pairs={{0,3},{1,0},{2,1},{3,2},{4,7},{5,4},{6,5},{7,6},{8,11},{9,8},{10,9... | collective-permute-start | bytes 1572872 | tf_op jit(solution)/shard_map/ppermute | solution.py:16
  40.5 1.9 %collective-permute-start.7 = (bf16[16,128,128]{2,1,0:T(8,128)(2,1)}, bf16[16,128,128]{2,1,0:T(8,128)(2,1)S(1)}, u32[]{:S(2)}, u32[]{:S(2)}) collective-permute-start(bf16[16,128,128]{2,1,0:T(8,128)(2,1)} %bitcast.14.right_ref), channel_id=1, source_target_pairs={{0,24},{4,28},{8,0},{12,4},{16,8},{20,12},{24,16},{28,20},{1,25},{... | collective-permute-start | bytes 1572872 | tf_op jit(solution)/shard_map/ppermute | solution.py:16
  42.4 0.8 copy-done.6
  43.2 8.6 %shard_map.65.refs_0_ = f32[16,128,128]{2,1,0:T(8,128)} custom-call(s32[4,4,384]{2,1,0:T(4,128)} %pad_add_fusion.stack_ref, s32[4,1]{1,0:T(4,128)} %jit_remainder_.2.map_ref, s32[4]{0:T(128)} %get-tuple-element.33.n_ref, s32[32]{0:T(128)} %bitcast.39, bf16[16,128,128]{2,1,0:T(8,128)(2,1)} %copy-done.2, ...), custom_call_target="tpu_custom_call", output_to_operand_aliasing={{}: (6, {})} | custom-call | tf_op jit(solution)/shard_map/pallas_call | solution.py:91
  51.8 2.1 %collective-permute-start.6 = (bf16[16,128,128]{2,1,0:T(8,128)(2,1)S(1)}, bf16[16,128,128]{2,1,0:T(8,128)(2,1)S(1)}, u32[]{:S(2)}, u32[]{:S(2)}) collective-permute-start(bf16[16,128,128]{2,1,0:T(8,128)(2,1)S(1)} %collective-permute-done.4.left_ref), channel_id=1, source_target_pairs={{0,3},{1,0},{2,1},{3,2},{4,7},{5,4},{6,5},{7,6},{8,11},{9,8},{10,9... | collective-permute-start | bytes 1572872 | tf_op jit(solution)/shard_map/ppermute | solution.py:16
  53.8 4.8 %collective-permute-start.8 = (bf16[16,128,128]{2,1,0:T(8,128)(2,1)}, bf16[16,128,128]{2,1,0:T(8,128)(2,1)S(1)}, u32[]{:S(2)}, u32[]{:S(2)}) collective-permute-start(bf16[16,128,128]{2,1,0:T(8,128)(2,1)} %bitcast.14.right_ref), channel_id=1, source_target_pairs={{0,20},{4,24},{8,28},{12,0},{16,4},{20,8},{24,12},{28,16},{1,21},{... | collective-permute-start | bytes 1572872 | tf_op jit(solution)/shard_map/ppermute | solution.py:16
  58.7 0.8 copy-done.4
  59.5 7.7 %shard_map.66.refs_0_ = f32[16,128,128]{2,1,0:T(8,128)} custom-call(s32[4,4,384]{2,1,0:T(4,128)} %pad_add_fusion.stack_ref, s32[4,1]{1,0:T(4,128)} %jit_remainder_.2.map_ref, s32[4]{0:T(128)} %get-tuple-element.33.n_ref, s32[32]{0:T(128)} %bitcast.40, bf16[16,128,128]{2,1,0:T(8,128)(2,1)} %copy-done.3, ...), custom_call_target="tpu_custom_call", output_to_operand_aliasing={{}: (6, {})} | custom-call | tf_op jit(solution)/shard_map/pallas_call | solution.py:91
  67.1 0.8 copy-done.5
  67.9 0.8 copy-done.7
  68.7 8.8 %shard_map.67 = bf16[32,128,128]{2,1,0:T(8,128)(2,1)} custom-call(s32[4,4,384]{2,1,0:T(4,128)} %pad_add_fusion.stack_ref, s32[4,1]{1,0:T(4,128)} %jit_remainder_.2.map_ref, s32[4]{0:T(128)} %get-tuple-element.33.n_ref, s32[32]{0:T(128)} %bitcast.41, bf16[16,128,128]{2,1,0:T(8,128)(2,1)} %copy-done.5, bf16[16,128,128]{2,1,0:T(8,128)(2,1)} %copy-done.7, ...), custom_call_target="tpu_custom_call" | custom-call | tf_op jit(solution)/shard_map/pallas_call | solution.py:91
  77.5 31.6 %all_to_all.10 = bf16[1,1,32,128,128]{4,3,1,0,2:T(8,128)(2,1)S(1)} all-to-all(bf16[1,1,32,128,128]{4,3,1,0,2:T(8,128)(2,1)} %bitcast.32), channel_id=1, replica_groups=mesh['row'=8,'col'=4] {'row','col'}, dimensions={2} | all-to-all | bytes 2097152 | tf_op jit(solution)/shard_map/all_to_all | solution.py:139
  109.1 1.0 copy.28
  (40 shorter events, 0.6 us)
Async XLA Ops:
  0.0 1.1 %copy-start = (bf16[1,1,16,128,128]{4,3,2,1,0:T(8,128)(2,1)S(1)}, bf16[1,1,16,128,128]{4,3,2,1,0:T(8,128)(2,1)}, u32[]{:S(2)}) copy-start(bf16[1,1,16,128,128]{4,3,2,1,0:T(8,128)(2,1)} %param.9) | copy-start | bytes 1572868
  0.0 0.8 copy-start.11
  2.7 5.4 %copy-start.10 = (s32[1,1,4,4]{3,2,1,0:T(4,128)S(1)}, s32[1,1,4,4]{3,2,1,0:T(4,128)}, u32[]{:S(2)}) copy-start(s32[1,1,4,4]{3,2,1,0:T(4,128)} %param.10) | copy-start | bytes 196
  2.7 5.5 %copy-start.8 = (bf16[1,1,16,128,128]{4,3,2,1,0:T(8,128)(2,1)S(1)}, bf16[1,1,16,128,128]{4,3,2,1,0:T(8,128)(2,1)}, u32[]{:S(2)}) copy-start(bf16[1,1,16,128,128]{4,3,2,1,0:T(8,128)(2,1)} %param.8) | copy-start | bytes 1572868
  2.7 19.8 %all-to-all-start = ((bf16[8,2,128,128]{3,2,1,0:T(8,128)(2,1)}), bf16[8,2,128,128]{3,2,1,0:T(8,128)(2,1)}, u32[]{:S(2)}, u32[]{:S(2)}) async-start(bf16[8,2,128,128]{3,2,1,0:T(8,128)(2,1)} %select_select_fusion), calls=%async_computation | async-start | bytes 1048576 | tf_op jit(solution)/shard_map/all_to_all | solution.py:124
  9.1 7.4 %collective-permute-start = (bf16[4,128,128]{2,1,0:T(8,128)(2,1)S(1)}, bf16[4,128,128]{2,1,0:T(8,128)(2,1)S(1)}, u32[]{:S(2)}, u32[]{:S(2)}) collective-permute-start(bf16[4,128,128]{2,1,0:T(8,128)(2,1)S(1)} %get-tuple-element.38), channel_id=1, source_target_pairs={{0,1},{1,2},{2,3},{3,0},{4,5},{5,6},{6,7},{7,4},{8,9},{9,10},{10,1... | collective-permute-start | bytes 393224 | tf_op jit(solution)/shard_map/ppermute | solution.py:16
  10.8 11.6 %collective-permute-start.1 = (bf16[4,128,128]{2,1,0:T(8,128)(2,1)S(1)}, bf16[4,128,128]{2,1,0:T(8,128)(2,1)S(1)}, u32[]{:S(2)}, u32[]{:S(2)}) collective-permute-start(bf16[4,128,128]{2,1,0:T(8,128)(2,1)S(1)} %get-tuple-element.37), channel_id=1, source_target_pairs={{0,2},{1,3},{2,0},{3,1},{4,6},{5,7},{6,4},{7,5},{8,10},{9,11},{10,... | collective-permute-start | bytes 393224 | tf_op jit(solution)/shard_map/ppermute | solution.py:16
  13.1 9.3 %collective-permute-start.2 = (bf16[4,128,128]{2,1,0:T(8,128)(2,1)S(1)}, bf16[4,128,128]{2,1,0:T(8,128)(2,1)S(1)}, u32[]{:S(2)}, u32[]{:S(2)}) collective-permute-start(bf16[4,128,128]{2,1,0:T(8,128)(2,1)S(1)} %get-tuple-element.36), channel_id=1, source_target_pairs={{0,3},{1,0},{2,1},{3,2},{4,7},{5,4},{6,5},{7,6},{8,11},{9,8},{10,9... | collective-permute-start | bytes 393224 | tf_op jit(solution)/shard_map/ppermute | solution.py:16
  22.4 3.8 %copy-start.9 = (s32[1,1,4,3,384]{4,2,3,1,0:T(4,128)S(1)}, s32[1,1,4,3,384]{4,2,3,1,0:T(4,128)}, u32[]{:S(2)}) copy-start(s32[1,1,4,3,384]{4,2,3,1,0:T(4,128)} %param.12) | copy-start | bytes 55300
  22.5 6.9 %copy-start.1 = (bf16[16,128,128]{2,1,0:T(8,128)(2,1)}, bf16[16,128,128]{2,1,0:T(8,128)(2,1)S(1)}, u32[]{:S(2)}) copy-start(bf16[16,128,128]{2,1,0:T(8,128)(2,1)S(1)} %pad_maximum_fusion.left_ref) | copy-start | bytes 1572868
  22.5 15.0 %collective-permute-start.3 = (bf16[16,128,128]{2,1,0:T(8,128)(2,1)S(1)}, bf16[16,128,128]{2,1,0:T(8,128)(2,1)S(1)}, u32[]{:S(2)}, u32[]{:S(2)}) collective-permute-start(bf16[16,128,128]{2,1,0:T(8,128)(2,1)S(1)} %pad_maximum_fusion.left_ref), channel_id=1, source_target_pairs={{0,3},{1,0},{2,1},{3,2},{4,7},{5,4},{6,5},{7,6},{8,11},{9,8},{10,9... | collective-permute-start | bytes 1572872 | tf_op jit(solution)/shard_map/ppermute | solution.py:16
  27.6 14.8 %collective-permute-start.5 = (bf16[16,128,128]{2,1,0:T(8,128)(2,1)}, bf16[16,128,128]{2,1,0:T(8,128)(2,1)S(1)}, u32[]{:S(2)}, u32[]{:S(2)}) collective-permute-start(bf16[16,128,128]{2,1,0:T(8,128)(2,1)} %bitcast.14.right_ref), channel_id=1, source_target_pairs={{0,28},{4,0},{8,4},{12,8},{16,12},{20,16},{24,20},{28,24},{1,29},{... | collective-permute-start | bytes 1572872 | tf_op jit(solution)/shard_map/ppermute | solution.py:16
  37.5 4.8 %copy-start.2 = (bf16[16,128,128]{2,1,0:T(8,128)(2,1)}, bf16[16,128,128]{2,1,0:T(8,128)(2,1)S(1)}, u32[]{:S(2)}) copy-start(bf16[16,128,128]{2,1,0:T(8,128)(2,1)S(1)} %collective-permute-done.3.left_ref) | copy-start | bytes 1572868
  37.5 14.3 %collective-permute-start.4 = (bf16[16,128,128]{2,1,0:T(8,128)(2,1)S(1)}, bf16[16,128,128]{2,1,0:T(8,128)(2,1)S(1)}, u32[]{:S(2)}, u32[]{:S(2)}) collective-permute-start(bf16[16,128,128]{2,1,0:T(8,128)(2,1)S(1)} %collective-permute-done.3.left_ref), channel_id=1, source_target_pairs={{0,3},{1,0},{2,1},{3,2},{4,7},{5,4},{6,5},{7,6},{8,11},{9,8},{10,9... | collective-permute-start | bytes 1572872 | tf_op jit(solution)/shard_map/ppermute | solution.py:16
  40.5 18.2 %collective-permute-start.7 = (bf16[16,128,128]{2,1,0:T(8,128)(2,1)}, bf16[16,128,128]{2,1,0:T(8,128)(2,1)S(1)}, u32[]{:S(2)}, u32[]{:S(2)}) collective-permute-start(bf16[16,128,128]{2,1,0:T(8,128)(2,1)} %bitcast.14.right_ref), channel_id=1, source_target_pairs={{0,24},{4,28},{8,0},{12,4},{16,8},{20,12},{24,16},{28,20},{1,25},{... | collective-permute-start | bytes 1572872 | tf_op jit(solution)/shard_map/ppermute | solution.py:16
  42.4 0.8 copy-start.6
  51.8 6.9 %copy-start.3 = (bf16[16,128,128]{2,1,0:T(8,128)(2,1)}, bf16[16,128,128]{2,1,0:T(8,128)(2,1)S(1)}, u32[]{:S(2)}) copy-start(bf16[16,128,128]{2,1,0:T(8,128)(2,1)S(1)} %collective-permute-done.4.left_ref) | copy-start | bytes 1572868
  51.8 15.3 %collective-permute-start.6 = (bf16[16,128,128]{2,1,0:T(8,128)(2,1)S(1)}, bf16[16,128,128]{2,1,0:T(8,128)(2,1)S(1)}, u32[]{:S(2)}, u32[]{:S(2)}) collective-permute-start(bf16[16,128,128]{2,1,0:T(8,128)(2,1)S(1)} %collective-permute-done.4.left_ref), channel_id=1, source_target_pairs={{0,3},{1,0},{2,1},{3,2},{4,7},{5,4},{6,5},{7,6},{8,11},{9,8},{10,9... | collective-permute-start | bytes 1572872 | tf_op jit(solution)/shard_map/ppermute | solution.py:16
  53.8 13.3 %collective-permute-start.8 = (bf16[16,128,128]{2,1,0:T(8,128)(2,1)}, bf16[16,128,128]{2,1,0:T(8,128)(2,1)S(1)}, u32[]{:S(2)}, u32[]{:S(2)}) collective-permute-start(bf16[16,128,128]{2,1,0:T(8,128)(2,1)} %bitcast.14.right_ref), channel_id=1, source_target_pairs={{0,20},{4,24},{8,28},{12,0},{16,4},{20,8},{24,12},{28,16},{1,21},{... | collective-permute-start | bytes 1572872 | tf_op jit(solution)/shard_map/ppermute | solution.py:16
  58.7 0.8 copy-start.4
  67.1 0.8 copy-start.5
  67.9 0.8 copy-start.7

commit v14 on v11

--- a/solution.py
+++ b/solution.py
@@ -26,9 +26,11 @@
 
 def stop_kernel(stop, first, last, stack_ref, map_ref, n_ref, send_ref, left_ref, right_ref, *refs):
     if first:
-        acc_out_ref, acc_ref = refs[0], refs[-1]
+        acc_out_ref = refs[0]
+        acc_ref = refs[-1] if last else acc_out_ref
     else:
-        acc_in_ref, acc_out_ref, acc_ref = refs[0], refs[1], refs[-1]
+        acc_in_ref, acc_out_ref = refs[0], refs[1]
+        acc_ref = refs[-1] if last else acc_out_ref
     live_count = n_ref[stop]
     slots = map_ref.shape[1]
     left_count = left_ref.shape[0]
@@ -65,8 +67,6 @@
             wanted = send_ref[e]
             block = acc_ref[jnp.clip(wanted, 0, result_count - 1)].astype(acc_out_ref.dtype)
             acc_out_ref[e] = jnp.where(wanted >= 0, block, jnp.zeros_like(block))
-    else:
-        acc_out_ref[...] = acc_ref[...]
 
 
 def run_stop(total, left, right, stacks, left_maps, live_counts, c_send, stop, last, result_shape):
@@ -81,7 +81,7 @@
         operands.append(total)
         if not last:
             aliases = {6: 0}
-    scratch = [pltpu.VMEM(result_shape, jnp.float32)]
+    scratch = [pltpu.VMEM(result_shape, jnp.float32)] if last else []
     out_dtype = jnp.bfloat16 if last else jnp.float32
     out_shape = (c_send.shape[0],) + result_shape[1:] if last else result_shape
     grid_spec = pltpu.PrefetchScalarGridSpec(

time: 105 us -> 106 us (level)
  waiting for transfers between devices: 5.02 us -> 7.11 us
  Pallas kernels: 35.8 us -> 37.4 us
  blocking collectives: 32.6 us -> 31 us
    ppermute x9, waiting for transfers between devices: 3.5 us -> 5.6 us  [passed_along(): return lax.ppermute(value, axis, pairs)]
    all_to_all x1, blocking collectives: 32.6 us -> 31 us  [on_device(): lax.all_to_all(outgoing[None, None], ('row', 'col'), split_axis=2, concat...]
    pallas_call x4, Pallas kernels: 35.8 us -> 37.4 us  [run_stop(): pl.pallas_call(functools.partial(stop_kernel, stop, first, last), grid_sp...]
  transfers between devices with their start and end apart: 10 -> 10, of which waited for: 3 -> 4; matrix products, arithmetic and copies ran while one was open for 3% -> 3% of each run, Pallas kernels for 26% -> 25%
where the time goes in v14:
time: 106 us
  Pallas kernels  37.4 us (35%)
  blocking collectives  31 us (29%)
  starting transfers between devices  20.6 us (19%)
  local copies, waits for them, and re-layouts  7.25 us (7%)
  waiting for transfers between devices  7.11 us (7%)
  other arithmetic  2.61 us (2%)
    pallas_call x4, Pallas kernels, run_stop(): pl.pallas_call(functools.partial(stop_kernel, stop, first, last), grid_sp...  37.4 us
    all_to_all x1, blocking collectives, on_device(): lax.all_to_all(outgoing[None, None], ('row', 'col'), split_axis=2, concat...  31 us
    ppermute x9, starting transfers between devices, passed_along(): return lax.ppermute(value, axis, pairs)  15 us
    ppermute x9, waiting for transfers between devices, passed_along(): return lax.ppermute(value, axis, pairs)  5.6 us
    all_to_all x1, starting transfers between devices, on_device(): lax.all_to_all(right_out, 'row', split_axis=0, concat_axis=0, tiled=True)  5.53 us
    unnamed x28, local copies, waits for them, and re-layouts  5.52 us
  transfers between devices with their start and end apart: 10, of which 4 were waited for; matrix products, arithmetic and copies ran while one was open for 3% of the time, Pallas kernels for 25%

profile of v14, /device:TPU:1, one launch (start us, length us, event | category | flops | bytes accessed | tf_op | source)
XLA Modules:
  0.0 106.0 jit_solution(10045117645717907963)
XLA Ops:
  0.0 0.7 copy-done.11
  0.8 0.2 copy-done
  1.1 0.6 gather_fusion
  1.7 0.1 select_select_fusion.1
  1.9 2.2 %collective-permute-start = (bf16[4,128,128]{2,1,0:T(8,128)(2,1)S(1)}, bf16[4,128,128]{2,1,0:T(8,128)(2,1)S(1)}, u32[]{:S(2)}, u32[]{:S(2)}) collective-permute-start(bf16[4,128,128]{2,1,0:T(8,128)(2,1)S(1)} %get-tuple-element.32), channel_id=1, source_target_pairs={{0,1},{1,2},{2,3},{3,0},{4,5},{5,6},{6,7},{7,4},{8,9},{9,10},{10,1... | collective-permute-start | bytes 393224 | tf_op jit(solution)/shard_map/ppermute | solution.py:16
  4.1 2.3 %collective-permute-start.1 = (bf16[4,128,128]{2,1,0:T(8,128)(2,1)S(1)}, bf16[4,128,128]{2,1,0:T(8,128)(2,1)S(1)}, u32[]{:S(2)}, u32[]{:S(2)}) collective-permute-start(bf16[4,128,128]{2,1,0:T(8,128)(2,1)S(1)} %get-tuple-element.31), channel_id=1, source_target_pairs={{0,2},{1,3},{2,0},{3,1},{4,6},{5,7},{6,4},{7,5},{8,10},{9,11},{10,... | collective-permute-start | bytes 393224 | tf_op jit(solution)/shard_map/ppermute | solution.py:16
  6.4 1.1 %collective-permute-start.2 = (bf16[4,128,128]{2,1,0:T(8,128)(2,1)S(1)}, bf16[4,128,128]{2,1,0:T(8,128)(2,1)S(1)}, u32[]{:S(2)}, u32[]{:S(2)}) collective-permute-start(bf16[4,128,128]{2,1,0:T(8,128)(2,1)S(1)} %get-tuple-element.30), channel_id=1, source_target_pairs={{0,3},{1,0},{2,1},{3,2},{4,7},{5,4},{6,5},{7,6},{8,11},{9,8},{10,9... | collective-permute-start | bytes 393224 | tf_op jit(solution)/shard_map/ppermute | solution.py:16
  7.9 0.6 gather_fusion.1
  8.6 0.9 select_select_fusion
  9.5 5.5 %all-to-all-start = ((bf16[8,2,128,128]{3,2,1,0:T(8,128)(2,1)}), bf16[8,2,128,128]{3,2,1,0:T(8,128)(2,1)}, u32[]{:S(2)}, u32[]{:S(2)}) async-start(bf16[8,2,128,128]{3,2,1,0:T(8,128)(2,1)} %select_select_fusion), calls=%async_computation | async-start | bytes 1048576 | tf_op jit(solution)/shard_map/all_to_all | solution.py:122
  15.0 0.7 collective-permute-done.1
  15.8 3.2 %collective-permute-start.3 = (bf16[16,128,128]{2,1,0:T(8,128)(2,1)S(1)}, bf16[16,128,128]{2,1,0:T(8,128)(2,1)S(1)}, u32[]{:S(2)}, u32[]{:S(2)}) collective-permute-start(bf16[16,128,128]{2,1,0:T(8,128)(2,1)S(1)} %pad_maximum_fusion.left_ref), channel_id=1, source_target_pairs={{0,3},{1,0},{2,1},{3,2},{4,7},{5,4},{6,5},{7,6},{8,11},{9,8},{10,9... | collective-permute-start | bytes 1572872 | tf_op jit(solution)/shard_map/ppermute | solution.py:16
  19.0 0.7 fusion.n_ref
  19.7 0.7 fusion.2.map_ref
  20.4 1.5 %all-to-all-done = bf16[8,2,128,128]{3,2,1,0:T(8,128)(2,1)} async-done(((bf16[8,2,128,128]{3,2,1,0:T(8,128)(2,1)}), bf16[8,2,128,128]{3,2,1,0:T(8,128)(2,1)}, u32[]{:S(2)}, u32[]{:S(2)}) %all-to-all-start) | async-done | bytes 524320 | tf_op jit(solution)/shard_map/all_to_all | solution.py:122
  21.9 3.0 %collective-permute-start.5 = (bf16[16,128,128]{2,1,0:T(8,128)(2,1)}, bf16[16,128,128]{2,1,0:T(8,128)(2,1)S(1)}, u32[]{:S(2)}, u32[]{:S(2)}) collective-permute-start(bf16[16,128,128]{2,1,0:T(8,128)(2,1)} %bitcast.14.right_ref), channel_id=1, source_target_pairs={{0,28},{4,0},{8,4},{12,8},{16,12},{20,16},{24,20},{28,24},{1,29},{... | collective-permute-start | bytes 1572872 | tf_op jit(solution)/shard_map/ppermute | solution.py:16
  24.9 10.0 %shard_map.64.refs_0_ = f32[16,128,128]{2,1,0:T(8,128)} custom-call(s32[4,3,384]{2,1,0:T(4,128)} %bitcast.37, s32[4,16]{1,0:T(4,128)} %fusion.2.map_ref, s32[4]{0:T(128)} %fusion.n_ref, s32[32]{0:T(128)} %bitcast.42, bf16[16,128,128]{2,1,0:T(8,128)(2,1)} %copy-done.1, bf16[16,128,128]{2,1,0:T(8,128)(2,1)} %bitcast.14.right_ref), custom_call_target="tpu_custom_call" | custom-call | tf_op jit(solution)/shard_map/pallas_call | solution.py:94
  35.0 0.4 collective-permute-start.7
  35.4 0.4 copy-done.3
  35.7 0.8 copy-done.8
  36.5 7.9 %shard_map.65.refs_0_ = f32[16,128,128]{2,1,0:T(8,128)} custom-call(s32[4,3,384]{2,1,0:T(4,128)} %bitcast.38, s32[4,16]{1,0:T(4,128)} %fusion.2.map_ref, s32[4]{0:T(128)} %fusion.n_ref, s32[32]{0:T(128)} %bitcast.43, bf16[16,128,128]{2,1,0:T(8,128)(2,1)} %copy-done.3, bf16[16,128,128]{2,1,0:T(8,128)(2,1)} %copy-done.8, ...), custom_call_target="tpu_custom_call", output_to_operand_aliasing={{}: (6, {})} | custom-call | tf_op jit(solution)/shard_map/pallas_call | solution.py:94
  44.4 4.4 %collective-permute-done.4.left_ref = bf16[16,128,128]{2,1,0:T(8,128)(2,1)S(1)} collective-permute-done((bf16[16,128,128]{2,1,0:T(8,128)(2,1)S(1)}, bf16[16,128,128]{2,1,0:T(8,128)(2,1)S(1)}, u32[]{:S(2)}, u32[]{:S(2)}) %collective-permute-start.4) | collective-permute-done | bytes 524320 | tf_op jit(solution)/shard_map/ppermute | solution.py:16
  48.8 1.3 %collective-permute-start.6 = (bf16[16,128,128]{2,1,0:T(8,128)(2,1)S(1)}, bf16[16,128,128]{2,1,0:T(8,128)(2,1)S(1)}, u32[]{:S(2)}, u32[]{:S(2)}) collective-permute-start(bf16[16,128,128]{2,1,0:T(8,128)(2,1)S(1)} %collective-permute-done.4.left_ref), channel_id=1, source_target_pairs={{0,3},{1,0},{2,1},{3,2},{4,7},{5,4},{6,5},{7,6},{8,11},{9,8},{10,9... | collective-permute-start | bytes 1572872 | tf_op jit(solution)/shard_map/ppermute | solution.py:16
  50.1 1.6 %collective-permute-start.8 = (bf16[16,128,128]{2,1,0:T(8,128)(2,1)}, bf16[16,128,128]{2,1,0:T(8,128)(2,1)S(1)}, u32[]{:S(2)}, u32[]{:S(2)}) collective-permute-start(bf16[16,128,128]{2,1,0:T(8,128)(2,1)} %bitcast.14.right_ref), channel_id=1, source_target_pairs={{0,20},{4,24},{8,28},{12,0},{16,4},{20,8},{24,12},{28,16},{1,21},{... | collective-permute-start | bytes 1572872 | tf_op jit(solution)/shard_map/ppermute | solution.py:16
  51.7 0.8 copy-done.5
  52.5 9.0 %shard_map.66.refs_0_ = f32[16,128,128]{2,1,0:T(8,128)} custom-call(s32[4,3,384]{2,1,0:T(4,128)} %bitcast.39, s32[4,16]{1,0:T(4,128)} %fusion.2.map_ref, s32[4]{0:T(128)} %fusion.n_ref, s32[32]{0:T(128)} %bitcast.44, bf16[16,128,128]{2,1,0:T(8,128)(2,1)} %copy-done.4, bf16[16,128,128]{2,1,0:T(8,128)(2,1)} %copy-done.5, ...), custom_call_target="tpu_custom_call", output_to_operand_aliasing={{}: (6, {})} | custom-call | tf_op jit(solution)/shard_map/pallas_call | solution.py:94
  61.5 0.5 collective-permute-done.6.left_ref
  62.0 0.8 copy-done.6
  62.8 0.8 copy-done.7
  63.6 10.4 %shard_map.67 = bf16[32,128,128]{2,1,0:T(8,128)(2,1)} custom-call(s32[4,3,384]{2,1,0:T(4,128)} %bitcast.40, s32[4,16]{1,0:T(4,128)} %fusion.2.map_ref, s32[4]{0:T(128)} %fusion.n_ref, s32[32]{0:T(128)} %bitcast.45, bf16[16,128,128]{2,1,0:T(8,128)(2,1)} %copy-done.6, bf16[16,128,128]{2,1,0:T(8,128)(2,1)} %copy-done.7, f32[16,128,128]{2,1,0:T(8,128)} %shard_map.66.refs_0_), custom_call_target="tpu_custom_call" | custom-call | tf_op jit(solution)/shard_map/pallas_call | solution.py:94
  74.1 31.0 %all_to_all.10 = bf16[1,1,32,128,128]{4,3,1,0,2:T(8,128)(2,1)S(1)} all-to-all(bf16[1,1,32,128,128]{4,3,1,0,2:T(8,128)(2,1)} %bitcast.32), channel_id=1, replica_groups=mesh['row'=8,'col'=4] {'row','col'}, dimensions={2} | all-to-all | bytes 2097152 | tf_op jit(solution)/shard_map/all_to_all | solution.py:136
  105.1 1.0 copy.28
  (42 shorter events, 0.7 us)
Async XLA Ops:
  0.0 1.1 copy-start
  0.0 0.7 copy-start.11
  1.9 6.0 %copy-start.9 = (bf16[1,1,16,128,128]{4,3,2,1,0:T(8,128)(2,1)S(1)}, bf16[1,1,16,128,128]{4,3,2,1,0:T(8,128)(2,1)}, u32[]{:S(2)}) copy-start(bf16[1,1,16,128,128]{4,3,2,1,0:T(8,128)(2,1)} %param.9) | copy-start | bytes 1572868
  1.9 13.1 %collective-permute-start = (bf16[4,128,128]{2,1,0:T(8,128)(2,1)S(1)}, bf16[4,128,128]{2,1,0:T(8,128)(2,1)S(1)}, u32[]{:S(2)}, u32[]{:S(2)}) collective-permute-start(bf16[4,128,128]{2,1,0:T(8,128)(2,1)S(1)} %get-tuple-element.32), channel_id=1, source_target_pairs={{0,1},{1,2},{2,3},{3,0},{4,5},{5,6},{6,7},{7,4},{8,9},{9,10},{10,1... | collective-permute-start | bytes 393224 | tf_op jit(solution)/shard_map/ppermute | solution.py:16
  4.1 3.4 %copy-start.12 = (s32[1,1,8,2]{2,3,1,0:T(2,128)S(1)}, s32[1,1,8,2]{2,3,1,0:T(2,128)}, u32[]{:S(2)}) copy-start(s32[1,1,8,2]{2,3,1,0:T(2,128)} %param.11) | copy-start | bytes 196
  4.1 11.6 %collective-permute-start.1 = (bf16[4,128,128]{2,1,0:T(8,128)(2,1)S(1)}, bf16[4,128,128]{2,1,0:T(8,128)(2,1)S(1)}, u32[]{:S(2)}, u32[]{:S(2)}) collective-permute-start(bf16[4,128,128]{2,1,0:T(8,128)(2,1)S(1)} %get-tuple-element.31), channel_id=1, source_target_pairs={{0,2},{1,3},{2,0},{3,1},{4,6},{5,7},{6,4},{7,5},{8,10},{9,11},{10,... | collective-permute-start | bytes 393224 | tf_op jit(solution)/shard_map/ppermute | solution.py:16
  6.4 9.3 %collective-permute-start.2 = (bf16[4,128,128]{2,1,0:T(8,128)(2,1)S(1)}, bf16[4,128,128]{2,1,0:T(8,128)(2,1)S(1)}, u32[]{:S(2)}, u32[]{:S(2)}) collective-permute-start(bf16[4,128,128]{2,1,0:T(8,128)(2,1)S(1)} %get-tuple-element.30), channel_id=1, source_target_pairs={{0,3},{1,0},{2,1},{3,2},{4,7},{5,4},{6,5},{7,6},{8,11},{9,8},{10,9... | collective-permute-start | bytes 393224 | tf_op jit(solution)/shard_map/ppermute | solution.py:16
  9.5 12.4 %all-to-all-start = ((bf16[8,2,128,128]{3,2,1,0:T(8,128)(2,1)}), bf16[8,2,128,128]{3,2,1,0:T(8,128)(2,1)}, u32[]{:S(2)}, u32[]{:S(2)}) async-start(bf16[8,2,128,128]{3,2,1,0:T(8,128)(2,1)} %select_select_fusion), calls=%async_computation | async-start | bytes 1048576 | tf_op jit(solution)/shard_map/all_to_all | solution.py:122
  15.7 3.3 %copy-start.10 = (s32[1,1,4,3,384]{4,2,3,1,0:T(4,128)S(1)}, s32[1,1,4,3,384]{4,2,3,1,0:T(4,128)}, u32[]{:S(2)}) copy-start(s32[1,1,4,3,384]{4,2,3,1,0:T(4,128)} %param.12) | copy-start | bytes 55300
  15.8 9.1 %copy-start.1 = (bf16[16,128,128]{2,1,0:T(8,128)(2,1)}, bf16[16,128,128]{2,1,0:T(8,128)(2,1)S(1)}, u32[]{:S(2)}) copy-start(bf16[16,128,128]{2,1,0:T(8,128)(2,1)S(1)} %pad_maximum_fusion.left_ref) | copy-start | bytes 1572868
  15.8 19.1 %collective-permute-start.3 = (bf16[16,128,128]{2,1,0:T(8,128)(2,1)S(1)}, bf16[16,128,128]{2,1,0:T(8,128)(2,1)S(1)}, u32[]{:S(2)}, u32[]{:S(2)}) collective-permute-start(bf16[16,128,128]{2,1,0:T(8,128)(2,1)S(1)} %pad_maximum_fusion.left_ref), channel_id=1, source_target_pairs={{0,3},{1,0},{2,1},{3,2},{4,7},{5,4},{6,5},{7,6},{8,11},{9,8},{10,9... | collective-permute-start | bytes 1572872 | tf_op jit(solution)/shard_map/ppermute | solution.py:16
  19.0 5.9 %copy-start.2 = (s32[1,1,4,3,384]{4,3,2,1,0:T(4,128)}, s32[1,1,4,3,384]{4,3,2,1,0:T(4,128)S(1)}, u32[]{:S(2)}) copy-start(s32[1,1,4,3,384]{4,3,2,1,0:T(4,128)S(1)} %copy.24) | copy-start | bytes 55300
  21.9 13.5 %collective-permute-start.5 = (bf16[16,128,128]{2,1,0:T(8,128)(2,1)}, bf16[16,128,128]{2,1,0:T(8,128)(2,1)S(1)}, u32[]{:S(2)}, u32[]{:S(2)}) collective-permute-start(bf16[16,128,128]{2,1,0:T(8,128)(2,1)} %bitcast.14.right_ref), channel_id=1, source_target_pairs={{0,28},{4,0},{8,4},{12,8},{16,12},{20,16},{24,20},{28,24},{1,29},{... | collective-permute-start | bytes 1572872 | tf_op jit(solution)/shard_map/ppermute | solution.py:16
  34.9 0.8 copy-start.3
  34.9 13.9 %collective-permute-start.4 = (bf16[16,128,128]{2,1,0:T(8,128)(2,1)S(1)}, bf16[16,128,128]{2,1,0:T(8,128)(2,1)S(1)}, u32[]{:S(2)}, u32[]{:S(2)}) collective-permute-start(bf16[16,128,128]{2,1,0:T(8,128)(2,1)S(1)} %collective-permute-done.3.left_ref), channel_id=1, source_target_pairs={{0,3},{1,0},{2,1},{3,2},{4,7},{5,4},{6,5},{7,6},{8,11},{9,8},{10,9... | collective-permute-start | bytes 1572872 | tf_op jit(solution)/shard_map/ppermute | solution.py:16
  35.0 16.7 %collective-permute-start.7 = (bf16[16,128,128]{2,1,0:T(8,128)(2,1)}, bf16[16,128,128]{2,1,0:T(8,128)(2,1)S(1)}, u32[]{:S(2)}, u32[]{:S(2)}) collective-permute-start(bf16[16,128,128]{2,1,0:T(8,128)(2,1)} %bitcast.14.right_ref), channel_id=1, source_target_pairs={{0,24},{4,28},{8,0},{12,4},{16,8},{20,12},{24,16},{28,20},{1,25},{... | collective-permute-start | bytes 1572872 | tf_op jit(solution)/shard_map/ppermute | solution.py:16
  35.7 0.8 copy-start.8
  48.8 2.9 %copy-start.4 = (bf16[16,128,128]{2,1,0:T(8,128)(2,1)}, bf16[16,128,128]{2,1,0:T(8,128)(2,1)S(1)}, u32[]{:S(2)}) copy-start(bf16[16,128,128]{2,1,0:T(8,128)(2,1)S(1)} %collective-permute-done.4.left_ref) | copy-start | bytes 1572868
  48.8 13.2 %collective-permute-start.6 = (bf16[16,128,128]{2,1,0:T(8,128)(2,1)S(1)}, bf16[16,128,128]{2,1,0:T(8,128)(2,1)S(1)}, u32[]{:S(2)}, u32[]{:S(2)}) collective-permute-start(bf16[16,128,128]{2,1,0:T(8,128)(2,1)S(1)} %collective-permute-done.4.left_ref), channel_id=1, source_target_pairs={{0,3},{1,0},{2,1},{3,2},{4,7},{5,4},{6,5},{7,6},{8,11},{9,8},{10,9... | collective-permute-start | bytes 1572872 | tf_op jit(solution)/shard_map/ppermute | solution.py:16
  50.1 11.9 %collective-permute-start.8 = (bf16[16,128,128]{2,1,0:T(8,128)(2,1)}, bf16[16,128,128]{2,1,0:T(8,128)(2,1)S(1)}, u32[]{:S(2)}, u32[]{:S(2)}) collective-permute-start(bf16[16,128,128]{2,1,0:T(8,128)(2,1)} %bitcast.14.right_ref), channel_id=1, source_target_pairs={{0,20},{4,24},{8,28},{12,0},{16,4},{20,8},{24,12},{28,16},{1,21},{... | collective-permute-start | bytes 1572872 | tf_op jit(solution)/shard_map/ppermute | solution.py:16
  51.7 0.8 copy-start.5
  62.0 0.8 copy-start.6
  62.8 0.8 copy-start.7

commit v15 on v14

--- a/solution.py
+++ b/solution.py
@@ -21,7 +21,7 @@
     return jnp.where((index >= 0)[..., None, None], picked, jnp.zeros_like(picked))
 
 
-GROUP = 32
+GROUP = 64
 
 
 def stop_kernel(stop, first, last, stack_ref, map_ref, n_ref, send_ref, left_ref, right_ref, *refs):

time: 106 us -> 105 us (level)
  waiting for transfers between devices: 7.11 us -> 5.91 us
    ppermute x9, waiting for transfers between devices: 5.6 us -> 4.39 us  [passed_along(): return lax.ppermute(value, axis, pairs)]
  transfers between devices with their start and end apart: 10 -> 10, of which waited for: 4 -> 3; matrix products, arithmetic and copies ran while one was open for 3% -> 3% of each run, Pallas kernels for 25% -> 27%
where the time goes in v15:
time: 105 us
  Pallas kernels  37.3 us (36%)
  blocking collectives  30.6 us (29%)
  starting transfers between devices  21.1 us (20%)
  local copies, waits for them, and re-layouts  7.21 us (7%)
  waiting for transfers between devices  5.91 us (6%)
  other arithmetic  2.61 us (2%)
    pallas_call x4, Pallas kernels, run_stop(): pl.pallas_call(functools.partial(stop_kernel, stop, first, last), grid_sp...  37.3 us
    all_to_all x1, blocking collectives, on_device(): lax.all_to_all(outgoing[None, None], ('row', 'col'), split_axis=2, concat...  30.6 us
    ppermute x9, starting transfers between devices, passed_along(): return lax.ppermute(value, axis, pairs)  15.6 us
    all_to_all x1, starting transfers between devices, on_device(): lax.all_to_all(right_out, 'row', split_axis=0, concat_axis=0, tiled=True)  5.53 us
    unnamed x28, local copies, waits for them, and re-layouts  5.48 us
    ppermute x9, waiting for transfers between devices, passed_along(): return lax.ppermute(value, axis, pairs)  4.39 us
  transfers between devices with their start and end apart: 10, of which 3 were waited for; matrix products, arithmetic and copies ran while one was open for 3% of the time, Pallas kernels for 27%

profile of v15, /device:TPU:1, one launch (start us, length us, event | category | flops | bytes accessed | tf_op | source)
XLA Modules:
  0.0 104.8 jit_solution(9210885873013336224)
XLA Ops:
  0.0 0.7 copy-done.11
  0.8 0.2 copy-done
  1.1 0.6 gather_fusion
  1.7 0.1 select_select_fusion.1
  1.9 2.2 %collective-permute-start = (bf16[4,128,128]{2,1,0:T(8,128)(2,1)S(1)}, bf16[4,128,128]{2,1,0:T(8,128)(2,1)S(1)}, u32[]{:S(2)}, u32[]{:S(2)}) collective-permute-start(bf16[4,128,128]{2,1,0:T(8,128)(2,1)S(1)} %get-tuple-element.32), channel_id=1, source_target_pairs={{0,1},{1,2},{2,3},{3,0},{4,5},{5,6},{6,7},{7,4},{8,9},{9,10},{10,1... | collective-permute-start | bytes 393224 | tf_op jit(solution)/shard_map/ppermute | solution.py:16
  4.1 2.3 %collective-permute-start.1 = (bf16[4,128,128]{2,1,0:T(8,128)(2,1)S(1)}, bf16[4,128,128]{2,1,0:T(8,128)(2,1)S(1)}, u32[]{:S(2)}, u32[]{:S(2)}) collective-permute-start(bf16[4,128,128]{2,1,0:T(8,128)(2,1)S(1)} %get-tuple-element.31), channel_id=1, source_target_pairs={{0,2},{1,3},{2,0},{3,1},{4,6},{5,7},{6,4},{7,5},{8,10},{9,11},{10,... | collective-permute-start | bytes 393224 | tf_op jit(solution)/shard_map/ppermute | solution.py:16
  6.4 1.1 %collective-permute-start.2 = (bf16[4,128,128]{2,1,0:T(8,128)(2,1)S(1)}, bf16[4,128,128]{2,1,0:T(8,128)(2,1)S(1)}, u32[]{:S(2)}, u32[]{:S(2)}) collective-permute-start(bf16[4,128,128]{2,1,0:T(8,128)(2,1)S(1)} %get-tuple-element.30), channel_id=1, source_target_pairs={{0,3},{1,0},{2,1},{3,2},{4,7},{5,4},{6,5},{7,6},{8,11},{9,8},{10,9... | collective-permute-start | bytes 393224 | tf_op jit(solution)/shard_map/ppermute | solution.py:16
  7.5 0.1 copy.18
  7.9 0.6 gather_fusion.1
  8.6 0.9 select_select_fusion
  9.5 5.5 %all-to-all-start = ((bf16[8,2,128,128]{3,2,1,0:T(8,128)(2,1)}), bf16[8,2,128,128]{3,2,1,0:T(8,128)(2,1)}, u32[]{:S(2)}, u32[]{:S(2)}) async-start(bf16[8,2,128,128]{3,2,1,0:T(8,128)(2,1)} %select_select_fusion), calls=%async_computation | async-start | bytes 1048576 | tf_op jit(solution)/shard_map/all_to_all | solution.py:122
  15.0 0.7 collective-permute-done.1
  15.8 3.2 %collective-permute-start.3 = (bf16[16,128,128]{2,1,0:T(8,128)(2,1)S(1)}, bf16[16,128,128]{2,1,0:T(8,128)(2,1)S(1)}, u32[]{:S(2)}, u32[]{:S(2)}) collective-permute-start(bf16[16,128,128]{2,1,0:T(8,128)(2,1)S(1)} %pad_maximum_fusion.left_ref), channel_id=1, source_target_pairs={{0,3},{1,0},{2,1},{3,2},{4,7},{5,4},{6,5},{7,6},{8,11},{9,8},{10,9... | collective-permute-start | bytes 1572872 | tf_op jit(solution)/shard_map/ppermute | solution.py:16
  19.0 0.7 fusion.n_ref
  19.7 0.7 fusion.2.map_ref
  20.4 1.5 %all-to-all-done = bf16[8,2,128,128]{3,2,1,0:T(8,128)(2,1)} async-done(((bf16[8,2,128,128]{3,2,1,0:T(8,128)(2,1)}), bf16[8,2,128,128]{3,2,1,0:T(8,128)(2,1)}, u32[]{:S(2)}, u32[]{:S(2)}) %all-to-all-start) | async-done | bytes 524320 | tf_op jit(solution)/shard_map/all_to_all | solution.py:122
  21.9 3.0 %collective-permute-start.5 = (bf16[16,128,128]{2,1,0:T(8,128)(2,1)}, bf16[16,128,128]{2,1,0:T(8,128)(2,1)S(1)}, u32[]{:S(2)}, u32[]{:S(2)}) collective-permute-start(bf16[16,128,128]{2,1,0:T(8,128)(2,1)} %bitcast.14.right_ref), channel_id=1, source_target_pairs={{0,28},{4,0},{8,4},{12,8},{16,12},{20,16},{24,20},{28,24},{1,29},{... | collective-permute-start | bytes 1572872 | tf_op jit(solution)/shard_map/ppermute | solution.py:16
  24.9 9.4 %shard_map.64.refs_0_ = f32[16,128,128]{2,1,0:T(8,128)} custom-call(s32[4,3,384]{2,1,0:T(4,128)} %bitcast.37, s32[4,16]{1,0:T(4,128)} %fusion.2.map_ref, s32[4]{0:T(128)} %fusion.n_ref, s32[32]{0:T(128)} %bitcast.42, bf16[16,128,128]{2,1,0:T(8,128)(2,1)} %copy-done.1, bf16[16,128,128]{2,1,0:T(8,128)(2,1)} %bitcast.14.right_ref), custom_call_target="tpu_custom_call" | custom-call | tf_op jit(solution)/shard_map/pallas_call | solution.py:94
  34.3 0.5 collective-permute-start.7
  34.8 0.3 copy-done.3
  35.1 0.8 copy-done.8
  35.9 8.1 %shard_map.65.refs_0_ = f32[16,128,128]{2,1,0:T(8,128)} custom-call(s32[4,3,384]{2,1,0:T(4,128)} %bitcast.38, s32[4,16]{1,0:T(4,128)} %fusion.2.map_ref, s32[4]{0:T(128)} %fusion.n_ref, s32[32]{0:T(128)} %bitcast.43, bf16[16,128,128]{2,1,0:T(8,128)(2,1)} %copy-done.3, bf16[16,128,128]{2,1,0:T(8,128)(2,1)} %copy-done.8, ...), custom_call_target="tpu_custom_call", output_to_operand_aliasing={{}: (6, {})} | custom-call | tf_op jit(solution)/shard_map/pallas_call | solution.py:94
  44.1 3.7 %collective-permute-done.4.left_ref = bf16[16,128,128]{2,1,0:T(8,128)(2,1)S(1)} collective-permute-done((bf16[16,128,128]{2,1,0:T(8,128)(2,1)S(1)}, bf16[16,128,128]{2,1,0:T(8,128)(2,1)S(1)}, u32[]{:S(2)}, u32[]{:S(2)}) %collective-permute-start.4) | collective-permute-done | bytes 524320 | tf_op jit(solution)/shard_map/ppermute | solution.py:16
  47.7 1.1 %collective-permute-start.6 = (bf16[16,128,128]{2,1,0:T(8,128)(2,1)S(1)}, bf16[16,128,128]{2,1,0:T(8,128)(2,1)S(1)}, u32[]{:S(2)}, u32[]{:S(2)}) collective-permute-start(bf16[16,128,128]{2,1,0:T(8,128)(2,1)S(1)} %collective-permute-done.4.left_ref), channel_id=1, source_target_pairs={{0,3},{1,0},{2,1},{3,2},{4,7},{5,4},{6,5},{7,6},{8,11},{9,8},{10,9... | collective-permute-start | bytes 1572872 | tf_op jit(solution)/shard_map/ppermute | solution.py:16
  48.8 2.3 %collective-permute-start.8 = (bf16[16,128,128]{2,1,0:T(8,128)(2,1)}, bf16[16,128,128]{2,1,0:T(8,128)(2,1)S(1)}, u32[]{:S(2)}, u32[]{:S(2)}) collective-permute-start(bf16[16,128,128]{2,1,0:T(8,128)(2,1)} %bitcast.14.right_ref), channel_id=1, source_target_pairs={{0,20},{4,24},{8,28},{12,0},{16,4},{20,8},{24,12},{28,16},{1,21},{... | collective-permute-start | bytes 1572872 | tf_op jit(solution)/shard_map/ppermute | solution.py:16
  51.1 0.8 copy-done.5
  51.9 10.3 %shard_map.66.refs_0_ = f32[16,128,128]{2,1,0:T(8,128)} custom-call(s32[4,3,384]{2,1,0:T(4,128)} %bitcast.39, s32[4,16]{1,0:T(4,128)} %fusion.2.map_ref, s32[4]{0:T(128)} %fusion.n_ref, s32[32]{0:T(128)} %bitcast.44, bf16[16,128,128]{2,1,0:T(8,128)(2,1)} %copy-done.4, bf16[16,128,128]{2,1,0:T(8,128)(2,1)} %copy-done.5, ...), custom_call_target="tpu_custom_call", output_to_operand_aliasing={{}: (6, {})} | custom-call | tf_op jit(solution)/shard_map/pallas_call | solution.py:94
  62.3 0.8 copy-done.6
  63.1 0.8 copy-done.7
  63.9 9.5 %shard_map.67 = bf16[32,128,128]{2,1,0:T(8,128)(2,1)} custom-call(s32[4,3,384]{2,1,0:T(4,128)} %bitcast.40, s32[4,16]{1,0:T(4,128)} %fusion.2.map_ref, s32[4]{0:T(128)} %fusion.n_ref, s32[32]{0:T(128)} %bitcast.45, bf16[16,128,128]{2,1,0:T(8,128)(2,1)} %copy-done.6, bf16[16,128,128]{2,1,0:T(8,128)(2,1)} %copy-done.7, f32[16,128,128]{2,1,0:T(8,128)} %shard_map.66.refs_0_), custom_call_target="tpu_custom_call" | custom-call | tf_op jit(solution)/shard_map/pallas_call | solution.py:94
  73.3 30.6 %all_to_all.10 = bf16[1,1,32,128,128]{4,3,1,0,2:T(8,128)(2,1)S(1)} all-to-all(bf16[1,1,32,128,128]{4,3,1,0,2:T(8,128)(2,1)} %bitcast.32), channel_id=1, replica_groups=mesh['row'=8,'col'=4] {'row','col'}, dimensions={2} | all-to-all | bytes 2097152 | tf_op jit(solution)/shard_map/all_to_all | solution.py:136
  103.9 1.0 copy.28
  (42 shorter events, 0.6 us)
Async XLA Ops:
  0.0 1.1 %copy-start = (bf16[1,1,16,128,128]{4,3,2,1,0:T(8,128)(2,1)S(1)}, bf16[1,1,16,128,128]{4,3,2,1,0:T(8,128)(2,1)}, u32[]{:S(2)}) copy-start(bf16[1,1,16,128,128]{4,3,2,1,0:T(8,128)(2,1)} %param.8) | copy-start | bytes 1572868
  0.0 0.7 copy-start.11
  1.9 6.0 %copy-start.9 = (bf16[1,1,16,128,128]{4,3,2,1,0:T(8,128)(2,1)S(1)}, bf16[1,1,16,128,128]{4,3,2,1,0:T(8,128)(2,1)}, u32[]{:S(2)}) copy-start(bf16[1,1,16,128,128]{4,3,2,1,0:T(8,128)(2,1)} %param.9) | copy-start | bytes 1572868
  1.9 13.1 %collective-permute-start = (bf16[4,128,128]{2,1,0:T(8,128)(2,1)S(1)}, bf16[4,128,128]{2,1,0:T(8,128)(2,1)S(1)}, u32[]{:S(2)}, u32[]{:S(2)}) collective-permute-start(bf16[4,128,128]{2,1,0:T(8,128)(2,1)S(1)} %get-tuple-element.32), channel_id=1, source_target_pairs={{0,1},{1,2},{2,3},{3,0},{4,5},{5,6},{6,7},{7,4},{8,9},{9,10},{10,1... | collective-permute-start | bytes 393224 | tf_op jit(solution)/shard_map/ppermute | solution.py:16
  4.1 3.4 %copy-start.12 = (s32[1,1,8,2]{2,3,1,0:T(2,128)S(1)}, s32[1,1,8,2]{2,3,1,0:T(2,128)}, u32[]{:S(2)}) copy-start(s32[1,1,8,2]{2,3,1,0:T(2,128)} %param.11) | copy-start | bytes 196
  4.1 11.6 %collective-permute-start.1 = (bf16[4,128,128]{2,1,0:T(8,128)(2,1)S(1)}, bf16[4,128,128]{2,1,0:T(8,128)(2,1)S(1)}, u32[]{:S(2)}, u32[]{:S(2)}) collective-permute-start(bf16[4,128,128]{2,1,0:T(8,128)(2,1)S(1)} %get-tuple-element.31), channel_id=1, source_target_pairs={{0,2},{1,3},{2,0},{3,1},{4,6},{5,7},{6,4},{7,5},{8,10},{9,11},{10,... | collective-permute-start | bytes 393224 | tf_op jit(solution)/shard_map/ppermute | solution.py:16
  6.4 9.3 %collective-permute-start.2 = (bf16[4,128,128]{2,1,0:T(8,128)(2,1)S(1)}, bf16[4,128,128]{2,1,0:T(8,128)(2,1)S(1)}, u32[]{:S(2)}, u32[]{:S(2)}) collective-permute-start(bf16[4,128,128]{2,1,0:T(8,128)(2,1)S(1)} %get-tuple-element.30), channel_id=1, source_target_pairs={{0,3},{1,0},{2,1},{3,2},{4,7},{5,4},{6,5},{7,6},{8,11},{9,8},{10,9... | collective-permute-start | bytes 393224 | tf_op jit(solution)/shard_map/ppermute | solution.py:16
  9.5 12.4 %all-to-all-start = ((bf16[8,2,128,128]{3,2,1,0:T(8,128)(2,1)}), bf16[8,2,128,128]{3,2,1,0:T(8,128)(2,1)}, u32[]{:S(2)}, u32[]{:S(2)}) async-start(bf16[8,2,128,128]{3,2,1,0:T(8,128)(2,1)} %select_select_fusion), calls=%async_computation | async-start | bytes 1048576 | tf_op jit(solution)/shard_map/all_to_all | solution.py:122
  15.7 3.3 %copy-start.10 = (s32[1,1,4,3,384]{4,2,3,1,0:T(4,128)S(1)}, s32[1,1,4,3,384]{4,2,3,1,0:T(4,128)}, u32[]{:S(2)}) copy-start(s32[1,1,4,3,384]{4,2,3,1,0:T(4,128)} %param.12) | copy-start | bytes 55300
  15.8 9.1 %copy-start.1 = (bf16[16,128,128]{2,1,0:T(8,128)(2,1)}, bf16[16,128,128]{2,1,0:T(8,128)(2,1)S(1)}, u32[]{:S(2)}) copy-start(bf16[16,128,128]{2,1,0:T(8,128)(2,1)S(1)} %pad_maximum_fusion.left_ref) | copy-start | bytes 1572868
  15.8 18.5 %collective-permute-start.3 = (bf16[16,128,128]{2,1,0:T(8,128)(2,1)S(1)}, bf16[16,128,128]{2,1,0:T(8,128)(2,1)S(1)}, u32[]{:S(2)}, u32[]{:S(2)}) collective-permute-start(bf16[16,128,128]{2,1,0:T(8,128)(2,1)S(1)} %pad_maximum_fusion.left_ref), channel_id=1, source_target_pairs={{0,3},{1,0},{2,1},{3,2},{4,7},{5,4},{6,5},{7,6},{8,11},{9,8},{10,9... | collective-permute-start | bytes 1572872 | tf_op jit(solution)/shard_map/ppermute | solution.py:16
  19.0 5.9 %copy-start.2 = (s32[1,1,4,3,384]{4,3,2,1,0:T(4,128)}, s32[1,1,4,3,384]{4,3,2,1,0:T(4,128)S(1)}, u32[]{:S(2)}) copy-start(s32[1,1,4,3,384]{4,3,2,1,0:T(4,128)S(1)} %copy.24) | copy-start | bytes 55300
  21.9 12.9 %collective-permute-start.5 = (bf16[16,128,128]{2,1,0:T(8,128)(2,1)}, bf16[16,128,128]{2,1,0:T(8,128)(2,1)S(1)}, u32[]{:S(2)}, u32[]{:S(2)}) collective-permute-start(bf16[16,128,128]{2,1,0:T(8,128)(2,1)} %bitcast.14.right_ref), channel_id=1, source_target_pairs={{0,28},{4,0},{8,4},{12,8},{16,12},{20,16},{24,20},{28,24},{1,29},{... | collective-permute-start | bytes 1572872 | tf_op jit(solution)/shard_map/ppermute | solution.py:16
  34.3 0.8 copy-start.3
  34.3 13.4 %collective-permute-start.4 = (bf16[16,128,128]{2,1,0:T(8,128)(2,1)S(1)}, bf16[16,128,128]{2,1,0:T(8,128)(2,1)S(1)}, u32[]{:S(2)}, u32[]{:S(2)}) collective-permute-start(bf16[16,128,128]{2,1,0:T(8,128)(2,1)S(1)} %collective-permute-done.3.left_ref), channel_id=1, source_target_pairs={{0,3},{1,0},{2,1},{3,2},{4,7},{5,4},{6,5},{7,6},{8,11},{9,8},{10,9... | collective-permute-start | bytes 1572872 | tf_op jit(solution)/shard_map/ppermute | solution.py:16
  34.3 16.8 %collective-permute-start.7 = (bf16[16,128,128]{2,1,0:T(8,128)(2,1)}, bf16[16,128,128]{2,1,0:T(8,128)(2,1)S(1)}, u32[]{:S(2)}, u32[]{:S(2)}) collective-permute-start(bf16[16,128,128]{2,1,0:T(8,128)(2,1)} %bitcast.14.right_ref), channel_id=1, source_target_pairs={{0,24},{4,28},{8,0},{12,4},{16,8},{20,12},{24,16},{28,20},{1,25},{... | collective-permute-start | bytes 1572872 | tf_op jit(solution)/shard_map/ppermute | solution.py:16
  35.1 0.8 copy-start.8
  47.7 3.4 %copy-start.4 = (bf16[16,128,128]{2,1,0:T(8,128)(2,1)}, bf16[16,128,128]{2,1,0:T(8,128)(2,1)S(1)}, u32[]{:S(2)}) copy-start(bf16[16,128,128]{2,1,0:T(8,128)(2,1)S(1)} %collective-permute-done.4.left_ref) | copy-start | bytes 1572868
  47.7 14.5 %collective-permute-start.6 = (bf16[16,128,128]{2,1,0:T(8,128)(2,1)S(1)}, bf16[16,128,128]{2,1,0:T(8,128)(2,1)S(1)}, u32[]{:S(2)}, u32[]{:S(2)}) collective-permute-start(bf16[16,128,128]{2,1,0:T(8,128)(2,1)S(1)} %collective-permute-done.4.left_ref), channel_id=1, source_target_pairs={{0,3},{1,0},{2,1},{3,2},{4,7},{5,4},{6,5},{7,6},{8,11},{9,8},{10,9... | collective-permute-start | bytes 1572872 | tf_op jit(solution)/shard_map/ppermute | solution.py:16
  48.8 13.4 %collective-permute-start.8 = (bf16[16,128,128]{2,1,0:T(8,128)(2,1)}, bf16[16,128,128]{2,1,0:T(8,128)(2,1)S(1)}, u32[]{:S(2)}, u32[]{:S(2)}) collective-permute-start(bf16[16,128,128]{2,1,0:T(8,128)(2,1)} %bitcast.14.right_ref), channel_id=1, source_target_pairs={{0,20},{4,24},{8,28},{12,0},{16,4},{20,8},{24,12},{28,16},{1,21},{... | collective-permute-start | bytes 1572872 | tf_op jit(solution)/shard_map/ppermute | solution.py:16
  51.1 0.8 copy-start.5
  62.3 0.8 copy-start.6
  63.1 0.8 copy-start.7

commit v16 on v15

--- a/solution.py
+++ b/solution.py
@@ -21,7 +21,7 @@
     return jnp.where((index >= 0)[..., None, None], picked, jnp.zeros_like(picked))
 
 
-GROUP = 64
+GROUP = 96
 
 
 def stop_kernel(stop, first, last, stack_ref, map_ref, n_ref, send_ref, left_ref, right_ref, *refs):

time: 105 us -> 105 us (level)
  Pallas kernels: 37.3 us -> 40.1 us
  waiting for transfers between devices: 5.91 us -> 3.99 us
  blocking collectives: 30.6 us -> 28.8 us
    pallas_call x4, Pallas kernels: 37.3 us -> 40.1 us  [run_stop(): pl.pallas_call(functools.partial(stop_kernel, stop, first, last), grid_sp...]
    ppermute x9, waiting for transfers between devices: 4.39 us -> 2.47 us  [passed_along(): return lax.ppermute(value, axis, pairs)]
    all_to_all x1, blocking collectives: 30.6 us -> 28.8 us  [on_device(): lax.all_to_all(outgoing[None, None], ('row', 'col'), split_axis=2, concat...]
  transfers between devices with their start and end apart: 10 -> 10, of which waited for: 3 -> 3; matrix products, arithmetic and copies ran while one was open for 3% -> 3% of each run, Pallas kernels for 27% -> 29%
where the time goes in v16:
time: 105 us; the launch traced here: 104 us
  Pallas kernels  40.1 us (38%)
  blocking collectives  28.8 us (27%)
  starting transfers between devices  21.2 us (20%)
  local copies, waits for them, and re-layouts  7.09 us (7%)
  waiting for transfers between devices  3.99 us (4%)
  other arithmetic  2.61 us (2%)
    pallas_call x4, Pallas kernels, run_stop(): pl.pallas_call(functools.partial(stop_kernel, stop, first, last), grid_sp...  40.1 us
    all_to_all x1, blocking collectives, on_device(): lax.all_to_all(outgoing[None, None], ('row', 'col'), split_axis=2, concat...  28.8 us
    ppermute x9, starting transfers between devices, passed_along(): return lax.ppermute(value, axis, pairs)  15.7 us
    all_to_all x1, starting transfers between devices, on_device(): lax.all_to_all(right_out, 'row', split_axis=0, concat_axis=0, tiled=True)  5.53 us
    unnamed x28, local copies, waits for them, and re-layouts  5.36 us
    ppermute x9, waiting for transfers between devices, passed_along(): return lax.ppermute(value, axis, pairs)  2.47 us
  transfers between devices with their start and end apart: 10, of which 3 were waited for; matrix products, arithmetic and copies ran while one was open for 3% of the time, Pallas kernels for 29%

profile of v16, /device:TPU:1, one launch (start us, length us, event | category | flops | bytes accessed | tf_op | source)
XLA Modules:
  0.0 104.0 jit_solution(11217470372495405610)
XLA Ops:
  0.0 0.7 copy-done.11
  0.8 0.2 copy-done
  1.1 0.6 gather_fusion
  1.7 0.1 select_select_fusion.1
  1.9 2.2 %collective-permute-start = (bf16[4,128,128]{2,1,0:T(8,128)(2,1)S(1)}, bf16[4,128,128]{2,1,0:T(8,128)(2,1)S(1)}, u32[]{:S(2)}, u32[]{:S(2)}) collective-permute-start(bf16[4,128,128]{2,1,0:T(8,128)(2,1)S(1)} %get-tuple-element.32), channel_id=1, source_target_pairs={{0,1},{1,2},{2,3},{3,0},{4,5},{5,6},{6,7},{7,4},{8,9},{9,10},{10,1... | collective-permute-start | bytes 393224 | tf_op jit(solution)/shard_map/ppermute | solution.py:16
  4.1 2.3 %collective-permute-start.1 = (bf16[4,128,128]{2,1,0:T(8,128)(2,1)S(1)}, bf16[4,128,128]{2,1,0:T(8,128)(2,1)S(1)}, u32[]{:S(2)}, u32[]{:S(2)}) collective-permute-start(bf16[4,128,128]{2,1,0:T(8,128)(2,1)S(1)} %get-tuple-element.31), channel_id=1, source_target_pairs={{0,2},{1,3},{2,0},{3,1},{4,6},{5,7},{6,4},{7,5},{8,10},{9,11},{10,... | collective-permute-start | bytes 393224 | tf_op jit(solution)/shard_map/ppermute | solution.py:16
  6.4 1.1 %collective-permute-start.2 = (bf16[4,128,128]{2,1,0:T(8,128)(2,1)S(1)}, bf16[4,128,128]{2,1,0:T(8,128)(2,1)S(1)}, u32[]{:S(2)}, u32[]{:S(2)}) collective-permute-start(bf16[4,128,128]{2,1,0:T(8,128)(2,1)S(1)} %get-tuple-element.30), channel_id=1, source_target_pairs={{0,3},{1,0},{2,1},{3,2},{4,7},{5,4},{6,5},{7,6},{8,11},{9,8},{10,9... | collective-permute-start | bytes 393224 | tf_op jit(solution)/shard_map/ppermute | solution.py:16
  7.5 0.1 copy.18
  7.9 0.6 gather_fusion.1
  8.6 0.9 select_select_fusion
  9.5 5.5 %all-to-all-start = ((bf16[8,2,128,128]{3,2,1,0:T(8,128)(2,1)}), bf16[8,2,128,128]{3,2,1,0:T(8,128)(2,1)}, u32[]{:S(2)}, u32[]{:S(2)}) async-start(bf16[8,2,128,128]{3,2,1,0:T(8,128)(2,1)} %select_select_fusion), calls=%async_computation | async-start | bytes 1048576 | tf_op jit(solution)/shard_map/all_to_all | solution.py:122
  15.0 0.7 collective-permute-done.1
  15.8 3.2 %collective-permute-start.3 = (bf16[16,128,128]{2,1,0:T(8,128)(2,1)S(1)}, bf16[16,128,128]{2,1,0:T(8,128)(2,1)S(1)}, u32[]{:S(2)}, u32[]{:S(2)}) collective-permute-start(bf16[16,128,128]{2,1,0:T(8,128)(2,1)S(1)} %pad_maximum_fusion.left_ref), channel_id=1, source_target_pairs={{0,3},{1,0},{2,1},{3,2},{4,7},{5,4},{6,5},{7,6},{8,11},{9,8},{10,9... | collective-permute-start | bytes 1572872 | tf_op jit(solution)/shard_map/ppermute | solution.py:16
  19.0 0.7 fusion.n_ref
  19.7 0.7 fusion.2.map_ref
  20.4 1.5 %all-to-all-done = bf16[8,2,128,128]{3,2,1,0:T(8,128)(2,1)} async-done(((bf16[8,2,128,128]{3,2,1,0:T(8,128)(2,1)}), bf16[8,2,128,128]{3,2,1,0:T(8,128)(2,1)}, u32[]{:S(2)}, u32[]{:S(2)}) %all-to-all-start) | async-done | bytes 524320 | tf_op jit(solution)/shard_map/all_to_all | solution.py:122
  21.9 3.0 %collective-permute-start.5 = (bf16[16,128,128]{2,1,0:T(8,128)(2,1)}, bf16[16,128,128]{2,1,0:T(8,128)(2,1)S(1)}, u32[]{:S(2)}, u32[]{:S(2)}) collective-permute-start(bf16[16,128,128]{2,1,0:T(8,128)(2,1)} %bitcast.14.right_ref), channel_id=1, source_target_pairs={{0,28},{4,0},{8,4},{12,8},{16,12},{20,16},{24,20},{28,24},{1,29},{... | collective-permute-start | bytes 1572872 | tf_op jit(solution)/shard_map/ppermute | solution.py:16
  24.9 9.3 %shard_map.64.refs_0_ = f32[16,128,128]{2,1,0:T(8,128)} custom-call(s32[4,3,384]{2,1,0:T(4,128)} %bitcast.37, s32[4,16]{1,0:T(4,128)} %fusion.2.map_ref, s32[4]{0:T(128)} %fusion.n_ref, s32[32]{0:T(128)} %bitcast.42, bf16[16,128,128]{2,1,0:T(8,128)(2,1)} %copy-done.1, bf16[16,128,128]{2,1,0:T(8,128)(2,1)} %bitcast.14.right_ref), custom_call_target="tpu_custom_call" | custom-call | tf_op jit(solution)/shard_map/pallas_call | solution.py:94
  34.2 0.6 collective-permute-start.7
  34.8 0.2 copy-done.3
  35.0 0.8 copy-done.8
  35.8 10.2 %shard_map.65.refs_0_ = f32[16,128,128]{2,1,0:T(8,128)} custom-call(s32[4,3,384]{2,1,0:T(4,128)} %bitcast.38, s32[4,16]{1,0:T(4,128)} %fusion.2.map_ref, s32[4]{0:T(128)} %fusion.n_ref, s32[32]{0:T(128)} %bitcast.43, bf16[16,128,128]{2,1,0:T(8,128)(2,1)} %copy-done.3, bf16[16,128,128]{2,1,0:T(8,128)(2,1)} %copy-done.8, ...), custom_call_target="tpu_custom_call", output_to_operand_aliasing={{}: (6, {})} | custom-call | tf_op jit(solution)/shard_map/pallas_call | solution.py:94
  46.0 1.8 %collective-permute-done.4.left_ref = bf16[16,128,128]{2,1,0:T(8,128)(2,1)S(1)} collective-permute-done((bf16[16,128,128]{2,1,0:T(8,128)(2,1)S(1)}, bf16[16,128,128]{2,1,0:T(8,128)(2,1)S(1)}, u32[]{:S(2)}, u32[]{:S(2)}) %collective-permute-start.4) | collective-permute-done | bytes 524320 | tf_op jit(solution)/shard_map/ppermute | solution.py:16
  47.8 0.8 collective-permute-start.6
  48.6 2.5 %collective-permute-start.8 = (bf16[16,128,128]{2,1,0:T(8,128)(2,1)}, bf16[16,128,128]{2,1,0:T(8,128)(2,1)S(1)}, u32[]{:S(2)}, u32[]{:S(2)}) collective-permute-start(bf16[16,128,128]{2,1,0:T(8,128)(2,1)} %bitcast.14.right_ref), channel_id=1, source_target_pairs={{0,20},{4,24},{8,28},{12,0},{16,4},{20,8},{24,12},{28,16},{1,21},{... | collective-permute-start | bytes 1572872 | tf_op jit(solution)/shard_map/ppermute | solution.py:16
  51.1 0.8 copy-done.5
  51.9 10.2 %shard_map.66.refs_0_ = f32[16,128,128]{2,1,0:T(8,128)} custom-call(s32[4,3,384]{2,1,0:T(4,128)} %bitcast.39, s32[4,16]{1,0:T(4,128)} %fusion.2.map_ref, s32[4]{0:T(128)} %fusion.n_ref, s32[32]{0:T(128)} %bitcast.44, bf16[16,128,128]{2,1,0:T(8,128)(2,1)} %copy-done.4, bf16[16,128,128]{2,1,0:T(8,128)(2,1)} %copy-done.5, ...), custom_call_target="tpu_custom_call", output_to_operand_aliasing={{}: (6, {})} | custom-call | tf_op jit(solution)/shard_map/pallas_call | solution.py:94
  62.1 0.8 copy-done.6
  62.9 0.8 copy-done.7
  63.7 10.4 %shard_map.67 = bf16[32,128,128]{2,1,0:T(8,128)(2,1)} custom-call(s32[4,3,384]{2,1,0:T(4,128)} %bitcast.40, s32[4,16]{1,0:T(4,128)} %fusion.2.map_ref, s32[4]{0:T(128)} %fusion.n_ref, s32[32]{0:T(128)} %bitcast.45, bf16[16,128,128]{2,1,0:T(8,128)(2,1)} %copy-done.6, bf16[16,128,128]{2,1,0:T(8,128)(2,1)} %copy-done.7, f32[16,128,128]{2,1,0:T(8,128)} %shard_map.66.refs_0_), custom_call_target="tpu_custom_call" | custom-call | tf_op jit(solution)/shard_map/pallas_call | solution.py:94
  74.1 28.8 %all_to_all.10 = bf16[1,1,32,128,128]{4,3,1,0,2:T(8,128)(2,1)S(1)} all-to-all(bf16[1,1,32,128,128]{4,3,1,0,2:T(8,128)(2,1)} %bitcast.32), channel_id=1, replica_groups=mesh['row'=8,'col'=4] {'row','col'}, dimensions={2} | all-to-all | bytes 2097152 | tf_op jit(solution)/shard_map/all_to_all | solution.py:136
  103.0 1.0 copy.28
  (42 shorter events, 0.6 us)
Async XLA Ops:
  0.0 1.1 %copy-start = (bf16[1,1,16,128,128]{4,3,2,1,0:T(8,128)(2,1)S(1)}, bf16[1,1,16,128,128]{4,3,2,1,0:T(8,128)(2,1)}, u32[]{:S(2)}) copy-start(bf16[1,1,16,128,128]{4,3,2,1,0:T(8,128)(2,1)} %param.8) | copy-start | bytes 1572868
  0.0 0.7 copy-start.11
  1.9 6.0 %copy-start.9 = (bf16[1,1,16,128,128]{4,3,2,1,0:T(8,128)(2,1)S(1)}, bf16[1,1,16,128,128]{4,3,2,1,0:T(8,128)(2,1)}, u32[]{:S(2)}) copy-start(bf16[1,1,16,128,128]{4,3,2,1,0:T(8,128)(2,1)} %param.9) | copy-start | bytes 1572868
  1.9 13.1 %collective-permute-start = (bf16[4,128,128]{2,1,0:T(8,128)(2,1)S(1)}, bf16[4,128,128]{2,1,0:T(8,128)(2,1)S(1)}, u32[]{:S(2)}, u32[]{:S(2)}) collective-permute-start(bf16[4,128,128]{2,1,0:T(8,128)(2,1)S(1)} %get-tuple-element.32), channel_id=1, source_target_pairs={{0,1},{1,2},{2,3},{3,0},{4,5},{5,6},{6,7},{7,4},{8,9},{9,10},{10,1... | collective-permute-start | bytes 393224 | tf_op jit(solution)/shard_map/ppermute | solution.py:16
  4.1 3.4 %copy-start.12 = (s32[1,1,8,2]{2,3,1,0:T(2,128)S(1)}, s32[1,1,8,2]{2,3,1,0:T(2,128)}, u32[]{:S(2)}) copy-start(s32[1,1,8,2]{2,3,1,0:T(2,128)} %param.11) | copy-start | bytes 196
  4.1 11.6 %collective-permute-start.1 = (bf16[4,128,128]{2,1,0:T(8,128)(2,1)S(1)}, bf16[4,128,128]{2,1,0:T(8,128)(2,1)S(1)}, u32[]{:S(2)}, u32[]{:S(2)}) collective-permute-start(bf16[4,128,128]{2,1,0:T(8,128)(2,1)S(1)} %get-tuple-element.31), channel_id=1, source_target_pairs={{0,2},{1,3},{2,0},{3,1},{4,6},{5,7},{6,4},{7,5},{8,10},{9,11},{10,... | collective-permute-start | bytes 393224 | tf_op jit(solution)/shard_map/ppermute | solution.py:16
  6.4 9.3 %collective-permute-start.2 = (bf16[4,128,128]{2,1,0:T(8,128)(2,1)S(1)}, bf16[4,128,128]{2,1,0:T(8,128)(2,1)S(1)}, u32[]{:S(2)}, u32[]{:S(2)}) collective-permute-start(bf16[4,128,128]{2,1,0:T(8,128)(2,1)S(1)} %get-tuple-element.30), channel_id=1, source_target_pairs={{0,3},{1,0},{2,1},{3,2},{4,7},{5,4},{6,5},{7,6},{8,11},{9,8},{10,9... | collective-permute-start | bytes 393224 | tf_op jit(solution)/shard_map/ppermute | solution.py:16
  9.5 12.4 %all-to-all-start = ((bf16[8,2,128,128]{3,2,1,0:T(8,128)(2,1)}), bf16[8,2,128,128]{3,2,1,0:T(8,128)(2,1)}, u32[]{:S(2)}, u32[]{:S(2)}) async-start(bf16[8,2,128,128]{3,2,1,0:T(8,128)(2,1)} %select_select_fusion), calls=%async_computation | async-start | bytes 1048576 | tf_op jit(solution)/shard_map/all_to_all | solution.py:122
  15.7 3.3 %copy-start.10 = (s32[1,1,4,3,384]{4,2,3,1,0:T(4,128)S(1)}, s32[1,1,4,3,384]{4,2,3,1,0:T(4,128)}, u32[]{:S(2)}) copy-start(s32[1,1,4,3,384]{4,2,3,1,0:T(4,128)} %param.12) | copy-start | bytes 55300
  15.8 9.1 %copy-start.1 = (bf16[16,128,128]{2,1,0:T(8,128)(2,1)}, bf16[16,128,128]{2,1,0:T(8,128)(2,1)S(1)}, u32[]{:S(2)}) copy-start(bf16[16,128,128]{2,1,0:T(8,128)(2,1)S(1)} %pad_maximum_fusion.left_ref) | copy-start | bytes 1572868
  15.8 18.4 %collective-permute-start.3 = (bf16[16,128,128]{2,1,0:T(8,128)(2,1)S(1)}, bf16[16,128,128]{2,1,0:T(8,128)(2,1)S(1)}, u32[]{:S(2)}, u32[]{:S(2)}) collective-permute-start(bf16[16,128,128]{2,1,0:T(8,128)(2,1)S(1)} %pad_maximum_fusion.left_ref), channel_id=1, source_target_pairs={{0,3},{1,0},{2,1},{3,2},{4,7},{5,4},{6,5},{7,6},{8,11},{9,8},{10,9... | collective-permute-start | bytes 1572872 | tf_op jit(solution)/shard_map/ppermute | solution.py:16
  19.0 5.9 %copy-start.2 = (s32[1,1,4,3,384]{4,3,2,1,0:T(4,128)}, s32[1,1,4,3,384]{4,3,2,1,0:T(4,128)S(1)}, u32[]{:S(2)}) copy-start(s32[1,1,4,3,384]{4,3,2,1,0:T(4,128)S(1)} %copy.24) | copy-start | bytes 55300
  21.9 12.9 %collective-permute-start.5 = (bf16[16,128,128]{2,1,0:T(8,128)(2,1)}, bf16[16,128,128]{2,1,0:T(8,128)(2,1)S(1)}, u32[]{:S(2)}, u32[]{:S(2)}) collective-permute-start(bf16[16,128,128]{2,1,0:T(8,128)(2,1)} %bitcast.14.right_ref), channel_id=1, source_target_pairs={{0,28},{4,0},{8,4},{12,8},{16,12},{20,16},{24,20},{28,24},{1,29},{... | collective-permute-start | bytes 1572872 | tf_op jit(solution)/shard_map/ppermute | solution.py:16
  34.2 0.8 copy-start.3
  34.2 13.5 %collective-permute-start.4 = (bf16[16,128,128]{2,1,0:T(8,128)(2,1)S(1)}, bf16[16,128,128]{2,1,0:T(8,128)(2,1)S(1)}, u32[]{:S(2)}, u32[]{:S(2)}) collective-permute-start(bf16[16,128,128]{2,1,0:T(8,128)(2,1)S(1)} %collective-permute-done.3.left_ref), channel_id=1, source_target_pairs={{0,3},{1,0},{2,1},{3,2},{4,7},{5,4},{6,5},{7,6},{8,11},{9,8},{10,9... | collective-permute-start | bytes 1572872 | tf_op jit(solution)/shard_map/ppermute | solution.py:16
  34.2 16.9 %collective-permute-start.7 = (bf16[16,128,128]{2,1,0:T(8,128)(2,1)}, bf16[16,128,128]{2,1,0:T(8,128)(2,1)S(1)}, u32[]{:S(2)}, u32[]{:S(2)}) collective-permute-start(bf16[16,128,128]{2,1,0:T(8,128)(2,1)} %bitcast.14.right_ref), channel_id=1, source_target_pairs={{0,24},{4,28},{8,0},{12,4},{16,8},{20,12},{24,16},{28,20},{1,25},{... | collective-permute-start | bytes 1572872 | tf_op jit(solution)/shard_map/ppermute | solution.py:16
  35.0 0.8 copy-start.8
  47.8 3.4 %copy-start.4 = (bf16[16,128,128]{2,1,0:T(8,128)(2,1)}, bf16[16,128,128]{2,1,0:T(8,128)(2,1)S(1)}, u32[]{:S(2)}) copy-start(bf16[16,128,128]{2,1,0:T(8,128)(2,1)S(1)} %collective-permute-done.4.left_ref) | copy-start | bytes 1572868
  47.8 14.3 %collective-permute-start.6 = (bf16[16,128,128]{2,1,0:T(8,128)(2,1)S(1)}, bf16[16,128,128]{2,1,0:T(8,128)(2,1)S(1)}, u32[]{:S(2)}, u32[]{:S(2)}) collective-permute-start(bf16[16,128,128]{2,1,0:T(8,128)(2,1)S(1)} %collective-permute-done.4.left_ref), channel_id=1, source_target_pairs={{0,3},{1,0},{2,1},{3,2},{4,7},{5,4},{6,5},{7,6},{8,11},{9,8},{10,9... | collective-permute-start | bytes 1572872 | tf_op jit(solution)/shard_map/ppermute | solution.py:16
  48.6 13.6 %collective-permute-start.8 = (bf16[16,128,128]{2,1,0:T(8,128)(2,1)}, bf16[16,128,128]{2,1,0:T(8,128)(2,1)S(1)}, u32[]{:S(2)}, u32[]{:S(2)}) collective-permute-start(bf16[16,128,128]{2,1,0:T(8,128)(2,1)} %bitcast.14.right_ref), channel_id=1, source_target_pairs={{0,20},{4,24},{8,28},{12,0},{16,4},{20,8},{24,12},{28,16},{1,21},{... | collective-permute-start | bytes 1572872 | tf_op jit(solution)/shard_map/ppermute | solution.py:16
  51.1 0.8 copy-start.5
  62.1 0.8 copy-start.6
  62.9 0.8 copy-start.7

commit v17 on v16

--- a/solution.py
+++ b/solution.py
@@ -21,7 +21,7 @@
     return jnp.where((index >= 0)[..., None, None], picked, jnp.zeros_like(picked))
 
 
-GROUP = 96
+GROUP = 48
 
 
 def stop_kernel(stop, first, last, stack_ref, map_ref, n_ref, send_ref, left_ref, right_ref, *refs):

time: 105 us -> 106 us (level); the launches traced: 104 us -> 104 us
  Pallas kernels: 40.1 us -> 37.1 us
  waiting for transfers between devices: 3.99 us -> 5.75 us
    pallas_call x4, Pallas kernels: 40.1 us -> 37.1 us  [run_stop(): pl.pallas_call(functools.partial(stop_kernel, stop, first, last), grid_sp...]
    ppermute x9, waiting for transfers between devices: 2.47 us -> 4.23 us  [passed_along(): return lax.ppermute(value, axis, pairs)]
  transfers between devices with their start and end apart: 10 -> 10, of which waited for: 3 -> 3; matrix products, arithmetic and copies ran while one was open for 3% -> 3% of each run, Pallas kernels for 29% -> 27%
where the time goes in v17:
time: 106 us; the launch traced here: 104 us
  Pallas kernels  37.1 us (35%)
  blocking collectives  29.8 us (28%)
  starting transfers between devices  21 us (20%)
  local copies, waits for them, and re-layouts  7.45 us (7%)
  waiting for transfers between devices  5.75 us (5%)
  other arithmetic  2.61 us (2%)
    pallas_call x4, Pallas kernels, run_stop(): pl.pallas_call(functools.partial(stop_kernel, stop, first, last), grid_sp...  37.1 us
    all_to_all x1, blocking collectives, on_device(): lax.all_to_all(outgoing[None, None], ('row', 'col'), split_axis=2, concat...  29.8 us
    ppermute x9, starting transfers between devices, passed_along(): return lax.ppermute(value, axis, pairs)  15.4 us
    unnamed x28, local copies, waits for them, and re-layouts  5.72 us
    all_to_all x1, starting transfers between devices, on_device(): lax.all_to_all(right_out, 'row', split_axis=0, concat_axis=0, tiled=True)  5.53 us
    ppermute x9, waiting for transfers between devices, passed_along(): return lax.ppermute(value, axis, pairs)  4.23 us
  transfers between devices with their start and end apart: 10, of which 3 were waited for; matrix products, arithmetic and copies ran while one was open for 3% of the time, Pallas kernels for 27%

profile of v17, /device:TPU:1, one launch (start us, length us, event | category | flops | bytes accessed | tf_op | source)
XLA Modules:
  0.0 103.8 jit_solution(12053492274572214868)
XLA Ops:
  0.0 0.7 copy-done.11
  0.8 0.2 copy-done
  1.1 0.6 gather_fusion
  1.7 0.1 select_select_fusion.1
  1.9 2.2 %collective-permute-start = (bf16[4,128,128]{2,1,0:T(8,128)(2,1)S(1)}, bf16[4,128,128]{2,1,0:T(8,128)(2,1)S(1)}, u32[]{:S(2)}, u32[]{:S(2)}) collective-permute-start(bf16[4,128,128]{2,1,0:T(8,128)(2,1)S(1)} %get-tuple-element.32), channel_id=1, source_target_pairs={{0,1},{1,2},{2,3},{3,0},{4,5},{5,6},{6,7},{7,4},{8,9},{9,10},{10,1... | collective-permute-start | bytes 393224 | tf_op jit(solution)/shard_map/ppermute | solution.py:16
  4.1 2.3 %collective-permute-start.1 = (bf16[4,128,128]{2,1,0:T(8,128)(2,1)S(1)}, bf16[4,128,128]{2,1,0:T(8,128)(2,1)S(1)}, u32[]{:S(2)}, u32[]{:S(2)}) collective-permute-start(bf16[4,128,128]{2,1,0:T(8,128)(2,1)S(1)} %get-tuple-element.31), channel_id=1, source_target_pairs={{0,2},{1,3},{2,0},{3,1},{4,6},{5,7},{6,4},{7,5},{8,10},{9,11},{10,... | collective-permute-start | bytes 393224 | tf_op jit(solution)/shard_map/ppermute | solution.py:16
  6.4 1.1 %collective-permute-start.2 = (bf16[4,128,128]{2,1,0:T(8,128)(2,1)S(1)}, bf16[4,128,128]{2,1,0:T(8,128)(2,1)S(1)}, u32[]{:S(2)}, u32[]{:S(2)}) collective-permute-start(bf16[4,128,128]{2,1,0:T(8,128)(2,1)S(1)} %get-tuple-element.30), channel_id=1, source_target_pairs={{0,3},{1,0},{2,1},{3,2},{4,7},{5,4},{6,5},{7,6},{8,11},{9,8},{10,9... | collective-permute-start | bytes 393224 | tf_op jit(solution)/shard_map/ppermute | solution.py:16
  7.5 0.1 copy.18
  7.9 0.6 gather_fusion.1
  8.6 0.9 select_select_fusion
  9.5 5.5 %all-to-all-start = ((bf16[8,2,128,128]{3,2,1,0:T(8,128)(2,1)}), bf16[8,2,128,128]{3,2,1,0:T(8,128)(2,1)}, u32[]{:S(2)}, u32[]{:S(2)}) async-start(bf16[8,2,128,128]{3,2,1,0:T(8,128)(2,1)} %select_select_fusion), calls=%async_computation | async-start | bytes 1048576 | tf_op jit(solution)/shard_map/all_to_all | solution.py:122
  15.0 0.7 collective-permute-done.1
  15.8 3.2 %collective-permute-start.3 = (bf16[16,128,128]{2,1,0:T(8,128)(2,1)S(1)}, bf16[16,128,128]{2,1,0:T(8,128)(2,1)S(1)}, u32[]{:S(2)}, u32[]{:S(2)}) collective-permute-start(bf16[16,128,128]{2,1,0:T(8,128)(2,1)S(1)} %pad_maximum_fusion.left_ref), channel_id=1, source_target_pairs={{0,3},{1,0},{2,1},{3,2},{4,7},{5,4},{6,5},{7,6},{8,11},{9,8},{10,9... | collective-permute-start | bytes 1572872 | tf_op jit(solution)/shard_map/ppermute | solution.py:16
  19.0 0.7 fusion.n_ref
  19.7 0.7 fusion.2.map_ref
  20.4 1.5 %all-to-all-done = bf16[8,2,128,128]{3,2,1,0:T(8,128)(2,1)} async-done(((bf16[8,2,128,128]{3,2,1,0:T(8,128)(2,1)}), bf16[8,2,128,128]{3,2,1,0:T(8,128)(2,1)}, u32[]{:S(2)}, u32[]{:S(2)}) %all-to-all-start) | async-done | bytes 524320 | tf_op jit(solution)/shard_map/all_to_all | solution.py:122
  21.9 3.0 %collective-permute-start.5 = (bf16[16,128,128]{2,1,0:T(8,128)(2,1)}, bf16[16,128,128]{2,1,0:T(8,128)(2,1)S(1)}, u32[]{:S(2)}, u32[]{:S(2)}) collective-permute-start(bf16[16,128,128]{2,1,0:T(8,128)(2,1)} %bitcast.14.right_ref), channel_id=1, source_target_pairs={{0,28},{4,0},{8,4},{12,8},{16,12},{20,16},{24,20},{28,24},{1,29},{... | collective-permute-start | bytes 1572872 | tf_op jit(solution)/shard_map/ppermute | solution.py:16
  24.9 9.6 %shard_map.64.refs_0_ = f32[16,128,128]{2,1,0:T(8,128)} custom-call(s32[4,3,384]{2,1,0:T(4,128)} %bitcast.37, s32[4,16]{1,0:T(4,128)} %fusion.2.map_ref, s32[4]{0:T(128)} %fusion.n_ref, s32[32]{0:T(128)} %bitcast.42, bf16[16,128,128]{2,1,0:T(8,128)(2,1)} %copy-done.1, bf16[16,128,128]{2,1,0:T(8,128)(2,1)} %bitcast.14.right_ref), custom_call_target="tpu_custom_call" | custom-call | tf_op jit(solution)/shard_map/pallas_call | solution.py:94
  34.6 0.2 collective-permute-start.7
  34.8 0.6 copy-done.3
  35.4 0.8 copy-done.8
  36.2 7.9 %shard_map.65.refs_0_ = f32[16,128,128]{2,1,0:T(8,128)} custom-call(s32[4,3,384]{2,1,0:T(4,128)} %bitcast.38, s32[4,16]{1,0:T(4,128)} %fusion.2.map_ref, s32[4]{0:T(128)} %fusion.n_ref, s32[32]{0:T(128)} %bitcast.43, bf16[16,128,128]{2,1,0:T(8,128)(2,1)} %copy-done.3, bf16[16,128,128]{2,1,0:T(8,128)(2,1)} %copy-done.8, ...), custom_call_target="tpu_custom_call", output_to_operand_aliasing={{}: (6, {})} | custom-call | tf_op jit(solution)/shard_map/pallas_call | solution.py:94
  44.1 3.5 %collective-permute-done.4.left_ref = bf16[16,128,128]{2,1,0:T(8,128)(2,1)S(1)} collective-permute-done((bf16[16,128,128]{2,1,0:T(8,128)(2,1)S(1)}, bf16[16,128,128]{2,1,0:T(8,128)(2,1)S(1)}, u32[]{:S(2)}, u32[]{:S(2)}) %collective-permute-start.4) | collective-permute-done | bytes 524320 | tf_op jit(solution)/shard_map/ppermute | solution.py:16
  47.6 1.7 %collective-permute-start.6 = (bf16[16,128,128]{2,1,0:T(8,128)(2,1)S(1)}, bf16[16,128,128]{2,1,0:T(8,128)(2,1)S(1)}, u32[]{:S(2)}, u32[]{:S(2)}) collective-permute-start(bf16[16,128,128]{2,1,0:T(8,128)(2,1)S(1)} %collective-permute-done.4.left_ref), channel_id=1, source_target_pairs={{0,3},{1,0},{2,1},{3,2},{4,7},{5,4},{6,5},{7,6},{8,11},{9,8},{10,9... | collective-permute-start | bytes 1572872 | tf_op jit(solution)/shard_map/ppermute | solution.py:16
  49.3 1.8 %collective-permute-start.8 = (bf16[16,128,128]{2,1,0:T(8,128)(2,1)}, bf16[16,128,128]{2,1,0:T(8,128)(2,1)S(1)}, u32[]{:S(2)}, u32[]{:S(2)}) collective-permute-start(bf16[16,128,128]{2,1,0:T(8,128)(2,1)} %bitcast.14.right_ref), channel_id=1, source_target_pairs={{0,20},{4,24},{8,28},{12,0},{16,4},{20,8},{24,12},{28,16},{1,21},{... | collective-permute-start | bytes 1572872 | tf_op jit(solution)/shard_map/ppermute | solution.py:16
  51.1 0.8 copy-done.5
  51.9 10.5 %shard_map.66.refs_0_ = f32[16,128,128]{2,1,0:T(8,128)} custom-call(s32[4,3,384]{2,1,0:T(4,128)} %bitcast.39, s32[4,16]{1,0:T(4,128)} %fusion.2.map_ref, s32[4]{0:T(128)} %fusion.n_ref, s32[32]{0:T(128)} %bitcast.44, bf16[16,128,128]{2,1,0:T(8,128)(2,1)} %copy-done.4, bf16[16,128,128]{2,1,0:T(8,128)(2,1)} %copy-done.5, ...), custom_call_target="tpu_custom_call", output_to_operand_aliasing={{}: (6, {})} | custom-call | tf_op jit(solution)/shard_map/pallas_call | solution.py:94
  62.4 0.8 copy-done.6
  63.2 0.8 copy-done.7
  64.0 9.0 %shard_map.67 = bf16[32,128,128]{2,1,0:T(8,128)(2,1)} custom-call(s32[4,3,384]{2,1,0:T(4,128)} %bitcast.40, s32[4,16]{1,0:T(4,128)} %fusion.2.map_ref, s32[4]{0:T(128)} %fusion.n_ref, s32[32]{0:T(128)} %bitcast.45, bf16[16,128,128]{2,1,0:T(8,128)(2,1)} %copy-done.6, bf16[16,128,128]{2,1,0:T(8,128)(2,1)} %copy-done.7, f32[16,128,128]{2,1,0:T(8,128)} %shard_map.66.refs_0_), custom_call_target="tpu_custom_call" | custom-call | tf_op jit(solution)/shard_map/pallas_call | solution.py:94
  73.0 29.8 %all_to_all.10 = bf16[1,1,32,128,128]{4,3,1,0,2:T(8,128)(2,1)S(1)} all-to-all(bf16[1,1,32,128,128]{4,3,1,0,2:T(8,128)(2,1)} %bitcast.32), channel_id=1, replica_groups=mesh['row'=8,'col'=4] {'row','col'}, dimensions={2} | all-to-all | bytes 2097152 | tf_op jit(solution)/shard_map/all_to_all | solution.py:136
  102.8 1.0 copy.28
  (42 shorter events, 0.6 us)
Async XLA Ops:
  0.0 1.1 %copy-start = (bf16[1,1,16,128,128]{4,3,2,1,0:T(8,128)(2,1)S(1)}, bf16[1,1,16,128,128]{4,3,2,1,0:T(8,128)(2,1)}, u32[]{:S(2)}) copy-start(bf16[1,1,16,128,128]{4,3,2,1,0:T(8,128)(2,1)} %param.8) | copy-start | bytes 1572868
  0.0 0.7 copy-start.11
  1.9 6.0 %copy-start.9 = (bf16[1,1,16,128,128]{4,3,2,1,0:T(8,128)(2,1)S(1)}, bf16[1,1,16,128,128]{4,3,2,1,0:T(8,128)(2,1)}, u32[]{:S(2)}) copy-start(bf16[1,1,16,128,128]{4,3,2,1,0:T(8,128)(2,1)} %param.9) | copy-start | bytes 1572868
  1.9 13.1 %collective-permute-start = (bf16[4,128,128]{2,1,0:T(8,128)(2,1)S(1)}, bf16[4,128,128]{2,1,0:T(8,128)(2,1)S(1)}, u32[]{:S(2)}, u32[]{:S(2)}) collective-permute-start(bf16[4,128,128]{2,1,0:T(8,128)(2,1)S(1)} %get-tuple-element.32), channel_id=1, source_target_pairs={{0,1},{1,2},{2,3},{3,0},{4,5},{5,6},{6,7},{7,4},{8,9},{9,10},{10,1... | collective-permute-start | bytes 393224 | tf_op jit(solution)/shard_map/ppermute | solution.py:16
  4.1 3.4 %copy-start.12 = (s32[1,1,8,2]{2,3,1,0:T(2,128)S(1)}, s32[1,1,8,2]{2,3,1,0:T(2,128)}, u32[]{:S(2)}) copy-start(s32[1,1,8,2]{2,3,1,0:T(2,128)} %param.11) | copy-start | bytes 196
  4.1 11.6 %collective-permute-start.1 = (bf16[4,128,128]{2,1,0:T(8,128)(2,1)S(1)}, bf16[4,128,128]{2,1,0:T(8,128)(2,1)S(1)}, u32[]{:S(2)}, u32[]{:S(2)}) collective-permute-start(bf16[4,128,128]{2,1,0:T(8,128)(2,1)S(1)} %get-tuple-element.31), channel_id=1, source_target_pairs={{0,2},{1,3},{2,0},{3,1},{4,6},{5,7},{6,4},{7,5},{8,10},{9,11},{10,... | collective-permute-start | bytes 393224 | tf_op jit(solution)/shard_map/ppermute | solution.py:16
  6.4 9.3 %collective-permute-start.2 = (bf16[4,128,128]{2,1,0:T(8,128)(2,1)S(1)}, bf16[4,128,128]{2,1,0:T(8,128)(2,1)S(1)}, u32[]{:S(2)}, u32[]{:S(2)}) collective-permute-start(bf16[4,128,128]{2,1,0:T(8,128)(2,1)S(1)} %get-tuple-element.30), channel_id=1, source_target_pairs={{0,3},{1,0},{2,1},{3,2},{4,7},{5,4},{6,5},{7,6},{8,11},{9,8},{10,9... | collective-permute-start | bytes 393224 | tf_op jit(solution)/shard_map/ppermute | solution.py:16
  9.5 12.4 %all-to-all-start = ((bf16[8,2,128,128]{3,2,1,0:T(8,128)(2,1)}), bf16[8,2,128,128]{3,2,1,0:T(8,128)(2,1)}, u32[]{:S(2)}, u32[]{:S(2)}) async-start(bf16[8,2,128,128]{3,2,1,0:T(8,128)(2,1)} %select_select_fusion), calls=%async_computation | async-start | bytes 1048576 | tf_op jit(solution)/shard_map/all_to_all | solution.py:122
  15.7 3.3 %copy-start.10 = (s32[1,1,4,3,384]{4,2,3,1,0:T(4,128)S(1)}, s32[1,1,4,3,384]{4,2,3,1,0:T(4,128)}, u32[]{:S(2)}) copy-start(s32[1,1,4,3,384]{4,2,3,1,0:T(4,128)} %param.12) | copy-start | bytes 55300
  15.8 9.1 %copy-start.1 = (bf16[16,128,128]{2,1,0:T(8,128)(2,1)}, bf16[16,128,128]{2,1,0:T(8,128)(2,1)S(1)}, u32[]{:S(2)}) copy-start(bf16[16,128,128]{2,1,0:T(8,128)(2,1)S(1)} %pad_maximum_fusion.left_ref) | copy-start | bytes 1572868
  15.8 18.8 %collective-permute-start.3 = (bf16[16,128,128]{2,1,0:T(8,128)(2,1)S(1)}, bf16[16,128,128]{2,1,0:T(8,128)(2,1)S(1)}, u32[]{:S(2)}, u32[]{:S(2)}) collective-permute-start(bf16[16,128,128]{2,1,0:T(8,128)(2,1)S(1)} %pad_maximum_fusion.left_ref), channel_id=1, source_target_pairs={{0,3},{1,0},{2,1},{3,2},{4,7},{5,4},{6,5},{7,6},{8,11},{9,8},{10,9... | collective-permute-start | bytes 1572872 | tf_op jit(solution)/shard_map/ppermute | solution.py:16
  19.0 5.9 %copy-start.2 = (s32[1,1,4,3,384]{4,3,2,1,0:T(4,128)}, s32[1,1,4,3,384]{4,3,2,1,0:T(4,128)S(1)}, u32[]{:S(2)}) copy-start(s32[1,1,4,3,384]{4,3,2,1,0:T(4,128)S(1)} %copy.24) | copy-start | bytes 55300
  21.9 12.9 %collective-permute-start.5 = (bf16[16,128,128]{2,1,0:T(8,128)(2,1)}, bf16[16,128,128]{2,1,0:T(8,128)(2,1)S(1)}, u32[]{:S(2)}, u32[]{:S(2)}) collective-permute-start(bf16[16,128,128]{2,1,0:T(8,128)(2,1)} %bitcast.14.right_ref), channel_id=1, source_target_pairs={{0,28},{4,0},{8,4},{12,8},{16,12},{20,16},{24,20},{28,24},{1,29},{... | collective-permute-start | bytes 1572872 | tf_op jit(solution)/shard_map/ppermute | solution.py:16
  34.6 0.8 copy-start.3
  34.6 13.1 %collective-permute-start.4 = (bf16[16,128,128]{2,1,0:T(8,128)(2,1)S(1)}, bf16[16,128,128]{2,1,0:T(8,128)(2,1)S(1)}, u32[]{:S(2)}, u32[]{:S(2)}) collective-permute-start(bf16[16,128,128]{2,1,0:T(8,128)(2,1)S(1)} %collective-permute-done.3.left_ref), channel_id=1, source_target_pairs={{0,3},{1,0},{2,1},{3,2},{4,7},{5,4},{6,5},{7,6},{8,11},{9,8},{10,9... | collective-permute-start | bytes 1572872 | tf_op jit(solution)/shard_map/ppermute | solution.py:16
  34.6 16.5 %collective-permute-start.7 = (bf16[16,128,128]{2,1,0:T(8,128)(2,1)}, bf16[16,128,128]{2,1,0:T(8,128)(2,1)S(1)}, u32[]{:S(2)}, u32[]{:S(2)}) collective-permute-start(bf16[16,128,128]{2,1,0:T(8,128)(2,1)} %bitcast.14.right_ref), channel_id=1, source_target_pairs={{0,24},{4,28},{8,0},{12,4},{16,8},{20,12},{24,16},{28,20},{1,25},{... | collective-permute-start | bytes 1572872 | tf_op jit(solution)/shard_map/ppermute | solution.py:16
  35.4 0.8 copy-start.8
  47.6 3.5 %copy-start.4 = (bf16[16,128,128]{2,1,0:T(8,128)(2,1)}, bf16[16,128,128]{2,1,0:T(8,128)(2,1)S(1)}, u32[]{:S(2)}) copy-start(bf16[16,128,128]{2,1,0:T(8,128)(2,1)S(1)} %collective-permute-done.4.left_ref) | copy-start | bytes 1572868
  47.6 14.8 %collective-permute-start.6 = (bf16[16,128,128]{2,1,0:T(8,128)(2,1)S(1)}, bf16[16,128,128]{2,1,0:T(8,128)(2,1)S(1)}, u32[]{:S(2)}, u32[]{:S(2)}) collective-permute-start(bf16[16,128,128]{2,1,0:T(8,128)(2,1)S(1)} %collective-permute-done.4.left_ref), channel_id=1, source_target_pairs={{0,3},{1,0},{2,1},{3,2},{4,7},{5,4},{6,5},{7,6},{8,11},{9,8},{10,9... | collective-permute-start | bytes 1572872 | tf_op jit(solution)/shard_map/ppermute | solution.py:16
  49.3 13.1 %collective-permute-start.8 = (bf16[16,128,128]{2,1,0:T(8,128)(2,1)}, bf16[16,128,128]{2,1,0:T(8,128)(2,1)S(1)}, u32[]{:S(2)}, u32[]{:S(2)}) collective-permute-start(bf16[16,128,128]{2,1,0:T(8,128)(2,1)} %bitcast.14.right_ref), channel_id=1, source_target_pairs={{0,20},{4,24},{8,28},{12,0},{16,4},{20,8},{24,12},{28,16},{1,21},{... | collective-permute-start | bytes 1572872 | tf_op jit(solution)/shard_map/ppermute | solution.py:16
  51.1 0.8 copy-start.5
  62.4 0.8 copy-start.6
  63.2 0.8 copy-start.7
